TPU v7x, 32 devices: a whole 2x2x4 slice. The times are simulated.
32 devices in a mesh: groups: 2 (over x), dp: 16 (over z, y, core).
Axes of the slice: x: 2, y: 2, z: 4, core: 2. Of those that a mesh axis runs over, the one named last changes fastest.
Arguments:
- hidden: bfloat16 [12288, 11008], P(('groups', 'dp')), parts along dimension 0, may hold values from -6 to 6
- out_grad: bfloat16 [12288, 4096], P(('groups', 'dp')), parts along dimension 0, may hold values from -0.75 to 0.75
- hidden_basis: bfloat16 [64, 11008], P(None, 'dp'), may hold values from -0.0546875 to 0.0546875
- output_basis: bfloat16 [64, 4096], P(None, 'dp'), may hold values from -0.09375 to 0.09375
- owner_ids: int32 [12288, 1], P(('groups', 'dp')), parts along dimension 0, may hold values from 0 to 15; in each aligned block of 384 rows (0 to 383, 384 to 767, ...) at most 48 rows name the same one
- doc_slot: int32 [12288], P(('groups', 'dp')), parts along dimension 0, may hold values from 0 to 7
Outputs:
- doc_grads: float32 [256, 4096], P(('groups', 'dp')), parts along dimension 0
There are 2 independent parts, one for each index of `groups`. A program takes and returns all parts, laid end to end along the dimension named above; an argument that names none is the same for every part. Nothing has to cross between parts.
Inputs may be any that keep to these rules, and one draw needn't show every extreme that they name: `owner_ids`: among the 384 tokens of one device, at most 48 have the same owner, and some owner gets exactly 48 of them.
All inputs are finite; a program needn't handle non-finite values.
Results may differ from a plain program's by a relative error of at most 0.0042.
Values may be sent and summed in bfloat16 or wider, within the bound.
No kernel may reach another device: no remote copies, remote signals or barrier semaphores. Data moves between devices by JAX's collectives and lax.ppermute only.
A program may use at most 128 MiB of HBM per device.

v0:
```python
import jax
import jax.numpy as jnp
from jax import lax
from jax.sharding import PartitionSpec as P

DOCS_DEV = 8


def folder(token_block, portion):
    return lax.dot_general(
        token_block, portion, (((1,), (1,)), ((), ())), preferred_element_type=jnp.float32
    )


def project_hidden(token_block, hidden_basis):
    summed = folder(token_block, lax.all_gather(hidden_basis, "dp", axis=1, tiled=True))
    return summed.astype(jnp.bfloat16)


def project_output(token_block, output_basis):
    summed = folder(token_block, lax.all_gather(output_basis, "dp", axis=1, tiled=True))
    return summed.astype(jnp.bfloat16)


def send_rows(first, second, labels):
    first_in, second_in, label_in = (
        lax.all_to_all(first, "dp", split_axis=0, concat_axis=0, tiled=True),
        lax.all_to_all(second, "dp", split_axis=0, concat_axis=0, tiled=True),
        lax.all_to_all(labels.astype(jnp.bfloat16), "dp", split_axis=0, concat_axis=0, tiled=True),
    )
    return (first_in, second_in, label_in.astype(jnp.int32))


def local(hidden, out_grad, hidden_basis, output_basis, owner_ids, doc_slot):
    devices = lax.axis_size("dp")
    local_tokens = hidden.shape[0]
    capacity = 2 * local_tokens // devices
    rank_width = hidden_basis.shape[0]
    buffer_len = devices * capacity
    targets = owner_ids[:, 0]
    member = (targets[:, None] == jnp.arange(devices, dtype=jnp.int32)[None, :]).astype(jnp.int32)
    before = jnp.cumsum(member, axis=0) - member
    position = jnp.sum(member * before, axis=1)
    slot_index = targets * capacity + position
    labels = jnp.full((buffer_len,), -1, jnp.int32).at[slot_index].set(doc_slot)
    left_source = project_hidden(hidden, hidden_basis)
    right_source = project_output(out_grad, output_basis)
    left_buffer = jnp.zeros((buffer_len, rank_width), jnp.bfloat16).at[slot_index].set(left_source)
    right_buffer = (
        jnp.zeros((buffer_len, rank_width), jnp.bfloat16).at[slot_index].set(right_source)
    )
    left, right, arrived = send_rows(left_buffer, right_buffer, labels)
    selector = (arrived[:, None] == jnp.arange(DOCS_DEV, dtype=jnp.int32)[None, :]).astype(
        jnp.bfloat16
    )
    weighted = (selector[:, :, None] * left[:, None, :]).reshape(buffer_len, DOCS_DEV * rank_width)
    grads = lax.dot_general(
        weighted, right, (((0,), (0,)), ((), ())), preferred_element_type=jnp.float32
    )
    return grads.reshape(DOCS_DEV, rank_width * rank_width)


def solution(mesh):
    placed = (
        P(("groups", "dp"), None),
        P(("groups", "dp"), None),
        P(None, "dp"),
        P(None, "dp"),
        P(("groups", "dp"), None),
        P(("groups", "dp")),
    )
    return jax.shard_map(
        local, mesh=mesh, in_specs=placed, out_specs=P(("groups", "dp"), None), check_vma=False
    )
```

profile of v0, /device:TPU:0, one launch (start us, length us, event | category | flops | bytes accessed | tf_op | source)
XLA Modules:
  0.0 91.8 jit_solution(4919744085502683929)
XLA Ops:
  6.5 0.7 all-gather.3.cloned.1.call-update
  7.3 0.9 %reduce = s32[384]{0:T(512)S(1)} reduce(s32[384,1]{0,1:T(1,128)} %param.10, s32[]{:T(128)} %constant.3.clone.1), dimensions={1}, to_apply=%param.10.reduce_sub_computation | reduce | bytes 3076 | tf_op args[4]
  8.2 0.9 reduce-window.6
  9.1 0.2 slice_reduce_fusion
  9.4 0.7 fusion.11
  10.1 3.1 %scatter_custom_fusion = s32[768]{0:T(1024)S(1)} fusion(s32[384]{0:T(512)S(1)} %fusion.11, s32[384]{0:T(512)} %param.11, s32[]{:T(128)} %constant.5.clone.1), kind=kCustom, calls=%fused_computation.23 | custom fusion | bytes 3584 | tf_op jit(solution)/shard_map/scatter | solution.py:45
  13.2 0.7 all_to_all.27
  13.9 7.4 %all-to-all-start = ((bf16[16,48,1]{1,2,0:T(2,128)(2,1)}), bf16[16,48,1]{1,2,0:T(2,128)(2,1)S(1)}, u32[]{:S(2)}, u32[]{:S(2)}) async-start(bf16[16,48,1]{1,2,0:T(2,128)(2,1)} %all_to_all.27), calls=%async_computation | async-start | bytes 16384 | tf_op jit(solution)/shard_map/all_to_all | solution.py:29
  21.3 24.1 %all_gather.7 = bf16[64,4096]{1,0:T(8,128)(2,1)S(1)} all-gather(bf16[64,256]{1,0:T(8,128)(2,1)} %param.9), channel_id=1, replica_groups=mesh['groups'=2,'dp'=16] {'dp'}, dimensions={1}, use_global_device_ids=true | all-gather | bytes 557056 | tf_op jit(solution)/shard_map/all_gather | solution.py:21
  45.4 1.1 %convolution_convert_fusion = bf16[384,64]{0,1:T(8,128)(2,1)S(1)} fusion(bf16[384,4096]{1,0:T(8,128)(2,1)S(1)} %copy-done, bf16[64,4096]{1,0:T(8,128)(2,1)S(1)} %all_gather.7), kind=kOutput, calls=%fused_computation.3 | convolution fusion | flops 201351168 | bytes 3719168 | tf_op jit(solution)/shard_map/dot_general | solution.py:10
  46.6 1.5 %scatter_custom_fusion.2 = bf16[768,64]{1,0:T(8,128)(2,1)S(1)} fusion(s32[384]{0:T(512)S(1)} %fusion.11, bf16[384,64]{1,0:T(8,128)(2,1)S(1)} %copy.18, bf16[]{:T(256)} %constant.14.clone.1), kind=kCustom, calls=%fused_computation.6 | custom fusion | bytes 98306 | tf_op jit(solution)/shard_map/scatter | solution.py:50
  48.2 0.8 reshape.117
  49.0 3.5 %all-to-all-start.2 = ((bf16[16,2,1536]{2,1,0:T(2,128)(2,1)}), bf16[16,2,1536]{2,1,0:T(2,128)(2,1)S(1)}, u32[]{:S(2)}, u32[]{:S(2)}) async-start(bf16[16,2,1536]{2,1,0:T(2,128)(2,1)} %reshape.117), calls=%async_computation.2 | async-start | bytes 196608 | tf_op jit(solution)/shard_map/all_to_all | solution.py:28
  52.6 3.4 %copy.15 = bf16[16,688,64]{1,0,2:T(8,128)(2,1)} copy(bf16[16,688,64]{1,2,0:T(8,128)(2,1)} %all-gather.3.cloned.1.call-done) | data formatting | bytes 2818048 | tf_op jit(solution)/shard_map/all_gather | solution.py:16
  56.0 4.2 %reshape.97 = bf16[11008,64]{0,1:T(8,128)(2,1)} reshape(bf16[16,688,64]{1,0,2:T(8,128)(2,1)} %copy.15) | data formatting | bytes 2818048
  60.3 6.4 %convolution_convert_fusion.1 = bf16[384,64]{0,1:T(8,128)(2,1)S(1)} fusion(bf16[384,11008]{1,0:T(8,128)(2,1)} %param.6, bf16[11008,64]{0,1:T(8,128)(2,1)} %reshape.97), kind=kOutput, calls=%fused_computation.4 | convolution fusion | flops 541089792 | bytes 9912320 | tf_op jit(solution)/shard_map/dot_general | solution.py:10
  66.8 1.5 %scatter_custom_fusion.1 = bf16[768,64]{1,0:T(8,128)(2,1)S(1)} fusion(s32[384]{0:T(512)S(1)} %fusion.11, bf16[384,64]{1,0:T(8,128)(2,1)S(1)} %copy.16, bf16[]{:T(256)} %constant.14.clone.1), kind=kCustom, calls=%fused_computation.8 | custom fusion | bytes 98306 | tf_op jit(solution)/shard_map/scatter | solution.py:48
  68.3 0.8 reshape.115
  69.1 6.0 %all-to-all-start.1 = ((bf16[16,2,1536]{2,1,0:T(2,128)(2,1)}), bf16[16,2,1536]{2,1,0:T(2,128)(2,1)S(1)}, u32[]{:S(2)}, u32[]{:S(2)}) async-start(bf16[16,2,1536]{2,1,0:T(2,128)(2,1)} %reshape.115), calls=%async_computation.1 | async-start | bytes 196608 | tf_op jit(solution)/shard_map/all_to_all | solution.py:27
  75.1 0.9 reshape.118
  76.0 6.5 %all-to-all-done.1 = bf16[16,2,1536]{2,1,0:T(2,128)(2,1)S(1)} async-done(((bf16[16,2,1536]{2,1,0:T(2,128)(2,1)}), bf16[16,2,1536]{2,1,0:T(2,128)(2,1)S(1)}, u32[]{:S(2)}, u32[]{:S(2)}) %all-to-all-start.1) | async-done | bytes 98336 | tf_op jit(solution)/shard_map/all_to_all | solution.py:27
  82.5 0.2 reshape.116
  82.9 1.3 %fusion.12 = f32[512,64]{1,0:T(8,128)S(1)} fusion(bf16[768,512]{0,1:T(8,128)(2,1)S(1)} %bitcast.40, bf16[768,64]{1,0:T(8,128)(2,1)} %bitcast.41), kind=kOutput, calls=%fused_computation.26 | convolution fusion | flops 50331648 | bytes 1015808 | tf_op jit(solution)/shard_map/dot_general | solution.py:57
  84.2 0.8 reshape.70
  (17 shorter events, 0.7 us)
Async XLA Ops:
  6.5 38.9 %copy-start = (bf16[384,4096]{1,0:T(8,128)(2,1)S(1)}, bf16[384,4096]{1,0:T(8,128)(2,1)}, u32[]{:S(2)}) copy-start(bf16[384,4096]{1,0:T(8,128)(2,1)} %param.7) | copy-start | bytes 9437188
  6.5 46.1 %all-gather.3.cloned.1.call-start = ((), (), s32[]{:S(2)}) async-start(), calls=%async_computation.3 | async-start | bytes 1671168 | tf_op jit(solution)/shard_map/all_gather | solution.py:16
  13.9 35.1 %all-to-all-start = ((bf16[16,48,1]{1,2,0:T(2,128)(2,1)}), bf16[16,48,1]{1,2,0:T(2,128)(2,1)S(1)}, u32[]{:S(2)}, u32[]{:S(2)}) async-start(bf16[16,48,1]{1,2,0:T(2,128)(2,1)} %all_to_all.27), calls=%async_computation | async-start | bytes 16384 | tf_op jit(solution)/shard_map/all_to_all | solution.py:29
  49.0 20.2 %all-to-all-start.2 = ((bf16[16,2,1536]{2,1,0:T(2,128)(2,1)}), bf16[16,2,1536]{2,1,0:T(2,128)(2,1)S(1)}, u32[]{:S(2)}, u32[]{:S(2)}) async-start(bf16[16,2,1536]{2,1,0:T(2,128)(2,1)} %reshape.117), calls=%async_computation.2 | async-start | bytes 196608 | tf_op jit(solution)/shard_map/all_to_all | solution.py:28
  69.1 13.4 %all-to-all-start.1 = ((bf16[16,2,1536]{2,1,0:T(2,128)(2,1)}), bf16[16,2,1536]{2,1,0:T(2,128)(2,1)S(1)}, u32[]{:S(2)}, u32[]{:S(2)}) async-start(bf16[16,2,1536]{2,1,0:T(2,128)(2,1)} %reshape.115), calls=%async_computation.1 | async-start | bytes 196608 | tf_op jit(solution)/shard_map/all_to_all | solution.py:27
Sparse Core Ops, SparseCore 0:
  9.6 42.6 all-gather.2
where the time goes:
time: 92.3 us; the launch traced here: 91.8 us
  blocking collectives  24.1 us (26%)
  local copies, waits for them, and re-layouts  18.6 us (20%)
  starting transfers between devices  16.9 us (18%)
  between operations  13.5 us (15%)
  matrix products  8.77 us (10%)
  waiting for transfers between devices  7.26 us (8%)
  other arithmetic  2.74 us (3%)
    all_gather x1, blocking collectives, project_output(): lax.all_gather(output_basis, 'dp', axis=1, tiled=True)  24.1 us
    dot_general x2, matrix products, folder(): lax.dot_general(token_block, portion, (((1,), (1,)), ((), ())), preferred...  7.48 us
    all_to_all x1, starting transfers between devices, send_rows(): lax.all_to_all(labels.astype(jnp.bfloat16), 'dp', split_axis=0, concat_ax...  7.39 us
    unnamed x7, local copies, waits for them, and re-layouts  6.88 us
    all_to_all x1, waiting for transfers between devices, send_rows(): lax.all_to_all(first, 'dp', split_axis=0, concat_axis=0, tiled=True)  6.54 us
    all_to_all x1, starting transfers between devices, send_rows(): lax.all_to_all(first, 'dp', split_axis=0, concat_axis=0, tiled=True)  5.97 us
    all_to_all x1, starting transfers between devices, send_rows(): lax.all_to_all(second, 'dp', split_axis=0, concat_axis=0, tiled=True)  3.51 us
    all_gather x1, local copies, waits for them, and re-layouts, project_hidden(): lax.all_gather(hidden_basis, 'dp', axis=1, tiled=True)  3.42 us
  transfers between devices with their start and end apart: 4, of which 1 were waited for; matrix products, arithmetic and copies ran while one was open for 29% of the time, Pallas kernels for 0%

commit v1 on v0

v1 whole, which is shorter than its diff:
```python
import jax
import jax.numpy as jnp
from jax import lax
from jax.sharding import PartitionSpec as P

DOCS_DEV = 8


def gather_bases(hidden_basis, output_basis, devices):
    rank_width, hidden_cols = hidden_basis.shape
    packed = jnp.concatenate([hidden_basis, output_basis], axis=1)[None]
    spread = jnp.broadcast_to(packed, (devices,) + packed.shape[1:])
    got = lax.all_to_all(spread, "dp", 0, 0, tiled=True)
    hidden_full = got[:, :, :hidden_cols].transpose(1, 0, 2).reshape(rank_width, -1)
    output_full = got[:, :, hidden_cols:].transpose(1, 0, 2).reshape(rank_width, -1)
    return hidden_full, output_full


def project(token_block, basis):
    summed = lax.dot_general(
        token_block, basis, (((1,), (1,)), ((), ())), preferred_element_type=jnp.float32
    )
    return summed.astype(jnp.bfloat16)


def local(hidden, out_grad, hidden_basis, output_basis, owner_ids, doc_slot):
    devices = lax.axis_size("dp")
    local_tokens = hidden.shape[0]
    capacity = 2 * local_tokens // devices
    rank_width = hidden_basis.shape[0]
    buffer_len = devices * capacity
    hidden_full, output_full = gather_bases(hidden_basis, output_basis, devices)
    left = project(hidden, hidden_full)
    right = project(out_grad, output_full)
    targets = owner_ids[:, 0]
    member = (targets[:, None] == jnp.arange(devices, dtype=jnp.int32)[None, :]).astype(jnp.bfloat16)
    token_ids = jnp.arange(local_tokens, dtype=jnp.int32)
    earlier = (token_ids[:, None] > token_ids[None, :]).astype(jnp.bfloat16)
    before = lax.dot_general(
        earlier, member, (((1,), (0,)), ((), ())), preferred_element_type=jnp.float32
    )
    position = jnp.sum(member.astype(jnp.float32) * before, axis=1).astype(jnp.int32)
    slot_index = targets * capacity + position
    dispatch = (
        jnp.arange(buffer_len, dtype=jnp.int32)[:, None] == slot_index[None, :]
    ).astype(jnp.bfloat16)
    label = (doc_slot + 1).astype(jnp.bfloat16)[:, None]
    rows = jnp.concatenate([left, right, label], axis=1)
    buffer = lax.dot_general(
        dispatch, rows, (((1,), (0,)), ((), ())), preferred_element_type=jnp.float32
    ).astype(jnp.bfloat16)
    arrived = lax.all_to_all(buffer, "dp", 0, 0, tiled=True)
    left_in = arrived[:, :rank_width]
    right_in = arrived[:, rank_width:2 * rank_width]
    label_in = arrived[:, 2 * rank_width:]
    selector = (label_in == (jnp.arange(DOCS_DEV, dtype=jnp.int32) + 1)[None, :].astype(jnp.bfloat16)).astype(
        jnp.bfloat16
    )
    weighted = (selector[:, :, None] * left_in[:, None, :]).reshape(buffer_len, DOCS_DEV * rank_width)
    grads = lax.dot_general(
        weighted, right_in, (((0,), (0,)), ((), ())), preferred_element_type=jnp.float32
    )
    return grads.reshape(DOCS_DEV, rank_width * rank_width)


def solution(mesh):
    placed = (
        P(("groups", "dp"), None),
        P(("groups", "dp"), None),
        P(None, "dp"),
        P(None, "dp"),
        P(("groups", "dp"), None),
        P(("groups", "dp")),
    )
    return jax.shard_map(
        local, mesh=mesh, in_specs=placed, out_specs=P(("groups", "dp"), None), check_vma=False
    )
```

time: 92.3 us -> 102 us (1.11)
  waiting for transfers between devices: 7.26 us -> 53.1 us
  blocking collectives: 24.1 us -> 0 us
  between operations: 13.5 us -> 0.12 us
  local copies, waits for them, and re-layouts: 18.6 us -> 16.7 us
  starting transfers between devices: 16.9 us -> 18.8 us
  matrix products: 8.77 us -> 10.1 us
    all_to_all x3 -> x2, waiting for transfers between devices: 6.55 us -> 53.1 us  [the longest x1 40.9 us: gather_bases(): got = lax.all_to_all(spread, 'dp', 0, 0, tiled=True)]
    all_gather x1 -> x0, blocking collectives: 24.1 us -> none  [project_output(): lax.all_gather(output_basis, 'dp', axis=1, tiled=True)]
    scatter x3 -> x0, local copies, waits for them, and re-layouts: 6.13 us -> none  [the longest x1 3.08 us: local(): labels = jnp.full((buffer_len,), -1, jnp.int32).at[slot_index].set(doc_slot)]
    reshape x0 -> x2, local copies, waits for them, and re-layouts: none -> 5.09 us  [the longest x1 4.26 us: gather_bases(): got[:, :, :hidden_cols].transpose(1, 0, 2).reshape(rank_width, -1)]
    unnamed x7 -> x10, local copies, waits for them, and re-layouts: 6.88 us -> 3.06 us
    transpose x0 -> x2, local copies, waits for them, and re-layouts: none -> 3.56 us  [gather_bases(): got[:, :, :hidden_cols].transpose(1, 0, 2).reshape(rank_width, -1)]
    all_gather x1 -> x0, local copies, waits for them, and re-layouts: 3.42 us -> none  [project_hidden(): lax.all_gather(hidden_basis, 'dp', axis=1, tiled=True)]
    all_to_all x3 -> x2, starting transfers between devices: 16.9 us -> 18.8 us  [the longest x1 11.2 us: local(): arrived = lax.all_to_all(buffer, 'dp', 0, 0, tiled=True)]
  transfers between devices with their start and end apart: 4 -> 2, of which waited for: 1 -> 2; matrix products, arithmetic and copies ran while one was open for 29% -> 0% of each run, Pallas kernels for 0% -> 0%
where the time goes in v1:
time: 102 us; the launch traced here: 101 us
  waiting for transfers between devices  53.1 us (52%)
  starting transfers between devices  18.8 us (18%)
  local copies, waits for them, and re-layouts  16.7 us (16%)
  matrix products  10.1 us (10%)
  other arithmetic  2.2 us (2%)
    all_to_all x1, waiting for transfers between devices, gather_bases(): got = lax.all_to_all(spread, 'dp', 0, 0, tiled=True)  40.9 us
    all_to_all x1, waiting for transfers between devices, local(): arrived = lax.all_to_all(buffer, 'dp', 0, 0, tiled=True)  12.2 us
    all_to_all x1, starting transfers between devices, local(): arrived = lax.all_to_all(buffer, 'dp', 0, 0, tiled=True)  11.2 us
    dot_general x2, matrix products, project(): lax.dot_general(token_block, basis, (((1,), (1,)), ((), ())), preferred_e...  8.29 us
    all_to_all x1, starting transfers between devices, gather_bases(): got = lax.all_to_all(spread, 'dp', 0, 0, tiled=True)  7.57 us
    reshape x1, local copies, waits for them, and re-layouts, gather_bases(): got[:, :, :hidden_cols].transpose(1, 0, 2).reshape(rank_width, -1)  4.26 us
    transpose x2, local copies, waits for them, and re-layouts, gather_bases(): got[:, :, :hidden_cols].transpose(1, 0, 2).reshape(rank_width, -1)  3.56 us
    unnamed x10, local copies, waits for them, and re-layouts  3.06 us
  transfers between devices with their start and end apart: 2, of which 2 were waited for; matrix products, arithmetic and copies ran while one was open for 0% of the time, Pallas kernels for 0%

profile of v1, /device:TPU:0, one launch (start us, length us, event | category | flops | bytes accessed | tf_op | source)
XLA Modules:
  0.0 101.0 jit_solution(2245879382301480565)
XLA Ops:
  0.0 0.0 copy-start
  0.0 1.1 %pad_maximum_fusion = bf16[64,944]{1,0:T(8,128)(2,1)S(1)} fusion(bf16[64,256]{1,0:T(8,128)(2,1)} %param.9, bf16[64,688]{1,0:T(8,128)(2,1)} %param.8), kind=kLoop, calls=%fused_computation.16 | loop fusion | flops 241664 | bytes 241664 | tf_op jit(solution)/shard_map/concatenate | solution.py:11
  1.2 1.6 %broadcast_in_dim.4 = bf16[16,64,944]{2,1,0:T(8,128)(2,1)} broadcast(bf16[64,944]{1,0:T(8,128)(2,1)S(1)} %pad_maximum_fusion), dimensions={1,2} | broadcast | bytes 2054144 | tf_op jit(solution)/shard_map/broadcast_in_dim | solution.py:12
  2.7 7.6 %all-to-all-start = ((bf16[16,64,944]{2,1,0:T(8,128)(2,1)}), bf16[16,64,944]{2,1,0:T(8,128)(2,1)}, u32[]{:S(2)}, u32[]{:S(2)}) async-start(bf16[16,64,944]{2,1,0:T(8,128)(2,1)} %broadcast_in_dim.4), calls=%async_computation | async-start | bytes 4194304 | tf_op jit(solution)/shard_map/all_to_all | solution.py:13
  10.4 0.2 fusion.2
  10.6 40.9 %all-to-all-done = bf16[16,64,944]{2,1,0:T(8,128)(2,1)} async-done(((bf16[16,64,944]{2,1,0:T(8,128)(2,1)}), bf16[16,64,944]{2,1,0:T(8,128)(2,1)}, u32[]{:S(2)}, u32[]{:S(2)}) %all-to-all-start) | async-done | bytes 1933344 | tf_op jit(solution)/shard_map/all_to_all | solution.py:13
  51.4 1.4 %slice_bitcast_fusion.1 = bf16[16,8,8,256]{3,2,1,0:T(8,128)(2,1)S(1)} fusion(bf16[16,64,944]{2,1,0:T(8,128)(2,1)} %all-to-all-done), kind=kLoop, calls=%fused_computation.11 | loop fusion | bytes 1048576
  52.8 0.8 copy.21
  53.6 1.5 %slice_bitcast_fusion = bf16[64,16,688]{2,0,1:T(8,128)(2,1)S(1)} fusion(bf16[16,64,944]{2,1,0:T(8,128)(2,1)} %all-to-all-done), kind=kLoop, calls=%fused_computation | loop fusion | bytes 2818048 | tf_op jit(solution)/shard_map/transpose | solution.py:14
  55.2 2.0 %copy.9 = bf16[64,16,688]{2,1,0:T(8,128)(2,1)} copy(bf16[64,16,688]{2,0,1:T(8,128)(2,1)S(1)} %slice_bitcast_fusion) | data formatting | bytes 2818048 | tf_op jit(solution)/shard_map/transpose | solution.py:14
  57.2 4.3 %reshape.62 = bf16[64,11008]{1,0:T(8,128)(2,1)} reshape(bf16[64,16,688]{2,1,0:T(8,128)(2,1)} %copy.9) | data formatting | bytes 2818048 | tf_op jit(solution)/shard_map/reshape | solution.py:14
  61.5 2.2 %fusion = bf16[384,64]{0,1:T(8,128)(2,1)S(1)} fusion(bf16[64,4096]{1,0:T(8,128)(2,1)} %bitcast.22, bf16[384,4096]{1,0:T(8,128)(2,1)S(1)} %copy-done), kind=kOutput, calls=%fused_computation.5 | convolution fusion | flops 201351168 | bytes 3719168 | tf_op jit(solution)/shard_map/dot_general | solution.py:20
  63.7 6.1 %fusion.1 = bf16[384,64]{0,1:T(8,128)(2,1)S(1)} fusion(bf16[64,11008]{1,0:T(8,128)(2,1)S(1)} %copy-done.1, bf16[384,11008]{1,0:T(8,128)(2,1)} %param.6), kind=kOutput, calls=%fused_computation.6 | convolution fusion | flops 541089792 | bytes 9912320 | tf_op jit(solution)/shard_map/dot_general | solution.py:20
  69.8 0.4 convolution_convert_fusion
  70.2 0.9 copy.15
  71.1 11.2 %all-to-all-start.1 = ((bf16[16,48,129]{2,1,0:T(8,128)(2,1)}), bf16[16,48,129]{2,1,0:T(8,128)(2,1)S(1)}, u32[]{:S(2)}, u32[]{:S(2)}) async-start(bf16[16,48,129]{2,1,0:T(8,128)(2,1)} %bitcast.23), calls=%async_computation.1 | async-start | bytes 786432 | tf_op jit(solution)/shard_map/all_to_all | solution.py:52
  82.4 12.2 %all-to-all-done.1 = bf16[16,48,129]{2,1,0:T(8,128)(2,1)S(1)} async-done(((bf16[16,48,129]{2,1,0:T(8,128)(2,1)}), bf16[16,48,129]{2,1,0:T(8,128)(2,1)S(1)}, u32[]{:S(2)}, u32[]{:S(2)}) %all-to-all-start.1) | async-done | bytes 198176 | tf_op jit(solution)/shard_map/all_to_all | solution.py:52
  94.5 0.7 slice.26
  95.2 0.1 slice_reduce_fusion
  95.4 1.7 %copy.18 = bf16[768,64]{0,1:T(8,128)(2,1)} copy(bf16[768,64]{1,0:T(8,128)(2,1)} %slice.26) | data formatting | bytes 196608
  97.1 0.1 compare_convert_fusion
  97.1 0.9 broadcast_multiply_fusion
  98.1 1.1 %fusion.4 = f32[512,64]{1,0:T(8,128)} fusion(bf16[768,512]{0,1:T(8,128)(2,1)S(1)} %bitcast.18, bf16[768,129]{1,0:T(8,128)(2,1)S(1)} %bitcast.21), kind=kOutput, calls=%fused_computation.13 | convolution fusion | flops 50331648 | bytes 1114112 | tf_op jit(solution)/shard_map/dot_general | solution.py:60
  99.2 1.7 %reshape.64 = f32[8,4096]{1,0:T(8,128)} reshape(f32[512,64]{1,0:T(8,128)} %fusion.4) | data formatting | bytes 262144 | tf_op jit(solution)/shard_map/reshape | solution.py:63
  (12 shorter events, 0.1 us)
Async XLA Ops:
  0.0 61.5 %copy-start = (bf16[384,4096]{1,0:T(8,128)(2,1)S(1)}, bf16[384,4096]{1,0:T(8,128)(2,1)}, u32[]{:S(2)}) copy-start(bf16[384,4096]{1,0:T(8,128)(2,1)} %param.7) | copy-start | bytes 9437188
  2.7 7.6 %copy-start.2 = (s32[384]{0:T(512)S(1)}, s32[384]{0:T(512)}, u32[]{:S(2)}) copy-start(s32[384]{0:T(512)} %param.11) | copy-start | bytes 4612
  2.7 7.6 %copy-start.3 = (s32[384,1]{0,1:T(1,128)S(1)}, s32[384,1]{0,1:T(1,128)}, u32[]{:S(2)}) copy-start(s32[384,1]{0,1:T(1,128)} %param.10) | copy-start | bytes 4612
  2.7 48.7 %all-to-all-start = ((bf16[16,64,944]{2,1,0:T(8,128)(2,1)}), bf16[16,64,944]{2,1,0:T(8,128)(2,1)}, u32[]{:S(2)}, u32[]{:S(2)}) async-start(bf16[16,64,944]{2,1,0:T(8,128)(2,1)} %broadcast_in_dim.4), calls=%async_computation | async-start | bytes 4194304 | tf_op jit(solution)/shard_map/all_to_all | solution.py:13
  61.5 2.2 %copy-start.1 = (bf16[64,11008]{1,0:T(8,128)(2,1)S(1)}, bf16[64,11008]{1,0:T(8,128)(2,1)}, u32[]{:S(2)}) copy-start(bf16[64,11008]{1,0:T(8,128)(2,1)} %reshape.62) | copy-start | bytes 4227076
  71.1 23.4 %all-to-all-start.1 = ((bf16[16,48,129]{2,1,0:T(8,128)(2,1)}), bf16[16,48,129]{2,1,0:T(8,128)(2,1)S(1)}, u32[]{:S(2)}, u32[]{:S(2)}) async-start(bf16[16,48,129]{2,1,0:T(8,128)(2,1)} %bitcast.23), calls=%async_computation.1 | async-start | bytes 786432 | tf_op jit(solution)/shard_map/all_to_all | solution.py:52

commit v2 on v1

v2 whole, which is shorter than its diff:
```python
import numpy as np
import jax
import jax.numpy as jnp
from jax import lax
from jax.sharding import PartitionSpec as P

DOCS_DEV = 8


def ring_planes(devices):
    chips = devices // 2
    if devices % 2 or chips < 2:
        return [list(range(devices))]
    if chips % 2 == 0 and chips >= 4:
        order = list(range(0, chips, 2)) + list(range(chips - 1, 0, -2))
    else:
        order = list(range(chips))
    return [[2 * chip + core for chip in order] for core in range(2)]


def ring_gather(block, devices):
    planes = ring_planes(devices)
    length = len(planes[0])
    me = lax.axis_index("dp")
    place = np.zeros(devices, np.int32)
    plane_of = np.zeros(devices, np.int32)
    for plane, members in enumerate(planes):
        for spot, member in enumerate(members):
            place[member] = spot
            plane_of[member] = plane
    spot = jnp.asarray(place)[me]
    forward = [(ring[t], ring[(t + 1) % length]) for ring in planes for t in range(length)]
    backward = [(ring[t], ring[(t - 1) % length]) for ring in planes for t in range(length)]
    ahead = [block]
    behind = []
    moving = block
    for _ in range(length // 2):
        moving = lax.ppermute(moving, "dp", forward)
        ahead.append(moving)
    moving = block
    for _ in range(length - 1 - length // 2):
        moving = lax.ppermute(moving, "dp", backward)
        behind.append(moving)
    by_distance = jnp.stack(ahead + behind[::-1])
    mine = by_distance[(spot - jnp.arange(length)) % length]
    if len(planes) == 1:
        stacks = [mine]
    else:
        swap = list(zip(planes[0], planes[1])) + list(zip(planes[1], planes[0]))
        other = lax.ppermute(mine, "dp", swap)
        first = jnp.asarray(plane_of)[me] == 0
        stacks = [jnp.where(first, mine, other), jnp.where(first, other, mine)]
    pieces = [None] * devices
    for plane, members in enumerate(planes):
        for at, member in enumerate(members):
            pieces[member] = stacks[plane][at]
    return pieces


def project(token_block, basis):
    summed = lax.dot_general(
        token_block, basis, (((1,), (1,)), ((), ())), preferred_element_type=jnp.float32
    )
    return summed.astype(jnp.bfloat16)


def local(hidden, out_grad, hidden_basis, output_basis, owner_ids, doc_slot):
    devices = lax.axis_size("dp")
    local_tokens = hidden.shape[0]
    capacity = 2 * local_tokens // devices
    rank_width = hidden_basis.shape[0]
    hidden_cols = hidden_basis.shape[1]
    buffer_len = devices * capacity
    pieces = ring_gather(jnp.concatenate([hidden_basis, output_basis], axis=1), devices)
    hidden_full = jnp.concatenate([piece[:, :hidden_cols] for piece in pieces], axis=1)
    output_full = jnp.concatenate([piece[:, hidden_cols:] for piece in pieces], axis=1)
    left = project(hidden, hidden_full)
    right = project(out_grad, output_full)
    targets = owner_ids[:, 0]
    member = (targets[:, None] == jnp.arange(devices, dtype=jnp.int32)[None, :]).astype(jnp.bfloat16)
    token_ids = jnp.arange(local_tokens, dtype=jnp.int32)
    earlier = (token_ids[:, None] > token_ids[None, :]).astype(jnp.bfloat16)
    before = lax.dot_general(
        earlier, member, (((1,), (0,)), ((), ())), preferred_element_type=jnp.float32
    )
    position = jnp.sum(member.astype(jnp.float32) * before, axis=1).astype(jnp.int32)
    slot_index = targets * capacity + position
    dispatch = (
        jnp.arange(buffer_len, dtype=jnp.int32)[:, None] == slot_index[None, :]
    ).astype(jnp.bfloat16)
    rows = jnp.concatenate([left, right], axis=1)
    buffer = lax.dot_general(
        dispatch, rows, (((1,), (0,)), ((), ())), preferred_element_type=jnp.float32
    ).astype(jnp.bfloat16)
    label = lax.dot_general(
        dispatch, (doc_slot + 1).astype(jnp.bfloat16), (((1,), (0,)), ((), ())),
        preferred_element_type=jnp.float32,
    ).astype(jnp.bfloat16)
    width = 2 * rank_width
    label_row = jnp.pad(label.reshape(devices, 1, capacity), ((0, 0), (0, 0), (0, width - capacity)))
    packed = jnp.concatenate([buffer.reshape(devices, capacity, width), label_row], axis=1)
    arrived = lax.all_to_all(packed, "dp", 0, 0, tiled=True)
    rows_in = arrived[:, :capacity, :].reshape(buffer_len, width)
    label_in = arrived[:, capacity, :capacity].reshape(buffer_len, 1)
    left_in = rows_in[:, :rank_width]
    right_in = rows_in[:, rank_width:]
    wanted = (jnp.arange(DOCS_DEV, dtype=jnp.int32) + 1).astype(jnp.bfloat16)[None, :]
    selector = (label_in == wanted).astype(jnp.bfloat16)
    weighted = (selector[:, :, None] * left_in[:, None, :]).reshape(buffer_len, DOCS_DEV * rank_width)
    grads = lax.dot_general(
        weighted, right_in, (((0,), (0,)), ((), ())), preferred_element_type=jnp.float32
    )
    return grads.reshape(DOCS_DEV, rank_width * rank_width)


def solution(mesh):
    placed = (
        P(("groups", "dp"), None),
        P(("groups", "dp"), None),
        P(None, "dp"),
        P(None, "dp"),
        P(("groups", "dp"), None),
        P(("groups", "dp")),
    )
    return jax.shard_map(
        local, mesh=mesh, in_specs=placed, out_specs=P(("groups", "dp"), None), check_vma=False
    )
```

time: 102 us -> 77.4 us (0.76)
  waiting for transfers between devices: 53.1 us -> 17.5 us
  local copies, waits for them, and re-layouts: 16.7 us -> 26.1 us
  other arithmetic: 2.2 us -> 6.01 us
  starting transfers between devices: 18.8 us -> 16 us
    all_to_all x2 -> x1, waiting for transfers between devices: 53.1 us -> 9.57 us  [local(): arrived = lax.all_to_all(packed, 'dp', 0, 0, tiled=True)]
    all_to_all x2 -> x1, starting transfers between devices: 18.8 us -> 6.49 us  [local(): arrived = lax.all_to_all(packed, 'dp', 0, 0, tiled=True)]
    ppermute x0 -> x8, starting transfers between devices: none -> 9.48 us  [the longest x4 9.45 us: ring_gather(): moving = lax.ppermute(moving, 'dp', forward)]
    slice x2 -> x19, local copies, waits for them, and re-layouts: 0.83 us -> 9.63 us  [the longest x16 7.77 us: local(): piece[:, :hidden_cols]]
    ppermute x0 -> x8, waiting for transfers between devices: none -> 7.98 us  [the longest x4 6.92 us: ring_gather(): moving = lax.ppermute(moving, 'dp', forward)]
    reshape x2 -> x1, local copies, waits for them, and re-layouts: 5.09 us -> 0.09 us  [local(): label.reshape(devices, 1, capacity)]
    concatenate x0 -> x2, local copies, waits for them, and re-layouts: none -> 3.88 us  [the longest x1 3.8 us: local(): jnp.concatenate([piece[:, :hidden_cols] for piece in pieces], axis=1)]
    transpose x2 -> x0, local copies, waits for them, and re-layouts: 3.56 us -> none  [gather_bases(): got[:, :, :hidden_cols].transpose(1, 0, 2).reshape(rank_width, -1)]
  transfers between devices with their start and end apart: 2 -> 9, of which waited for: 2 -> 5; matrix products, arithmetic and copies ran while one was open for 0% -> 10% of each run, Pallas kernels for 0% -> 0%
where the time goes in v2:
time: 77.4 us; the launch traced here: 76.7 us
  local copies, waits for them, and re-layouts  26.1 us (34%)
  waiting for transfers between devices  17.5 us (23%)
  starting transfers between devices  16 us (21%)
  matrix products  10.2 us (13%)
  other arithmetic  6.01 us (8%)
  between operations  0.83 us (1%)
    all_to_all x1, waiting for transfers between devices, local(): arrived = lax.all_to_all(packed, 'dp', 0, 0, tiled=True)  9.57 us
    ppermute x4, starting transfers between devices, ring_gather(): moving = lax.ppermute(moving, 'dp', forward)  9.45 us
    dot_general x2, matrix products, project(): lax.dot_general(token_block, basis, (((1,), (1,)), ((), ())), preferred_e...  8.2 us
    slice x16, local copies, waits for them, and re-layouts, local(): piece[:, :hidden_cols]  7.77 us
    ppermute x4, waiting for transfers between devices, ring_gather(): moving = lax.ppermute(moving, 'dp', forward)  6.92 us
    all_to_all x1, starting transfers between devices, local(): arrived = lax.all_to_all(packed, 'dp', 0, 0, tiled=True)  6.49 us
    unnamed x31, local copies, waits for them, and re-layouts  5.17 us
    concatenate x1, local copies, waits for them, and re-layouts, local(): jnp.concatenate([piece[:, :hidden_cols] for piece in pieces], axis=1)  3.8 us
  transfers between devices with their start and end apart: 9, of which 5 were waited for; matrix products, arithmetic and copies ran while one was open for 10% of the time, Pallas kernels for 0%

profile of v2, /device:TPU:0, one launch (start us, length us, event | category | flops | bytes accessed | tf_op | source)
XLA Modules:
  0.0 76.7 jit_solution(4851038061599206636)
XLA Ops:
  0.0 1.1 %pad_maximum_fusion = bf16[64,944]{1,0:T(8,128)(2,1)S(1)} fusion(bf16[64,256]{1,0:T(8,128)(2,1)} %param.11, bf16[64,688]{1,0:T(8,128)(2,1)} %param.10), kind=kLoop, calls=%fused_computation.39 | loop fusion | flops 241664 | bytes 241664 | tf_op jit(solution)/shard_map/concatenate | solution.py:74
  1.2 3.1 %collective-permute-start = (bf16[64,944]{1,0:T(8,128)(2,1)S(1)}, bf16[64,944]{1,0:T(8,128)(2,1)S(1)}, u32[]{:S(2)}, u32[]{:S(2)}) collective-permute-start(bf16[64,944]{1,0:T(8,128)(2,1)S(1)} %pad_maximum_fusion), channel_id=1, source_target_pairs={{0,4},{4,8},{8,12},{12,14},{14,10},{10,6},{6,2},{2,0},{1,5},{5,9},... | collective-permute-start | bytes 362504 | tf_op jit(solution)/shard_map/ppermute | solution.py:38
  4.3 1.2 %dynamic_slice.7 = s32[1]{0:T(128)} dynamic-slice(s32[16]{0:T(128)} %constant.39.clone, s32[]{:T(128)S(6)} %select_n.40), dynamic_slice_sizes={1} | dynamic-slice | bytes 12 | tf_op jit(solution)/shard_map/dynamic_slice | solution.py:31
  6.2 1.6 %bitcast_dynamic-update-slice_fusion.7 = bf16[8,64,944]{2,1,0:T(8,128)(2,1)} fusion(bf16[64,256]{1,0:T(8,128)(2,1)} %param.11, bf16[64,688]{1,0:T(8,128)(2,1)} %param.10), kind=kLoop, calls=%fused_computation.47 | loop fusion | flops 241663 | bytes 251904
  7.8 2.0 %collective-permute-start.1 = (bf16[64,944]{1,0:T(8,128)(2,1)S(1)}, bf16[64,944]{1,0:T(8,128)(2,1)S(1)}, u32[]{:S(2)}, u32[]{:S(2)}) collective-permute-start(bf16[64,944]{1,0:T(8,128)(2,1)S(1)} %collective-permute-done), channel_id=1, source_target_pairs={{0,4},{4,8},{8,12},{12,14},{14,10},{10,6},{6,2},{2,0},{1,5},{5,9},... | collective-permute-start | bytes 362504 | tf_op jit(solution)/shard_map/ppermute | solution.py:38
  10.5 2.3 %collective-permute-done.1 = bf16[64,944]{1,0:T(8,128)(2,1)S(1)} collective-permute-done((bf16[64,944]{1,0:T(8,128)(2,1)S(1)}, bf16[64,944]{1,0:T(8,128)(2,1)S(1)}, u32[]{:S(2)}, u32[]{:S(2)}) %collective-permute-start.1) | collective-permute-done | bytes 120864 | tf_op jit(solution)/shard_map/ppermute | solution.py:38
  12.8 2.0 %collective-permute-start.2 = (bf16[64,944]{1,0:T(8,128)(2,1)S(1)}, bf16[64,944]{1,0:T(8,128)(2,1)S(1)}, u32[]{:S(2)}, u32[]{:S(2)}) collective-permute-start(bf16[64,944]{1,0:T(8,128)(2,1)S(1)} %collective-permute-done.1), channel_id=1, source_target_pairs={{0,4},{4,8},{8,12},{12,14},{14,10},{10,6},{6,2},{2,0},{1,5},{5,9},... | collective-permute-start | bytes 362504 | tf_op jit(solution)/shard_map/ppermute | solution.py:38
  15.5 2.4 %collective-permute-done.2 = bf16[64,944]{1,0:T(8,128)(2,1)S(1)} collective-permute-done((bf16[64,944]{1,0:T(8,128)(2,1)S(1)}, bf16[64,944]{1,0:T(8,128)(2,1)S(1)}, u32[]{:S(2)}, u32[]{:S(2)}) %collective-permute-start.2) | collective-permute-done | bytes 120864 | tf_op jit(solution)/shard_map/ppermute | solution.py:38
  17.9 2.3 %collective-permute-start.3 = (bf16[64,944]{1,0:T(8,128)(2,1)S(1)}, bf16[64,944]{1,0:T(8,128)(2,1)S(1)}, u32[]{:S(2)}, u32[]{:S(2)}) collective-permute-start(bf16[64,944]{1,0:T(8,128)(2,1)S(1)} %collective-permute-done.2), channel_id=1, source_target_pairs={{0,4},{4,8},{8,12},{12,14},{14,10},{10,6},{6,2},{2,0},{1,5},{5,9},... | collective-permute-start | bytes 362504 | tf_op jit(solution)/shard_map/ppermute | solution.py:38
  20.8 2.2 %collective-permute-done.3 = bf16[64,944]{1,0:T(8,128)(2,1)S(1)} collective-permute-done((bf16[64,944]{1,0:T(8,128)(2,1)S(1)}, bf16[64,944]{1,0:T(8,128)(2,1)S(1)}, u32[]{:S(2)}, u32[]{:S(2)}) %collective-permute-start.3) | collective-permute-done | bytes 120864 | tf_op jit(solution)/shard_map/ppermute | solution.py:38
  24.4 0.7 bitcast_dynamic-update-slice_fusion.1
  25.7 2.8 %gather_fusion = bf16[8,64,944]{2,1,0:T(8,128)(2,1)} fusion(bf16[8,64,944]{2,1,0:T(8,128)(2,1)} %bitcast_dynamic-update-slice_fusion, s32[1024]{0:T(1024)S(1)} %pad_clamp_fusion), kind=kCustom, calls=%fused_computation | custom fusion | bytes 1933344 | tf_op jit(solution)/shard_map/gather | solution.py:45
  30.5 1.1 %collective-permute-done.7 = bf16[8,64,944]{2,1,0:T(8,128)(2,1)} collective-permute-done((bf16[8,64,944]{2,1,0:T(8,128)(2,1)}, bf16[8,64,944]{2,1,0:T(8,128)(2,1)}, u32[]{:S(2)}, u32[]{:S(2)}) %collective-permute-start.7) | collective-permute-done | bytes 966688 | tf_op jit(solution)/shard_map/ppermute | solution.py:50
  31.5 1.7 %broadcast_select_fusion = (bf16[8,64,944]{2,1,0:T(8,128)(2,1)S(1)}, bf16[8,64,944]{2,1,0:T(8,128)(2,1)S(1)}) fusion(bf16[8,64,944]{2,1,0:T(8,128)(2,1)} %collective-permute-done.7, bf16[8,64,944]{2,1,0:T(8,128)(2,1)} %gather_fusion, pred[]{:T(512)} %bitcast), kind=kLoop, calls=%fused_computation.12 | loop fusion | flops 966656 | bytes 3866625 | tf_op jit(solution)/shard_map/jit(_where)/select_n | solution.py:52
  42.6 1.7 %fusion.3 = bf16[384,64]{0,1:T(8,128)(2,1)} fusion(bf16[64,4096]{1,0:T(8,128)(2,1)S(1)} %constant_dynamic-update-slice_fusion, bf16[384,4096]{1,0:T(8,128)(2,1)S(1)} %copy-done), kind=kOutput, calls=%fused_computation.7 | convolution fusion | flops 201351168 | bytes 3719168 | tf_op jit(solution)/shard_map/dot_general | solution.py:61
  44.3 3.8 %concatenate.16 = bf16[64,11008]{1,0:T(8,128)(2,1)} concatenate(bf16[64,688]{1,0:T(8,128)(2,1)S(1)} %slice.211, bf16[64,688]{1,0:T(8,128)(2,1)S(1)} %slice.213, bf16[64,688]{1,0:T(8,128)(2,1)S(1)} %slice.215, bf16[64,688]{1,0:T(8,128)(2,1)S(1)} %slice.217, bf16[64,688]{1,0:T(8,128)(2,1)} %slice.219, bf16[64,688]{1,0:T(8,128)(2,1)} %slice.221, bf16[64,688]{1,0:T(8,128)(2,1)} %slice.223, ...), dimensions={1} | concatenate | bytes 2818048 | tf_op jit(solution)/shard_map/concatenate | solution.py:75
  48.1 6.5 %fusion.4 = bf16[384,64]{0,1:T(8,128)(2,1)S(1)} fusion(bf16[64,11008]{1,0:T(8,128)(2,1)} %concatenate.16, bf16[384,11008]{1,0:T(8,128)(2,1)} %param.8), kind=kOutput, calls=%fused_computation.8 | convolution fusion | flops 541089792 | bytes 9912320 | tf_op jit(solution)/shard_map/dot_general | solution.py:61
  54.9 0.7 fusion.10
  55.6 6.5 %all-to-all-start = ((bf16[16,49,128]{2,1,0:T(8,128)(2,1)}), bf16[16,49,128]{2,1,0:T(8,128)(2,1)}, u32[]{:S(2)}, u32[]{:S(2)}) async-start(bf16[16,49,128]{2,1,0:T(8,128)(2,1)} %fusion.10), calls=%async_computation | async-start | bytes 458752 | tf_op jit(solution)/shard_map/all_to_all | solution.py:102
  62.1 9.6 %all-to-all-done = bf16[16,49,128]{2,1,0:T(8,128)(2,1)} async-done(((bf16[16,49,128]{2,1,0:T(8,128)(2,1)}), bf16[16,49,128]{2,1,0:T(8,128)(2,1)}, u32[]{:S(2)}, u32[]{:S(2)}) %all-to-all-start) | async-done | bytes 200736 | tf_op jit(solution)/shard_map/all_to_all | solution.py:102
  71.7 0.9 %slice.259 = bf16[16,48,128]{2,1,0:T(8,128)(2,1)S(1)} slice(bf16[16,49,128]{2,1,0:T(8,128)(2,1)} %all-to-all-done), slice={[0:16], [0:48], [0:128]} | slice | bytes 393216 | tf_op jit(solution)/shard_map/slice | solution.py:103
  72.8 0.8 %slice_reduce_fusion = bf16[16,48]{1,0:T(8,128)(2,1)S(1)} fusion(bf16[16,49,128]{2,1,0:T(8,128)(2,1)} %all-to-all-done), kind=kLoop, calls=%fused_computation.71 | loop fusion | bytes 3072 | tf_op jit(solution)/shard_map/slice | solution.py:104
  73.8 1.1 %fusion.11 = f32[512,64]{1,0:T(8,128)} fusion(bf16[768,512]{0,1:T(8,128)(2,1)S(1)} %bitcast.66, bf16[768,128]{1,0:T(8,128)(2,1)S(1)} %bitcast.68), kind=kOutput, calls=%fused_computation.21 | convolution fusion | flops 50331648 | bytes 1114112 | tf_op jit(solution)/shard_map/dot_general | solution.py:110
  74.9 1.7 %reshape.117 = f32[8,4096]{1,0:T(8,128)} reshape(f32[512,64]{1,0:T(8,128)} %fusion.11) | data formatting | bytes 262144 | tf_op jit(solution)/shard_map/reshape | solution.py:113
  (73 shorter events, 15.9 us)
Async XLA Ops:
  0.0 42.6 %copy-start = (bf16[384,4096]{1,0:T(8,128)(2,1)S(1)}, bf16[384,4096]{1,0:T(8,128)(2,1)}, u32[]{:S(2)}) copy-start(bf16[384,4096]{1,0:T(8,128)(2,1)} %param.9) | copy-start | bytes 9437188
  0.0 29.2 %copy-start.4 = (s32[16]{0:T(128)S(1)}, s32[16]{0:T(128)}, u32[]{:S(2)}) copy-start(s32[16]{0:T(128)} %constant.40.clone) | copy-start | bytes 196
  0.0 28.5 %copy-start.2 = (s32[384]{0:T(512)S(1)}, s32[384]{0:T(512)}, u32[]{:S(2)}) copy-start(s32[384]{0:T(512)} %param.13) | copy-start | bytes 4612
  0.0 28.6 %copy-start.3 = (s32[384,1]{0,1:T(1,128)S(1)}, s32[384,1]{0,1:T(1,128)}, u32[]{:S(2)}) copy-start(s32[384,1]{0,1:T(1,128)} %param.12) | copy-start | bytes 4612
  1.2 6.6 %collective-permute-start = (bf16[64,944]{1,0:T(8,128)(2,1)S(1)}, bf16[64,944]{1,0:T(8,128)(2,1)S(1)}, u32[]{:S(2)}, u32[]{:S(2)}) collective-permute-start(bf16[64,944]{1,0:T(8,128)(2,1)S(1)} %pad_maximum_fusion), channel_id=1, source_target_pairs={{0,4},{4,8},{8,12},{12,14},{14,10},{10,6},{6,2},{2,0},{1,5},{5,9},... | collective-permute-start | bytes 362504 | tf_op jit(solution)/shard_map/ppermute | solution.py:38
  4.2 5.6 %collective-permute-start.4 = (bf16[64,944]{1,0:T(8,128)(2,1)S(1)}, bf16[64,944]{1,0:T(8,128)(2,1)S(1)}, u32[]{:S(2)}, u32[]{:S(2)}) collective-permute-start(bf16[64,944]{1,0:T(8,128)(2,1)S(1)} %pad_maximum_fusion), channel_id=1, source_target_pairs={{0,2},{4,0},{8,4},{12,8},{14,12},{10,14},{6,10},{2,6},{1,3},{5,1},... | collective-permute-start | bytes 362504 | tf_op jit(solution)/shard_map/ppermute | solution.py:42
  7.8 5.0 %collective-permute-start.1 = (bf16[64,944]{1,0:T(8,128)(2,1)S(1)}, bf16[64,944]{1,0:T(8,128)(2,1)S(1)}, u32[]{:S(2)}, u32[]{:S(2)}) collective-permute-start(bf16[64,944]{1,0:T(8,128)(2,1)S(1)} %collective-permute-done), channel_id=1, source_target_pairs={{0,4},{4,8},{8,12},{12,14},{14,10},{10,6},{6,2},{2,0},{1,5},{5,9},... | collective-permute-start | bytes 362504 | tf_op jit(solution)/shard_map/ppermute | solution.py:38
  9.8 5.0 %collective-permute-start.5 = (bf16[64,944]{1,0:T(8,128)(2,1)S(1)}, bf16[64,944]{1,0:T(8,128)(2,1)S(1)}, u32[]{:S(2)}, u32[]{:S(2)}) collective-permute-start(bf16[64,944]{1,0:T(8,128)(2,1)S(1)} %collective-permute-done.4), channel_id=1, source_target_pairs={{0,2},{4,0},{8,4},{12,8},{14,12},{10,14},{6,10},{2,6},{1,3},{5,1},... | collective-permute-start | bytes 362504 | tf_op jit(solution)/shard_map/ppermute | solution.py:42
  12.8 5.1 %collective-permute-start.2 = (bf16[64,944]{1,0:T(8,128)(2,1)S(1)}, bf16[64,944]{1,0:T(8,128)(2,1)S(1)}, u32[]{:S(2)}, u32[]{:S(2)}) collective-permute-start(bf16[64,944]{1,0:T(8,128)(2,1)S(1)} %collective-permute-done.1), channel_id=1, source_target_pairs={{0,4},{4,8},{8,12},{12,14},{14,10},{10,6},{6,2},{2,0},{1,5},{5,9},... | collective-permute-start | bytes 362504 | tf_op jit(solution)/shard_map/ppermute | solution.py:38
  14.8 8.9 %collective-permute-start.6 = (bf16[64,944]{1,0:T(8,128)(2,1)S(1)}, bf16[64,944]{1,0:T(8,128)(2,1)S(1)}, u32[]{:S(2)}, u32[]{:S(2)}) collective-permute-start(bf16[64,944]{1,0:T(8,128)(2,1)S(1)} %collective-permute-done.5), channel_id=1, source_target_pairs={{0,2},{4,0},{8,4},{12,8},{14,12},{10,14},{6,10},{2,6},{1,3},{5,1},... | collective-permute-start | bytes 362504 | tf_op jit(solution)/shard_map/ppermute | solution.py:42
  17.9 5.2 %collective-permute-start.3 = (bf16[64,944]{1,0:T(8,128)(2,1)S(1)}, bf16[64,944]{1,0:T(8,128)(2,1)S(1)}, u32[]{:S(2)}, u32[]{:S(2)}) collective-permute-start(bf16[64,944]{1,0:T(8,128)(2,1)S(1)} %collective-permute-done.2), channel_id=1, source_target_pairs={{0,4},{4,8},{8,12},{12,14},{14,10},{10,6},{6,2},{2,0},{1,5},{5,9},... | collective-permute-start | bytes 362504 | tf_op jit(solution)/shard_map/ppermute | solution.py:38
  28.5 3.0 %collective-permute-start.7 = (bf16[8,64,944]{2,1,0:T(8,128)(2,1)}, bf16[8,64,944]{2,1,0:T(8,128)(2,1)}, u32[]{:S(2)}, u32[]{:S(2)}) collective-permute-start(bf16[8,64,944]{2,1,0:T(8,128)(2,1)} %gather_fusion), channel_id=1, source_target_pairs={{0,1},{4,5},{8,9},{12,13},{14,15},{10,11},{6,7},{2,3},{1,0},{5,4},... | collective-permute-start | bytes 2899976 | tf_op jit(solution)/shard_map/ppermute | solution.py:50
  48.1 6.5 %copy-start.1 = (bf16[384,64]{0,1:T(8,128)(2,1)S(1)}, bf16[384,64]{0,1:T(8,128)(2,1)}, u32[]{:S(2)}) copy-start(bf16[384,64]{0,1:T(8,128)(2,1)} %fusion.3) | copy-start | bytes 147460
  55.6 16.1 %all-to-all-start = ((bf16[16,49,128]{2,1,0:T(8,128)(2,1)}), bf16[16,49,128]{2,1,0:T(8,128)(2,1)}, u32[]{:S(2)}, u32[]{:S(2)}) async-start(bf16[16,49,128]{2,1,0:T(8,128)(2,1)} %fusion.10), calls=%async_computation | async-start | bytes 458752 | tf_op jit(solution)/shard_map/all_to_all | solution.py:102

commit v3 on v2

--- a/solution.py
+++ b/solution.py
@@ -42,19 +42,17 @@
         moving = lax.ppermute(moving, "dp", backward)
         behind.append(moving)
     by_distance = jnp.stack(ahead + behind[::-1])
-    mine = by_distance[(spot - jnp.arange(length)) % length]
+    chip_spot = np.zeros(length, np.int32)
+    for at, member in enumerate(planes[0]):
+        chip_spot[member // len(planes)] = at
+    mine = by_distance[(spot - jnp.asarray(chip_spot)) % length]
     if len(planes) == 1:
-        stacks = [mine]
-    else:
-        swap = list(zip(planes[0], planes[1])) + list(zip(planes[1], planes[0]))
-        other = lax.ppermute(mine, "dp", swap)
-        first = jnp.asarray(plane_of)[me] == 0
-        stacks = [jnp.where(first, mine, other), jnp.where(first, other, mine)]
-    pieces = [None] * devices
-    for plane, members in enumerate(planes):
-        for at, member in enumerate(members):
-            pieces[member] = stacks[plane][at]
-    return pieces
+        return mine
+    swap = list(zip(planes[0], planes[1])) + list(zip(planes[1], planes[0]))
+    other = lax.ppermute(mine, "dp", swap)
+    first = jnp.asarray(plane_of)[me] == 0
+    both = jnp.where(first, jnp.stack([mine, other], axis=1), jnp.stack([other, mine], axis=1))
+    return both.reshape((devices,) + block.shape)
 
 
 def project(token_block, basis):
@@ -71,9 +69,9 @@
     rank_width = hidden_basis.shape[0]
     hidden_cols = hidden_basis.shape[1]
     buffer_len = devices * capacity
-    pieces = ring_gather(jnp.concatenate([hidden_basis, output_basis], axis=1), devices)
-    hidden_full = jnp.concatenate([piece[:, :hidden_cols] for piece in pieces], axis=1)
-    output_full = jnp.concatenate([piece[:, hidden_cols:] for piece in pieces], axis=1)
+    stacked = ring_gather(jnp.concatenate([hidden_basis, output_basis], axis=1), devices)
+    hidden_full = stacked[:, :, :hidden_cols].transpose(1, 0, 2).reshape(rank_width, -1)
+    output_full = stacked[:, :, hidden_cols:].transpose(1, 0, 2).reshape(rank_width, -1)
     left = project(hidden, hidden_full)
     right = project(out_grad, output_full)
     targets = owner_ids[:, 0]

time: 77.4 us -> 73.3 us (0.947)
  local copies, waits for them, and re-layouts: 26.1 us -> 20.5 us
  other arithmetic: 6.01 us -> 7.64 us
    slice x16 -> x0, local copies, waits for them, and re-layouts: 7.77 us -> none  [local(): piece[:, :hidden_cols]]
    reshape x0 -> x2, local copies, waits for them, and re-layouts: none -> 5.09 us  [the longest x1 4.26 us: local(): stacked[:, :, :hidden_cols].transpose(1, 0, 2).reshape(rank_width, -1)]
    concatenate x2 -> x0, local copies, waits for them, and re-layouts: 3.88 us -> none  [the longest x1 3.8 us: local(): jnp.concatenate([piece[:, :hidden_cols] for piece in pieces], axis=1)]
    transpose x0 -> x2, local copies, waits for them, and re-layouts: none -> 2.19 us  [local(): stacked[:, :, :hidden_cols].transpose(1, 0, 2).reshape(rank_width, -1)]
    select_n x2, other arithmetic: 2.34 us -> 3.95 us  [the longest x1 2.64 us: ring_gather(): jnp.where(first, jnp.stack([mine, other], axis=1), jnp.stack([other, mine...]
    unnamed x31 -> x17, local copies, waits for them, and re-layouts: 5.17 us -> 4.2 us
  transfers between devices with their start and end apart: 9 -> 9, of which waited for: 5 -> 5; matrix products, arithmetic and copies ran while one was open for 10% -> 11% of each run, Pallas kernels for 0% -> 0%
where the time goes in v3:
time: 73.3 us; the launch traced here: 72.8 us
  local copies, waits for them, and re-layouts  20.5 us (28%)
  waiting for transfers between devices  17.5 us (24%)
  starting transfers between devices  16 us (22%)
  matrix products  10.3 us (14%)
  other arithmetic  7.64 us (10%)
  between operations  0.8 us (1%)
    all_to_all x1, waiting for transfers between devices, local(): arrived = lax.all_to_all(packed, 'dp', 0, 0, tiled=True)  9.57 us
    ppermute x4, starting transfers between devices, ring_gather(): moving = lax.ppermute(moving, 'dp', forward)  9.45 us
    dot_general x2, matrix products, project(): lax.dot_general(token_block, basis, (((1,), (1,)), ((), ())), preferred_e...  8.29 us
    ppermute x4, waiting for transfers between devices, ring_gather(): moving = lax.ppermute(moving, 'dp', forward)  6.91 us
    all_to_all x1, starting transfers between devices, local(): arrived = lax.all_to_all(packed, 'dp', 0, 0, tiled=True)  6.49 us
    reshape x1, local copies, waits for them, and re-layouts, local(): stacked[:, :, :hidden_cols].transpose(1, 0, 2).reshape(rank_width, -1)  4.26 us
    unnamed x17, local copies, waits for them, and re-layouts  4.2 us
    gather x1, local copies, waits for them, and re-layouts, ring_gather(): mine = by_distance[(spot - jnp.asarray(chip_spot)) % length]  2.8 us
  transfers between devices with their start and end apart: 9, of which 5 were waited for; matrix products, arithmetic and copies ran while one was open for 11% of the time, Pallas kernels for 0%

profile of v3, /device:TPU:0, one launch (start us, length us, event | category | flops | bytes accessed | tf_op | source)
XLA Modules:
  0.0 72.8 jit_solution(4974229422743421009)
XLA Ops:
  0.0 1.1 %pad_maximum_fusion = bf16[64,944]{1,0:T(8,128)(2,1)S(1)} fusion(bf16[64,256]{1,0:T(8,128)(2,1)} %param.12, bf16[64,688]{1,0:T(8,128)(2,1)} %param.11), kind=kLoop, calls=%fused_computation.24 | loop fusion | flops 241664 | bytes 241664 | tf_op jit(solution)/shard_map/concatenate | solution.py:72
  1.2 3.1 %collective-permute-start = (bf16[64,944]{1,0:T(8,128)(2,1)S(1)}, bf16[64,944]{1,0:T(8,128)(2,1)S(1)}, u32[]{:S(2)}, u32[]{:S(2)}) collective-permute-start(bf16[64,944]{1,0:T(8,128)(2,1)S(1)} %pad_maximum_fusion), channel_id=1, source_target_pairs={{0,4},{4,8},{8,12},{12,14},{14,10},{10,6},{6,2},{2,0},{1,5},{5,9},... | collective-permute-start | bytes 362504 | tf_op jit(solution)/shard_map/ppermute | solution.py:38
  4.2 1.2 %dynamic_slice.7 = s32[1]{0:T(128)} dynamic-slice(s32[16]{0:T(128)} %constant.41.clone, s32[]{:T(128)S(6)} %select_n.26), dynamic_slice_sizes={1} | dynamic-slice | bytes 12 | tf_op jit(solution)/shard_map/dynamic_slice | solution.py:31
  5.5 1.3 %compare_select_fusion = s32[8]{0:T(128)S(1)} fusion(s32[8]{0:T(128)} %constant.46, s32[]{:T(128)} %bitcast.9), kind=kLoop, calls=%fused_computation.42 | loop fusion | flops 120 | bytes 68 | tf_op jit(solution)/shard_map/select_n | solution.py:48
  6.8 1.7 %bitcast_dynamic-update-slice_fusion.7 = bf16[8,64,944]{2,1,0:T(8,128)(2,1)} fusion(bf16[64,256]{1,0:T(8,128)(2,1)} %param.12, bf16[64,688]{1,0:T(8,128)(2,1)} %param.11), kind=kLoop, calls=%fused_computation.32 | loop fusion | flops 241663 | bytes 251904
  8.5 2.0 %collective-permute-start.1 = (bf16[64,944]{1,0:T(8,128)(2,1)S(1)}, bf16[64,944]{1,0:T(8,128)(2,1)S(1)}, u32[]{:S(2)}, u32[]{:S(2)}) collective-permute-start(bf16[64,944]{1,0:T(8,128)(2,1)S(1)} %collective-permute-done), channel_id=1, source_target_pairs={{0,4},{4,8},{8,12},{12,14},{14,10},{10,6},{6,2},{2,0},{1,5},{5,9},... | collective-permute-start | bytes 362504 | tf_op jit(solution)/shard_map/ppermute | solution.py:38
  11.2 2.3 %collective-permute-done.1 = bf16[64,944]{1,0:T(8,128)(2,1)S(1)} collective-permute-done((bf16[64,944]{1,0:T(8,128)(2,1)S(1)}, bf16[64,944]{1,0:T(8,128)(2,1)S(1)}, u32[]{:S(2)}, u32[]{:S(2)}) %collective-permute-start.1) | collective-permute-done | bytes 120864 | tf_op jit(solution)/shard_map/ppermute | solution.py:38
  13.4 2.0 %collective-permute-start.2 = (bf16[64,944]{1,0:T(8,128)(2,1)S(1)}, bf16[64,944]{1,0:T(8,128)(2,1)S(1)}, u32[]{:S(2)}, u32[]{:S(2)}) collective-permute-start(bf16[64,944]{1,0:T(8,128)(2,1)S(1)} %collective-permute-done.1), channel_id=1, source_target_pairs={{0,4},{4,8},{8,12},{12,14},{14,10},{10,6},{6,2},{2,0},{1,5},{5,9},... | collective-permute-start | bytes 362504 | tf_op jit(solution)/shard_map/ppermute | solution.py:38
  16.1 2.4 %collective-permute-done.2 = bf16[64,944]{1,0:T(8,128)(2,1)S(1)} collective-permute-done((bf16[64,944]{1,0:T(8,128)(2,1)S(1)}, bf16[64,944]{1,0:T(8,128)(2,1)S(1)}, u32[]{:S(2)}, u32[]{:S(2)}) %collective-permute-start.2) | collective-permute-done | bytes 120864 | tf_op jit(solution)/shard_map/ppermute | solution.py:38
  18.5 2.3 %collective-permute-start.3 = (bf16[64,944]{1,0:T(8,128)(2,1)S(1)}, bf16[64,944]{1,0:T(8,128)(2,1)S(1)}, u32[]{:S(2)}, u32[]{:S(2)}) collective-permute-start(bf16[64,944]{1,0:T(8,128)(2,1)S(1)} %collective-permute-done.2), channel_id=1, source_target_pairs={{0,4},{4,8},{8,12},{12,14},{14,10},{10,6},{6,2},{2,0},{1,5},{5,9},... | collective-permute-start | bytes 362504 | tf_op jit(solution)/shard_map/ppermute | solution.py:38
  21.5 2.2 %collective-permute-done.3 = bf16[64,944]{1,0:T(8,128)(2,1)S(1)} collective-permute-done((bf16[64,944]{1,0:T(8,128)(2,1)S(1)}, bf16[64,944]{1,0:T(8,128)(2,1)S(1)}, u32[]{:S(2)}, u32[]{:S(2)}) %collective-permute-start.3) | collective-permute-done | bytes 120864 | tf_op jit(solution)/shard_map/ppermute | solution.py:38
  26.4 2.8 %gather_fusion = bf16[8,64,944]{2,1,0:T(8,128)(2,1)} fusion(bf16[8,64,944]{2,1,0:T(8,128)(2,1)} %bitcast_dynamic-update-slice_fusion, s32[1024]{0:T(1024)S(1)} %pad_clamp_fusion), kind=kCustom, calls=%fused_computation | custom fusion | bytes 1933344 | tf_op jit(solution)/shard_map/gather | solution.py:48
  31.2 1.1 %collective-permute-done.7 = bf16[8,64,944]{2,1,0:T(8,128)(2,1)} collective-permute-done((bf16[8,64,944]{2,1,0:T(8,128)(2,1)}, bf16[8,64,944]{2,1,0:T(8,128)(2,1)}, u32[]{:S(2)}, u32[]{:S(2)}) %collective-permute-start.7) | collective-permute-done | bytes 966688 | tf_op jit(solution)/shard_map/ppermute | solution.py:52
  32.2 2.6 %maximum_select_fusion = bf16[8,2,64,944]{3,2,1,0:T(8,128)(2,1)S(1)} fusion(bf16[8,1,64,944]{3,2,1,0:T(8,128)(2,1)} %bitcast.11, bf16[8,1,64,944]{3,2,1,0:T(8,128)(2,1)} %bitcast.43, pred[]{:T(512)} %bitcast), kind=kLoop, calls=%fused_computation.1 | loop fusion | flops 2899968 | bytes 3866625 | tf_op jit(solution)/shard_map/jit(_where)/select_n | solution.py:54
  35.2 0.8 %copy.21 = bf16[16,8,8,256]{3,2,0,1:T(8,128)(2,1)} copy(bf16[16,8,8,256]{3,2,1,0:T(8,128)(2,1)S(1)} %slice_bitcast_fusion.1) | data formatting | bytes 1048576 | tf_op jit(solution)/shard_map/reshape | solution.py:74
  36.1 2.0 %copy.14 = bf16[64,16,688]{2,1,0:T(8,128)(2,1)} copy(bf16[64,16,688]{2,0,1:T(8,128)(2,1)S(1)} %slice_bitcast_fusion) | data formatting | bytes 2818048 | tf_op jit(solution)/shard_map/transpose | solution.py:73
  38.1 4.3 %reshape.76 = bf16[64,11008]{1,0:T(8,128)(2,1)} reshape(bf16[64,16,688]{2,1,0:T(8,128)(2,1)} %copy.14) | data formatting | bytes 2818048 | tf_op jit(solution)/shard_map/reshape | solution.py:73
  42.4 2.2 %fusion.3 = bf16[384,64]{0,1:T(8,128)(2,1)S(1)} fusion(bf16[64,4096]{1,0:T(8,128)(2,1)} %bitcast.45, bf16[384,4096]{1,0:T(8,128)(2,1)S(1)} %copy-done), kind=kOutput, calls=%fused_computation.9 | convolution fusion | flops 201351168 | bytes 3719168 | tf_op jit(solution)/shard_map/dot_general | solution.py:59
  44.6 6.1 %fusion.4 = bf16[384,64]{0,1:T(8,128)(2,1)S(1)} fusion(bf16[64,11008]{1,0:T(8,128)(2,1)S(1)} %copy-done.1, bf16[384,11008]{1,0:T(8,128)(2,1)} %param.9), kind=kOutput, calls=%fused_computation.10 | convolution fusion | flops 541089792 | bytes 9912320 | tf_op jit(solution)/shard_map/dot_general | solution.py:59
  51.7 6.5 %all-to-all-start = ((bf16[16,49,128]{2,1,0:T(8,128)(2,1)}), bf16[16,49,128]{2,1,0:T(8,128)(2,1)}, u32[]{:S(2)}, u32[]{:S(2)}) async-start(bf16[16,49,128]{2,1,0:T(8,128)(2,1)} %fusion.10), calls=%async_computation | async-start | bytes 458752 | tf_op jit(solution)/shard_map/all_to_all | solution.py:100
  58.2 9.6 %all-to-all-done = bf16[16,49,128]{2,1,0:T(8,128)(2,1)} async-done(((bf16[16,49,128]{2,1,0:T(8,128)(2,1)}), bf16[16,49,128]{2,1,0:T(8,128)(2,1)}, u32[]{:S(2)}, u32[]{:S(2)}) %all-to-all-start) | async-done | bytes 200736 | tf_op jit(solution)/shard_map/all_to_all | solution.py:100
  67.8 0.9 %slice.29 = bf16[16,48,128]{2,1,0:T(8,128)(2,1)S(1)} slice(bf16[16,49,128]{2,1,0:T(8,128)(2,1)} %all-to-all-done), slice={[0:16], [0:48], [0:128]} | slice | bytes 393216 | tf_op jit(solution)/shard_map/slice | solution.py:101
  69.9 1.1 %fusion.11 = f32[512,64]{1,0:T(8,128)} fusion(bf16[768,512]{0,1:T(8,128)(2,1)S(1)} %bitcast.44, bf16[768,128]{1,0:T(8,128)(2,1)S(1)} %bitcast.47), kind=kOutput, calls=%fused_computation.22 | convolution fusion | flops 50331648 | bytes 1114112 | tf_op jit(solution)/shard_map/dot_general | solution.py:108
  71.1 1.7 %reshape.81 = f32[8,4096]{1,0:T(8,128)} reshape(f32[512,64]{1,0:T(8,128)} %fusion.11) | data formatting | bytes 262144 | tf_op jit(solution)/shard_map/reshape | solution.py:111
  (44 shorter events, 8.5 us)
Async XLA Ops:
  0.0 42.4 %copy-start = (bf16[384,4096]{1,0:T(8,128)(2,1)S(1)}, bf16[384,4096]{1,0:T(8,128)(2,1)}, u32[]{:S(2)}) copy-start(bf16[384,4096]{1,0:T(8,128)(2,1)} %param.10) | copy-start | bytes 9437188
  1.2 7.3 %collective-permute-start = (bf16[64,944]{1,0:T(8,128)(2,1)S(1)}, bf16[64,944]{1,0:T(8,128)(2,1)S(1)}, u32[]{:S(2)}, u32[]{:S(2)}) collective-permute-start(bf16[64,944]{1,0:T(8,128)(2,1)S(1)} %pad_maximum_fusion), channel_id=1, source_target_pairs={{0,4},{4,8},{8,12},{12,14},{14,10},{10,6},{6,2},{2,0},{1,5},{5,9},... | collective-permute-start | bytes 362504 | tf_op jit(solution)/shard_map/ppermute | solution.py:38
  4.2 6.3 %collective-permute-start.4 = (bf16[64,944]{1,0:T(8,128)(2,1)S(1)}, bf16[64,944]{1,0:T(8,128)(2,1)S(1)}, u32[]{:S(2)}, u32[]{:S(2)}) collective-permute-start(bf16[64,944]{1,0:T(8,128)(2,1)S(1)} %pad_maximum_fusion), channel_id=1, source_target_pairs={{0,2},{4,0},{8,4},{12,8},{14,12},{10,14},{6,10},{2,6},{1,3},{5,1},... | collective-permute-start | bytes 362504 | tf_op jit(solution)/shard_map/ppermute | solution.py:42
  6.8 22.4 %copy-start.2 = (s32[384]{0:T(512)S(1)}, s32[384]{0:T(512)}, u32[]{:S(2)}) copy-start(s32[384]{0:T(512)} %param.14) | copy-start | bytes 4612
  6.8 22.4 %copy-start.3 = (s32[384,1]{0,1:T(1,128)S(1)}, s32[384,1]{0,1:T(1,128)}, u32[]{:S(2)}) copy-start(s32[384,1]{0,1:T(1,128)} %param.13) | copy-start | bytes 4612
  8.5 5.0 %collective-permute-start.1 = (bf16[64,944]{1,0:T(8,128)(2,1)S(1)}, bf16[64,944]{1,0:T(8,128)(2,1)S(1)}, u32[]{:S(2)}, u32[]{:S(2)}) collective-permute-start(bf16[64,944]{1,0:T(8,128)(2,1)S(1)} %collective-permute-done), channel_id=1, source_target_pairs={{0,4},{4,8},{8,12},{12,14},{14,10},{10,6},{6,2},{2,0},{1,5},{5,9},... | collective-permute-start | bytes 362504 | tf_op jit(solution)/shard_map/ppermute | solution.py:38
  10.5 5.0 %collective-permute-start.5 = (bf16[64,944]{1,0:T(8,128)(2,1)S(1)}, bf16[64,944]{1,0:T(8,128)(2,1)S(1)}, u32[]{:S(2)}, u32[]{:S(2)}) collective-permute-start(bf16[64,944]{1,0:T(8,128)(2,1)S(1)} %collective-permute-done.4), channel_id=1, source_target_pairs={{0,2},{4,0},{8,4},{12,8},{14,12},{10,14},{6,10},{2,6},{1,3},{5,1},... | collective-permute-start | bytes 362504 | tf_op jit(solution)/shard_map/ppermute | solution.py:42
  11.1 18.8 %copy-start.4 = (s32[16]{0:T(128)S(1)}, s32[16]{0:T(128)}, u32[]{:S(2)}) copy-start(s32[16]{0:T(128)} %constant.43.clone) | copy-start | bytes 196
  13.4 5.1 %collective-permute-start.2 = (bf16[64,944]{1,0:T(8,128)(2,1)S(1)}, bf16[64,944]{1,0:T(8,128)(2,1)S(1)}, u32[]{:S(2)}, u32[]{:S(2)}) collective-permute-start(bf16[64,944]{1,0:T(8,128)(2,1)S(1)} %collective-permute-done.1), channel_id=1, source_target_pairs={{0,4},{4,8},{8,12},{12,14},{14,10},{10,6},{6,2},{2,0},{1,5},{5,9},... | collective-permute-start | bytes 362504 | tf_op jit(solution)/shard_map/ppermute | solution.py:38
  15.5 8.9 %collective-permute-start.6 = (bf16[64,944]{1,0:T(8,128)(2,1)S(1)}, bf16[64,944]{1,0:T(8,128)(2,1)S(1)}, u32[]{:S(2)}, u32[]{:S(2)}) collective-permute-start(bf16[64,944]{1,0:T(8,128)(2,1)S(1)} %collective-permute-done.5), channel_id=1, source_target_pairs={{0,2},{4,0},{8,4},{12,8},{14,12},{10,14},{6,10},{2,6},{1,3},{5,1},... | collective-permute-start | bytes 362504 | tf_op jit(solution)/shard_map/ppermute | solution.py:42
  18.5 5.2 %collective-permute-start.3 = (bf16[64,944]{1,0:T(8,128)(2,1)S(1)}, bf16[64,944]{1,0:T(8,128)(2,1)S(1)}, u32[]{:S(2)}, u32[]{:S(2)}) collective-permute-start(bf16[64,944]{1,0:T(8,128)(2,1)S(1)} %collective-permute-done.2), channel_id=1, source_target_pairs={{0,4},{4,8},{8,12},{12,14},{14,10},{10,6},{6,2},{2,0},{1,5},{5,9},... | collective-permute-start | bytes 362504 | tf_op jit(solution)/shard_map/ppermute | solution.py:38
  29.2 3.0 %collective-permute-start.7 = (bf16[8,64,944]{2,1,0:T(8,128)(2,1)}, bf16[8,64,944]{2,1,0:T(8,128)(2,1)}, u32[]{:S(2)}, u32[]{:S(2)}) collective-permute-start(bf16[8,64,944]{2,1,0:T(8,128)(2,1)} %gather_fusion), channel_id=1, source_target_pairs={{0,1},{4,5},{8,9},{12,13},{14,15},{10,11},{6,7},{2,3},{1,0},{5,4},... | collective-permute-start | bytes 2899976 | tf_op jit(solution)/shard_map/ppermute | solution.py:52
  42.4 2.2 %copy-start.1 = (bf16[64,11008]{1,0:T(8,128)(2,1)S(1)}, bf16[64,11008]{1,0:T(8,128)(2,1)}, u32[]{:S(2)}) copy-start(bf16[64,11008]{1,0:T(8,128)(2,1)} %reshape.76) | copy-start | bytes 4227076
  51.7 16.1 %all-to-all-start = ((bf16[16,49,128]{2,1,0:T(8,128)(2,1)}), bf16[16,49,128]{2,1,0:T(8,128)(2,1)}, u32[]{:S(2)}, u32[]{:S(2)}) async-start(bf16[16,49,128]{2,1,0:T(8,128)(2,1)} %fusion.10), calls=%async_computation | async-start | bytes 458752 | tf_op jit(solution)/shard_map/all_to_all | solution.py:100

commit v4 on v3

--- a/solution.py
+++ b/solution.py
@@ -2,6 +2,8 @@
 import jax
 import jax.numpy as jnp
 from jax import lax
+from jax.experimental import pallas as pl
+from jax.experimental.pallas import tpu as pltpu
 from jax.sharding import PartitionSpec as P
 
 DOCS_DEV = 8
@@ -29,37 +31,79 @@
             place[member] = spot
             plane_of[member] = plane
     spot = jnp.asarray(place)[me]
+    plane = jnp.asarray(plane_of)[me]
     forward = [(ring[t], ring[(t + 1) % length]) for ring in planes for t in range(length)]
     backward = [(ring[t], ring[(t - 1) % length]) for ring in planes for t in range(length)]
-    ahead = [block]
-    behind = []
+    blocks = [block]
+    shifts = [0]
     moving = block
-    for _ in range(length // 2):
+    for step in range(1, length // 2 + 1):
         moving = lax.ppermute(moving, "dp", forward)
-        ahead.append(moving)
+        blocks.append(moving)
+        shifts.append(-step)
     moving = block
-    for _ in range(length - 1 - length // 2):
+    for step in range(1, length - length // 2):
         moving = lax.ppermute(moving, "dp", backward)
-        behind.append(moving)
-    by_distance = jnp.stack(ahead + behind[::-1])
-    chip_spot = np.zeros(length, np.int32)
-    for at, member in enumerate(planes[0]):
-        chip_spot[member // len(planes)] = at
-    mine = by_distance[(spot - jnp.asarray(chip_spot)) % length]
-    if len(planes) == 1:
-        return mine
-    swap = list(zip(planes[0], planes[1])) + list(zip(planes[1], planes[0]))
-    other = lax.ppermute(mine, "dp", swap)
-    first = jnp.asarray(plane_of)[me] == 0
-    both = jnp.where(first, jnp.stack([mine, other], axis=1), jnp.stack([other, mine], axis=1))
-    return both.reshape((devices,) + block.shape)
+        blocks.append(moving)
+        shifts.append(step)
+    ring_table = jnp.asarray(np.array(planes, np.int32))
+    owners = [ring_table[plane, (spot + shift) % length] for shift in shifts]
+    if len(planes) > 1:
+        swap = list(zip(planes[0], planes[1])) + list(zip(planes[1], planes[0]))
+        blocks = blocks + [lax.ppermute(got, "dp", swap) for got in blocks]
+        owners = owners + [ring_table[1 - plane, (spot + shift) % length] for shift in shifts]
+    return blocks, jnp.stack(owners).astype(jnp.int32)
 
 
-def project(token_block, basis):
-    summed = lax.dot_general(
-        token_block, basis, (((1,), (1,)), ((), ())), preferred_element_type=jnp.float32
+def projection_kernel(count, hidden_cols, output_cols, rank_width):
+    def kernel(owners, *refs):
+        blocks = refs[:count]
+        hidden_ref, grad_ref, rows_ref, stacked, hidden_full, output_full = refs[count:]
+
+        @pl.when(pl.program_id(0) == 0)
+        def _():
+            for k in range(count):
+                stacked[owners[k]] = blocks[k][...]
+            for d in range(count):
+                hidden_full[:, d * hidden_cols:(d + 1) * hidden_cols] = stacked[d, :, :hidden_cols]
+                output_full[:, d * output_cols:(d + 1) * output_cols] = stacked[d, :, hidden_cols:]
+
+        dims = (((1,), (1,)), ((), ()))
+        left = lax.dot_general(hidden_ref[...], hidden_full[...], dims, preferred_element_type=jnp.float32)
+        right = lax.dot_general(grad_ref[...], output_full[...], dims, preferred_element_type=jnp.float32)
+        rows_ref[:, :rank_width] = left.astype(jnp.bfloat16)
+        rows_ref[:, rank_width:] = right.astype(jnp.bfloat16)
+
+    return kernel
+
+
+def project_rows(blocks, owners, hidden, out_grad):
+    count = len(blocks)
+    rank_width, width = blocks[0].shape
+    local_tokens, features = hidden.shape
+    outputs = out_grad.shape[1]
+    tile = 128 if local_tokens % 128 == 0 else local_tokens
+    whole = pl.BlockSpec((rank_width, width), lambda i, owners: (0, 0))
+    grid_spec = pltpu.PrefetchScalarGridSpec(
+        num_scalar_prefetch=1,
+        grid=(local_tokens // tile,),
+        in_specs=[whole] * count + [
+            pl.BlockSpec((tile, features), lambda i, owners: (i, 0)),
+            pl.BlockSpec((tile, outputs), lambda i, owners: (i, 0)),
+        ],
+        out_specs=pl.BlockSpec((tile, 2 * rank_width), lambda i, owners: (i, 0)),
+        scratch_shapes=[
+            pltpu.VMEM((count, rank_width, width), jnp.bfloat16),
+            pltpu.VMEM((rank_width, features), jnp.bfloat16),
+            pltpu.VMEM((rank_width, outputs), jnp.bfloat16),
+        ],
     )
-    return summed.astype(jnp.bfloat16)
+    return pl.pallas_call(
+        projection_kernel(count, features // count, outputs // count, rank_width),
+        grid_spec=grid_spec,
+        out_shape=jax.ShapeDtypeStruct((local_tokens, 2 * rank_width), jnp.bfloat16),
+        compiler_params=pltpu.CompilerParams(dimension_semantics=("arbitrary",)),
+    )(owners, *blocks, hidden, out_grad)
 
 
 def local(hidden, out_grad, hidden_basis, output_basis, owner_ids, doc_slot):
@@ -67,13 +111,9 @@
     local_tokens = hidden.shape[0]
     capacity = 2 * local_tokens // devices
     rank_width = hidden_basis.shape[0]
-    hidden_cols = hidden_basis.shape[1]
     buffer_len = devices * capacity
-    stacked = ring_gather(jnp.concatenate([hidden_basis, output_basis], axis=1), devices)
-    hidden_full = stacked[:, :, :hidden_cols].transpose(1, 0, 2).reshape(rank_width, -1)
-    output_full = stacked[:, :, hidden_cols:].transpose(1, 0, 2).reshape(rank_width, -1)
-    left = project(hidden, hidden_full)
-    right = project(out_grad, output_full)
+    blocks, owners = ring_gather(jnp.concatenate([hidden_basis, output_basis], axis=1), devices)
+    rows = project_rows(blocks, owners, hidden, out_grad)
     targets = owner_ids[:, 0]
     member = (targets[:, None] == jnp.arange(devices, dtype=jnp.int32)[None, :]).astype(jnp.bfloat16)
     token_ids = jnp.arange(local_tokens, dtype=jnp.int32)
@@ -86,7 +126,6 @@
     dispatch = (
         jnp.arange(buffer_len, dtype=jnp.int32)[:, None] == slot_index[None, :]
     ).astype(jnp.bfloat16)
-    rows = jnp.concatenate([left, right], axis=1)
     buffer = lax.dot_general(
         dispatch, rows, (((1,), (0,)), ((), ())), preferred_element_type=jnp.float32
     ).astype(jnp.bfloat16)

time: 73.3 us -> 74.2 us (1.012)
  Pallas kernels: 0 us -> 9.31 us
  between operations: 0.8 us -> 9.06 us
  matrix products: 10.3 us -> 2.19 us
  other arithmetic: 7.64 us -> 3.25 us
  local copies, waits for them, and re-layouts: 20.5 us -> 17.6 us
  waiting for transfers between devices: 17.5 us -> 15.8 us
    another operation x1, local copies, waits for them, and re-layouts: 0.66 us -> 10.7 us  [ring_gather(): return (blocks, jnp.stack(owners).astype(jnp.int32))]
    pallas_call x0 -> x1, Pallas kernels: none -> 9.31 us  [project_rows(): pl.pallas_call(projection_kernel(count, features // count, outputs // cou...]
    dot_general x2 -> x0, matrix products: 8.29 us -> none  [project(): lax.dot_general(token_block, basis, (((1,), (1,)), ((), ())), preferred_e...]
    reshape x2 -> x0, local copies, waits for them, and re-layouts: 5.09 us -> none  [the longest x1 4.26 us: local(): stacked[:, :, :hidden_cols].transpose(1, 0, 2).reshape(rank_width, -1)]
    select_n x2 -> x0, other arithmetic: 3.95 us -> none  [the longest x1 2.64 us: ring_gather(): jnp.where(first, jnp.stack([mine, other], axis=1), jnp.stack([other, mine...]
    ppermute x4, waiting for transfers between devices: 6.91 us -> 3.49 us  [ring_gather(): moving = lax.ppermute(moving, 'dp', forward)]
    unnamed x17 -> x32, local copies, waits for them, and re-layouts: 4.2 us -> 1.35 us
    gather x1 -> x0, local copies, waits for them, and re-layouts: 2.8 us -> none  [ring_gather(): mine = by_distance[(spot - jnp.asarray(chip_spot)) % length]]
  transfers between devices with their start and end apart: 9 -> 16, of which waited for: 5 -> 4; matrix products, arithmetic and copies ran while one was open for 11% -> 23% of each run, Pallas kernels for 0% -> 0%
where the time goes in v4:
time: 74.2 us; the launch traced here: 73.6 us
  local copies, waits for them, and re-layouts  17.6 us (24%)
  starting transfers between devices  16.4 us (22%)
  waiting for transfers between devices  15.8 us (21%)
  Pallas kernels  9.31 us (13%)
  between operations  9.06 us (12%)
  other arithmetic  3.25 us (4%)
  matrix products  2.19 us (3%)
    another operation x1, local copies, waits for them, and re-layouts, ring_gather(): return (blocks, jnp.stack(owners).astype(jnp.int32))  10.7 us
    all_to_all x1, waiting for transfers between devices, local(): arrived = lax.all_to_all(packed, 'dp', 0, 0, tiled=True)  9.51 us
    pallas_call x1, Pallas kernels, project_rows(): pl.pallas_call(projection_kernel(count, features // count, outputs // cou...  9.31 us
    ppermute x4, starting transfers between devices, ring_gather(): moving = lax.ppermute(moving, 'dp', forward)  8.74 us
    all_to_all x1, starting transfers between devices, local(): arrived = lax.all_to_all(packed, 'dp', 0, 0, tiled=True)  5.72 us
    ppermute x4, waiting for transfers between devices, ring_gather(): moving = lax.ppermute(moving, 'dp', forward)  3.49 us
    ppermute x3, waiting for transfers between devices, ring_gather(): moving = lax.ppermute(moving, 'dp', backward)  2.76 us
    dynamic_slice x1, local copies, waits for them, and re-layouts, ring_gather(): ring_table[1 - plane, (spot + shift) % length]  2 us
  transfers between devices with their start and end apart: 16, of which 4 were waited for; matrix products, arithmetic and copies ran while one was open for 23% of the time, Pallas kernels for 0%

profile of v4, /device:TPU:0, one launch (start us, length us, event | category | flops | bytes accessed | tf_op | source)
XLA Modules:
  0.0 73.6 jit_solution(5404754062304821884)
XLA Ops:
  0.0 1.0 %pad_maximum_fusion.refs_0_ = bf16[64,944]{1,0:T(8,128)(2,1)S(1)} fusion(bf16[64,256]{1,0:T(8,128)(2,1)} %param.12, bf16[64,688]{1,0:T(8,128)(2,1)} %param.11), kind=kLoop, calls=%fused_computation.16 | loop fusion | flops 241664 | bytes 241664 | tf_op jit(solution)/shard_map/concatenate | solution.py:115
  1.0 3.1 %collective-permute-start = (bf16[64,944]{1,0:T(8,128)(2,1)S(1)}, bf16[64,944]{1,0:T(8,128)(2,1)S(1)}, u32[]{:S(2)}, u32[]{:S(2)}) collective-permute-start(bf16[64,944]{1,0:T(8,128)(2,1)S(1)} %pad_maximum_fusion.refs_0_), channel_id=1, source_target_pairs={{0,4},{4,8},{8,12},{12,14},{14,10},{10,6},{6,2},{2,0},{1,5},{5,9},... | collective-permute-start | bytes 362504 | tf_op jit(solution)/shard_map/ppermute | solution.py:41
  4.1 1.2 %dynamic_slice.55 = s32[1]{0:T(128)} dynamic-slice(s32[16]{0:T(128)} %constant.93.clone, s32[]{:T(128)S(6)} %select_n.107), dynamic_slice_sizes={1} | dynamic-slice | bytes 12 | tf_op jit(solution)/shard_map/dynamic_slice | solution.py:33
  8.7 2.1 %collective-permute-start.1 = (bf16[64,944]{1,0:T(8,128)(2,1)S(1)}, bf16[64,944]{1,0:T(8,128)(2,1)S(1)}, u32[]{:S(2)}, u32[]{:S(2)}) collective-permute-start(bf16[64,944]{1,0:T(8,128)(2,1)S(1)} %collective-permute-done.refs_1_), channel_id=1, source_target_pairs={{0,4},{4,8},{8,12},{12,14},{14,10},{10,6},{6,2},{2,0},{1,5},{5,9},... | collective-permute-start | bytes 362504 | tf_op jit(solution)/shard_map/ppermute | solution.py:41
  10.7 0.7 add_convert_fusion
  11.4 3.4 %collective-permute-done.1.refs_2_ = bf16[64,944]{1,0:T(8,128)(2,1)S(1)} collective-permute-done((bf16[64,944]{1,0:T(8,128)(2,1)S(1)}, bf16[64,944]{1,0:T(8,128)(2,1)S(1)}, u32[]{:S(2)}, u32[]{:S(2)}) %collective-permute-start.1) | collective-permute-done | bytes 120864 | tf_op jit(solution)/shard_map/ppermute | solution.py:41
  14.8 1.8 %collective-permute-start.2 = (bf16[64,944]{1,0:T(8,128)(2,1)S(1)}, bf16[64,944]{1,0:T(8,128)(2,1)S(1)}, u32[]{:S(2)}, u32[]{:S(2)}) collective-permute-start(bf16[64,944]{1,0:T(8,128)(2,1)S(1)} %collective-permute-done.1.refs_2_), channel_id=1, source_target_pairs={{0,4},{4,8},{8,12},{12,14},{14,10},{10,6},{6,2},{2,0},{1,5},{5,9},... | collective-permute-start | bytes 362504 | tf_op jit(solution)/shard_map/ppermute | solution.py:41
  18.9 1.3 %dynamic_slice.54 = s32[1]{0:T(128)} dynamic-slice(s32[16]{0:T(128)} %constant.94.clone, s32[]{:T(128)S(6)} %select_n.107), dynamic_slice_sizes={1} | dynamic-slice | bytes 12 | tf_op jit(solution)/shard_map/dynamic_slice | solution.py:34
  22.8 0.7 reduce
  23.7 0.5 collective-permute-start.8
  24.5 1.8 %collective-permute-start.3 = (bf16[64,944]{1,0:T(8,128)(2,1)S(1)}, bf16[64,944]{1,0:T(8,128)(2,1)S(1)}, u32[]{:S(2)}, u32[]{:S(2)}) collective-permute-start(bf16[64,944]{1,0:T(8,128)(2,1)S(1)} %collective-permute-done.2.refs_3_), channel_id=1, source_target_pairs={{0,4},{4,8},{8,12},{12,14},{14,10},{10,6},{6,2},{2,0},{1,5},{5,9},... | collective-permute-start | bytes 362504 | tf_op jit(solution)/shard_map/ppermute | solution.py:41
  26.4 0.5 collective-permute-start.9
  27.0 2.8 %collective-permute-done.6.refs_7_ = bf16[64,944]{1,0:T(8,128)(2,1)S(1)} collective-permute-done((bf16[64,944]{1,0:T(8,128)(2,1)S(1)}, bf16[64,944]{1,0:T(8,128)(2,1)S(1)}, u32[]{:S(2)}, u32[]{:S(2)}) %collective-permute-start.6) | collective-permute-done | bytes 120864 | tf_op jit(solution)/shard_map/ppermute | solution.py:46
  31.3 2.0 %fusion.13 = (s32[1,1]{1,0:T(1,128)}, s32[1,1]{1,0:T(1,128)}, s32[1,1]{1,0:T(1,128)}, s32[1,1]{1,0:T(1,128)}, s32[1,1]{1,0:T(1,128)}, /*index=5*/s32[1,1]{1,0:T(...) fusion(s32[2,8]{1,0:T(2,128)} %constant.95.clone, ...), kind=kLoop, calls=%fused_computation.25 | loop fusion | bytes 168 | tf_op jit(solution)/shard_map/dynamic_slice | solution.py:54
  33.3 10.7 %stack.3.owners = s32[16]{0:T(128)} concatenate(s32[1]{0:T(128)} %bitcast.2, s32[1]{0:T(128)} %bitcast.3, s32[1]{0:T(128)} %bitcast.4, s32[1]{0:T(128)} %bitcast.5, s32[1]{0:T(128)} %bitcast.6, s32[1]{0:T(128)} %bitcast.7, s32[1]{0:T(128)} %bitcast.8, s32[1]{0:T(128)} %bitcast.9, s32[1]{0:T(128)} %bitcast.10, s32[1]{0:T(128)} %bitcast.11, s32[1]{0:T(128)} %bitcast.12, ...), dimensions={0} | concatenate | bytes 128 | tf_op jit(solution)/shard_map/stack | solution.py:55
  44.2 0.5 copy-done.11
  44.8 0.7 copy-done.15
  45.5 9.3 %shard_map.91 = bf16[384,128]{1,0:T(8,128)(2,1)} custom-call(s32[16]{0:T(128)} %stack.3.owners, bf16[64,944]{1,0:T(8,128)(2,1)} %copy-done, bf16[64,944]{1,0:T(8,128)(2,1)} %copy-done.1, bf16[64,944]{1,0:T(8,128)(2,1)} %copy-done.4, bf16[64,944]{1,0:T(8,128)(2,1)} %copy-done.6, bf16[64,944]{1,0:T(8,128)(2,1)} %copy-done.10, bf16[64,944]{1,0:T(8,128)(2,1)} %copy-done.2, ...), custom_call_target="tpu_custom_call" | custom-call | tf_op jit(solution)/shard_map/pallas_call | solution.py:101
  54.8 1.2 %fusion.2 = bf16[768,128]{1,0:T(8,128)(2,1)S(1)} fusion(bf16[384,128]{1,0:T(8,128)(2,1)} %shard_map.91, s32[384]{0:T(512)S(1)} %convert_add_fusion), kind=kOutput, calls=%fused_computation.3 | convolution fusion | flops 75890688 | bytes 296448 | tf_op jit(solution)/shard_map/dot_general | solution.py:129
  56.0 0.7 fusion.8
  56.7 5.7 %all-to-all-start = ((bf16[16,49,128]{2,1,0:T(8,128)(2,1)}), bf16[16,49,128]{2,1,0:T(8,128)(2,1)S(1)}, u32[]{:S(2)}, u32[]{:S(2)}) async-start(bf16[16,49,128]{2,1,0:T(8,128)(2,1)} %fusion.8), calls=%async_computation | async-start | bytes 458752 | tf_op jit(solution)/shard_map/all_to_all | solution.py:139
  62.4 9.5 %all-to-all-done = bf16[16,49,128]{2,1,0:T(8,128)(2,1)S(1)} async-done(((bf16[16,49,128]{2,1,0:T(8,128)(2,1)}), bf16[16,49,128]{2,1,0:T(8,128)(2,1)S(1)}, u32[]{:S(2)}, u32[]{:S(2)}) %all-to-all-start) | async-done | bytes 200736 | tf_op jit(solution)/shard_map/all_to_all | solution.py:139
  72.4 0.4 fusion.9
  72.8 0.8 %reshape.66 = f32[8,4096]{1,0:T(8,128)} reshape(f32[512,64]{1,0:T(8,128)S(1)} %fusion.9) | data formatting | bytes 262144 | tf_op jit(solution)/shard_map/reshape | solution.py:150
  (64 shorter events, 2.3 us)
Async XLA Ops:
  1.0 43.0 %copy-start = (bf16[64,944]{1,0:T(8,128)(2,1)}, bf16[64,944]{1,0:T(8,128)(2,1)S(1)}, u32[]{:S(2)}) copy-start(bf16[64,944]{1,0:T(8,128)(2,1)S(1)} %pad_maximum_fusion.refs_0_) | copy-start | bytes 362500
  1.0 7.6 %collective-permute-start = (bf16[64,944]{1,0:T(8,128)(2,1)S(1)}, bf16[64,944]{1,0:T(8,128)(2,1)S(1)}, u32[]{:S(2)}, u32[]{:S(2)}) collective-permute-start(bf16[64,944]{1,0:T(8,128)(2,1)S(1)} %pad_maximum_fusion.refs_0_), channel_id=1, source_target_pairs={{0,4},{4,8},{8,12},{12,14},{14,10},{10,6},{6,2},{2,0},{1,5},{5,9},... | collective-permute-start | bytes 362504 | tf_op jit(solution)/shard_map/ppermute | solution.py:41
  4.1 7.3 %collective-permute-start.4 = (bf16[64,944]{1,0:T(8,128)(2,1)S(1)}, bf16[64,944]{1,0:T(8,128)(2,1)S(1)}, u32[]{:S(2)}, u32[]{:S(2)}) collective-permute-start(bf16[64,944]{1,0:T(8,128)(2,1)S(1)} %pad_maximum_fusion.refs_0_), channel_id=1, source_target_pairs={{0,2},{4,0},{8,4},{12,8},{14,12},{10,14},{6,10},{2,6},{1,3},{5,1},... | collective-permute-start | bytes 362504 | tf_op jit(solution)/shard_map/ppermute | solution.py:46
  4.1 22.2 %collective-permute-start.7 = (bf16[64,944]{1,0:T(8,128)(2,1)S(1)}, bf16[64,944]{1,0:T(8,128)(2,1)S(1)}, u32[]{:S(2)}, u32[]{:S(2)}) collective-permute-start(bf16[64,944]{1,0:T(8,128)(2,1)S(1)} %pad_maximum_fusion.refs_0_), channel_id=1, source_target_pairs={{0,1},{4,5},{8,9},{12,13},{14,15},{10,11},{6,7},{2,3},{1,0},{5,4},... | collective-permute-start | bytes 362504 | tf_op jit(solution)/shard_map/ppermute | solution.py:53
  8.7 35.4 %copy-start.1 = (bf16[64,944]{1,0:T(8,128)(2,1)}, bf16[64,944]{1,0:T(8,128)(2,1)S(1)}, u32[]{:S(2)}) copy-start(bf16[64,944]{1,0:T(8,128)(2,1)S(1)} %collective-permute-done.refs_1_) | copy-start | bytes 362500
  8.7 6.2 %collective-permute-start.1 = (bf16[64,944]{1,0:T(8,128)(2,1)S(1)}, bf16[64,944]{1,0:T(8,128)(2,1)S(1)}, u32[]{:S(2)}, u32[]{:S(2)}) collective-permute-start(bf16[64,944]{1,0:T(8,128)(2,1)S(1)} %collective-permute-done.refs_1_), channel_id=1, source_target_pairs={{0,4},{4,8},{8,12},{12,14},{14,10},{10,6},{6,2},{2,0},{1,5},{5,9},... | collective-permute-start | bytes 362504 | tf_op jit(solution)/shard_map/ppermute | solution.py:41
  11.4 32.6 %copy-start.2 = (bf16[64,944]{1,0:T(8,128)(2,1)}, bf16[64,944]{1,0:T(8,128)(2,1)S(1)}, u32[]{:S(2)}) copy-start(bf16[64,944]{1,0:T(8,128)(2,1)S(1)} %collective-permute-done.4.refs_5_) | copy-start | bytes 362500
  11.4 12.8 %collective-permute-start.5 = (bf16[64,944]{1,0:T(8,128)(2,1)S(1)}, bf16[64,944]{1,0:T(8,128)(2,1)S(1)}, u32[]{:S(2)}, u32[]{:S(2)}) collective-permute-start(bf16[64,944]{1,0:T(8,128)(2,1)S(1)} %collective-permute-done.4.refs_5_), channel_id=1, source_target_pairs={{0,2},{4,0},{8,4},{12,8},{14,12},{10,14},{6,10},{2,6},{1,3},{5,1},... | collective-permute-start | bytes 362504 | tf_op jit(solution)/shard_map/ppermute | solution.py:46
  14.8 29.2 %copy-start.4 = (bf16[64,944]{1,0:T(8,128)(2,1)}, bf16[64,944]{1,0:T(8,128)(2,1)S(1)}, u32[]{:S(2)}) copy-start(bf16[64,944]{1,0:T(8,128)(2,1)S(1)} %collective-permute-done.1.refs_2_) | copy-start | bytes 362500
  14.8 9.6 %collective-permute-start.2 = (bf16[64,944]{1,0:T(8,128)(2,1)S(1)}, bf16[64,944]{1,0:T(8,128)(2,1)S(1)}, u32[]{:S(2)}, u32[]{:S(2)}) collective-permute-start(bf16[64,944]{1,0:T(8,128)(2,1)S(1)} %collective-permute-done.1.refs_2_), channel_id=1, source_target_pairs={{0,4},{4,8},{8,12},{12,14},{14,10},{10,6},{6,2},{2,0},{1,5},{5,9},... | collective-permute-start | bytes 362504 | tf_op jit(solution)/shard_map/ppermute | solution.py:41
  23.7 2.7 %collective-permute-start.12 = (bf16[64,944]{1,0:T(8,128)(2,1)S(1)}, bf16[64,944]{1,0:T(8,128)(2,1)S(1)}, u32[]{:S(2)}, u32[]{:S(2)}) collective-permute-start(bf16[64,944]{1,0:T(8,128)(2,1)S(1)} %collective-permute-done.4.refs_5_), channel_id=1, source_target_pairs={{0,1},{4,5},{8,9},{12,13},{14,15},{10,11},{6,7},{2,3},{1,0},{5,4},... | collective-permute-start | bytes 362504 | tf_op jit(solution)/shard_map/ppermute | solution.py:53
  23.7 3.1 %collective-permute-start.8 = (bf16[64,944]{1,0:T(8,128)(2,1)S(1)}, bf16[64,944]{1,0:T(8,128)(2,1)S(1)}, u32[]{:S(2)}, u32[]{:S(2)}) collective-permute-start(bf16[64,944]{1,0:T(8,128)(2,1)S(1)} %collective-permute-done.refs_1_), channel_id=1, source_target_pairs={{0,1},{4,5},{8,9},{12,13},{14,15},{10,11},{6,7},{2,3},{1,0},{5,4},... | collective-permute-start | bytes 362504 | tf_op jit(solution)/shard_map/ppermute | solution.py:53
  24.2 19.8 %copy-start.5 = (bf16[64,944]{1,0:T(8,128)(2,1)}, bf16[64,944]{1,0:T(8,128)(2,1)S(1)}, u32[]{:S(2)}) copy-start(bf16[64,944]{1,0:T(8,128)(2,1)S(1)} %collective-permute-done.5.refs_6_) | copy-start | bytes 362500
  24.2 5.5 %collective-permute-start.6 = (bf16[64,944]{1,0:T(8,128)(2,1)S(1)}, bf16[64,944]{1,0:T(8,128)(2,1)S(1)}, u32[]{:S(2)}, u32[]{:S(2)}) collective-permute-start(bf16[64,944]{1,0:T(8,128)(2,1)S(1)} %collective-permute-done.5.refs_6_), channel_id=1, source_target_pairs={{0,2},{4,0},{8,4},{12,8},{14,12},{10,14},{6,10},{2,6},{1,3},{5,1},... | collective-permute-start | bytes 362504 | tf_op jit(solution)/shard_map/ppermute | solution.py:46
  24.5 19.6 %copy-start.6 = (bf16[64,944]{1,0:T(8,128)(2,1)}, bf16[64,944]{1,0:T(8,128)(2,1)S(1)}, u32[]{:S(2)}) copy-start(bf16[64,944]{1,0:T(8,128)(2,1)S(1)} %collective-permute-done.2.refs_3_) | copy-start | bytes 362500
  24.5 5.3 %collective-permute-start.3 = (bf16[64,944]{1,0:T(8,128)(2,1)S(1)}, bf16[64,944]{1,0:T(8,128)(2,1)S(1)}, u32[]{:S(2)}, u32[]{:S(2)}) collective-permute-start(bf16[64,944]{1,0:T(8,128)(2,1)S(1)} %collective-permute-done.2.refs_3_), channel_id=1, source_target_pairs={{0,4},{4,8},{8,12},{12,14},{14,10},{10,6},{6,2},{2,0},{1,5},{5,9},... | collective-permute-start | bytes 362504 | tf_op jit(solution)/shard_map/ppermute | solution.py:41
  26.3 17.8 %copy-start.3 = (bf16[64,944]{1,0:T(8,128)(2,1)}, bf16[64,944]{1,0:T(8,128)(2,1)S(1)}, u32[]{:S(2)}) copy-start(bf16[64,944]{1,0:T(8,128)(2,1)S(1)} %collective-permute-done.7.refs_8_) | copy-start | bytes 362500
  26.3 17.7 %collective-permute-start.13 = (bf16[64,944]{1,0:T(8,128)(2,1)S(1)}, bf16[64,944]{1,0:T(8,128)(2,1)S(1)}, u32[]{:S(2)}, u32[]{:S(2)}) collective-permute-start(bf16[64,944]{1,0:T(8,128)(2,1)S(1)} %collective-permute-done.5.refs_6_), channel_id=1, source_target_pairs={{0,1},{4,5},{8,9},{12,13},{14,15},{10,11},{6,7},{2,3},{1,0},{5,4},... | collective-permute-start | bytes 362504 | tf_op jit(solution)/shard_map/ppermute | solution.py:53
  26.4 17.7 %copy-start.7 = (bf16[64,944]{1,0:T(8,128)(2,1)}, bf16[64,944]{1,0:T(8,128)(2,1)S(1)}, u32[]{:S(2)}) copy-start(bf16[64,944]{1,0:T(8,128)(2,1)S(1)} %collective-permute-done.12.refs_13_) | copy-start | bytes 362500
  26.4 17.6 %collective-permute-start.9 = (bf16[64,944]{1,0:T(8,128)(2,1)S(1)}, bf16[64,944]{1,0:T(8,128)(2,1)S(1)}, u32[]{:S(2)}, u32[]{:S(2)}) collective-permute-start(bf16[64,944]{1,0:T(8,128)(2,1)S(1)} %collective-permute-done.1.refs_2_), channel_id=1, source_target_pairs={{0,1},{4,5},{8,9},{12,13},{14,15},{10,11},{6,7},{2,3},{1,0},{5,4},... | collective-permute-start | bytes 362504 | tf_op jit(solution)/shard_map/ppermute | solution.py:53
  26.9 17.1 %collective-permute-start.10 = (bf16[64,944]{1,0:T(8,128)(2,1)S(1)}, bf16[64,944]{1,0:T(8,128)(2,1)S(1)}, u32[]{:S(2)}, u32[]{:S(2)}) collective-permute-start(bf16[64,944]{1,0:T(8,128)(2,1)S(1)} %collective-permute-done.2.refs_3_), channel_id=1, source_target_pairs={{0,1},{4,5},{8,9},{12,13},{14,15},{10,11},{6,7},{2,3},{1,0},{5,4},... | collective-permute-start | bytes 362504 | tf_op jit(solution)/shard_map/ppermute | solution.py:53
  29.7 14.3 %collective-permute-start.14 = (bf16[64,944]{1,0:T(8,128)(2,1)S(1)}, bf16[64,944]{1,0:T(8,128)(2,1)S(1)}, u32[]{:S(2)}, u32[]{:S(2)}) collective-permute-start(bf16[64,944]{1,0:T(8,128)(2,1)S(1)} %collective-permute-done.6.refs_7_), channel_id=1, source_target_pairs={{0,1},{4,5},{8,9},{12,13},{14,15},{10,11},{6,7},{2,3},{1,0},{5,4},... | collective-permute-start | bytes 362504 | tf_op jit(solution)/shard_map/ppermute | solution.py:53
  29.8 14.2 %collective-permute-start.11 = (bf16[64,944]{1,0:T(8,128)(2,1)S(1)}, bf16[64,944]{1,0:T(8,128)(2,1)S(1)}, u32[]{:S(2)}, u32[]{:S(2)}) collective-permute-start(bf16[64,944]{1,0:T(8,128)(2,1)S(1)} %collective-permute-done.3.refs_4_), channel_id=1, source_target_pairs={{0,1},{4,5},{8,9},{12,13},{14,15},{10,11},{6,7},{2,3},{1,0},{5,4},... | collective-permute-start | bytes 362504 | tf_op jit(solution)/shard_map/ppermute | solution.py:53
  56.7 15.2 %all-to-all-start = ((bf16[16,49,128]{2,1,0:T(8,128)(2,1)}), bf16[16,49,128]{2,1,0:T(8,128)(2,1)S(1)}, u32[]{:S(2)}, u32[]{:S(2)}) async-start(bf16[16,49,128]{2,1,0:T(8,128)(2,1)} %fusion.8), calls=%async_computation | async-start | bytes 458752 | tf_op jit(solution)/shard_map/all_to_all | solution.py:139
  (8 other events, 49.6 us)

commit v5 on v4

--- a/solution.py
+++ b/solution.py
@@ -46,25 +46,34 @@
         moving = lax.ppermute(moving, "dp", backward)
         blocks.append(moving)
         shifts.append(step)
-    ring_table = jnp.asarray(np.array(planes, np.int32))
-    owners = [ring_table[plane, (spot + shift) % length] for shift in shifts]
-    if len(planes) > 1:
-        swap = list(zip(planes[0], planes[1])) + list(zip(planes[1], planes[0]))
-        blocks = blocks + [lax.ppermute(got, "dp", swap) for got in blocks]
-        owners = owners + [ring_table[1 - plane, (spot + shift) % length] for shift in shifts]
-    return blocks, jnp.stack(owners).astype(jnp.int32)
+    spots = (spot + jnp.asarray(np.array(shifts, np.int32))) % length
+    chips = jnp.asarray(np.array(planes[0], np.int32) // len(planes))
+    hit = spots[:, None] == jnp.arange(length, dtype=jnp.int32)[None, :]
+    chip_of = jnp.sum(jnp.where(hit, chips[None, :], 0), axis=1)
+    if len(planes) == 1:
+        return blocks, None, chip_of.astype(jnp.int32)
+    mine = jnp.stack(blocks)
+    swap = list(zip(planes[0], planes[1])) + list(zip(planes[1], planes[0]))
+    other = lax.ppermute(mine, "dp", swap)
+    owners = jnp.concatenate([chip_of * 2 + plane, chip_of * 2 + 1 - plane])
+    return blocks, other, owners.astype(jnp.int32)
 
 
-def projection_kernel(count, hidden_cols, output_cols, rank_width):
+def projection_kernel(count, devices, hidden_cols, output_cols, rank_width, paired):
     def kernel(owners, *refs):
         blocks = refs[:count]
-        hidden_ref, grad_ref, rows_ref, stacked, hidden_full, output_full = refs[count:]
+        rest = refs[count:]
+        if paired:
+            other_ref, rest = rest[0], rest[1:]
+        hidden_ref, grad_ref, rows_ref, stacked, hidden_full, output_full = rest
 
         @pl.when(pl.program_id(0) == 0)
         def _():
             for k in range(count):
                 stacked[owners[k]] = blocks[k][...]
-            for d in range(count):
+                if paired:
+                    stacked[owners[count + k]] = other_ref[k]
+            for d in range(devices):
                 hidden_full[:, d * hidden_cols:(d + 1) * hidden_cols] = stacked[d, :, :hidden_cols]
                 output_full[:, d * output_cols:(d + 1) * output_cols] = stacked[d, :, hidden_cols:]
 
@@ -77,8 +86,9 @@
     return kernel
 
 
-def project_rows(blocks, owners, hidden, out_grad):
+def project_rows(blocks, other, owners, hidden, out_grad, devices):
     count = len(blocks)
+    paired = other is not None
     rank_width, width = blocks[0].shape
     local_tokens, features = hidden.shape
     outputs = out_grad.shape[1]
@@ -87,23 +97,23 @@
     grid_spec = pltpu.PrefetchScalarGridSpec(
         num_scalar_prefetch=1,
         grid=(local_tokens // tile,),
-        in_specs=[whole] * count + [
+        in_specs=[whole] * count + [pl.BlockSpec((count, rank_width, width), lambda i, owners: (0, 0, 0))] * paired + [
             pl.BlockSpec((tile, features), lambda i, owners: (i, 0)),
             pl.BlockSpec((tile, outputs), lambda i, owners: (i, 0)),
         ],
         out_specs=pl.BlockSpec((tile, 2 * rank_width), lambda i, owners: (i, 0)),
         scratch_shapes=[
-            pltpu.VMEM((count, rank_width, width), jnp.bfloat16),
+            pltpu.VMEM((devices, rank_width, width), jnp.bfloat16),
             pltpu.VMEM((rank_width, features), jnp.bfloat16),
             pltpu.VMEM((rank_width, outputs), jnp.bfloat16),
         ],
     )
     return pl.pallas_call(
-        projection_kernel(count, features // count, outputs // count, rank_width),
+        projection_kernel(count, devices, features // devices, outputs // devices, rank_width, paired),
         grid_spec=grid_spec,
         out_shape=jax.ShapeDtypeStruct((local_tokens, 2 * rank_width), jnp.bfloat16),
         compiler_params=pltpu.CompilerParams(dimension_semantics=("arbitrary",)),
-    )(owners, *blocks, hidden, out_grad)
+    )(owners, *blocks, *([other] if paired else []), hidden, out_grad)
 
 
 def local(hidden, out_grad, hidden_basis, output_basis, owner_ids, doc_slot):
@@ -112,8 +122,8 @@
     capacity = 2 * local_tokens // devices
     rank_width = hidden_basis.shape[0]
     buffer_len = devices * capacity
-    blocks, owners = ring_gather(jnp.concatenate([hidden_basis, output_basis], axis=1), devices)
-    rows = project_rows(blocks, owners, hidden, out_grad)
+    blocks, other, owners = ring_gather(jnp.concatenate([hidden_basis, output_basis], axis=1), devices)
+    rows = project_rows(blocks, other, owners, hidden, out_grad, devices)
     targets = owner_ids[:, 0]
     member = (targets[:, None] == jnp.arange(devices, dtype=jnp.int32)[None, :]).astype(jnp.bfloat16)
     token_ids = jnp.arange(local_tokens, dtype=jnp.int32)

time: 74.2 us -> 57.7 us (0.78)
  local copies, waits for them, and re-layouts: 17.6 us -> 4.75 us
  between operations: 9.06 us -> 0.26 us
  other arithmetic: 3.25 us -> 6.26 us
  waiting for transfers between devices: 15.8 us -> 18.5 us
    another operation x1, local copies, waits for them, and re-layouts: 10.7 us -> 0.01 us  [ring_gather(): mine = jnp.stack(blocks)]
    ppermute x4, waiting for transfers between devices: 3.49 us -> 8.8 us  [ring_gather(): moving = lax.ppermute(moving, 'dp', forward)]
    ppermute x3, waiting for transfers between devices: 2.76 us -> 0.01 us  [ring_gather(): moving = lax.ppermute(moving, 'dp', backward)]
    dynamic_slice x1 -> x0, local copies, waits for them, and re-layouts: 2 us -> none  [ring_gather(): ring_table[1 - plane, (spot + shift) % length]]
    ppermute x8 -> x1, starting transfers between devices: 1.66 us -> 0.07 us  [ring_gather(): other = lax.ppermute(mine, 'dp', swap)]
    unnamed x1 -> x2, other arithmetic: 0.7 us -> 1.7 us
    ppermute x4, starting transfers between devices: 8.74 us -> 9.5 us  [ring_gather(): moving = lax.ppermute(moving, 'dp', forward)]
  transfers between devices with their start and end apart: 16 -> 9, of which waited for: 4 -> 5; matrix products, arithmetic and copies ran while one was open for 23% -> 13% of each run, Pallas kernels for 0% -> 0%
where the time goes in v5:
time: 57.7 us; the launch traced here: 57.4 us
  waiting for transfers between devices  18.5 us (32%)
  starting transfers between devices  16.1 us (28%)
  Pallas kernels  9.33 us (16%)
  other arithmetic  6.26 us (11%)
  local copies, waits for them, and re-layouts  4.75 us (8%)
  matrix products  2.2 us (4%)
    all_to_all x1, waiting for transfers between devices, local(): arrived = lax.all_to_all(packed, 'dp', 0, 0, tiled=True)  9.51 us
    ppermute x4, starting transfers between devices, ring_gather(): moving = lax.ppermute(moving, 'dp', forward)  9.5 us
    pallas_call x1, Pallas kernels, project_rows(): pl.pallas_call(projection_kernel(count, devices, features // devices, out...  9.33 us
    ppermute x4, waiting for transfers between devices, ring_gather(): moving = lax.ppermute(moving, 'dp', forward)  8.8 us
    all_to_all x1, starting transfers between devices, local(): arrived = lax.all_to_all(packed, 'dp', 0, 0, tiled=True)  6.44 us
    unnamed x2, other arithmetic  1.7 us
    dynamic_slice x1, local copies, waits for them, and re-layouts, ring_gather(): plane = jnp.asarray(plane_of)[me]  1.31 us
    dynamic_slice x1, local copies, waits for them, and re-layouts, ring_gather(): spot = jnp.asarray(place)[me]  1.24 us
  transfers between devices with their start and end apart: 9, of which 5 were waited for; matrix products, arithmetic and copies ran while one was open for 13% of the time, Pallas kernels for 0%

profile of v5, /device:TPU:0, one launch (start us, length us, event | category | flops | bytes accessed | tf_op | source)
XLA Modules:
  0.0 57.4 jit_solution(14782318502715631336)
XLA Ops:
  0.0 1.0 %pad_maximum_fusion.refs_0_ = bf16[64,944]{1,0:T(8,128)(2,1)S(1)} fusion(bf16[64,256]{1,0:T(8,128)(2,1)} %param.13, bf16[64,688]{1,0:T(8,128)(2,1)} %param.12), kind=kLoop, calls=%fused_computation.16 | loop fusion | flops 241664 | bytes 241664 | tf_op jit(solution)/shard_map/concatenate | solution.py:125
  1.0 3.1 %collective-permute-start = (bf16[64,944]{1,0:T(8,128)(2,1)S(1)}, bf16[64,944]{1,0:T(8,128)(2,1)S(1)}, u32[]{:S(2)}, u32[]{:S(2)}) collective-permute-start(bf16[64,944]{1,0:T(8,128)(2,1)S(1)} %pad_maximum_fusion.refs_0_), channel_id=1, source_target_pairs={{0,4},{4,8},{8,12},{12,14},{14,10},{10,6},{6,2},{2,0},{1,5},{5,9},... | collective-permute-start | bytes 362504 | tf_op jit(solution)/shard_map/ppermute | solution.py:41
  4.1 0.7 %add_convert_fusion = bf16[384]{0:T(512)(128)(2,1)S(1)} fusion(s32[384]{0:T(512)} %param.15), kind=kLoop, calls=%fused_computation.34 | loop fusion | flops 768 | bytes 2304 | tf_op jit(solution)/shard_map/convert_element_type | solution.py:143
  4.8 1.0 %bitcast_dynamic-update-slice_fusion.7 = bf16[8,64,944]{2,1,0:T(8,128)(2,1)S(1)} fusion(bf16[64,256]{1,0:T(8,128)(2,1)} %param.13, bf16[64,688]{1,0:T(8,128)(2,1)} %param.12), kind=kLoop, calls=%fused_computation.24 | loop fusion | flops 241663 | bytes 251904
  5.8 1.2 %dynamic_slice.6 = s32[1]{0:T(128)} dynamic-slice(s32[16]{0:T(128)} %constant.41.clone, s32[]{:T(128)S(6)} %select_n.15), dynamic_slice_sizes={1} | dynamic-slice | bytes 12 | tf_op jit(solution)/shard_map/dynamic_slice | solution.py:33
  7.1 1.3 %dynamic_slice.7 = s32[1]{0:T(128)} dynamic-slice(s32[16]{0:T(128)} %constant.42.clone, s32[]{:T(128)S(6)} %select_n.15), dynamic_slice_sizes={1} | dynamic-slice | bytes 12 | tf_op jit(solution)/shard_map/dynamic_slice | solution.py:34
  8.4 0.7 %reduce = s32[384]{0:T(512)S(1)} reduce(s32[384,1]{0,1:T(1,128)} %param.14, s32[]{:T(128)} %constant.34.clone.1), dimensions={1}, to_apply=%param.14.reduce_sub_computation | reduce | bytes 3076 | tf_op args[4]
  9.3 2.1 %collective-permute-start.1 = (bf16[64,944]{1,0:T(8,128)(2,1)S(1)}, bf16[64,944]{1,0:T(8,128)(2,1)S(1)}, u32[]{:S(2)}, u32[]{:S(2)}) collective-permute-start(bf16[64,944]{1,0:T(8,128)(2,1)S(1)} %collective-permute-done.refs_1_), channel_id=1, source_target_pairs={{0,4},{4,8},{8,12},{12,14},{14,10},{10,6},{6,2},{2,0},{1,5},{5,9},... | collective-permute-start | bytes 362504 | tf_op jit(solution)/shard_map/ppermute | solution.py:41
  11.4 2.9 %collective-permute-done.1.refs_2_ = bf16[64,944]{1,0:T(8,128)(2,1)S(1)} collective-permute-done((bf16[64,944]{1,0:T(8,128)(2,1)S(1)}, bf16[64,944]{1,0:T(8,128)(2,1)S(1)}, u32[]{:S(2)}, u32[]{:S(2)}) %collective-permute-start.1) | collective-permute-done | bytes 120864 | tf_op jit(solution)/shard_map/ppermute | solution.py:41
  14.3 2.0 %collective-permute-start.2 = (bf16[64,944]{1,0:T(8,128)(2,1)S(1)}, bf16[64,944]{1,0:T(8,128)(2,1)S(1)}, u32[]{:S(2)}, u32[]{:S(2)}) collective-permute-start(bf16[64,944]{1,0:T(8,128)(2,1)S(1)} %collective-permute-done.1.refs_2_), channel_id=1, source_target_pairs={{0,4},{4,8},{8,12},{12,14},{14,10},{10,6},{6,2},{2,0},{1,5},{5,9},... | collective-permute-start | bytes 362504 | tf_op jit(solution)/shard_map/ppermute | solution.py:41
  16.4 3.0 %collective-permute-done.2.refs_3_ = bf16[64,944]{1,0:T(8,128)(2,1)S(1)} collective-permute-done((bf16[64,944]{1,0:T(8,128)(2,1)S(1)}, bf16[64,944]{1,0:T(8,128)(2,1)S(1)}, u32[]{:S(2)}, u32[]{:S(2)}) %collective-permute-start.2) | collective-permute-done | bytes 120864 | tf_op jit(solution)/shard_map/ppermute | solution.py:41
  19.4 2.3 %collective-permute-start.3 = (bf16[64,944]{1,0:T(8,128)(2,1)S(1)}, bf16[64,944]{1,0:T(8,128)(2,1)S(1)}, u32[]{:S(2)}, u32[]{:S(2)}) collective-permute-start(bf16[64,944]{1,0:T(8,128)(2,1)S(1)} %collective-permute-done.2.refs_3_), channel_id=1, source_target_pairs={{0,4},{4,8},{8,12},{12,14},{14,10},{10,6},{6,2},{2,0},{1,5},{5,9},... | collective-permute-start | bytes 362504 | tf_op jit(solution)/shard_map/ppermute | solution.py:41
  21.8 2.9 %collective-permute-done.3.refs_4_ = bf16[64,944]{1,0:T(8,128)(2,1)S(1)} collective-permute-done((bf16[64,944]{1,0:T(8,128)(2,1)S(1)}, bf16[64,944]{1,0:T(8,128)(2,1)S(1)}, u32[]{:S(2)}, u32[]{:S(2)}) %collective-permute-start.3) | collective-permute-done | bytes 120864 | tf_op jit(solution)/shard_map/ppermute | solution.py:41
  25.2 0.6 and_select_fusion
  26.0 0.7 %multiply_add_fusion = (s32[8]{0:T(128)S(1)}, s32[8]{0:T(128)S(1)}) fusion(s32[8]{0:T(128)S(1)} %select_reduce_fusion, s32[]{:T(128)} %bitcast.1), kind=kLoop, calls=%fused_computation.41 | loop fusion | flops 32 | bytes 100 | tf_op jit(solution)/shard_map/add | solution.py:58
  26.7 0.6 %pad_add_fusion.owners = s32[16]{0:T(128)} fusion(s32[8]{0:T(128)S(1)} %get-tuple-element.6, s32[8]{0:T(128)S(1)} %get-tuple-element.5), kind=kLoop, calls=%fused_computation.38 | loop fusion | flops 16 | bytes 128 | tf_op jit(solution)/shard_map/concatenate | solution.py:58
  27.5 1.0 %copy-done = bf16[8,64,944]{2,1,0:T(8,128)(2,1)} copy-done((bf16[8,64,944]{2,1,0:T(8,128)(2,1)}, bf16[8,64,944]{2,1,0:T(8,128)(2,1)S(1)}, u32[]{:S(2)}) %copy-start) | copy-done | bytes 966680
  28.5 9.3 %shard_map.100 = bf16[384,128]{1,0:T(8,128)(2,1)} custom-call(s32[16]{0:T(128)} %pad_add_fusion.owners, bf16[64,944]{1,0:T(8,128)(2,1)} %copy-done.1, bf16[64,944]{1,0:T(8,128)(2,1)} %copy-done.2, bf16[64,944]{1,0:T(8,128)(2,1)} %copy-done.4, bf16[64,944]{1,0:T(8,128)(2,1)} %copy-done.6, bf16[64,944]{1,0:T(8,128)(2,1)} %copy-done.8, ...), custom_call_target="tpu_custom_call" | custom-call | tf_op jit(solution)/shard_map/pallas_call | solution.py:111
  37.8 1.2 %fusion.2 = bf16[768,128]{1,0:T(8,128)(2,1)S(1)} fusion(bf16[384,128]{1,0:T(8,128)(2,1)} %shard_map.100, s32[384]{0:T(512)S(1)} %convert_add_fusion), kind=kOutput, calls=%fused_computation.3 | convolution fusion | flops 75890688 | bytes 296448 | tf_op jit(solution)/shard_map/dot_general | solution.py:139
  39.0 0.7 %fusion.8 = bf16[16,49,128]{2,1,0:T(8,128)(2,1)} fusion(bf16[16,1,48]{2,1,0:T(2,128)(2,1)S(1)} %reshape.73, bf16[16,48,128]{2,1,0:T(8,128)(2,1)S(1)} %bitcast.28), kind=kLoop, calls=%fused_computation.13 | loop fusion | flops 602112 | bytes 398848 | tf_op jit(solution)/shard_map/concatenate | solution.py:148
  39.7 6.4 %all-to-all-start = ((bf16[16,49,128]{2,1,0:T(8,128)(2,1)}), bf16[16,49,128]{2,1,0:T(8,128)(2,1)S(1)}, u32[]{:S(2)}, u32[]{:S(2)}) async-start(bf16[16,49,128]{2,1,0:T(8,128)(2,1)} %fusion.8), calls=%async_computation | async-start | bytes 458752 | tf_op jit(solution)/shard_map/all_to_all | solution.py:149
  46.2 9.5 %all-to-all-done = bf16[16,49,128]{2,1,0:T(8,128)(2,1)S(1)} async-done(((bf16[16,49,128]{2,1,0:T(8,128)(2,1)}), bf16[16,49,128]{2,1,0:T(8,128)(2,1)S(1)}, u32[]{:S(2)}, u32[]{:S(2)}) %all-to-all-start) | async-done | bytes 200736 | tf_op jit(solution)/shard_map/all_to_all | solution.py:149
  56.1 0.4 fusion.9
  56.6 0.8 %reshape.68 = f32[8,4096]{1,0:T(8,128)} reshape(f32[512,64]{1,0:T(8,128)S(1)} %fusion.9) | data formatting | bytes 262144 | tf_op jit(solution)/shard_map/reshape | solution.py:160
  (50 shorter events, 1.6 us)
Async XLA Ops:
  1.0 24.1 %copy-start.1 = (bf16[64,944]{1,0:T(8,128)(2,1)}, bf16[64,944]{1,0:T(8,128)(2,1)S(1)}, u32[]{:S(2)}) copy-start(bf16[64,944]{1,0:T(8,128)(2,1)S(1)} %pad_maximum_fusion.refs_0_) | copy-start | bytes 362500
  1.0 8.3 %collective-permute-start = (bf16[64,944]{1,0:T(8,128)(2,1)S(1)}, bf16[64,944]{1,0:T(8,128)(2,1)S(1)}, u32[]{:S(2)}, u32[]{:S(2)}) collective-permute-start(bf16[64,944]{1,0:T(8,128)(2,1)S(1)} %pad_maximum_fusion.refs_0_), channel_id=1, source_target_pairs={{0,4},{4,8},{8,12},{12,14},{14,10},{10,6},{6,2},{2,0},{1,5},{5,9},... | collective-permute-start | bytes 362504 | tf_op jit(solution)/shard_map/ppermute | solution.py:41
  4.1 7.3 %collective-permute-start.4 = (bf16[64,944]{1,0:T(8,128)(2,1)S(1)}, bf16[64,944]{1,0:T(8,128)(2,1)S(1)}, u32[]{:S(2)}, u32[]{:S(2)}) collective-permute-start(bf16[64,944]{1,0:T(8,128)(2,1)S(1)} %pad_maximum_fusion.refs_0_), channel_id=1, source_target_pairs={{0,2},{4,0},{8,4},{12,8},{14,12},{10,14},{6,10},{2,6},{1,3},{5,1},... | collective-permute-start | bytes 362504 | tf_op jit(solution)/shard_map/ppermute | solution.py:46
  5.8 19.5 %copy-start.10 = (s32[8]{0:T(128)S(1)}, s32[8]{0:T(128)}, u32[]{:S(2)}) copy-start(s32[8]{0:T(128)} %constant.43.clone) | copy-start | bytes 100
  5.8 20.0 %copy-start.9 = (s32[8]{0:T(128)S(1)}, s32[8]{0:T(128)}, u32[]{:S(2)}) copy-start(s32[8]{0:T(128)} %constant.44.clone) | copy-start | bytes 100
  9.3 18.2 %copy-start.2 = (bf16[64,944]{1,0:T(8,128)(2,1)}, bf16[64,944]{1,0:T(8,128)(2,1)S(1)}, u32[]{:S(2)}) copy-start(bf16[64,944]{1,0:T(8,128)(2,1)S(1)} %collective-permute-done.refs_1_) | copy-start | bytes 362500
  9.3 5.0 %collective-permute-start.1 = (bf16[64,944]{1,0:T(8,128)(2,1)S(1)}, bf16[64,944]{1,0:T(8,128)(2,1)S(1)}, u32[]{:S(2)}, u32[]{:S(2)}) collective-permute-start(bf16[64,944]{1,0:T(8,128)(2,1)S(1)} %collective-permute-done.refs_1_), channel_id=1, source_target_pairs={{0,4},{4,8},{8,12},{12,14},{14,10},{10,6},{6,2},{2,0},{1,5},{5,9},... | collective-permute-start | bytes 362504 | tf_op jit(solution)/shard_map/ppermute | solution.py:41
  11.4 16.1 %copy-start.3 = (bf16[64,944]{1,0:T(8,128)(2,1)}, bf16[64,944]{1,0:T(8,128)(2,1)S(1)}, u32[]{:S(2)}) copy-start(bf16[64,944]{1,0:T(8,128)(2,1)S(1)} %collective-permute-done.4.refs_5_) | copy-start | bytes 362500
  11.4 5.0 %collective-permute-start.5 = (bf16[64,944]{1,0:T(8,128)(2,1)S(1)}, bf16[64,944]{1,0:T(8,128)(2,1)S(1)}, u32[]{:S(2)}, u32[]{:S(2)}) collective-permute-start(bf16[64,944]{1,0:T(8,128)(2,1)S(1)} %collective-permute-done.4.refs_5_), channel_id=1, source_target_pairs={{0,2},{4,0},{8,4},{12,8},{14,12},{10,14},{6,10},{2,6},{1,3},{5,1},... | collective-permute-start | bytes 362504 | tf_op jit(solution)/shard_map/ppermute | solution.py:46
  14.3 13.1 %copy-start.4 = (bf16[64,944]{1,0:T(8,128)(2,1)}, bf16[64,944]{1,0:T(8,128)(2,1)S(1)}, u32[]{:S(2)}) copy-start(bf16[64,944]{1,0:T(8,128)(2,1)S(1)} %collective-permute-done.1.refs_2_) | copy-start | bytes 362500
  14.3 5.1 %collective-permute-start.2 = (bf16[64,944]{1,0:T(8,128)(2,1)S(1)}, bf16[64,944]{1,0:T(8,128)(2,1)S(1)}, u32[]{:S(2)}, u32[]{:S(2)}) collective-permute-start(bf16[64,944]{1,0:T(8,128)(2,1)S(1)} %collective-permute-done.1.refs_2_), channel_id=1, source_target_pairs={{0,4},{4,8},{8,12},{12,14},{14,10},{10,6},{6,2},{2,0},{1,5},{5,9},... | collective-permute-start | bytes 362504 | tf_op jit(solution)/shard_map/ppermute | solution.py:41
  16.3 11.1 %copy-start.5 = (bf16[64,944]{1,0:T(8,128)(2,1)}, bf16[64,944]{1,0:T(8,128)(2,1)S(1)}, u32[]{:S(2)}) copy-start(bf16[64,944]{1,0:T(8,128)(2,1)S(1)} %collective-permute-done.5.refs_6_) | copy-start | bytes 362500
  16.3 8.3 %collective-permute-start.6 = (bf16[64,944]{1,0:T(8,128)(2,1)S(1)}, bf16[64,944]{1,0:T(8,128)(2,1)S(1)}, u32[]{:S(2)}, u32[]{:S(2)}) collective-permute-start(bf16[64,944]{1,0:T(8,128)(2,1)S(1)} %collective-permute-done.5.refs_6_), channel_id=1, source_target_pairs={{0,2},{4,0},{8,4},{12,8},{14,12},{10,14},{6,10},{2,6},{1,3},{5,1},... | collective-permute-start | bytes 362504 | tf_op jit(solution)/shard_map/ppermute | solution.py:46
  19.4 8.1 %copy-start.6 = (bf16[64,944]{1,0:T(8,128)(2,1)}, bf16[64,944]{1,0:T(8,128)(2,1)S(1)}, u32[]{:S(2)}) copy-start(bf16[64,944]{1,0:T(8,128)(2,1)S(1)} %collective-permute-done.2.refs_3_) | copy-start | bytes 362500
  19.4 5.2 %collective-permute-start.3 = (bf16[64,944]{1,0:T(8,128)(2,1)S(1)}, bf16[64,944]{1,0:T(8,128)(2,1)S(1)}, u32[]{:S(2)}, u32[]{:S(2)}) collective-permute-start(bf16[64,944]{1,0:T(8,128)(2,1)S(1)} %collective-permute-done.2.refs_3_), channel_id=1, source_target_pairs={{0,4},{4,8},{8,12},{12,14},{14,10},{10,6},{6,2},{2,0},{1,5},{5,9},... | collective-permute-start | bytes 362504 | tf_op jit(solution)/shard_map/ppermute | solution.py:41
  24.6 2.9 %copy-start.8 = (bf16[64,944]{1,0:T(8,128)(2,1)}, bf16[64,944]{1,0:T(8,128)(2,1)S(1)}, u32[]{:S(2)}) copy-start(bf16[64,944]{1,0:T(8,128)(2,1)S(1)} %collective-permute-done.3.refs_4_) | copy-start | bytes 362500
  24.7 2.8 %copy-start.7 = (bf16[64,944]{1,0:T(8,128)(2,1)}, bf16[64,944]{1,0:T(8,128)(2,1)S(1)}, u32[]{:S(2)}) copy-start(bf16[64,944]{1,0:T(8,128)(2,1)S(1)} %collective-permute-done.6.refs_7_) | copy-start | bytes 362500
  24.7 2.7 %collective-permute-start.7 = (bf16[8,64,944]{2,1,0:T(8,128)(2,1)S(1)}, bf16[8,64,944]{2,1,0:T(8,128)(2,1)S(1)}, u32[]{:S(2)}, u32[]{:S(2)}) collective-permute-start(bf16[8,64,944]{2,1,0:T(8,128)(2,1)S(1)} %bitcast_dynamic-update-slice_fusion), channel_id=1, source_target_pairs={{0,1},{4,5},{8,9},{12,13},{14,15},{10,11},{6,7},{2,3},{1,0},{5,4},... | collective-permute-start | bytes 2899976 | tf_op jit(solution)/shard_map/ppermute | solution.py:57
  27.5 1.0 %copy-start = (bf16[8,64,944]{2,1,0:T(8,128)(2,1)}, bf16[8,64,944]{2,1,0:T(8,128)(2,1)S(1)}, u32[]{:S(2)}) copy-start(bf16[8,64,944]{2,1,0:T(8,128)(2,1)S(1)} %collective-permute-done.7.refs_8_) | copy-start | bytes 2899972
  39.7 16.0 %all-to-all-start = ((bf16[16,49,128]{2,1,0:T(8,128)(2,1)}), bf16[16,49,128]{2,1,0:T(8,128)(2,1)S(1)}, u32[]{:S(2)}, u32[]{:S(2)}) async-start(bf16[16,49,128]{2,1,0:T(8,128)(2,1)} %fusion.8), calls=%async_computation | async-start | bytes 458752 | tf_op jit(solution)/shard_map/all_to_all | solution.py:149

commit v6 on v3

--- a/solution.py
+++ b/solution.py
@@ -29,37 +29,57 @@
             place[member] = spot
             plane_of[member] = plane
     spot = jnp.asarray(place)[me]
+    plane = jnp.asarray(plane_of)[me]
     forward = [(ring[t], ring[(t + 1) % length]) for ring in planes for t in range(length)]
     backward = [(ring[t], ring[(t - 1) % length]) for ring in planes for t in range(length)]
-    ahead = [block]
-    behind = []
+    blocks = [block]
+    shifts = [0]
     moving = block
-    for _ in range(length // 2):
+    for step in range(1, length // 2 + 1):
         moving = lax.ppermute(moving, "dp", forward)
-        ahead.append(moving)
+        blocks.append(moving)
+        shifts.append(-step)
     moving = block
-    for _ in range(length - 1 - length // 2):
+    for step in range(1, length - length // 2):
         moving = lax.ppermute(moving, "dp", backward)
-        behind.append(moving)
-    by_distance = jnp.stack(ahead + behind[::-1])
-    chip_spot = np.zeros(length, np.int32)
-    for at, member in enumerate(planes[0]):
-        chip_spot[member // len(planes)] = at
-    mine = by_distance[(spot - jnp.asarray(chip_spot)) % length]
+        blocks.append(moving)
+        shifts.append(step)
+    spots = (spot + jnp.asarray(np.array(shifts, np.int32))) % length
+    chips = jnp.asarray(np.array(planes[0], np.int32) // len(planes))
+    hit = spots[:, None] == jnp.arange(length, dtype=jnp.int32)[None, :]
+    chip_of = jnp.sum(jnp.where(hit, chips[None, :], 0), axis=1)
     if len(planes) == 1:
-        return mine
+        return blocks, None, chip_of.astype(jnp.int32)
+    mine = jnp.stack(blocks)
     swap = list(zip(planes[0], planes[1])) + list(zip(planes[1], planes[0]))
     other = lax.ppermute(mine, "dp", swap)
-    first = jnp.asarray(plane_of)[me] == 0
-    both = jnp.where(first, jnp.stack([mine, other], axis=1), jnp.stack([other, mine], axis=1))
-    return both.reshape((devices,) + block.shape)
+    owners = jnp.concatenate([chip_of * 2 + plane, chip_of * 2 + 1 - plane])
+    return blocks, other, owners.astype(jnp.int32)
 
 
-def project(token_block, basis):
-    summed = lax.dot_general(
-        token_block, basis, (((1,), (1,)), ((), ())), preferred_element_type=jnp.float32
-    )
-    return summed.astype(jnp.bfloat16)
+def partial_rows(hidden_parts, grad_parts, block, owner, hidden_cols):
+    dims = (((1,), (1,)), ((), ()))
+    left = lax.dot_general(hidden_parts[owner], block[:, :hidden_cols], dims, preferred_element_type=jnp.float32)
+    right = lax.dot_general(grad_parts[owner], block[:, hidden_cols:], dims, preferred_element_type=jnp.float32)
+    return left, right
+
+
+def project_rows(blocks, other, owners, hidden, out_grad, devices):
+    local_tokens, features = hidden.shape
+    hidden_cols = features // devices
+    output_cols = out_grad.shape[1] // devices
+    hidden_parts = hidden.reshape(local_tokens, devices, hidden_cols).transpose(1, 0, 2)
+    grad_parts = out_grad.reshape(local_tokens, devices, output_cols).transpose(1, 0, 2)
+    pieces = list(blocks)
+    if other is not None:
+        pieces = pieces + [other[k] for k in range(len(blocks))]
+    left = None
+    right = None
+    for k, block in enumerate(pieces):
+        part_left, part_right = partial_rows(hidden_parts, grad_parts, block, owners[k], hidden_cols)
+        left = part_left if left is None else left + part_left
+        right = part_right if right is None else right + part_right
+    return jnp.concatenate([left, right], axis=1).astype(jnp.bfloat16)
 
 
 def local(hidden, out_grad, hidden_basis, output_basis, owner_ids, doc_slot):
@@ -67,13 +87,9 @@
     local_tokens = hidden.shape[0]
     capacity = 2 * local_tokens // devices
     rank_width = hidden_basis.shape[0]
-    hidden_cols = hidden_basis.shape[1]
     buffer_len = devices * capacity
-    stacked = ring_gather(jnp.concatenate([hidden_basis, output_basis], axis=1), devices)
-    hidden_full = stacked[:, :, :hidden_cols].transpose(1, 0, 2).reshape(rank_width, -1)
-    output_full = stacked[:, :, hidden_cols:].transpose(1, 0, 2).reshape(rank_width, -1)
-    left = project(hidden, hidden_full)
-    right = project(out_grad, output_full)
+    blocks, other, owners = ring_gather(jnp.concatenate([hidden_basis, output_basis], axis=1), devices)
+    rows = project_rows(blocks, other, owners, hidden, out_grad, devices)
     targets = owner_ids[:, 0]
     member = (targets[:, None] == jnp.arange(devices, dtype=jnp.int32)[None, :]).astype(jnp.bfloat16)
     token_ids = jnp.arange(local_tokens, dtype=jnp.int32)
@@ -86,7 +102,6 @@
     dispatch = (
         jnp.arange(buffer_len, dtype=jnp.int32)[:, None] == slot_index[None, :]
     ).astype(jnp.bfloat16)
-    rows = jnp.concatenate([left, right], axis=1)
     buffer = lax.dot_general(
         dispatch, rows, (((1,), (0,)), ((), ())), preferred_element_type=jnp.float32
     ).astype(jnp.bfloat16)

time: 73.3 us -> 104 us (1.42)
  between operations: 0.8 us -> 30.2 us
  matrix products: 10.3 us -> 17.1 us
  waiting for transfers between devices: 17.5 us -> 12.7 us
    unnamed x17 -> x14, local copies, waits for them, and re-layouts: 4.2 us -> 15.6 us
    dot_general x2 -> x32, matrix products: 8.29 us -> 15.8 us  [the longest x16 10.7 us: partial_rows(): lax.dot_general(hidden_parts[owner], block[:, :hidden_cols], dims, prefer...]
    reshape x2 -> x0, local copies, waits for them, and re-layouts: 5.09 us -> none  [the longest x1 4.26 us: local(): stacked[:, :, :hidden_cols].transpose(1, 0, 2).reshape(rank_width, -1)]
    ppermute x4, waiting for transfers between devices: 6.91 us -> 2.71 us  [ring_gather(): moving = lax.ppermute(moving, 'dp', forward)]
    gather x1 -> x0, local copies, waits for them, and re-layouts: 2.8 us -> none  [ring_gather(): mine = by_distance[(spot - jnp.asarray(chip_spot)) % length]]
    select_n x2 -> x1, other arithmetic: 3.95 us -> 1.3 us  [ring_gather(): spots = (spot + jnp.asarray(np.array(shifts, np.int32))) % length]
    transpose x2 -> x0, local copies, waits for them, and re-layouts: 2.19 us -> none  [local(): stacked[:, :, :hidden_cols].transpose(1, 0, 2).reshape(rank_width, -1)]
  transfers between devices with their start and end apart: 9 -> 9, of which waited for: 5 -> 4; matrix products, arithmetic and copies ran while one was open for 11% -> 35% of each run, Pallas kernels for 0% -> 0%
where the time goes in v6:
time: 104 us; the launch traced here: 103 us
  between operations  30.2 us (29%)
  local copies, waits for them, and re-layouts  20.1 us (19%)
  matrix products  17.1 us (16%)
  starting transfers between devices  16.3 us (16%)
  waiting for transfers between devices  12.7 us (12%)
  other arithmetic  6.75 us (6%)
    unnamed x14, local copies, waits for them, and re-layouts  15.6 us
    dot_general x16, matrix products, partial_rows(): lax.dot_general(hidden_parts[owner], block[:, :hidden_cols], dims, prefer...  10.7 us
    ppermute x4, starting transfers between devices, ring_gather(): moving = lax.ppermute(moving, 'dp', forward)  9.52 us
    all_to_all x1, waiting for transfers between devices, local(): arrived = lax.all_to_all(packed, 'dp', 0, 0, tiled=True)  9.51 us
    all_to_all x1, starting transfers between devices, local(): arrived = lax.all_to_all(packed, 'dp', 0, 0, tiled=True)  6.55 us
    dot_general x16, matrix products, partial_rows(): lax.dot_general(grad_parts[owner], block[:, hidden_cols:], dims, preferre...  5.13 us
    ppermute x4, waiting for transfers between devices, ring_gather(): moving = lax.ppermute(moving, 'dp', forward)  2.71 us
  transfers between devices with their start and end apart: 9, of which 4 were waited for; matrix products, arithmetic and copies ran while one was open for 35% of the time, Pallas kernels for 0%

profile of v6, /device:TPU:0, one launch (start us, length us, event | category | flops | bytes accessed | tf_op | source)
XLA Modules:
  0.0 103.2 jit_solution(8044717085472356795)
XLA Ops:
  0.0 1.7 %pad_maximum_fusion = bf16[64,944]{1,0:T(8,128)(2,1)} fusion(bf16[64,256]{1,0:T(8,128)(2,1)} %param.13, bf16[64,688]{1,0:T(8,128)(2,1)} %param.12), kind=kLoop, calls=%fused_computation.140 | loop fusion | flops 241664 | bytes 241664 | tf_op jit(solution)/shard_map/concatenate | solution.py:91
  1.7 3.0 %collective-permute-start = (bf16[64,944]{1,0:T(8,128)(2,1)}, bf16[64,944]{1,0:T(8,128)(2,1)S(1)}, u32[]{:S(2)}, u32[]{:S(2)}) collective-permute-start(bf16[64,944]{1,0:T(8,128)(2,1)} %pad_maximum_fusion), channel_id=1, source_target_pairs={{0,4},{4,8},{8,12},{12,14},{14,10},{10,6},{6,2},{2,0},{1,5},{5,9},... | collective-permute-start | bytes 362504 | tf_op jit(solution)/shard_map/ppermute | solution.py:39
  4.7 1.3 %dynamic_slice.4 = s32[1]{0:T(128)} dynamic-slice(s32[16]{0:T(128)} %constant.41.clone, s32[]{:T(128)S(6)} %select_n.79), dynamic_slice_sizes={1} | dynamic-slice | bytes 12 | tf_op jit(solution)/shard_map/dynamic_slice | solution.py:31
  5.9 1.3 %dynamic_slice.5 = s32[1]{0:T(128)} dynamic-slice(s32[16]{0:T(128)} %constant.42.clone, s32[]{:T(128)S(6)} %select_n.79), dynamic_slice_sizes={1} | dynamic-slice | bytes 12 | tf_op jit(solution)/shard_map/dynamic_slice | solution.py:32
  7.2 1.3 %and_select_fusion = s32[8]{0:T(128)S(1)} fusion(s32[8]{0:T(128)} %constant.43.clone, s32[]{:T(128)} %bitcast.1), kind=kLoop, calls=%fused_computation.225 | loop fusion | flops 96 | bytes 68 | tf_op jit(solution)/shard_map/jit(remainder)/select_n | solution.py:47
  8.5 0.8 select_reduce_fusion
  13.6 3.4 %copy.36 = bf16[384,4096]{0,1:T(8,128)(2,1)S(1)} copy(bf16[384,4096]{1,0:T(8,128)(2,1)} %param.11) | data formatting | bytes 6291456 | tf_op args[1]
  17.1 12.1 %copy.35 = bf16[384,11008]{0,1:T(8,128)(2,1)} copy(bf16[384,11008]{1,0:T(8,128)(2,1)} %param.10) | data formatting | bytes 16908288 | tf_op args[0]
  29.8 0.8 fusion.97
  30.6 1.9 %fusion.51 = f32[384,64]{0,1:T(8,128)} fusion(bf16[64,688]{1,0:T(8,128)(2,1)S(1)} %copy-done.1, bf16[384,16,688]{0,2,1:T(8,128)(2,1)} %bitcast.172, s32[]{:T(128)S(6)} %select_n.82), kind=kOutput, calls=%fused_computation.66 | convolution fusion | flops 33816576 | bytes 714756 | tf_op jit(solution)/shard_map/dot_general | solution.py:62
  61.0 2.1 %collective-permute-start.1 = (bf16[64,944]{1,0:T(8,128)(2,1)S(1)}, bf16[64,944]{1,0:T(8,128)(2,1)S(1)}, u32[]{:S(2)}, u32[]{:S(2)}) collective-permute-start(bf16[64,944]{1,0:T(8,128)(2,1)S(1)} %collective-permute-done), channel_id=1, source_target_pairs={{0,4},{4,8},{8,12},{12,14},{14,10},{10,6},{6,2},{2,0},{1,5},{5,9},... | collective-permute-start | bytes 362504 | tf_op jit(solution)/shard_map/ppermute | solution.py:39
  63.1 1.4 %fusion.45 = f32[384,64]{0,1:T(8,128)S(1)} fusion(bf16[384,16,688]{0,2,1:T(8,128)(2,1)} %bitcast.173, s32[]{:T(128)S(6)} %select_n.87, bf16[64,944]{1,0:T(8,128)(2,1)S(1)} %collective-permute-done.4), kind=kOutput, calls=%fused_computation.60 | convolution fusion | flops 33816576 | bytes 724996 | tf_op jit(solution)/shard_map/dot_general | solution.py:62
  64.6 1.4 %convolution_add_fusion.5 = f32[384,64]{0,1:T(8,128)S(1)} fusion(f32[384,64]{0,1:T(8,128)} %fusion.97, bf16[384,16,256]{0,2,1:T(8,128)(2,1)S(1)} %bitcast.189, s32[]{:T(128)S(6)} %select_n.83, bf16[64,944]{1,0:T(8,128)(2,1)S(1)} %collective-permute-done), kind=kOutput, calls=%fused_computation.9 | convolution fusion | flops 12607488 | bytes 425988 | tf_op jit(solution)/shard_map/dot_general | solution.py:63
  66.0 1.3 %convolution_add_fusion.11 = f32[384,64]{0,1:T(8,128)S(1)} fusion(f32[384,64]{0,1:T(8,128)} %fusion.51, bf16[384,16,688]{0,2,1:T(8,128)(2,1)} %bitcast.174, s32[]{:T(128)S(6)} %select_n.83, bf16[64,944]{1,0:T(8,128)(2,1)S(1)} %collective-permute-done), kind=kOutput, calls=%fused_computation.33 | convolution fusion | flops 33841152 | bytes 823300 | tf_op jit(solution)/shard_map/dot_general | solution.py:62
  67.5 2.2 %collective-permute-start.2 = (bf16[64,944]{1,0:T(8,128)(2,1)S(1)}, bf16[64,944]{1,0:T(8,128)(2,1)S(1)}, u32[]{:S(2)}, u32[]{:S(2)}) collective-permute-start(bf16[64,944]{1,0:T(8,128)(2,1)S(1)} %collective-permute-done.1), channel_id=1, source_target_pairs={{0,4},{4,8},{8,12},{12,14},{14,10},{10,6},{6,2},{2,0},{1,5},{5,9},... | collective-permute-start | bytes 362504 | tf_op jit(solution)/shard_map/ppermute | solution.py:39
  69.8 1.3 %convolution_add_fusion.10 = f32[384,64]{0,1:T(8,128)S(1)} fusion(f32[384,64]{0,1:T(8,128)S(1)} %convolution_add_fusion.11, bf16[384,16,688]{0,2,1:T(8,128)(2,1)} %bitcast.175, s32[]{:T(128)S(6)} %select_n.84, bf16[64,944]{1,0:T(8,128)(2,1)S(1)} %collective-permute-done.1), kind=kOutput, calls=%fused_computation.32 | convolution fusion | flops 33841152 | bytes 823300 | tf_op jit(solution)/shard_map/dot_general | solution.py:62
  71.3 1.2 %collective-permute-done.2 = bf16[64,944]{1,0:T(8,128)(2,1)S(1)} collective-permute-done((bf16[64,944]{1,0:T(8,128)(2,1)S(1)}, bf16[64,944]{1,0:T(8,128)(2,1)S(1)}, u32[]{:S(2)}, u32[]{:S(2)}) %collective-permute-start.2) | collective-permute-done | bytes 120864 | tf_op jit(solution)/shard_map/ppermute | solution.py:39
  72.5 2.2 %collective-permute-start.3 = (bf16[64,944]{1,0:T(8,128)(2,1)S(1)}, bf16[64,944]{1,0:T(8,128)(2,1)S(1)}, u32[]{:S(2)}, u32[]{:S(2)}) collective-permute-start(bf16[64,944]{1,0:T(8,128)(2,1)S(1)} %collective-permute-done.2), channel_id=1, source_target_pairs={{0,4},{4,8},{8,12},{12,14},{14,10},{10,6},{6,2},{2,0},{1,5},{5,9},... | collective-permute-start | bytes 362504 | tf_op jit(solution)/shard_map/ppermute | solution.py:39
  74.7 1.3 %convolution_add_fusion.9 = f32[384,64]{0,1:T(8,128)S(1)} fusion(f32[384,64]{0,1:T(8,128)S(1)} %convolution_add_fusion.10, bf16[384,16,688]{0,2,1:T(8,128)(2,1)} %bitcast.176, s32[]{:T(128)S(6)} %select_n.85, bf16[64,944]{1,0:T(8,128)(2,1)S(1)} %collective-permute-done.2), kind=kOutput, calls=%fused_computation.31 | convolution fusion | flops 33841152 | bytes 823300 | tf_op jit(solution)/shard_map/dot_general | solution.py:62
  76.0 1.5 %collective-permute-done.3 = bf16[64,944]{1,0:T(8,128)(2,1)S(1)} collective-permute-done((bf16[64,944]{1,0:T(8,128)(2,1)S(1)}, bf16[64,944]{1,0:T(8,128)(2,1)S(1)}, u32[]{:S(2)}, u32[]{:S(2)}) %collective-permute-start.3) | collective-permute-done | bytes 120864 | tf_op jit(solution)/shard_map/ppermute | solution.py:39
  78.3 1.3 %fusion.20 = f32[384,64]{0,1:T(8,128)S(1)} fusion(f32[384,64]{0,1:T(8,128)S(1)} %fusion.45, f32[384,64]{0,1:T(8,128)S(1)} %convolution_add_fusion.9, bf16[384,16,688]{0,2,1:T(8,128)(2,1)} %bitcast.177, s32[]{:T(128)S(6)} %select_n.86, bf16[64,944]{1,0:T(8,128)(2,1)S(1)} %collective-permute-done.3), kind=kOutput, calls=%fused_computation.30 | convolution fusion | flops 33865728 | bytes 921604 | tf_op jit(solution)/shard_map/dot_general | solution.py:62
  85.5 6.5 %all-to-all-start = ((bf16[16,49,128]{2,1,0:T(8,128)(2,1)}), bf16[16,49,128]{2,1,0:T(8,128)(2,1)S(1)}, u32[]{:S(2)}, u32[]{:S(2)}) async-start(bf16[16,49,128]{2,1,0:T(8,128)(2,1)} %fusion.70), calls=%async_computation | async-start | bytes 458752 | tf_op jit(solution)/shard_map/all_to_all | solution.py:115
  92.0 9.5 %all-to-all-done = bf16[16,49,128]{2,1,0:T(8,128)(2,1)S(1)} async-done(((bf16[16,49,128]{2,1,0:T(8,128)(2,1)}), bf16[16,49,128]{2,1,0:T(8,128)(2,1)S(1)}, u32[]{:S(2)}, u32[]{:S(2)}) %all-to-all-start) | async-done | bytes 200736 | tf_op jit(solution)/shard_map/all_to_all | solution.py:115
  102.4 0.8 reshape.140
  (68 shorter events, 11.4 us)
Async XLA Ops:
  1.7 59.3 %collective-permute-start = (bf16[64,944]{1,0:T(8,128)(2,1)}, bf16[64,944]{1,0:T(8,128)(2,1)S(1)}, u32[]{:S(2)}, u32[]{:S(2)}) collective-permute-start(bf16[64,944]{1,0:T(8,128)(2,1)} %pad_maximum_fusion), channel_id=1, source_target_pairs={{0,4},{4,8},{8,12},{12,14},{14,10},{10,6},{6,2},{2,0},{1,5},{5,9},... | collective-permute-start | bytes 362504 | tf_op jit(solution)/shard_map/ppermute | solution.py:39
  4.7 58.4 %collective-permute-start.4 = (bf16[64,944]{1,0:T(8,128)(2,1)}, bf16[64,944]{1,0:T(8,128)(2,1)S(1)}, u32[]{:S(2)}, u32[]{:S(2)}) collective-permute-start(bf16[64,944]{1,0:T(8,128)(2,1)} %pad_maximum_fusion), channel_id=1, source_target_pairs={{0,2},{4,0},{8,4},{12,8},{14,12},{10,14},{6,10},{2,6},{1,3},{5,1},... | collective-permute-start | bytes 362504 | tf_op jit(solution)/shard_map/ppermute | solution.py:44
  17.0 12.8 %copy-start.2 = (bf16[64,256]{1,0:T(8,128)(2,1)S(1)}, bf16[64,256]{1,0:T(8,128)(2,1)}, u32[]{:S(2)}) copy-start(bf16[64,256]{1,0:T(8,128)(2,1)} %param.13) | copy-start | bytes 98308
  17.1 13.6 %copy-start.1 = (bf16[64,688]{1,0:T(8,128)(2,1)S(1)}, bf16[64,688]{1,0:T(8,128)(2,1)}, u32[]{:S(2)}) copy-start(bf16[64,688]{1,0:T(8,128)(2,1)} %param.12) | copy-start | bytes 264196
  61.0 6.5 %collective-permute-start.1 = (bf16[64,944]{1,0:T(8,128)(2,1)S(1)}, bf16[64,944]{1,0:T(8,128)(2,1)S(1)}, u32[]{:S(2)}, u32[]{:S(2)}) collective-permute-start(bf16[64,944]{1,0:T(8,128)(2,1)S(1)} %collective-permute-done), channel_id=1, source_target_pairs={{0,4},{4,8},{8,12},{12,14},{14,10},{10,6},{6,2},{2,0},{1,5},{5,9},... | collective-permute-start | bytes 362504 | tf_op jit(solution)/shard_map/ppermute | solution.py:39
  63.1 16.5 %copy-start = (bf16[384,11008]{0,1:T(8,128)(2,1)S(1)}, bf16[384,11008]{0,1:T(8,128)(2,1)}, u32[]{:S(2)}) copy-start(bf16[384,11008]{0,1:T(8,128)(2,1)} %copy.35) | copy-start | bytes 25362436
  63.1 6.7 %collective-permute-start.5 = (bf16[64,944]{1,0:T(8,128)(2,1)S(1)}, bf16[64,944]{1,0:T(8,128)(2,1)S(1)}, u32[]{:S(2)}, u32[]{:S(2)}) collective-permute-start(bf16[64,944]{1,0:T(8,128)(2,1)S(1)} %collective-permute-done.4), channel_id=1, source_target_pairs={{0,2},{4,0},{8,4},{12,8},{14,12},{10,14},{6,10},{2,6},{1,3},{5,1},... | collective-permute-start | bytes 362504 | tf_op jit(solution)/shard_map/ppermute | solution.py:44
  67.5 5.0 %collective-permute-start.2 = (bf16[64,944]{1,0:T(8,128)(2,1)S(1)}, bf16[64,944]{1,0:T(8,128)(2,1)S(1)}, u32[]{:S(2)}, u32[]{:S(2)}) collective-permute-start(bf16[64,944]{1,0:T(8,128)(2,1)S(1)} %collective-permute-done.1), channel_id=1, source_target_pairs={{0,4},{4,8},{8,12},{12,14},{14,10},{10,6},{6,2},{2,0},{1,5},{5,9},... | collective-permute-start | bytes 362504 | tf_op jit(solution)/shard_map/ppermute | solution.py:39
  69.8 7.8 %collective-permute-start.6 = (bf16[64,944]{1,0:T(8,128)(2,1)S(1)}, bf16[64,944]{1,0:T(8,128)(2,1)S(1)}, u32[]{:S(2)}, u32[]{:S(2)}) collective-permute-start(bf16[64,944]{1,0:T(8,128)(2,1)S(1)} %collective-permute-done.5), channel_id=1, source_target_pairs={{0,2},{4,0},{8,4},{12,8},{14,12},{10,14},{6,10},{2,6},{1,3},{5,1},... | collective-permute-start | bytes 362504 | tf_op jit(solution)/shard_map/ppermute | solution.py:44
  72.5 5.0 %collective-permute-start.3 = (bf16[64,944]{1,0:T(8,128)(2,1)S(1)}, bf16[64,944]{1,0:T(8,128)(2,1)S(1)}, u32[]{:S(2)}, u32[]{:S(2)}) collective-permute-start(bf16[64,944]{1,0:T(8,128)(2,1)S(1)} %collective-permute-done.2), channel_id=1, source_target_pairs={{0,4},{4,8},{8,12},{12,14},{14,10},{10,6},{6,2},{2,0},{1,5},{5,9},... | collective-permute-start | bytes 362504 | tf_op jit(solution)/shard_map/ppermute | solution.py:39
  77.6 2.7 %collective-permute-start.7 = (bf16[8,64,944]{2,1,0:T(8,128)(2,1)S(1)}, bf16[8,64,944]{2,1,0:T(8,128)(2,1)S(1)}, u32[]{:S(2)}, u32[]{:S(2)}) collective-permute-start(bf16[8,64,944]{2,1,0:T(8,128)(2,1)S(1)} %bitcast_dynamic-update-slice_fusion), channel_id=1, source_target_pairs={{0,1},{4,5},{8,9},{12,13},{14,15},{10,11},{6,7},{2,3},{1,0},{5,4},... | collective-permute-start | bytes 2899976 | tf_op jit(solution)/shard_map/ppermute | solution.py:55
  85.5 16.1 %all-to-all-start = ((bf16[16,49,128]{2,1,0:T(8,128)(2,1)}), bf16[16,49,128]{2,1,0:T(8,128)(2,1)S(1)}, u32[]{:S(2)}, u32[]{:S(2)}) async-start(bf16[16,49,128]{2,1,0:T(8,128)(2,1)} %fusion.70), calls=%async_computation | async-start | bytes 458752 | tf_op jit(solution)/shard_map/all_to_all | solution.py:115

commit v7 on v5

--- a/solution.py
+++ b/solution.py
@@ -30,8 +30,6 @@
         for spot, member in enumerate(members):
             place[member] = spot
             plane_of[member] = plane
-    spot = jnp.asarray(place)[me]
-    plane = jnp.asarray(plane_of)[me]
     forward = [(ring[t], ring[(t + 1) % length]) for ring in planes for t in range(length)]
     backward = [(ring[t], ring[(t - 1) % length]) for ring in planes for t in range(length)]
     blocks = [block]
@@ -46,17 +44,19 @@
         moving = lax.ppermute(moving, "dp", backward)
         blocks.append(moving)
         shifts.append(step)
-    spots = (spot + jnp.asarray(np.array(shifts, np.int32))) % length
-    chips = jnp.asarray(np.array(planes[0], np.int32) // len(planes))
-    hit = spots[:, None] == jnp.arange(length, dtype=jnp.int32)[None, :]
-    chip_of = jnp.sum(jnp.where(hit, chips[None, :], 0), axis=1)
+    table = np.zeros((devices, len(shifts) * len(planes)), np.int32)
+    for member in range(devices):
+        for k, shift in enumerate(shifts):
+            for side in range(len(planes)):
+                ring = planes[(plane_of[member] + side) % len(planes)]
+                table[member, side * len(shifts) + k] = ring[(place[member] + shift) % length]
+    owners = jnp.asarray(table)[me]
     if len(planes) == 1:
-        return blocks, None, chip_of.astype(jnp.int32)
+        return blocks, None, owners
     mine = jnp.stack(blocks)
     swap = list(zip(planes[0], planes[1])) + list(zip(planes[1], planes[0]))
     other = lax.ppermute(mine, "dp", swap)
-    owners = jnp.concatenate([chip_of * 2 + plane, chip_of * 2 + 1 - plane])
-    return blocks, other, owners.astype(jnp.int32)
+    return blocks, other, owners
 
 
 def projection_kernel(count, devices, hidden_cols, output_cols, rank_width, paired):
@@ -65,7 +65,9 @@
         rest = refs[count:]
         if paired:
             other_ref, rest = rest[0], rest[1:]
-        hidden_ref, grad_ref, rows_ref, stacked, hidden_full, output_full = rest
+        hidden_ref, grad_ref, dispatch_ref, buffer_ref, rows, stacked, hidden_full, output_full = rest
+        step = pl.program_id(0)
+        tile = hidden_ref.shape[0]
 
         @pl.when(pl.program_id(0) == 0)
         def _():
@@ -80,13 +82,21 @@
         dims = (((1,), (1,)), ((), ()))
         left = lax.dot_general(hidden_ref[...], hidden_full[...], dims, preferred_element_type=jnp.float32)
         right = lax.dot_general(grad_ref[...], output_full[...], dims, preferred_element_type=jnp.float32)
-        rows_ref[:, :rank_width] = left.astype(jnp.bfloat16)
-        rows_ref[:, rank_width:] = right.astype(jnp.bfloat16)
+        at = pl.multiple_of(step * tile, tile)
+        rows[pl.ds(at, tile), :rank_width] = left.astype(jnp.bfloat16)
+        rows[pl.ds(at, tile), rank_width:] = right.astype(jnp.bfloat16)
+
+        @pl.when(step == pl.num_programs(0) - 1)
+        def _():
+            placed = lax.dot_general(
+                dispatch_ref[...], rows[...], (((1,), (0,)), ((), ())), preferred_element_type=jnp.float32
+            )
+            buffer_ref[...] = placed.astype(jnp.bfloat16)
 
     return kernel
 
 
-def project_rows(blocks, other, owners, hidden, out_grad, devices):
+def project_rows(blocks, other, owners, hidden, out_grad, dispatch, devices):
     count = len(blocks)
     paired = other is not None
     rank_width, width = blocks[0].shape
@@ -100,9 +110,11 @@
         in_specs=[whole] * count + [pl.BlockSpec((count, rank_width, width), lambda i, owners: (0, 0, 0))] * paired + [
             pl.BlockSpec((tile, features), lambda i, owners: (i, 0)),
             pl.BlockSpec((tile, outputs), lambda i, owners: (i, 0)),
+            pl.BlockSpec(dispatch.shape, lambda i, owners: (0, 0)),
         ],
-        out_specs=pl.BlockSpec((tile, 2 * rank_width), lambda i, owners: (i, 0)),
+        out_specs=pl.BlockSpec((dispatch.shape[0], 2 * rank_width), lambda i, owners: (0, 0)),
         scratch_shapes=[
+            pltpu.VMEM((local_tokens, 2 * rank_width), jnp.bfloat16),
             pltpu.VMEM((devices, rank_width, width), jnp.bfloat16),
             pltpu.VMEM((rank_width, features), jnp.bfloat16),
             pltpu.VMEM((rank_width, outputs), jnp.bfloat16),
@@ -111,9 +123,9 @@
     return pl.pallas_call(
         projection_kernel(count, devices, features // devices, outputs // devices, rank_width, paired),
         grid_spec=grid_spec,
-        out_shape=jax.ShapeDtypeStruct((local_tokens, 2 * rank_width), jnp.bfloat16),
+        out_shape=jax.ShapeDtypeStruct((dispatch.shape[0], 2 * rank_width), jnp.bfloat16),
         compiler_params=pltpu.CompilerParams(dimension_semantics=("arbitrary",)),
-    )(owners, *blocks, *([other] if paired else []), hidden, out_grad)
+    )(owners, *blocks, *([other] if paired else []), hidden, out_grad, dispatch)
 
 
 def local(hidden, out_grad, hidden_basis, output_basis, owner_ids, doc_slot):
@@ -123,7 +135,6 @@
     rank_width = hidden_basis.shape[0]
     buffer_len = devices * capacity
     blocks, other, owners = ring_gather(jnp.concatenate([hidden_basis, output_basis], axis=1), devices)
-    rows = project_rows(blocks, other, owners, hidden, out_grad, devices)
     targets = owner_ids[:, 0]
     member = (targets[:, None] == jnp.arange(devices, dtype=jnp.int32)[None, :]).astype(jnp.bfloat16)
     token_ids = jnp.arange(local_tokens, dtype=jnp.int32)
@@ -136,9 +147,7 @@
     dispatch = (
         jnp.arange(buffer_len, dtype=jnp.int32)[:, None] == slot_index[None, :]
     ).astype(jnp.bfloat16)
-    buffer = lax.dot_general(
-        dispatch, rows, (((1,), (0,)), ((), ())), preferred_element_type=jnp.float32
-    ).astype(jnp.bfloat16)
+    buffer = project_rows(blocks, other, owners, hidden, out_grad, dispatch, devices)
     label = lax.dot_general(
         dispatch, (doc_slot + 1).astype(jnp.bfloat16), (((1,), (0,)), ((), ())),
         preferred_element_type=jnp.float32,

time: 57.7 us -> 56.6 us (0.981)
  waiting for transfers between devices: 18.5 us -> 20.5 us
  local copies, waits for them, and re-layouts: 4.75 us -> 3.39 us
  matrix products: 2.2 us -> 0.98 us
  other arithmetic: 6.26 us -> 5.54 us
    dynamic_slice x2 -> x0, local copies, waits for them, and re-layouts: 2.54 us -> none  [the longest x1 1.31 us: ring_gather(): plane = jnp.asarray(plane_of)[me]]
    ppermute x4, waiting for transfers between devices: 8.8 us -> 10.9 us  [ring_gather(): moving = lax.ppermute(moving, 'dp', forward)]
    dot_general x1 -> x0, matrix products: 1.22 us -> none  [local(): lax.dot_general(dispatch, rows, (((1,), (0,)), ((), ())), preferred_eleme...]
    squeeze x0 -> x1, local copies, waits for them, and re-layouts: none -> 1.2 us  [ring_gather(): owners = jnp.asarray(table)[me]]
    convert_element_type x0 -> x1, other arithmetic: none -> 1.04 us  [local(): dispatch = (jnp.arange(buffer_len, dtype=jnp.int32)[:, None] == slot_inde...]
    concatenate x1, other arithmetic: 0.71 us -> 1.63 us  [local(): jnp.concatenate([buffer.reshape(devices, capacity, width), label_row], ax...]
    ppermute x4, starting transfers between devices: 9.5 us -> 8.76 us  [ring_gather(): moving = lax.ppermute(moving, 'dp', forward)]
    add x1 -> x0, other arithmetic: 0.69 us -> none  [ring_gather(): owners = jnp.concatenate([chip_of * 2 + plane, chip_of * 2 + 1 - plane])]
  transfers between devices with their start and end apart: 9 -> 9, of which waited for: 5 -> 5; matrix products, arithmetic and copies ran while one was open for 13% -> 8% of each run, Pallas kernels for 0% -> 0%
where the time goes in v7:
time: 56.6 us; the launch traced here: 56.3 us
  waiting for transfers between devices  20.5 us (36%)
  starting transfers between devices  15.8 us (28%)
  Pallas kernels  9.84 us (17%)
  other arithmetic  5.54 us (10%)
  local copies, waits for them, and re-layouts  3.39 us (6%)
  matrix products  0.98 us (2%)
    ppermute x4, waiting for transfers between devices, ring_gather(): moving = lax.ppermute(moving, 'dp', forward)  10.9 us
    pallas_call x1, Pallas kernels, project_rows(): pl.pallas_call(projection_kernel(count, devices, features // devices, out...  9.84 us
    all_to_all x1, waiting for transfers between devices, local(): arrived = lax.all_to_all(packed, 'dp', 0, 0, tiled=True)  9.51 us
    ppermute x4, starting transfers between devices, ring_gather(): moving = lax.ppermute(moving, 'dp', forward)  8.76 us
    all_to_all x1, starting transfers between devices, local(): arrived = lax.all_to_all(packed, 'dp', 0, 0, tiled=True)  6.53 us
    unnamed x2, other arithmetic  1.7 us
    concatenate x1, other arithmetic, local(): jnp.concatenate([buffer.reshape(devices, capacity, width), label_row], ax...  1.63 us
    squeeze x1, local copies, waits for them, and re-layouts, ring_gather(): owners = jnp.asarray(table)[me]  1.2 us
  transfers between devices with their start and end apart: 9, of which 5 were waited for; matrix products, arithmetic and copies ran while one was open for 8% of the time, Pallas kernels for 0%

profile of v7, /device:TPU:0, one launch (start us, length us, event | category | flops | bytes accessed | tf_op | source)
XLA Modules:
  0.0 56.3 jit_solution(18258067075367646169)
XLA Ops:
  0.0 1.0 %pad_maximum_fusion.refs_0_ = bf16[64,944]{1,0:T(8,128)(2,1)S(1)} fusion(bf16[64,256]{1,0:T(8,128)(2,1)} %param.10, bf16[64,688]{1,0:T(8,128)(2,1)} %param.9), kind=kLoop, calls=%fused_computation.14 | loop fusion | flops 241664 | bytes 241664 | tf_op jit(solution)/shard_map/concatenate | solution.py:137
  1.0 3.1 %collective-permute-start = (bf16[64,944]{1,0:T(8,128)(2,1)S(1)}, bf16[64,944]{1,0:T(8,128)(2,1)S(1)}, u32[]{:S(2)}, u32[]{:S(2)}) collective-permute-start(bf16[64,944]{1,0:T(8,128)(2,1)S(1)} %pad_maximum_fusion.refs_0_), channel_id=1, source_target_pairs={{0,4},{4,8},{8,12},{12,14},{14,10},{10,6},{6,2},{2,0},{1,5},{5,9},... | collective-permute-start | bytes 362504 | tf_op jit(solution)/shard_map/ppermute | solution.py:39
  4.1 0.7 %reduce = s32[384]{0:T(512)S(1)} reduce(s32[384,1]{0,1:T(1,128)} %param.11, s32[]{:T(128)} %constant.3.clone.1), dimensions={1}, to_apply=%param.11.reduce_sub_computation | reduce | bytes 3076 | tf_op args[4]
  4.8 1.0 %bitcast_dynamic-update-slice_fusion.7 = bf16[8,64,944]{2,1,0:T(8,128)(2,1)S(1)} fusion(bf16[64,256]{1,0:T(8,128)(2,1)} %param.10, bf16[64,688]{1,0:T(8,128)(2,1)} %param.9), kind=kLoop, calls=%fused_computation.22 | loop fusion | flops 241663 | bytes 251904
  5.8 1.7 %collective-permute-done.refs_1_ = bf16[64,944]{1,0:T(8,128)(2,1)S(1)} collective-permute-done((bf16[64,944]{1,0:T(8,128)(2,1)S(1)}, bf16[64,944]{1,0:T(8,128)(2,1)S(1)}, u32[]{:S(2)}, u32[]{:S(2)}) %collective-permute-start) | collective-permute-done | bytes 120864 | tf_op jit(solution)/shard_map/ppermute | solution.py:39
  7.5 1.8 %collective-permute-start.1 = (bf16[64,944]{1,0:T(8,128)(2,1)S(1)}, bf16[64,944]{1,0:T(8,128)(2,1)S(1)}, u32[]{:S(2)}, u32[]{:S(2)}) collective-permute-start(bf16[64,944]{1,0:T(8,128)(2,1)S(1)} %collective-permute-done.refs_1_), channel_id=1, source_target_pairs={{0,4},{4,8},{8,12},{12,14},{14,10},{10,6},{6,2},{2,0},{1,5},{5,9},... | collective-permute-start | bytes 362504 | tf_op jit(solution)/shard_map/ppermute | solution.py:39
  9.3 0.2 collective-permute-start.5
  9.6 2.9 %collective-permute-done.1.refs_2_ = bf16[64,944]{1,0:T(8,128)(2,1)S(1)} collective-permute-done((bf16[64,944]{1,0:T(8,128)(2,1)S(1)}, bf16[64,944]{1,0:T(8,128)(2,1)S(1)}, u32[]{:S(2)}, u32[]{:S(2)}) %collective-permute-start.1) | collective-permute-done | bytes 120864 | tf_op jit(solution)/shard_map/ppermute | solution.py:39
  12.5 1.8 %collective-permute-start.2 = (bf16[64,944]{1,0:T(8,128)(2,1)S(1)}, bf16[64,944]{1,0:T(8,128)(2,1)S(1)}, u32[]{:S(2)}, u32[]{:S(2)}) collective-permute-start(bf16[64,944]{1,0:T(8,128)(2,1)S(1)} %collective-permute-done.1.refs_2_), channel_id=1, source_target_pairs={{0,4},{4,8},{8,12},{12,14},{14,10},{10,6},{6,2},{2,0},{1,5},{5,9},... | collective-permute-start | bytes 362504 | tf_op jit(solution)/shard_map/ppermute | solution.py:39
  14.3 0.2 collective-permute-start.6
  14.6 3.3 %collective-permute-done.2.refs_3_ = bf16[64,944]{1,0:T(8,128)(2,1)S(1)} collective-permute-done((bf16[64,944]{1,0:T(8,128)(2,1)S(1)}, bf16[64,944]{1,0:T(8,128)(2,1)S(1)}, u32[]{:S(2)}, u32[]{:S(2)}) %collective-permute-start.2) | collective-permute-done | bytes 120864 | tf_op jit(solution)/shard_map/ppermute | solution.py:39
  17.9 2.1 %collective-permute-start.3 = (bf16[64,944]{1,0:T(8,128)(2,1)S(1)}, bf16[64,944]{1,0:T(8,128)(2,1)S(1)}, u32[]{:S(2)}, u32[]{:S(2)}) collective-permute-start(bf16[64,944]{1,0:T(8,128)(2,1)S(1)} %collective-permute-done.2.refs_3_), channel_id=1, source_target_pairs={{0,4},{4,8},{8,12},{12,14},{14,10},{10,6},{6,2},{2,0},{1,5},{5,9},... | collective-permute-start | bytes 362504 | tf_op jit(solution)/shard_map/ppermute | solution.py:39
  20.0 2.9 %collective-permute-done.3.refs_4_ = bf16[64,944]{1,0:T(8,128)(2,1)S(1)} collective-permute-done((bf16[64,944]{1,0:T(8,128)(2,1)S(1)}, bf16[64,944]{1,0:T(8,128)(2,1)S(1)}, u32[]{:S(2)}, u32[]{:S(2)}) %collective-permute-start.3) | collective-permute-done | bytes 120864 | tf_op jit(solution)/shard_map/ppermute | solution.py:39
  23.2 0.2 fusion.2
  23.4 0.3 fusion.3
  23.8 1.2 %dynamic-slice_bitcast_fusion.owners = s32[16]{0:T(128)} fusion(s32[16,16]{1,0:T(8,128)} %constant.19.clone, s32[]{:T(128)S(6)} %select_n.3), kind=kLoop, calls=%fused_computation.31 | loop fusion | bytes 132 | tf_op jit(solution)/shard_map/squeeze | solution.py:53
  25.0 1.0 %fusion.1.refs_11_ = bf16[768,384]{1,0:T(8,128)(2,1)} fusion(s32[384]{0:T(512)S(1)} %convert_add_fusion), kind=kLoop, calls=%fused_computation.2 | loop fusion | flops 589824 | bytes 591360 | tf_op jit(solution)/shard_map/convert_element_type | solution.py:149
  26.1 1.0 %copy-done = bf16[8,64,944]{2,1,0:T(8,128)(2,1)} copy-done((bf16[8,64,944]{2,1,0:T(8,128)(2,1)}, bf16[8,64,944]{2,1,0:T(8,128)(2,1)S(1)}, u32[]{:S(2)}) %copy-start) | copy-done | bytes 966680
  27.1 9.8 %shard_map.73 = bf16[768,128]{1,0:T(8,128)(2,1)} custom-call(s32[16]{0:T(128)} %dynamic-slice_bitcast_fusion.owners, bf16[64,944]{1,0:T(8,128)(2,1)} %copy-done.1, bf16[64,944]{1,0:T(8,128)(2,1)} %copy-done.2, bf16[64,944]{1,0:T(8,128)(2,1)} %copy-done.4, bf16[64,944]{1,0:T(8,128)(2,1)} %copy-done.6, bf16[64,944]{1,0:T(8,128)(2,1)} %copy-done.8, ...), custom_call_target="tpu_custom_call" | custom-call | tf_op jit(solution)/shard_map/pallas_call | solution.py:123
  36.9 1.6 %fusion.6 = bf16[16,49,128]{2,1,0:T(8,128)(2,1)} fusion(bf16[16,1,48]{2,1,0:T(2,128)(2,1)S(1)} %reshape.71, bf16[16,48,128]{2,1,0:T(8,128)(2,1)} %bitcast.27), kind=kLoop, calls=%fused_computation.11 | loop fusion | flops 602112 | bytes 398848 | tf_op jit(solution)/shard_map/concatenate | solution.py:157
  38.5 6.5 %all-to-all-start = ((bf16[16,49,128]{2,1,0:T(8,128)(2,1)}), bf16[16,49,128]{2,1,0:T(8,128)(2,1)S(1)}, u32[]{:S(2)}, u32[]{:S(2)}) async-start(bf16[16,49,128]{2,1,0:T(8,128)(2,1)} %fusion.6), calls=%async_computation | async-start | bytes 458752 | tf_op jit(solution)/shard_map/all_to_all | solution.py:158
  45.1 9.5 %all-to-all-done = bf16[16,49,128]{2,1,0:T(8,128)(2,1)S(1)} async-done(((bf16[16,49,128]{2,1,0:T(8,128)(2,1)}), bf16[16,49,128]{2,1,0:T(8,128)(2,1)S(1)}, u32[]{:S(2)}, u32[]{:S(2)}) %all-to-all-start) | async-done | bytes 200736 | tf_op jit(solution)/shard_map/all_to_all | solution.py:158
  55.0 0.4 fusion.7
  55.5 0.8 %reshape.66 = f32[8,4096]{1,0:T(8,128)} reshape(f32[512,64]{1,0:T(8,128)S(1)} %fusion.7) | data formatting | bytes 262144 | tf_op jit(solution)/shard_map/reshape | solution.py:169
  (43 shorter events, 0.7 us)
Async XLA Ops:
  0.0 23.1 %copy-start.9 = (s32[384]{0:T(512)S(1)}, s32[384]{0:T(512)}, u32[]{:S(2)}) copy-start(s32[384]{0:T(512)} %param.12) | copy-start | bytes 4612
  1.0 22.7 %copy-start.1 = (bf16[64,944]{1,0:T(8,128)(2,1)}, bf16[64,944]{1,0:T(8,128)(2,1)S(1)}, u32[]{:S(2)}) copy-start(bf16[64,944]{1,0:T(8,128)(2,1)S(1)} %pad_maximum_fusion.refs_0_) | copy-start | bytes 362500
  1.0 6.5 %collective-permute-start = (bf16[64,944]{1,0:T(8,128)(2,1)S(1)}, bf16[64,944]{1,0:T(8,128)(2,1)S(1)}, u32[]{:S(2)}, u32[]{:S(2)}) collective-permute-start(bf16[64,944]{1,0:T(8,128)(2,1)S(1)} %pad_maximum_fusion.refs_0_), channel_id=1, source_target_pairs={{0,4},{4,8},{8,12},{12,14},{14,10},{10,6},{6,2},{2,0},{1,5},{5,9},... | collective-permute-start | bytes 362504 | tf_op jit(solution)/shard_map/ppermute | solution.py:39
  4.1 5.2 %collective-permute-start.4 = (bf16[64,944]{1,0:T(8,128)(2,1)S(1)}, bf16[64,944]{1,0:T(8,128)(2,1)S(1)}, u32[]{:S(2)}, u32[]{:S(2)}) collective-permute-start(bf16[64,944]{1,0:T(8,128)(2,1)S(1)} %pad_maximum_fusion.refs_0_), channel_id=1, source_target_pairs={{0,2},{4,0},{8,4},{12,8},{14,12},{10,14},{6,10},{2,6},{1,3},{5,1},... | collective-permute-start | bytes 362504 | tf_op jit(solution)/shard_map/ppermute | solution.py:44
  7.5 18.5 %copy-start.2 = (bf16[64,944]{1,0:T(8,128)(2,1)}, bf16[64,944]{1,0:T(8,128)(2,1)S(1)}, u32[]{:S(2)}) copy-start(bf16[64,944]{1,0:T(8,128)(2,1)S(1)} %collective-permute-done.refs_1_) | copy-start | bytes 362500
  7.5 5.0 %collective-permute-start.1 = (bf16[64,944]{1,0:T(8,128)(2,1)S(1)}, bf16[64,944]{1,0:T(8,128)(2,1)S(1)}, u32[]{:S(2)}, u32[]{:S(2)}) collective-permute-start(bf16[64,944]{1,0:T(8,128)(2,1)S(1)} %collective-permute-done.refs_1_), channel_id=1, source_target_pairs={{0,4},{4,8},{8,12},{12,14},{14,10},{10,6},{6,2},{2,0},{1,5},{5,9},... | collective-permute-start | bytes 362504 | tf_op jit(solution)/shard_map/ppermute | solution.py:39
  9.3 16.7 %copy-start.3 = (bf16[64,944]{1,0:T(8,128)(2,1)}, bf16[64,944]{1,0:T(8,128)(2,1)S(1)}, u32[]{:S(2)}) copy-start(bf16[64,944]{1,0:T(8,128)(2,1)S(1)} %collective-permute-done.4.refs_5_) | copy-start | bytes 362500
  9.3 5.0 %collective-permute-start.5 = (bf16[64,944]{1,0:T(8,128)(2,1)S(1)}, bf16[64,944]{1,0:T(8,128)(2,1)S(1)}, u32[]{:S(2)}, u32[]{:S(2)}) collective-permute-start(bf16[64,944]{1,0:T(8,128)(2,1)S(1)} %collective-permute-done.4.refs_5_), channel_id=1, source_target_pairs={{0,2},{4,0},{8,4},{12,8},{14,12},{10,14},{6,10},{2,6},{1,3},{5,1},... | collective-permute-start | bytes 362504 | tf_op jit(solution)/shard_map/ppermute | solution.py:44
  12.5 13.5 %copy-start.4 = (bf16[64,944]{1,0:T(8,128)(2,1)}, bf16[64,944]{1,0:T(8,128)(2,1)S(1)}, u32[]{:S(2)}) copy-start(bf16[64,944]{1,0:T(8,128)(2,1)S(1)} %collective-permute-done.1.refs_2_) | copy-start | bytes 362500
  12.5 5.4 %collective-permute-start.2 = (bf16[64,944]{1,0:T(8,128)(2,1)S(1)}, bf16[64,944]{1,0:T(8,128)(2,1)S(1)}, u32[]{:S(2)}, u32[]{:S(2)}) collective-permute-start(bf16[64,944]{1,0:T(8,128)(2,1)S(1)} %collective-permute-done.1.refs_2_), channel_id=1, source_target_pairs={{0,4},{4,8},{8,12},{12,14},{14,10},{10,6},{6,2},{2,0},{1,5},{5,9},... | collective-permute-start | bytes 362504 | tf_op jit(solution)/shard_map/ppermute | solution.py:39
  14.3 11.7 %copy-start.5 = (bf16[64,944]{1,0:T(8,128)(2,1)}, bf16[64,944]{1,0:T(8,128)(2,1)S(1)}, u32[]{:S(2)}) copy-start(bf16[64,944]{1,0:T(8,128)(2,1)S(1)} %collective-permute-done.5.refs_6_) | copy-start | bytes 362500
  14.3 8.7 %collective-permute-start.6 = (bf16[64,944]{1,0:T(8,128)(2,1)S(1)}, bf16[64,944]{1,0:T(8,128)(2,1)S(1)}, u32[]{:S(2)}, u32[]{:S(2)}) collective-permute-start(bf16[64,944]{1,0:T(8,128)(2,1)S(1)} %collective-permute-done.5.refs_6_), channel_id=1, source_target_pairs={{0,2},{4,0},{8,4},{12,8},{14,12},{10,14},{6,10},{2,6},{1,3},{5,1},... | collective-permute-start | bytes 362504 | tf_op jit(solution)/shard_map/ppermute | solution.py:44
  17.9 8.2 %copy-start.6 = (bf16[64,944]{1,0:T(8,128)(2,1)}, bf16[64,944]{1,0:T(8,128)(2,1)S(1)}, u32[]{:S(2)}) copy-start(bf16[64,944]{1,0:T(8,128)(2,1)S(1)} %collective-permute-done.2.refs_3_) | copy-start | bytes 362500
  17.9 5.0 %collective-permute-start.3 = (bf16[64,944]{1,0:T(8,128)(2,1)S(1)}, bf16[64,944]{1,0:T(8,128)(2,1)S(1)}, u32[]{:S(2)}, u32[]{:S(2)}) collective-permute-start(bf16[64,944]{1,0:T(8,128)(2,1)S(1)} %collective-permute-done.2.refs_3_), channel_id=1, source_target_pairs={{0,4},{4,8},{8,12},{12,14},{14,10},{10,6},{6,2},{2,0},{1,5},{5,9},... | collective-permute-start | bytes 362504 | tf_op jit(solution)/shard_map/ppermute | solution.py:39
  23.0 3.1 %copy-start.8 = (bf16[64,944]{1,0:T(8,128)(2,1)}, bf16[64,944]{1,0:T(8,128)(2,1)S(1)}, u32[]{:S(2)}) copy-start(bf16[64,944]{1,0:T(8,128)(2,1)S(1)} %collective-permute-done.3.refs_4_) | copy-start | bytes 362500
  23.0 3.1 %copy-start.7 = (bf16[64,944]{1,0:T(8,128)(2,1)}, bf16[64,944]{1,0:T(8,128)(2,1)S(1)}, u32[]{:S(2)}) copy-start(bf16[64,944]{1,0:T(8,128)(2,1)S(1)} %collective-permute-done.6.refs_7_) | copy-start | bytes 362500
  23.1 3.0 %collective-permute-start.7 = (bf16[8,64,944]{2,1,0:T(8,128)(2,1)S(1)}, bf16[8,64,944]{2,1,0:T(8,128)(2,1)S(1)}, u32[]{:S(2)}, u32[]{:S(2)}) collective-permute-start(bf16[8,64,944]{2,1,0:T(8,128)(2,1)S(1)} %bitcast_dynamic-update-slice_fusion), channel_id=1, source_target_pairs={{0,1},{4,5},{8,9},{12,13},{14,15},{10,11},{6,7},{2,3},{1,0},{5,4},... | collective-permute-start | bytes 2899976 | tf_op jit(solution)/shard_map/ppermute | solution.py:58
  26.1 1.0 %copy-start = (bf16[8,64,944]{2,1,0:T(8,128)(2,1)}, bf16[8,64,944]{2,1,0:T(8,128)(2,1)S(1)}, u32[]{:S(2)}) copy-start(bf16[8,64,944]{2,1,0:T(8,128)(2,1)S(1)} %collective-permute-done.7.refs_8_) | copy-start | bytes 2899972
  38.5 16.1 %all-to-all-start = ((bf16[16,49,128]{2,1,0:T(8,128)(2,1)}), bf16[16,49,128]{2,1,0:T(8,128)(2,1)S(1)}, u32[]{:S(2)}, u32[]{:S(2)}) async-start(bf16[16,49,128]{2,1,0:T(8,128)(2,1)} %fusion.6), calls=%async_computation | async-start | bytes 458752 | tf_op jit(solution)/shard_map/all_to_all | solution.py:158

commit v8 on v7

v8 whole, which is shorter than its diff:
```python
import numpy as np
import jax
import jax.numpy as jnp
from jax import lax
from jax.experimental import pallas as pl
from jax.experimental.pallas import tpu as pltpu
from jax.sharding import PartitionSpec as P

DOCS_DEV = 8


def ring_planes(devices):
    chips = devices // 2
    if devices % 2 or chips < 2:
        return [list(range(devices))]
    if chips % 2 == 0 and chips >= 4:
        order = list(range(0, chips, 2)) + list(range(chips - 1, 0, -2))
    else:
        order = list(range(chips))
    return [[2 * chip + core for chip in order] for core in range(2)]


def ring_gather(block, devices):
    planes = ring_planes(devices)
    length = len(planes[0])
    place = np.zeros(devices, np.int32)
    plane_of = np.zeros(devices, np.int32)
    for plane, members in enumerate(planes):
        for spot, member in enumerate(members):
            place[member] = spot
            plane_of[member] = plane
    forward = [(ring[t], ring[(t + 1) % length]) for ring in planes for t in range(length)]
    backward = [(ring[t], ring[(t - 1) % length]) for ring in planes for t in range(length)]
    blocks = [block]
    shifts = [0]
    moving = block
    for step in range(1, length // 2 + 1):
        moving = lax.ppermute(moving, "dp", forward)
        blocks.append(moving)
        shifts.append(-step)
    moving = block
    for step in range(1, length - length // 2):
        moving = lax.ppermute(moving, "dp", backward)
        blocks.append(moving)
        shifts.append(step)
    table = np.zeros((devices, len(shifts) * len(planes)), np.int32)
    for member in range(devices):
        for k, shift in enumerate(shifts):
            for side in range(len(planes)):
                ring = planes[(plane_of[member] + side) % len(planes)]
                table[member, side * len(shifts) + k] = ring[(place[member] + shift) % length]
    owners = jnp.asarray(table.reshape(-1))
    if len(planes) == 1:
        return blocks, None, owners
    mine = jnp.stack(blocks)
    swap = list(zip(planes[0], planes[1])) + list(zip(planes[1], planes[0]))
    other = lax.ppermute(mine, "dp", swap)
    return blocks, other, owners


def projection_kernel(count, devices, hidden_cols, output_cols, rank_width, paired, capacity):
    width = count * (2 if paired else 1)

    def kernel(table, *refs):
        blocks = refs[:count]
        rest = refs[count:]
        if paired:
            other_ref, rest = rest[0], rest[1:]
        hidden_ref, grad_ref, owner_ref, slot_ref, out_ref, rows, stacked, hidden_full, output_full = rest
        step = pl.program_id(0)
        tile = hidden_ref.shape[0]
        me = lax.axis_index("dp")

        @pl.when(step == 0)
        def _():
            for k in range(count):
                stacked[table[me * width + k]] = blocks[k][...]
                if paired:
                    stacked[table[me * width + count + k]] = other_ref[k]
            for d in range(devices):
                hidden_full[:, d * hidden_cols:(d + 1) * hidden_cols] = stacked[d, :, :hidden_cols]
                output_full[:, d * output_cols:(d + 1) * output_cols] = stacked[d, :, hidden_cols:]

        dims = (((1,), (1,)), ((), ()))
        left = lax.dot_general(hidden_ref[...], hidden_full[...], dims, preferred_element_type=jnp.float32)
        right = lax.dot_general(grad_ref[...], output_full[...], dims, preferred_element_type=jnp.float32)
        at = pl.multiple_of(step * tile, tile)
        rows[pl.ds(at, tile), :rank_width] = left.astype(jnp.bfloat16)
        rows[pl.ds(at, tile), rank_width:] = right.astype(jnp.bfloat16)

        @pl.when(step == pl.num_programs(0) - 1)
        def _():
            tokens, lanes = rows.shape
            targets = owner_ref[...]
            member = (targets == lax.broadcasted_iota(jnp.int32, (tokens, devices), 1)).astype(jnp.bfloat16)
            earlier = (
                lax.broadcasted_iota(jnp.int32, (tokens, tokens), 0)
                > lax.broadcasted_iota(jnp.int32, (tokens, tokens), 1)
            ).astype(jnp.bfloat16)
            before = jnp.dot(earlier, member, preferred_element_type=jnp.float32)
            position = jnp.sum(member.astype(jnp.float32) * before, axis=1, keepdims=True).astype(jnp.int32)
            slot_index = targets * capacity + position
            spread = (
                slot_index == lax.broadcasted_iota(jnp.int32, (tokens, devices * capacity), 1)
            ).astype(jnp.bfloat16)
            down = (((0,), (0,)), ((), ()))
            placed = lax.dot_general(spread, rows[...], down, preferred_element_type=jnp.float32)
            placed = placed.astype(jnp.bfloat16)
            slots = jnp.broadcast_to(slot_ref[...].astype(jnp.float32), (8, tokens)).T[:, :1]
            tagged = member * (slots + 1.0).astype(jnp.bfloat16)
            spot = (position == lax.broadcasted_iota(jnp.int32, (tokens, lanes), 1)).astype(jnp.bfloat16)
            labels = lax.dot_general(tagged, spot, down, preferred_element_type=jnp.float32)
            labels = labels.astype(jnp.bfloat16)
            for d in range(devices):
                out_ref[d, :capacity, :] = placed[d * capacity:(d + 1) * capacity, :]
                out_ref[d, capacity:, :] = labels[d:d + 1, :]

    return kernel


def project_rows(blocks, other, table, hidden, out_grad, owner_ids, doc_slot, devices, capacity):
    count = len(blocks)
    paired = other is not None
    rank_width, width = blocks[0].shape
    local_tokens, features = hidden.shape
    outputs = out_grad.shape[1]
    tile = 128 if local_tokens % 128 == 0 else local_tokens
    whole = pl.BlockSpec((rank_width, width), lambda i, table: (0, 0))
    grid_spec = pltpu.PrefetchScalarGridSpec(
        num_scalar_prefetch=1,
        grid=(local_tokens // tile,),
        in_specs=[whole] * count + [pl.BlockSpec((count, rank_width, width), lambda i, table: (0, 0, 0))] * paired + [
            pl.BlockSpec((tile, features), lambda i, table: (i, 0)),
            pl.BlockSpec((tile, outputs), lambda i, table: (i, 0)),
            pl.BlockSpec((local_tokens, 1), lambda i, table: (0, 0)),
            pl.BlockSpec((1, local_tokens), lambda i, table: (0, 0)),
        ],
        out_specs=pl.BlockSpec((devices, capacity + 1, 2 * rank_width), lambda i, table: (0, 0, 0)),
        scratch_shapes=[
            pltpu.VMEM((local_tokens, 2 * rank_width), jnp.bfloat16),
            pltpu.VMEM((devices, rank_width, width), jnp.bfloat16),
            pltpu.VMEM((rank_width, features), jnp.bfloat16),
            pltpu.VMEM((rank_width, outputs), jnp.bfloat16),
        ],
    )
    return pl.pallas_call(
        projection_kernel(count, devices, features // devices, outputs // devices, rank_width, paired, capacity),
        grid_spec=grid_spec,
        out_shape=jax.ShapeDtypeStruct((devices, capacity + 1, 2 * rank_width), jnp.bfloat16),
        compiler_params=pltpu.CompilerParams(dimension_semantics=("arbitrary",)),
    )(table, *blocks, *([other] if paired else []), hidden, out_grad, owner_ids, doc_slot.reshape(1, -1))


def local(hidden, out_grad, hidden_basis, output_basis, owner_ids, doc_slot):
    devices = lax.axis_size("dp")
    local_tokens = hidden.shape[0]
    capacity = 2 * local_tokens // devices
    rank_width = hidden_basis.shape[0]
    buffer_len = devices * capacity
    blocks, other, table = ring_gather(jnp.concatenate([hidden_basis, output_basis], axis=1), devices)
    packed = project_rows(blocks, other, table, hidden, out_grad, owner_ids, doc_slot, devices, capacity)
    arrived = lax.all_to_all(packed, "dp", 0, 0, tiled=True)
    rows_in = arrived[:, :capacity, :].reshape(buffer_len, 2 * rank_width)
    label_in = arrived[:, capacity, :capacity].reshape(buffer_len, 1)
    left_in = rows_in[:, :rank_width]
    right_in = rows_in[:, rank_width:]
    wanted = (jnp.arange(DOCS_DEV, dtype=jnp.int32) + 1).astype(jnp.bfloat16)[None, :]
    selector = (label_in == wanted).astype(jnp.bfloat16)
    weighted = (selector[:, :, None] * left_in[:, None, :]).reshape(buffer_len, DOCS_DEV * rank_width)
    grads = lax.dot_general(
        weighted, right_in, (((0,), (0,)), ((), ())), preferred_element_type=jnp.float32
    )
    return grads.reshape(DOCS_DEV, rank_width * rank_width)


def solution(mesh):
    placed = (
        P(("groups", "dp"), None),
        P(("groups", "dp"), None),
        P(None, "dp"),
        P(None, "dp"),
        P(("groups", "dp"), None),
        P(("groups", "dp")),
    )
    return jax.shard_map(
        local, mesh=mesh, in_specs=placed, out_specs=P(("groups", "dp"), None), check_vma=False
    )
```

time: 56.6 us -> 55.5 us (0.981)
  other arithmetic: 5.54 us -> 2.14 us
  local copies, waits for them, and re-layouts: 3.39 us -> 4.86 us
  Pallas kernels: 9.84 us -> 10.6 us
  waiting for transfers between devices: 20.5 us -> 21.2 us
    concatenate x1 -> x0, other arithmetic: 1.63 us -> none  [local(): jnp.concatenate([buffer.reshape(devices, capacity, width), label_row], ax...]
    unnamed x26 -> x25, local copies, waits for them, and re-layouts: 1.06 us -> 2.56 us
    squeeze x1 -> x0, local copies, waits for them, and re-layouts: 1.2 us -> none  [ring_gather(): owners = jnp.asarray(table)[me]]
    reshape x1, local copies, waits for them, and re-layouts: 0.09 us -> 1.25 us  [project_rows(): doc_slot.reshape(1, -1)]
    convert_element_type x2 -> x0, other arithmetic: 1.04 us -> none  [the longest x1 1.04 us: local(): dispatch = (jnp.arange(buffer_len, dtype=jnp.int32)[:, None] == slot_inde...]
    pallas_call x1, Pallas kernels: 9.84 us -> 10.6 us  [project_rows(): pl.pallas_call(projection_kernel(count, devices, features // devices, out...]
    ppermute x4, waiting for transfers between devices: 10.9 us -> 11.6 us  [ring_gather(): moving = lax.ppermute(moving, 'dp', forward)]
    unnamed x2 -> x1, other arithmetic: 1.7 us -> 1 us
  transfers between devices with their start and end apart: 9 -> 9, of which waited for: 5 -> 5; matrix products, arithmetic and copies ran while one was open for 8% -> 7% of each run, Pallas kernels for 0% -> 0%
where the time goes in v8:
time: 55.5 us; the launch traced here: 55.2 us
  waiting for transfers between devices  21.2 us (38%)
  starting transfers between devices  15.8 us (28%)
  Pallas kernels  10.6 us (19%)
  local copies, waits for them, and re-layouts  4.86 us (9%)
  other arithmetic  2.14 us (4%)
    ppermute x4, waiting for transfers between devices, ring_gather(): moving = lax.ppermute(moving, 'dp', forward)  11.6 us
    pallas_call x1, Pallas kernels, project_rows(): pl.pallas_call(projection_kernel(count, devices, features // devices, out...  10.6 us
    all_to_all x1, waiting for transfers between devices, local(): arrived = lax.all_to_all(packed, 'dp', 0, 0, tiled=True)  9.51 us
    ppermute x4, starting transfers between devices, ring_gather(): moving = lax.ppermute(moving, 'dp', forward)  8.76 us
    all_to_all x1, starting transfers between devices, local(): arrived = lax.all_to_all(packed, 'dp', 0, 0, tiled=True)  6.54 us
    unnamed x25, local copies, waits for them, and re-layouts  2.56 us
    reshape x1, local copies, waits for them, and re-layouts, project_rows(): doc_slot.reshape(1, -1)  1.25 us
  transfers between devices with their start and end apart: 9, of which 5 were waited for; matrix products, arithmetic and copies ran while one was open for 7% of the time, Pallas kernels for 0%

profile of v8, /device:TPU:0, one launch (start us, length us, event | category | flops | bytes accessed | tf_op | source)
XLA Modules:
  0.0 55.2 jit_solution(9785273478520661652)
XLA Ops:
  0.0 1.0 %pad_maximum_fusion.refs_0_ = bf16[64,944]{1,0:T(8,128)(2,1)S(1)} fusion(bf16[64,256]{1,0:T(8,128)(2,1)} %param.10, bf16[64,688]{1,0:T(8,128)(2,1)} %param.9), kind=kLoop, calls=%fused_computation.3 | loop fusion | flops 241664 | bytes 241664 | tf_op jit(solution)/shard_map/concatenate | solution.py:160
  1.0 3.1 %collective-permute-start = (bf16[64,944]{1,0:T(8,128)(2,1)S(1)}, bf16[64,944]{1,0:T(8,128)(2,1)S(1)}, u32[]{:S(2)}, u32[]{:S(2)}) collective-permute-start(bf16[64,944]{1,0:T(8,128)(2,1)S(1)} %pad_maximum_fusion.refs_0_), channel_id=1, source_target_pairs={{0,4},{4,8},{8,12},{12,14},{14,10},{10,6},{6,2},{2,0},{1,5},{5,9},... | collective-permute-start | bytes 362504 | tf_op jit(solution)/shard_map/ppermute | solution.py:38
  4.1 1.0 %bitcast_dynamic-update-slice_fusion.7 = bf16[8,64,944]{2,1,0:T(8,128)(2,1)S(1)} fusion(bf16[64,256]{1,0:T(8,128)(2,1)} %param.10, bf16[64,688]{1,0:T(8,128)(2,1)} %param.9), kind=kLoop, calls=%fused_computation.11 | loop fusion | flops 241663 | bytes 251904
  5.1 2.4 %collective-permute-done.refs_1_ = bf16[64,944]{1,0:T(8,128)(2,1)S(1)} collective-permute-done((bf16[64,944]{1,0:T(8,128)(2,1)S(1)}, bf16[64,944]{1,0:T(8,128)(2,1)S(1)}, u32[]{:S(2)}, u32[]{:S(2)}) %collective-permute-start) | collective-permute-done | bytes 120864 | tf_op jit(solution)/shard_map/ppermute | solution.py:38
  7.5 1.8 %collective-permute-start.1 = (bf16[64,944]{1,0:T(8,128)(2,1)S(1)}, bf16[64,944]{1,0:T(8,128)(2,1)S(1)}, u32[]{:S(2)}, u32[]{:S(2)}) collective-permute-start(bf16[64,944]{1,0:T(8,128)(2,1)S(1)} %collective-permute-done.refs_1_), channel_id=1, source_target_pairs={{0,4},{4,8},{8,12},{12,14},{14,10},{10,6},{6,2},{2,0},{1,5},{5,9},... | collective-permute-start | bytes 362504 | tf_op jit(solution)/shard_map/ppermute | solution.py:38
  9.3 0.2 collective-permute-start.5
  9.6 2.9 %collective-permute-done.1.refs_2_ = bf16[64,944]{1,0:T(8,128)(2,1)S(1)} collective-permute-done((bf16[64,944]{1,0:T(8,128)(2,1)S(1)}, bf16[64,944]{1,0:T(8,128)(2,1)S(1)}, u32[]{:S(2)}, u32[]{:S(2)}) %collective-permute-start.1) | collective-permute-done | bytes 120864 | tf_op jit(solution)/shard_map/ppermute | solution.py:38
  12.5 1.8 %collective-permute-start.2 = (bf16[64,944]{1,0:T(8,128)(2,1)S(1)}, bf16[64,944]{1,0:T(8,128)(2,1)S(1)}, u32[]{:S(2)}, u32[]{:S(2)}) collective-permute-start(bf16[64,944]{1,0:T(8,128)(2,1)S(1)} %collective-permute-done.1.refs_2_), channel_id=1, source_target_pairs={{0,4},{4,8},{8,12},{12,14},{14,10},{10,6},{6,2},{2,0},{1,5},{5,9},... | collective-permute-start | bytes 362504 | tf_op jit(solution)/shard_map/ppermute | solution.py:38
  14.3 0.2 collective-permute-start.6
  14.5 3.3 %collective-permute-done.2.refs_3_ = bf16[64,944]{1,0:T(8,128)(2,1)S(1)} collective-permute-done((bf16[64,944]{1,0:T(8,128)(2,1)S(1)}, bf16[64,944]{1,0:T(8,128)(2,1)S(1)}, u32[]{:S(2)}, u32[]{:S(2)}) %collective-permute-start.2) | collective-permute-done | bytes 120864 | tf_op jit(solution)/shard_map/ppermute | solution.py:38
  17.9 2.1 %collective-permute-start.3 = (bf16[64,944]{1,0:T(8,128)(2,1)S(1)}, bf16[64,944]{1,0:T(8,128)(2,1)S(1)}, u32[]{:S(2)}, u32[]{:S(2)}) collective-permute-start(bf16[64,944]{1,0:T(8,128)(2,1)S(1)} %collective-permute-done.2.refs_3_), channel_id=1, source_target_pairs={{0,4},{4,8},{8,12},{12,14},{14,10},{10,6},{6,2},{2,0},{1,5},{5,9},... | collective-permute-start | bytes 362504 | tf_op jit(solution)/shard_map/ppermute | solution.py:38
  20.0 2.9 %collective-permute-done.3.refs_4_ = bf16[64,944]{1,0:T(8,128)(2,1)S(1)} collective-permute-done((bf16[64,944]{1,0:T(8,128)(2,1)S(1)}, bf16[64,944]{1,0:T(8,128)(2,1)S(1)}, u32[]{:S(2)}, u32[]{:S(2)}) %collective-permute-start.3) | collective-permute-done | bytes 120864 | tf_op jit(solution)/shard_map/ppermute | solution.py:38
  23.0 0.1 collective-permute-start.7
  23.1 1.5 %copy.9.refs_11_ = s32[384,1]{1,0:T(8,128)} copy(s32[384,1]{0,1:T(1,128)} %param.11) | data formatting | bytes 3072 | tf_op args[4]
  24.6 1.3 %reshape.51.refs_12_ = s32[1,384]{1,0:T(1,128)} reshape(s32[384]{0:T(512)} %param.12) | data formatting | bytes 3072 | tf_op jit(solution)/shard_map/reshape | solution.py:151
  25.9 1.0 %copy-done = bf16[8,64,944]{2,1,0:T(8,128)(2,1)} copy-done((bf16[8,64,944]{2,1,0:T(8,128)(2,1)}, bf16[8,64,944]{2,1,0:T(8,128)(2,1)S(1)}, u32[]{:S(2)}) %copy-start) | copy-done | bytes 966680
  26.9 10.6 %shard_map.73 = bf16[16,49,128]{2,1,0:T(8,128)(2,1)} custom-call(s32[256]{0:T(256)} %constant.4.clone.table, bf16[64,944]{1,0:T(8,128)(2,1)} %copy-done.1, bf16[64,944]{1,0:T(8,128)(2,1)} %copy-done.2, bf16[64,944]{1,0:T(8,128)(2,1)} %copy-done.4, bf16[64,944]{1,0:T(8,128)(2,1)} %copy-done.6, bf16[64,944]{1,0:T(8,128)(2,1)} %copy-done.8, ...), custom_call_target="tpu_custom_call" | custom-call | tf_op jit(solution)/shard_map/pallas_call | solution.py:146
  37.5 6.5 %all-to-all-start = ((bf16[16,49,128]{2,1,0:T(8,128)(2,1)}), bf16[16,49,128]{2,1,0:T(8,128)(2,1)S(1)}, u32[]{:S(2)}, u32[]{:S(2)}) async-start(bf16[16,49,128]{2,1,0:T(8,128)(2,1)} %shard_map.73), calls=%async_computation | async-start | bytes 458752 | tf_op jit(solution)/shard_map/all_to_all | solution.py:162
  44.0 9.5 %all-to-all-done = bf16[16,49,128]{2,1,0:T(8,128)(2,1)S(1)} async-done(((bf16[16,49,128]{2,1,0:T(8,128)(2,1)}), bf16[16,49,128]{2,1,0:T(8,128)(2,1)S(1)}, u32[]{:S(2)}, u32[]{:S(2)}) %all-to-all-start) | async-done | bytes 200736 | tf_op jit(solution)/shard_map/all_to_all | solution.py:162
  53.6 0.1 copy.10
  53.7 0.1 eq.19
  53.8 0.1 compare_convert_fusion
  54.0 0.4 fusion
  54.4 0.8 %reshape.53 = f32[8,4096]{1,0:T(8,128)} reshape(f32[512,64]{1,0:T(8,128)S(1)} %fusion) | data formatting | bytes 262144 | tf_op jit(solution)/shard_map/reshape | solution.py:173
  (33 shorter events, 0.2 us)
Async XLA Ops:
  1.0 24.9 %copy-start.1 = (bf16[64,944]{1,0:T(8,128)(2,1)}, bf16[64,944]{1,0:T(8,128)(2,1)S(1)}, u32[]{:S(2)}) copy-start(bf16[64,944]{1,0:T(8,128)(2,1)S(1)} %pad_maximum_fusion.refs_0_) | copy-start | bytes 362500
  1.0 6.5 %collective-permute-start = (bf16[64,944]{1,0:T(8,128)(2,1)S(1)}, bf16[64,944]{1,0:T(8,128)(2,1)S(1)}, u32[]{:S(2)}, u32[]{:S(2)}) collective-permute-start(bf16[64,944]{1,0:T(8,128)(2,1)S(1)} %pad_maximum_fusion.refs_0_), channel_id=1, source_target_pairs={{0,4},{4,8},{8,12},{12,14},{14,10},{10,6},{6,2},{2,0},{1,5},{5,9},... | collective-permute-start | bytes 362504 | tf_op jit(solution)/shard_map/ppermute | solution.py:38
  4.1 5.2 %collective-permute-start.4 = (bf16[64,944]{1,0:T(8,128)(2,1)S(1)}, bf16[64,944]{1,0:T(8,128)(2,1)S(1)}, u32[]{:S(2)}, u32[]{:S(2)}) collective-permute-start(bf16[64,944]{1,0:T(8,128)(2,1)S(1)} %pad_maximum_fusion.refs_0_), channel_id=1, source_target_pairs={{0,2},{4,0},{8,4},{12,8},{14,12},{10,14},{6,10},{2,6},{1,3},{5,1},... | collective-permute-start | bytes 362504 | tf_op jit(solution)/shard_map/ppermute | solution.py:43
  7.5 18.3 %copy-start.2 = (bf16[64,944]{1,0:T(8,128)(2,1)}, bf16[64,944]{1,0:T(8,128)(2,1)S(1)}, u32[]{:S(2)}) copy-start(bf16[64,944]{1,0:T(8,128)(2,1)S(1)} %collective-permute-done.refs_1_) | copy-start | bytes 362500
  7.5 5.0 %collective-permute-start.1 = (bf16[64,944]{1,0:T(8,128)(2,1)S(1)}, bf16[64,944]{1,0:T(8,128)(2,1)S(1)}, u32[]{:S(2)}, u32[]{:S(2)}) collective-permute-start(bf16[64,944]{1,0:T(8,128)(2,1)S(1)} %collective-permute-done.refs_1_), channel_id=1, source_target_pairs={{0,4},{4,8},{8,12},{12,14},{14,10},{10,6},{6,2},{2,0},{1,5},{5,9},... | collective-permute-start | bytes 362504 | tf_op jit(solution)/shard_map/ppermute | solution.py:38
  9.3 16.5 %copy-start.3 = (bf16[64,944]{1,0:T(8,128)(2,1)}, bf16[64,944]{1,0:T(8,128)(2,1)S(1)}, u32[]{:S(2)}) copy-start(bf16[64,944]{1,0:T(8,128)(2,1)S(1)} %collective-permute-done.4.refs_5_) | copy-start | bytes 362500
  9.3 5.0 %collective-permute-start.5 = (bf16[64,944]{1,0:T(8,128)(2,1)S(1)}, bf16[64,944]{1,0:T(8,128)(2,1)S(1)}, u32[]{:S(2)}, u32[]{:S(2)}) collective-permute-start(bf16[64,944]{1,0:T(8,128)(2,1)S(1)} %collective-permute-done.4.refs_5_), channel_id=1, source_target_pairs={{0,2},{4,0},{8,4},{12,8},{14,12},{10,14},{6,10},{2,6},{1,3},{5,1},... | collective-permute-start | bytes 362504 | tf_op jit(solution)/shard_map/ppermute | solution.py:43
  12.5 13.4 %copy-start.4 = (bf16[64,944]{1,0:T(8,128)(2,1)}, bf16[64,944]{1,0:T(8,128)(2,1)S(1)}, u32[]{:S(2)}) copy-start(bf16[64,944]{1,0:T(8,128)(2,1)S(1)} %collective-permute-done.1.refs_2_) | copy-start | bytes 362500
  12.5 5.4 %collective-permute-start.2 = (bf16[64,944]{1,0:T(8,128)(2,1)S(1)}, bf16[64,944]{1,0:T(8,128)(2,1)S(1)}, u32[]{:S(2)}, u32[]{:S(2)}) collective-permute-start(bf16[64,944]{1,0:T(8,128)(2,1)S(1)} %collective-permute-done.1.refs_2_), channel_id=1, source_target_pairs={{0,4},{4,8},{8,12},{12,14},{14,10},{10,6},{6,2},{2,0},{1,5},{5,9},... | collective-permute-start | bytes 362504 | tf_op jit(solution)/shard_map/ppermute | solution.py:38
  14.3 11.6 %copy-start.5 = (bf16[64,944]{1,0:T(8,128)(2,1)}, bf16[64,944]{1,0:T(8,128)(2,1)S(1)}, u32[]{:S(2)}) copy-start(bf16[64,944]{1,0:T(8,128)(2,1)S(1)} %collective-permute-done.5.refs_6_) | copy-start | bytes 362500
  14.3 8.7 %collective-permute-start.6 = (bf16[64,944]{1,0:T(8,128)(2,1)S(1)}, bf16[64,944]{1,0:T(8,128)(2,1)S(1)}, u32[]{:S(2)}, u32[]{:S(2)}) collective-permute-start(bf16[64,944]{1,0:T(8,128)(2,1)S(1)} %collective-permute-done.5.refs_6_), channel_id=1, source_target_pairs={{0,2},{4,0},{8,4},{12,8},{14,12},{10,14},{6,10},{2,6},{1,3},{5,1},... | collective-permute-start | bytes 362504 | tf_op jit(solution)/shard_map/ppermute | solution.py:43
  17.9 8.0 %copy-start.6 = (bf16[64,944]{1,0:T(8,128)(2,1)}, bf16[64,944]{1,0:T(8,128)(2,1)S(1)}, u32[]{:S(2)}) copy-start(bf16[64,944]{1,0:T(8,128)(2,1)S(1)} %collective-permute-done.2.refs_3_) | copy-start | bytes 362500
  17.9 5.0 %collective-permute-start.3 = (bf16[64,944]{1,0:T(8,128)(2,1)S(1)}, bf16[64,944]{1,0:T(8,128)(2,1)S(1)}, u32[]{:S(2)}, u32[]{:S(2)}) collective-permute-start(bf16[64,944]{1,0:T(8,128)(2,1)S(1)} %collective-permute-done.2.refs_3_), channel_id=1, source_target_pairs={{0,4},{4,8},{8,12},{12,14},{14,10},{10,6},{6,2},{2,0},{1,5},{5,9},... | collective-permute-start | bytes 362504 | tf_op jit(solution)/shard_map/ppermute | solution.py:38
  22.9 3.0 %copy-start.8 = (bf16[64,944]{1,0:T(8,128)(2,1)}, bf16[64,944]{1,0:T(8,128)(2,1)S(1)}, u32[]{:S(2)}) copy-start(bf16[64,944]{1,0:T(8,128)(2,1)S(1)} %collective-permute-done.3.refs_4_) | copy-start | bytes 362500
  23.0 2.9 %copy-start.7 = (bf16[64,944]{1,0:T(8,128)(2,1)}, bf16[64,944]{1,0:T(8,128)(2,1)S(1)}, u32[]{:S(2)}) copy-start(bf16[64,944]{1,0:T(8,128)(2,1)S(1)} %collective-permute-done.6.refs_7_) | copy-start | bytes 362500
  23.0 2.8 %collective-permute-start.7 = (bf16[8,64,944]{2,1,0:T(8,128)(2,1)S(1)}, bf16[8,64,944]{2,1,0:T(8,128)(2,1)S(1)}, u32[]{:S(2)}, u32[]{:S(2)}) collective-permute-start(bf16[8,64,944]{2,1,0:T(8,128)(2,1)S(1)} %bitcast_dynamic-update-slice_fusion), channel_id=1, source_target_pairs={{0,1},{4,5},{8,9},{12,13},{14,15},{10,11},{6,7},{2,3},{1,0},{5,4},... | collective-permute-start | bytes 2899976 | tf_op jit(solution)/shard_map/ppermute | solution.py:57
  25.9 1.0 %copy-start = (bf16[8,64,944]{2,1,0:T(8,128)(2,1)}, bf16[8,64,944]{2,1,0:T(8,128)(2,1)S(1)}, u32[]{:S(2)}) copy-start(bf16[8,64,944]{2,1,0:T(8,128)(2,1)S(1)} %collective-permute-done.7.refs_8_) | copy-start | bytes 2899972
  37.5 16.1 %all-to-all-start = ((bf16[16,49,128]{2,1,0:T(8,128)(2,1)}), bf16[16,49,128]{2,1,0:T(8,128)(2,1)S(1)}, u32[]{:S(2)}, u32[]{:S(2)}) async-start(bf16[16,49,128]{2,1,0:T(8,128)(2,1)} %shard_map.73), calls=%async_computation | async-start | bytes 458752 | tf_op jit(solution)/shard_map/all_to_all | solution.py:162

commit v9 on v8

--- a/solution.py
+++ b/solution.py
@@ -91,7 +91,10 @@
         @pl.when(step == pl.num_programs(0) - 1)
         def _():
             tokens, lanes = rows.shape
-            targets = owner_ref[...]
+            rows_of = lambda ref: jnp.broadcast_to(ref[...].reshape(1, tokens).astype(jnp.float32), (8, tokens))
+            columns = jnp.concatenate([rows_of(owner_ref), rows_of(slot_ref)], axis=0).T
+            targets = columns[:, 0:1].astype(jnp.int32)
+            slots = columns[:, 8:9]
             member = (targets == lax.broadcasted_iota(jnp.int32, (tokens, devices), 1)).astype(jnp.bfloat16)
             earlier = (
                 lax.broadcasted_iota(jnp.int32, (tokens, tokens), 0)
@@ -106,7 +109,6 @@
             down = (((0,), (0,)), ((), ()))
             placed = lax.dot_general(spread, rows[...], down, preferred_element_type=jnp.float32)
             placed = placed.astype(jnp.bfloat16)
-            slots = jnp.broadcast_to(slot_ref[...].astype(jnp.float32), (8, tokens)).T[:, :1]
             tagged = member * (slots + 1.0).astype(jnp.bfloat16)
             spot = (position == lax.broadcasted_iota(jnp.int32, (tokens, lanes), 1)).astype(jnp.bfloat16)
             labels = lax.dot_general(tagged, spot, down, preferred_element_type=jnp.float32)
@@ -132,8 +134,8 @@
         in_specs=[whole] * count + [pl.BlockSpec((count, rank_width, width), lambda i, table: (0, 0, 0))] * paired + [
             pl.BlockSpec((tile, features), lambda i, table: (i, 0)),
             pl.BlockSpec((tile, outputs), lambda i, table: (i, 0)),
-            pl.BlockSpec((local_tokens, 1), lambda i, table: (0, 0)),
             pl.BlockSpec((1, local_tokens), lambda i, table: (0, 0)),
+            pl.BlockSpec((local_tokens,), lambda i, table: (0,)),
         ],
         out_specs=pl.BlockSpec((devices, capacity + 1, 2 * rank_width), lambda i, table: (0, 0, 0)),
         scratch_shapes=[
@@ -148,7 +150,7 @@
         grid_spec=grid_spec,
         out_shape=jax.ShapeDtypeStruct((devices, capacity + 1, 2 * rank_width), jnp.bfloat16),
         compiler_params=pltpu.CompilerParams(dimension_semantics=("arbitrary",)),
-    )(table, *blocks, *([other] if paired else []), hidden, out_grad, owner_ids, doc_slot.reshape(1, -1))
+    )(table, *blocks, *([other] if paired else []), hidden, out_grad, owner_ids.reshape(1, -1), doc_slot)
 
 
 def local(hidden, out_grad, hidden_basis, output_basis, owner_ids, doc_slot):

time: 55.5 us -> 55.2 us (level)
  local copies, waits for them, and re-layouts: 4.86 us -> 2.05 us
  waiting for transfers between devices: 21.2 us -> 23.8 us
    ppermute x1, waiting for transfers between devices: 0.01 us -> 2.65 us  [ring_gather(): other = lax.ppermute(mine, 'dp', swap)]
    unnamed x25 -> x24, local copies, waits for them, and re-layouts: 2.56 us -> 1.01 us
    reshape x1 -> x0, local copies, waits for them, and re-layouts: 1.25 us -> none  [project_rows(): doc_slot.reshape(1, -1)]
  transfers between devices with their start and end apart: 9 -> 9, of which waited for: 5 -> 6; matrix products, arithmetic and copies ran while one was open for 7% -> 2% of each run, Pallas kernels for 0% -> 0%
where the time goes in v9:
time: 55.2 us; the launch traced here: 55 us
  waiting for transfers between devices  23.8 us (43%)
  starting transfers between devices  15.7 us (28%)
  Pallas kernels  10.6 us (19%)
  other arithmetic  2.14 us (4%)
  local copies, waits for them, and re-layouts  2.05 us (4%)
    ppermute x4, waiting for transfers between devices, ring_gather(): moving = lax.ppermute(moving, 'dp', forward)  11.6 us
    pallas_call x1, Pallas kernels, project_rows(): pl.pallas_call(projection_kernel(count, devices, features // devices, out...  10.6 us
    all_to_all x1, waiting for transfers between devices, local(): arrived = lax.all_to_all(packed, 'dp', 0, 0, tiled=True)  9.51 us
    ppermute x4, starting transfers between devices, ring_gather(): moving = lax.ppermute(moving, 'dp', forward)  8.76 us
    all_to_all x1, starting transfers between devices, local(): arrived = lax.all_to_all(packed, 'dp', 0, 0, tiled=True)  6.44 us
    ppermute x1, waiting for transfers between devices, ring_gather(): other = lax.ppermute(mine, 'dp', swap)  2.65 us
  transfers between devices with their start and end apart: 9, of which 6 were waited for; matrix products, arithmetic and copies ran while one was open for 2% of the time, Pallas kernels for 0%

profile of v9, /device:TPU:0, one launch (start us, length us, event | category | flops | bytes accessed | tf_op | source)
XLA Modules:
  0.0 55.0 jit_solution(16002822851369167134)
XLA Ops:
  0.0 1.0 %pad_maximum_fusion.refs_0_ = bf16[64,944]{1,0:T(8,128)(2,1)S(1)} fusion(bf16[64,256]{1,0:T(8,128)(2,1)} %param.10, bf16[64,688]{1,0:T(8,128)(2,1)} %param.9), kind=kLoop, calls=%fused_computation.3 | loop fusion | flops 241664 | bytes 241664 | tf_op jit(solution)/shard_map/concatenate | solution.py:162
  1.0 3.1 %collective-permute-start = (bf16[64,944]{1,0:T(8,128)(2,1)S(1)}, bf16[64,944]{1,0:T(8,128)(2,1)S(1)}, u32[]{:S(2)}, u32[]{:S(2)}) collective-permute-start(bf16[64,944]{1,0:T(8,128)(2,1)S(1)} %pad_maximum_fusion.refs_0_), channel_id=1, source_target_pairs={{0,4},{4,8},{8,12},{12,14},{14,10},{10,6},{6,2},{2,0},{1,5},{5,9},... | collective-permute-start | bytes 362504 | tf_op jit(solution)/shard_map/ppermute | solution.py:38
  4.1 1.0 %bitcast_dynamic-update-slice_fusion.7 = bf16[8,64,944]{2,1,0:T(8,128)(2,1)S(1)} fusion(bf16[64,256]{1,0:T(8,128)(2,1)} %param.10, bf16[64,688]{1,0:T(8,128)(2,1)} %param.9), kind=kLoop, calls=%fused_computation.11 | loop fusion | flops 241663 | bytes 251904
  5.1 2.4 %collective-permute-done.refs_1_ = bf16[64,944]{1,0:T(8,128)(2,1)S(1)} collective-permute-done((bf16[64,944]{1,0:T(8,128)(2,1)S(1)}, bf16[64,944]{1,0:T(8,128)(2,1)S(1)}, u32[]{:S(2)}, u32[]{:S(2)}) %collective-permute-start) | collective-permute-done | bytes 120864 | tf_op jit(solution)/shard_map/ppermute | solution.py:38
  7.5 1.8 %collective-permute-start.1 = (bf16[64,944]{1,0:T(8,128)(2,1)S(1)}, bf16[64,944]{1,0:T(8,128)(2,1)S(1)}, u32[]{:S(2)}, u32[]{:S(2)}) collective-permute-start(bf16[64,944]{1,0:T(8,128)(2,1)S(1)} %collective-permute-done.refs_1_), channel_id=1, source_target_pairs={{0,4},{4,8},{8,12},{12,14},{14,10},{10,6},{6,2},{2,0},{1,5},{5,9},... | collective-permute-start | bytes 362504 | tf_op jit(solution)/shard_map/ppermute | solution.py:38
  9.3 0.2 collective-permute-start.5
  9.6 2.9 %collective-permute-done.1.refs_2_ = bf16[64,944]{1,0:T(8,128)(2,1)S(1)} collective-permute-done((bf16[64,944]{1,0:T(8,128)(2,1)S(1)}, bf16[64,944]{1,0:T(8,128)(2,1)S(1)}, u32[]{:S(2)}, u32[]{:S(2)}) %collective-permute-start.1) | collective-permute-done | bytes 120864 | tf_op jit(solution)/shard_map/ppermute | solution.py:38
  12.5 1.8 %collective-permute-start.2 = (bf16[64,944]{1,0:T(8,128)(2,1)S(1)}, bf16[64,944]{1,0:T(8,128)(2,1)S(1)}, u32[]{:S(2)}, u32[]{:S(2)}) collective-permute-start(bf16[64,944]{1,0:T(8,128)(2,1)S(1)} %collective-permute-done.1.refs_2_), channel_id=1, source_target_pairs={{0,4},{4,8},{8,12},{12,14},{14,10},{10,6},{6,2},{2,0},{1,5},{5,9},... | collective-permute-start | bytes 362504 | tf_op jit(solution)/shard_map/ppermute | solution.py:38
  14.3 0.2 collective-permute-start.6
  14.5 3.3 %collective-permute-done.2.refs_3_ = bf16[64,944]{1,0:T(8,128)(2,1)S(1)} collective-permute-done((bf16[64,944]{1,0:T(8,128)(2,1)S(1)}, bf16[64,944]{1,0:T(8,128)(2,1)S(1)}, u32[]{:S(2)}, u32[]{:S(2)}) %collective-permute-start.2) | collective-permute-done | bytes 120864 | tf_op jit(solution)/shard_map/ppermute | solution.py:38
  17.9 2.1 %collective-permute-start.3 = (bf16[64,944]{1,0:T(8,128)(2,1)S(1)}, bf16[64,944]{1,0:T(8,128)(2,1)S(1)}, u32[]{:S(2)}, u32[]{:S(2)}) collective-permute-start(bf16[64,944]{1,0:T(8,128)(2,1)S(1)} %collective-permute-done.2.refs_3_), channel_id=1, source_target_pairs={{0,4},{4,8},{8,12},{12,14},{14,10},{10,6},{6,2},{2,0},{1,5},{5,9},... | collective-permute-start | bytes 362504 | tf_op jit(solution)/shard_map/ppermute | solution.py:38
  20.0 2.9 %collective-permute-done.3.refs_4_ = bf16[64,944]{1,0:T(8,128)(2,1)S(1)} collective-permute-done((bf16[64,944]{1,0:T(8,128)(2,1)S(1)}, bf16[64,944]{1,0:T(8,128)(2,1)S(1)}, u32[]{:S(2)}, u32[]{:S(2)}) %collective-permute-start.3) | collective-permute-done | bytes 120864 | tf_op jit(solution)/shard_map/ppermute | solution.py:38
  23.0 0.1 collective-permute-start.7
  23.1 2.6 %collective-permute-done.7.refs_8_ = bf16[8,64,944]{2,1,0:T(8,128)(2,1)S(1)} collective-permute-done((bf16[8,64,944]{2,1,0:T(8,128)(2,1)S(1)}, bf16[8,64,944]{2,1,0:T(8,128)(2,1)S(1)}, u32[]{:S(2)}, u32[]{:S(2)}) %collective-permute-start.7) | collective-permute-done | bytes 966688 | tf_op jit(solution)/shard_map/ppermute | solution.py:57
  25.8 0.9 %copy-done = bf16[8,64,944]{2,1,0:T(8,128)(2,1)} copy-done((bf16[8,64,944]{2,1,0:T(8,128)(2,1)}, bf16[8,64,944]{2,1,0:T(8,128)(2,1)S(1)}, u32[]{:S(2)}) %copy-start) | copy-done | bytes 966680
  26.7 10.6 %shard_map.73 = bf16[16,49,128]{2,1,0:T(8,128)(2,1)} custom-call(s32[256]{0:T(256)} %constant.4.clone.table, bf16[64,944]{1,0:T(8,128)(2,1)} %copy-done.1, bf16[64,944]{1,0:T(8,128)(2,1)} %copy-done.2, bf16[64,944]{1,0:T(8,128)(2,1)} %copy-done.4, bf16[64,944]{1,0:T(8,128)(2,1)} %copy-done.6, bf16[64,944]{1,0:T(8,128)(2,1)} %copy-done.8, ...), custom_call_target="tpu_custom_call" | custom-call | tf_op jit(solution)/shard_map/pallas_call | solution.py:148
  37.4 6.4 %all-to-all-start = ((bf16[16,49,128]{2,1,0:T(8,128)(2,1)}), bf16[16,49,128]{2,1,0:T(8,128)(2,1)S(1)}, u32[]{:S(2)}, u32[]{:S(2)}) async-start(bf16[16,49,128]{2,1,0:T(8,128)(2,1)} %shard_map.73), calls=%async_computation | async-start | bytes 458752 | tf_op jit(solution)/shard_map/all_to_all | solution.py:164
  43.8 9.5 %all-to-all-done = bf16[16,49,128]{2,1,0:T(8,128)(2,1)S(1)} async-done(((bf16[16,49,128]{2,1,0:T(8,128)(2,1)}), bf16[16,49,128]{2,1,0:T(8,128)(2,1)S(1)}, u32[]{:S(2)}, u32[]{:S(2)}) %all-to-all-start) | async-done | bytes 200736 | tf_op jit(solution)/shard_map/all_to_all | solution.py:164
  53.3 0.1 copy.8
  53.5 0.1 eq.19
  53.6 0.1 compare_convert_fusion
  53.7 0.1 broadcast_multiply_fusion
  53.7 0.4 fusion
  54.2 0.8 %reshape.53 = f32[8,4096]{1,0:T(8,128)} reshape(f32[512,64]{1,0:T(8,128)S(1)} %fusion) | data formatting | bytes 262144 | tf_op jit(solution)/shard_map/reshape | solution.py:175
  (31 shorter events, 0.2 us)
Async XLA Ops:
  1.0 24.8 %copy-start.1 = (bf16[64,944]{1,0:T(8,128)(2,1)}, bf16[64,944]{1,0:T(8,128)(2,1)S(1)}, u32[]{:S(2)}) copy-start(bf16[64,944]{1,0:T(8,128)(2,1)S(1)} %pad_maximum_fusion.refs_0_) | copy-start | bytes 362500
  1.0 6.5 %collective-permute-start = (bf16[64,944]{1,0:T(8,128)(2,1)S(1)}, bf16[64,944]{1,0:T(8,128)(2,1)S(1)}, u32[]{:S(2)}, u32[]{:S(2)}) collective-permute-start(bf16[64,944]{1,0:T(8,128)(2,1)S(1)} %pad_maximum_fusion.refs_0_), channel_id=1, source_target_pairs={{0,4},{4,8},{8,12},{12,14},{14,10},{10,6},{6,2},{2,0},{1,5},{5,9},... | collective-permute-start | bytes 362504 | tf_op jit(solution)/shard_map/ppermute | solution.py:38
  4.1 5.2 %collective-permute-start.4 = (bf16[64,944]{1,0:T(8,128)(2,1)S(1)}, bf16[64,944]{1,0:T(8,128)(2,1)S(1)}, u32[]{:S(2)}, u32[]{:S(2)}) collective-permute-start(bf16[64,944]{1,0:T(8,128)(2,1)S(1)} %pad_maximum_fusion.refs_0_), channel_id=1, source_target_pairs={{0,2},{4,0},{8,4},{12,8},{14,12},{10,14},{6,10},{2,6},{1,3},{5,1},... | collective-permute-start | bytes 362504 | tf_op jit(solution)/shard_map/ppermute | solution.py:43
  7.5 18.2 %copy-start.2 = (bf16[64,944]{1,0:T(8,128)(2,1)}, bf16[64,944]{1,0:T(8,128)(2,1)S(1)}, u32[]{:S(2)}) copy-start(bf16[64,944]{1,0:T(8,128)(2,1)S(1)} %collective-permute-done.refs_1_) | copy-start | bytes 362500
  7.5 5.0 %collective-permute-start.1 = (bf16[64,944]{1,0:T(8,128)(2,1)S(1)}, bf16[64,944]{1,0:T(8,128)(2,1)S(1)}, u32[]{:S(2)}, u32[]{:S(2)}) collective-permute-start(bf16[64,944]{1,0:T(8,128)(2,1)S(1)} %collective-permute-done.refs_1_), channel_id=1, source_target_pairs={{0,4},{4,8},{8,12},{12,14},{14,10},{10,6},{6,2},{2,0},{1,5},{5,9},... | collective-permute-start | bytes 362504 | tf_op jit(solution)/shard_map/ppermute | solution.py:38
  9.3 16.4 %copy-start.3 = (bf16[64,944]{1,0:T(8,128)(2,1)}, bf16[64,944]{1,0:T(8,128)(2,1)S(1)}, u32[]{:S(2)}) copy-start(bf16[64,944]{1,0:T(8,128)(2,1)S(1)} %collective-permute-done.4.refs_5_) | copy-start | bytes 362500
  9.3 5.0 %collective-permute-start.5 = (bf16[64,944]{1,0:T(8,128)(2,1)S(1)}, bf16[64,944]{1,0:T(8,128)(2,1)S(1)}, u32[]{:S(2)}, u32[]{:S(2)}) collective-permute-start(bf16[64,944]{1,0:T(8,128)(2,1)S(1)} %collective-permute-done.4.refs_5_), channel_id=1, source_target_pairs={{0,2},{4,0},{8,4},{12,8},{14,12},{10,14},{6,10},{2,6},{1,3},{5,1},... | collective-permute-start | bytes 362504 | tf_op jit(solution)/shard_map/ppermute | solution.py:43
  12.5 13.3 %copy-start.4 = (bf16[64,944]{1,0:T(8,128)(2,1)}, bf16[64,944]{1,0:T(8,128)(2,1)S(1)}, u32[]{:S(2)}) copy-start(bf16[64,944]{1,0:T(8,128)(2,1)S(1)} %collective-permute-done.1.refs_2_) | copy-start | bytes 362500
  12.5 5.4 %collective-permute-start.2 = (bf16[64,944]{1,0:T(8,128)(2,1)S(1)}, bf16[64,944]{1,0:T(8,128)(2,1)S(1)}, u32[]{:S(2)}, u32[]{:S(2)}) collective-permute-start(bf16[64,944]{1,0:T(8,128)(2,1)S(1)} %collective-permute-done.1.refs_2_), channel_id=1, source_target_pairs={{0,4},{4,8},{8,12},{12,14},{14,10},{10,6},{6,2},{2,0},{1,5},{5,9},... | collective-permute-start | bytes 362504 | tf_op jit(solution)/shard_map/ppermute | solution.py:38
  14.3 11.5 %copy-start.5 = (bf16[64,944]{1,0:T(8,128)(2,1)}, bf16[64,944]{1,0:T(8,128)(2,1)S(1)}, u32[]{:S(2)}) copy-start(bf16[64,944]{1,0:T(8,128)(2,1)S(1)} %collective-permute-done.5.refs_6_) | copy-start | bytes 362500
  14.3 8.7 %collective-permute-start.6 = (bf16[64,944]{1,0:T(8,128)(2,1)S(1)}, bf16[64,944]{1,0:T(8,128)(2,1)S(1)}, u32[]{:S(2)}, u32[]{:S(2)}) collective-permute-start(bf16[64,944]{1,0:T(8,128)(2,1)S(1)} %collective-permute-done.5.refs_6_), channel_id=1, source_target_pairs={{0,2},{4,0},{8,4},{12,8},{14,12},{10,14},{6,10},{2,6},{1,3},{5,1},... | collective-permute-start | bytes 362504 | tf_op jit(solution)/shard_map/ppermute | solution.py:43
  17.9 7.9 %copy-start.6 = (bf16[64,944]{1,0:T(8,128)(2,1)}, bf16[64,944]{1,0:T(8,128)(2,1)S(1)}, u32[]{:S(2)}) copy-start(bf16[64,944]{1,0:T(8,128)(2,1)S(1)} %collective-permute-done.2.refs_3_) | copy-start | bytes 362500
  17.9 5.0 %collective-permute-start.3 = (bf16[64,944]{1,0:T(8,128)(2,1)S(1)}, bf16[64,944]{1,0:T(8,128)(2,1)S(1)}, u32[]{:S(2)}, u32[]{:S(2)}) collective-permute-start(bf16[64,944]{1,0:T(8,128)(2,1)S(1)} %collective-permute-done.2.refs_3_), channel_id=1, source_target_pairs={{0,4},{4,8},{8,12},{12,14},{14,10},{10,6},{6,2},{2,0},{1,5},{5,9},... | collective-permute-start | bytes 362504 | tf_op jit(solution)/shard_map/ppermute | solution.py:38
  22.9 2.9 %copy-start.8 = (bf16[64,944]{1,0:T(8,128)(2,1)}, bf16[64,944]{1,0:T(8,128)(2,1)S(1)}, u32[]{:S(2)}) copy-start(bf16[64,944]{1,0:T(8,128)(2,1)S(1)} %collective-permute-done.3.refs_4_) | copy-start | bytes 362500
  23.0 2.8 %copy-start.7 = (bf16[64,944]{1,0:T(8,128)(2,1)}, bf16[64,944]{1,0:T(8,128)(2,1)S(1)}, u32[]{:S(2)}) copy-start(bf16[64,944]{1,0:T(8,128)(2,1)S(1)} %collective-permute-done.6.refs_7_) | copy-start | bytes 362500
  23.0 2.7 %collective-permute-start.7 = (bf16[8,64,944]{2,1,0:T(8,128)(2,1)S(1)}, bf16[8,64,944]{2,1,0:T(8,128)(2,1)S(1)}, u32[]{:S(2)}, u32[]{:S(2)}) collective-permute-start(bf16[8,64,944]{2,1,0:T(8,128)(2,1)S(1)} %bitcast_dynamic-update-slice_fusion), channel_id=1, source_target_pairs={{0,1},{4,5},{8,9},{12,13},{14,15},{10,11},{6,7},{2,3},{1,0},{5,4},... | collective-permute-start | bytes 2899976 | tf_op jit(solution)/shard_map/ppermute | solution.py:57
  25.8 1.0 %copy-start = (bf16[8,64,944]{2,1,0:T(8,128)(2,1)}, bf16[8,64,944]{2,1,0:T(8,128)(2,1)S(1)}, u32[]{:S(2)}) copy-start(bf16[8,64,944]{2,1,0:T(8,128)(2,1)S(1)} %collective-permute-done.7.refs_8_) | copy-start | bytes 2899972
  37.4 16.0 %all-to-all-start = ((bf16[16,49,128]{2,1,0:T(8,128)(2,1)}), bf16[16,49,128]{2,1,0:T(8,128)(2,1)S(1)}, u32[]{:S(2)}, u32[]{:S(2)}) async-start(bf16[16,49,128]{2,1,0:T(8,128)(2,1)} %shard_map.73), calls=%async_computation | async-start | bytes 458752 | tf_op jit(solution)/shard_map/all_to_all | solution.py:164

commit v10 on v9

--- a/solution.py
+++ b/solution.py
@@ -153,6 +153,131 @@
     )(table, *blocks, *([other] if paired else []), hidden, out_grad, owner_ids.reshape(1, -1), doc_slot)
 
 
+def half_kernel(count, hidden_cols, output_cols, rank_width, first, capacity, devices):
+    def kernel(table, *refs):
+        if first:
+            blocks = refs[:count]
+            hidden_ref, grad_ref, acc_ref, stacked = refs[count:]
+        else:
+            other_ref, hidden_ref, grad_ref, part_ref, owner_ref, slot_ref, out_ref, rows, stacked = refs
+        step = pl.program_id(0)
+        tile = hidden_ref.shape[0]
+        me = lax.axis_index("dp")
+        core = me % 2
+
+        @pl.when(step == 0)
+        def _():
+            for k in range(count):
+                if first:
+                    stacked[table[me * 2 * count + k] // 2] = blocks[k][...]
+                else:
+                    stacked[table[me * 2 * count + count + k] // 2] = other_ref[k]
+
+        dims = (((1,), (1,)), ((), ()))
+
+        def partial(side):
+            left = None
+            right = None
+            for chip in range(count):
+                d = 2 * chip + side
+                part = stacked[chip]
+                one = lax.dot_general(
+                    hidden_ref[:, d * hidden_cols:(d + 1) * hidden_cols], part[:, :hidden_cols], dims,
+                    preferred_element_type=jnp.float32,
+                )
+                two = lax.dot_general(
+                    grad_ref[:, d * output_cols:(d + 1) * output_cols], part[:, hidden_cols:], dims,
+                    preferred_element_type=jnp.float32,
+                )
+                left = one if left is None else left + one
+                right = two if right is None else right + two
+            return jnp.concatenate([left, right], axis=1)
+
+        mine_side = core if first else 1 - core
+        summed = lax.cond(mine_side == 0, lambda: partial(0), lambda: partial(1))
+        if first:
+            acc_ref[...] = summed
+            return
+        at = pl.multiple_of(step * tile, tile)
+        rows[pl.ds(at, tile), :] = (summed + part_ref[...]).astype(jnp.bfloat16)
+
+        @pl.when(step == pl.num_programs(0) - 1)
+        def _():
+            tokens, lanes = rows.shape
+            rows_of = lambda ref: jnp.broadcast_to(ref[...].reshape(1, tokens).astype(jnp.float32), (8, tokens))
+            columns = jnp.concatenate([rows_of(owner_ref), rows_of(slot_ref)], axis=0).T
+            targets = columns[:, 0:1].astype(jnp.int32)
+            slots = columns[:, 8:9]
+            member = (targets == lax.broadcasted_iota(jnp.int32, (tokens, devices), 1)).astype(jnp.bfloat16)
+            earlier = (
+                lax.broadcasted_iota(jnp.int32, (tokens, tokens), 0)
+                > lax.broadcasted_iota(jnp.int32, (tokens, tokens), 1)
+            ).astype(jnp.bfloat16)
+            before = jnp.dot(earlier, member, preferred_element_type=jnp.float32)
+            position = jnp.sum(member.astype(jnp.float32) * before, axis=1, keepdims=True).astype(jnp.int32)
+            slot_index = targets * capacity + position
+            spread = (
+                slot_index == lax.broadcasted_iota(jnp.int32, (tokens, devices * capacity), 1)
+            ).astype(jnp.bfloat16)
+            down = (((0,), (0,)), ((), ()))
+            placed = lax.dot_general(spread, rows[...], down, preferred_element_type=jnp.float32)
+            placed = placed.astype(jnp.bfloat16)
+            tagged = member * (slots + 1.0).astype(jnp.bfloat16)
+            spot = (position == lax.broadcasted_iota(jnp.int32, (tokens, lanes), 1)).astype(jnp.bfloat16)
+            labels = lax.dot_general(tagged, spot, down, preferred_element_type=jnp.float32)
+            labels = labels.astype(jnp.bfloat16)
+            for d in range(devices):
+                out_ref[d, :capacity, :] = placed[d * capacity:(d + 1) * capacity, :]
+                out_ref[d, capacity:, :] = labels[d:d + 1, :]
+
+    return kernel
+
+
+def project_in_halves(blocks, other, table, hidden, out_grad, owner_ids, doc_slot, devices, capacity):
+    count = len(blocks)
+    rank_width, width = blocks[0].shape
+    local_tokens, features = hidden.shape
+    outputs = out_grad.shape[1]
+    tile = 128 if local_tokens % 128 == 0 else local_tokens
+    grid = (local_tokens // tile,)
+    token_specs = [
+        pl.BlockSpec((tile, features), lambda i, table: (i, 0)),
+        pl.BlockSpec((tile, outputs), lambda i, table: (i, 0)),
+    ]
+    part_spec = pl.BlockSpec((tile, 2 * rank_width), lambda i, table: (i, 0))
+    stacked = pltpu.VMEM((count, rank_width, width), jnp.bfloat16)
+    params = pltpu.CompilerParams(dimension_semantics=("arbitrary",))
+    shape = (features // devices, outputs // devices, rank_width)
+    first = pl.pallas_call(
+        half_kernel(count, *shape, True, capacity, devices),
+        grid_spec=pltpu.PrefetchScalarGridSpec(
+            num_scalar_prefetch=1,
+            grid=grid,
+            in_specs=[pl.BlockSpec((rank_width, width), lambda i, table: (0, 0))] * count + token_specs,
+            out_specs=part_spec,
+            scratch_shapes=[stacked],
+        ),
+        out_shape=jax.ShapeDtypeStruct((local_tokens, 2 * rank_width), jnp.float32),
+        compiler_params=params,
+    )(table, *blocks, hidden, out_grad)
+    return pl.pallas_call(
+        half_kernel(count, *shape, False, capacity, devices),
+        grid_spec=pltpu.PrefetchScalarGridSpec(
+            num_scalar_prefetch=1,
+            grid=grid,
+            in_specs=[pl.BlockSpec((count, rank_width, width), lambda i, table: (0, 0, 0))] + token_specs + [
+                part_spec,
+                pl.BlockSpec((1, local_tokens), lambda i, table: (0, 0)),
+                pl.BlockSpec((local_tokens,), lambda i, table: (0,)),
+            ],
+            out_specs=pl.BlockSpec((devices, capacity + 1, 2 * rank_width), lambda i, table: (0, 0, 0)),
+            scratch_shapes=[pltpu.VMEM((local_tokens, 2 * rank_width), jnp.bfloat16), stacked],
+        ),
+        out_shape=jax.ShapeDtypeStruct((devices, capacity + 1, 2 * rank_width), jnp.bfloat16),
+        compiler_params=params,
+    )(table, other, hidden, out_grad, first, owner_ids.reshape(1, -1), doc_slot)
+
+
 def local(hidden, out_grad, hidden_basis, output_basis, owner_ids, doc_slot):
     devices = lax.axis_size("dp")
     local_tokens = hidden.shape[0]
@@ -160,7 +285,10 @@
     rank_width = hidden_basis.shape[0]
     buffer_len = devices * capacity
     blocks, other, table = ring_gather(jnp.concatenate([hidden_basis, output_basis], axis=1), devices)
-    packed = project_rows(blocks, other, table, hidden, out_grad, owner_ids, doc_slot, devices, capacity)
+    if other is None:
+        packed = project_rows(blocks, other, table, hidden, out_grad, owner_ids, doc_slot, devices, capacity)
+    else:
+        packed = project_in_halves(blocks, other, table, hidden, out_grad, owner_ids, doc_slot, devices, capacity)
     arrived = lax.all_to_all(packed, "dp", 0, 0, tiled=True)
     rows_in = arrived[:, :capacity, :].reshape(buffer_len, 2 * rank_width)
     label_in = arrived[:, capacity, :capacity].reshape(buffer_len, 1)

time: 55.2 us -> 59.4 us (1.076)
  Pallas kernels: 10.6 us -> 16.8 us
  waiting for transfers between devices: 23.8 us -> 21.2 us
    pallas_call x1 -> x2, Pallas kernels: 10.6 us -> 16.8 us  [the longest x1 9.17 us: project_in_halves(): pl.pallas_call(half_kernel(count, *shape, False, capacity, devices), grid...]
    ppermute x1, waiting for transfers between devices: 2.65 us -> 0.01 us  [ring_gather(): other = lax.ppermute(mine, 'dp', swap)]
  transfers between devices with their start and end apart: 9 -> 9, of which waited for: 6 -> 5; matrix products, arithmetic and copies ran while one was open for 2% -> 2% of each run, Pallas kernels for 0% -> 13%
where the time goes in v10:
time: 59.4 us; the launch traced here: 59.1 us
  waiting for transfers between devices  21.2 us (36%)
  Pallas kernels  16.8 us (28%)
  starting transfers between devices  15.7 us (26%)
  local copies, waits for them, and re-layouts  2.59 us (4%)
  other arithmetic  2.14 us (4%)
    ppermute x4, waiting for transfers between devices, ring_gather(): moving = lax.ppermute(moving, 'dp', forward)  11.6 us
    all_to_all x1, waiting for transfers between devices, local(): arrived = lax.all_to_all(packed, 'dp', 0, 0, tiled=True)  9.51 us
    pallas_call x1, Pallas kernels, project_in_halves(): pl.pallas_call(half_kernel(count, *shape, False, capacity, devices), grid...  9.17 us
    ppermute x4, starting transfers between devices, ring_gather(): moving = lax.ppermute(moving, 'dp', forward)  8.76 us
    pallas_call x1, Pallas kernels, project_in_halves(): pl.pallas_call(half_kernel(count, *shape, True, capacity, devices), grid_...  7.63 us
    all_to_all x1, starting transfers between devices, local(): arrived = lax.all_to_all(packed, 'dp', 0, 0, tiled=True)  6.44 us
    unnamed x24, local copies, waits for them, and re-layouts  1.54 us
  transfers between devices with their start and end apart: 9, of which 5 were waited for; matrix products, arithmetic and copies ran while one was open for 2% of the time, Pallas kernels for 13%

profile of v10, /device:TPU:0, one launch (start us, length us, event | category | flops | bytes accessed | tf_op | source)
XLA Modules:
  0.0 59.1 jit_solution(1123955410890642803)
XLA Ops:
  0.0 1.0 %pad_maximum_fusion.refs_0_ = bf16[64,944]{1,0:T(8,128)(2,1)S(1)} fusion(bf16[64,256]{1,0:T(8,128)(2,1)} %param.10, bf16[64,688]{1,0:T(8,128)(2,1)} %param.9), kind=kLoop, calls=%fused_computation.3 | loop fusion | flops 241664 | bytes 241664 | tf_op jit(solution)/shard_map/concatenate | solution.py:287
  1.0 3.1 %collective-permute-start = (bf16[64,944]{1,0:T(8,128)(2,1)S(1)}, bf16[64,944]{1,0:T(8,128)(2,1)S(1)}, u32[]{:S(2)}, u32[]{:S(2)}) collective-permute-start(bf16[64,944]{1,0:T(8,128)(2,1)S(1)} %pad_maximum_fusion.refs_0_), channel_id=1, source_target_pairs={{0,4},{4,8},{8,12},{12,14},{14,10},{10,6},{6,2},{2,0},{1,5},{5,9},... | collective-permute-start | bytes 362504 | tf_op jit(solution)/shard_map/ppermute | solution.py:38
  4.1 1.0 %bitcast_dynamic-update-slice_fusion.7 = bf16[8,64,944]{2,1,0:T(8,128)(2,1)S(1)} fusion(bf16[64,256]{1,0:T(8,128)(2,1)} %param.10, bf16[64,688]{1,0:T(8,128)(2,1)} %param.9), kind=kLoop, calls=%fused_computation.11 | loop fusion | flops 241663 | bytes 251904
  5.1 2.4 %collective-permute-done.refs_1_ = bf16[64,944]{1,0:T(8,128)(2,1)S(1)} collective-permute-done((bf16[64,944]{1,0:T(8,128)(2,1)S(1)}, bf16[64,944]{1,0:T(8,128)(2,1)S(1)}, u32[]{:S(2)}, u32[]{:S(2)}) %collective-permute-start) | collective-permute-done | bytes 120864 | tf_op jit(solution)/shard_map/ppermute | solution.py:38
  7.5 1.8 %collective-permute-start.1 = (bf16[64,944]{1,0:T(8,128)(2,1)S(1)}, bf16[64,944]{1,0:T(8,128)(2,1)S(1)}, u32[]{:S(2)}, u32[]{:S(2)}) collective-permute-start(bf16[64,944]{1,0:T(8,128)(2,1)S(1)} %collective-permute-done.refs_1_), channel_id=1, source_target_pairs={{0,4},{4,8},{8,12},{12,14},{14,10},{10,6},{6,2},{2,0},{1,5},{5,9},... | collective-permute-start | bytes 362504 | tf_op jit(solution)/shard_map/ppermute | solution.py:38
  9.3 0.2 collective-permute-start.5
  9.6 2.9 %collective-permute-done.1.refs_2_ = bf16[64,944]{1,0:T(8,128)(2,1)S(1)} collective-permute-done((bf16[64,944]{1,0:T(8,128)(2,1)S(1)}, bf16[64,944]{1,0:T(8,128)(2,1)S(1)}, u32[]{:S(2)}, u32[]{:S(2)}) %collective-permute-start.1) | collective-permute-done | bytes 120864 | tf_op jit(solution)/shard_map/ppermute | solution.py:38
  12.5 1.8 %collective-permute-start.2 = (bf16[64,944]{1,0:T(8,128)(2,1)S(1)}, bf16[64,944]{1,0:T(8,128)(2,1)S(1)}, u32[]{:S(2)}, u32[]{:S(2)}) collective-permute-start(bf16[64,944]{1,0:T(8,128)(2,1)S(1)} %collective-permute-done.1.refs_2_), channel_id=1, source_target_pairs={{0,4},{4,8},{8,12},{12,14},{14,10},{10,6},{6,2},{2,0},{1,5},{5,9},... | collective-permute-start | bytes 362504 | tf_op jit(solution)/shard_map/ppermute | solution.py:38
  14.3 0.2 collective-permute-start.6
  14.5 3.3 %collective-permute-done.2.refs_3_ = bf16[64,944]{1,0:T(8,128)(2,1)S(1)} collective-permute-done((bf16[64,944]{1,0:T(8,128)(2,1)S(1)}, bf16[64,944]{1,0:T(8,128)(2,1)S(1)}, u32[]{:S(2)}, u32[]{:S(2)}) %collective-permute-start.2) | collective-permute-done | bytes 120864 | tf_op jit(solution)/shard_map/ppermute | solution.py:38
  17.9 2.1 %collective-permute-start.3 = (bf16[64,944]{1,0:T(8,128)(2,1)S(1)}, bf16[64,944]{1,0:T(8,128)(2,1)S(1)}, u32[]{:S(2)}, u32[]{:S(2)}) collective-permute-start(bf16[64,944]{1,0:T(8,128)(2,1)S(1)} %collective-permute-done.2.refs_3_), channel_id=1, source_target_pairs={{0,4},{4,8},{8,12},{12,14},{14,10},{10,6},{6,2},{2,0},{1,5},{5,9},... | collective-permute-start | bytes 362504 | tf_op jit(solution)/shard_map/ppermute | solution.py:38
  20.0 2.9 %collective-permute-done.3.refs_4_ = bf16[64,944]{1,0:T(8,128)(2,1)S(1)} collective-permute-done((bf16[64,944]{1,0:T(8,128)(2,1)S(1)}, bf16[64,944]{1,0:T(8,128)(2,1)S(1)}, u32[]{:S(2)}, u32[]{:S(2)}) %collective-permute-start.3) | collective-permute-done | bytes 120864 | tf_op jit(solution)/shard_map/ppermute | solution.py:38
  23.0 0.1 collective-permute-start.7
  23.2 0.4 copy-done.8
  23.7 7.6 %shard_map.73.refs_3_ = f32[384,128]{1,0:T(8,128)} custom-call(s32[256]{0:T(256)} %constant.4.clone.table, bf16[64,944]{1,0:T(8,128)(2,1)} %copy-done.1, bf16[64,944]{1,0:T(8,128)(2,1)} %copy-done.2, bf16[64,944]{1,0:T(8,128)(2,1)} %copy-done.4, bf16[64,944]{1,0:T(8,128)(2,1)} %copy-done.6, bf16[64,944]{1,0:T(8,128)(2,1)} %copy-done.8, ...), custom_call_target="tpu_custom_call" | custom-call | tf_op jit(solution)/shard_map/pallas_call | solution.py:251
  31.3 1.0 %copy-done = bf16[8,64,944]{2,1,0:T(8,128)(2,1)} copy-done((bf16[8,64,944]{2,1,0:T(8,128)(2,1)}, bf16[8,64,944]{2,1,0:T(8,128)(2,1)S(1)}, u32[]{:S(2)}) %copy-start) | copy-done | bytes 966680
  32.3 9.2 %shard_map.74 = bf16[16,49,128]{2,1,0:T(8,128)(2,1)} custom-call(s32[256]{0:T(256)} %constant.4.clone.table, bf16[8,64,944]{2,1,0:T(8,128)(2,1)} %copy-done, bf16[384,11008]{1,0:T(8,128)(2,1)} %refs_1_.1, bf16[384,4096]{1,0:T(8,128)(2,1)} %refs_2_.1, f32[384,128]{1,0:T(8,128)} %shard_map.73.refs_3_, s32[1,384]{1,0:T(1,128)} %bitcast.24, s32[384]{0:T(512)} %refs_5_.1), custom_call_target="tpu_custom_call" | custom-call | tf_op jit(solution)/shard_map/pallas_call | solution.py:263
  41.4 6.4 %all-to-all-start = ((bf16[16,49,128]{2,1,0:T(8,128)(2,1)}), bf16[16,49,128]{2,1,0:T(8,128)(2,1)S(1)}, u32[]{:S(2)}, u32[]{:S(2)}) async-start(bf16[16,49,128]{2,1,0:T(8,128)(2,1)} %shard_map.74), calls=%async_computation | async-start | bytes 458752 | tf_op jit(solution)/shard_map/all_to_all | solution.py:292
  47.9 9.5 %all-to-all-done = bf16[16,49,128]{2,1,0:T(8,128)(2,1)S(1)} async-done(((bf16[16,49,128]{2,1,0:T(8,128)(2,1)}), bf16[16,49,128]{2,1,0:T(8,128)(2,1)S(1)}, u32[]{:S(2)}, u32[]{:S(2)}) %all-to-all-start) | async-done | bytes 200736 | tf_op jit(solution)/shard_map/all_to_all | solution.py:292
  57.4 0.1 copy.8
  57.6 0.1 eq.19
  57.7 0.1 compare_convert_fusion
  57.8 0.4 fusion
  58.3 0.8 %reshape.53 = f32[8,4096]{1,0:T(8,128)} reshape(f32[512,64]{1,0:T(8,128)S(1)} %fusion) | data formatting | bytes 262144 | tf_op jit(solution)/shard_map/reshape | solution.py:303
  (32 shorter events, 0.3 us)
Async XLA Ops:
  1.0 22.1 %copy-start.1 = (bf16[64,944]{1,0:T(8,128)(2,1)}, bf16[64,944]{1,0:T(8,128)(2,1)S(1)}, u32[]{:S(2)}) copy-start(bf16[64,944]{1,0:T(8,128)(2,1)S(1)} %pad_maximum_fusion.refs_0_) | copy-start | bytes 362500
  1.0 6.5 %collective-permute-start = (bf16[64,944]{1,0:T(8,128)(2,1)S(1)}, bf16[64,944]{1,0:T(8,128)(2,1)S(1)}, u32[]{:S(2)}, u32[]{:S(2)}) collective-permute-start(bf16[64,944]{1,0:T(8,128)(2,1)S(1)} %pad_maximum_fusion.refs_0_), channel_id=1, source_target_pairs={{0,4},{4,8},{8,12},{12,14},{14,10},{10,6},{6,2},{2,0},{1,5},{5,9},... | collective-permute-start | bytes 362504 | tf_op jit(solution)/shard_map/ppermute | solution.py:38
  4.1 5.2 %collective-permute-start.4 = (bf16[64,944]{1,0:T(8,128)(2,1)S(1)}, bf16[64,944]{1,0:T(8,128)(2,1)S(1)}, u32[]{:S(2)}, u32[]{:S(2)}) collective-permute-start(bf16[64,944]{1,0:T(8,128)(2,1)S(1)} %pad_maximum_fusion.refs_0_), channel_id=1, source_target_pairs={{0,2},{4,0},{8,4},{12,8},{14,12},{10,14},{6,10},{2,6},{1,3},{5,1},... | collective-permute-start | bytes 362504 | tf_op jit(solution)/shard_map/ppermute | solution.py:43
  7.5 15.6 %copy-start.2 = (bf16[64,944]{1,0:T(8,128)(2,1)}, bf16[64,944]{1,0:T(8,128)(2,1)S(1)}, u32[]{:S(2)}) copy-start(bf16[64,944]{1,0:T(8,128)(2,1)S(1)} %collective-permute-done.refs_1_) | copy-start | bytes 362500
  7.5 5.0 %collective-permute-start.1 = (bf16[64,944]{1,0:T(8,128)(2,1)S(1)}, bf16[64,944]{1,0:T(8,128)(2,1)S(1)}, u32[]{:S(2)}, u32[]{:S(2)}) collective-permute-start(bf16[64,944]{1,0:T(8,128)(2,1)S(1)} %collective-permute-done.refs_1_), channel_id=1, source_target_pairs={{0,4},{4,8},{8,12},{12,14},{14,10},{10,6},{6,2},{2,0},{1,5},{5,9},... | collective-permute-start | bytes 362504 | tf_op jit(solution)/shard_map/ppermute | solution.py:38
  9.3 13.8 %copy-start.3 = (bf16[64,944]{1,0:T(8,128)(2,1)}, bf16[64,944]{1,0:T(8,128)(2,1)S(1)}, u32[]{:S(2)}) copy-start(bf16[64,944]{1,0:T(8,128)(2,1)S(1)} %collective-permute-done.4.refs_5_) | copy-start | bytes 362500
  9.3 5.0 %collective-permute-start.5 = (bf16[64,944]{1,0:T(8,128)(2,1)S(1)}, bf16[64,944]{1,0:T(8,128)(2,1)S(1)}, u32[]{:S(2)}, u32[]{:S(2)}) collective-permute-start(bf16[64,944]{1,0:T(8,128)(2,1)S(1)} %collective-permute-done.4.refs_5_), channel_id=1, source_target_pairs={{0,2},{4,0},{8,4},{12,8},{14,12},{10,14},{6,10},{2,6},{1,3},{5,1},... | collective-permute-start | bytes 362504 | tf_op jit(solution)/shard_map/ppermute | solution.py:43
  12.5 10.6 %copy-start.4 = (bf16[64,944]{1,0:T(8,128)(2,1)}, bf16[64,944]{1,0:T(8,128)(2,1)S(1)}, u32[]{:S(2)}) copy-start(bf16[64,944]{1,0:T(8,128)(2,1)S(1)} %collective-permute-done.1.refs_2_) | copy-start | bytes 362500
  12.5 5.4 %collective-permute-start.2 = (bf16[64,944]{1,0:T(8,128)(2,1)S(1)}, bf16[64,944]{1,0:T(8,128)(2,1)S(1)}, u32[]{:S(2)}, u32[]{:S(2)}) collective-permute-start(bf16[64,944]{1,0:T(8,128)(2,1)S(1)} %collective-permute-done.1.refs_2_), channel_id=1, source_target_pairs={{0,4},{4,8},{8,12},{12,14},{14,10},{10,6},{6,2},{2,0},{1,5},{5,9},... | collective-permute-start | bytes 362504 | tf_op jit(solution)/shard_map/ppermute | solution.py:38
  14.3 8.9 %copy-start.5 = (bf16[64,944]{1,0:T(8,128)(2,1)}, bf16[64,944]{1,0:T(8,128)(2,1)S(1)}, u32[]{:S(2)}) copy-start(bf16[64,944]{1,0:T(8,128)(2,1)S(1)} %collective-permute-done.5.refs_6_) | copy-start | bytes 362500
  14.3 8.7 %collective-permute-start.6 = (bf16[64,944]{1,0:T(8,128)(2,1)S(1)}, bf16[64,944]{1,0:T(8,128)(2,1)S(1)}, u32[]{:S(2)}, u32[]{:S(2)}) collective-permute-start(bf16[64,944]{1,0:T(8,128)(2,1)S(1)} %collective-permute-done.5.refs_6_), channel_id=1, source_target_pairs={{0,2},{4,0},{8,4},{12,8},{14,12},{10,14},{6,10},{2,6},{1,3},{5,1},... | collective-permute-start | bytes 362504 | tf_op jit(solution)/shard_map/ppermute | solution.py:43
  17.9 5.3 %copy-start.6 = (bf16[64,944]{1,0:T(8,128)(2,1)}, bf16[64,944]{1,0:T(8,128)(2,1)S(1)}, u32[]{:S(2)}) copy-start(bf16[64,944]{1,0:T(8,128)(2,1)S(1)} %collective-permute-done.2.refs_3_) | copy-start | bytes 362500
  17.9 5.0 %collective-permute-start.3 = (bf16[64,944]{1,0:T(8,128)(2,1)S(1)}, bf16[64,944]{1,0:T(8,128)(2,1)S(1)}, u32[]{:S(2)}, u32[]{:S(2)}) collective-permute-start(bf16[64,944]{1,0:T(8,128)(2,1)S(1)} %collective-permute-done.2.refs_3_), channel_id=1, source_target_pairs={{0,4},{4,8},{8,12},{12,14},{14,10},{10,6},{6,2},{2,0},{1,5},{5,9},... | collective-permute-start | bytes 362504 | tf_op jit(solution)/shard_map/ppermute | solution.py:38
  22.9 0.7 %copy-start.8 = (bf16[64,944]{1,0:T(8,128)(2,1)}, bf16[64,944]{1,0:T(8,128)(2,1)S(1)}, u32[]{:S(2)}) copy-start(bf16[64,944]{1,0:T(8,128)(2,1)S(1)} %collective-permute-done.3.refs_4_) | copy-start | bytes 362500
  23.0 0.7 %copy-start.7 = (bf16[64,944]{1,0:T(8,128)(2,1)}, bf16[64,944]{1,0:T(8,128)(2,1)S(1)}, u32[]{:S(2)}) copy-start(bf16[64,944]{1,0:T(8,128)(2,1)S(1)} %collective-permute-done.6.refs_7_) | copy-start | bytes 362500
  23.0 8.3 %collective-permute-start.7 = (bf16[8,64,944]{2,1,0:T(8,128)(2,1)S(1)}, bf16[8,64,944]{2,1,0:T(8,128)(2,1)S(1)}, u32[]{:S(2)}, u32[]{:S(2)}) collective-permute-start(bf16[8,64,944]{2,1,0:T(8,128)(2,1)S(1)} %bitcast_dynamic-update-slice_fusion), channel_id=1, source_target_pairs={{0,1},{4,5},{8,9},{12,13},{14,15},{10,11},{6,7},{2,3},{1,0},{5,4},... | collective-permute-start | bytes 2899976 | tf_op jit(solution)/shard_map/ppermute | solution.py:57
  31.3 1.0 %copy-start = (bf16[8,64,944]{2,1,0:T(8,128)(2,1)}, bf16[8,64,944]{2,1,0:T(8,128)(2,1)S(1)}, u32[]{:S(2)}) copy-start(bf16[8,64,944]{2,1,0:T(8,128)(2,1)S(1)} %collective-permute-done.7.refs_0_) | copy-start | bytes 2899972
  41.4 16.0 %all-to-all-start = ((bf16[16,49,128]{2,1,0:T(8,128)(2,1)}), bf16[16,49,128]{2,1,0:T(8,128)(2,1)S(1)}, u32[]{:S(2)}, u32[]{:S(2)}) async-start(bf16[16,49,128]{2,1,0:T(8,128)(2,1)} %shard_map.74), calls=%async_computation | async-start | bytes 458752 | tf_op jit(solution)/shard_map/all_to_all | solution.py:292

commit v11 on v9

--- a/solution.py
+++ b/solution.py
@@ -82,36 +82,33 @@
                 output_full[:, d * output_cols:(d + 1) * output_cols] = stacked[d, :, hidden_cols:]
 
         dims = (((1,), (1,)), ((), ()))
-        left = lax.dot_general(hidden_ref[...], hidden_full[...], dims, preferred_element_type=jnp.float32)
-        right = lax.dot_general(grad_ref[...], output_full[...], dims, preferred_element_type=jnp.float32)
+        left = lax.dot_general(hidden_full[...], hidden_ref[...], dims, preferred_element_type=jnp.float32)
+        right = lax.dot_general(output_full[...], grad_ref[...], dims, preferred_element_type=jnp.float32)
         at = pl.multiple_of(step * tile, tile)
-        rows[pl.ds(at, tile), :rank_width] = left.astype(jnp.bfloat16)
-        rows[pl.ds(at, tile), rank_width:] = right.astype(jnp.bfloat16)
+        rows[:rank_width, pl.ds(at, tile)] = left.astype(jnp.bfloat16)
+        rows[rank_width:, pl.ds(at, tile)] = right.astype(jnp.bfloat16)
 
         @pl.when(step == pl.num_programs(0) - 1)
         def _():
-            tokens, lanes = rows.shape
-            rows_of = lambda ref: jnp.broadcast_to(ref[...].reshape(1, tokens).astype(jnp.float32), (8, tokens))
-            columns = jnp.concatenate([rows_of(owner_ref), rows_of(slot_ref)], axis=0).T
-            targets = columns[:, 0:1].astype(jnp.int32)
-            slots = columns[:, 8:9]
-            member = (targets == lax.broadcasted_iota(jnp.int32, (tokens, devices), 1)).astype(jnp.bfloat16)
-            earlier = (
+            lanes, tokens = rows.shape
+            targets = owner_ref[...]
+            slots = slot_ref[...].reshape(1, tokens)
+            member = (targets == lax.broadcasted_iota(jnp.int32, (devices, tokens), 0)).astype(jnp.bfloat16)
+            later = (
                 lax.broadcasted_iota(jnp.int32, (tokens, tokens), 0)
-                > lax.broadcasted_iota(jnp.int32, (tokens, tokens), 1)
+                < lax.broadcasted_iota(jnp.int32, (tokens, tokens), 1)
             ).astype(jnp.bfloat16)
-            before = jnp.dot(earlier, member, preferred_element_type=jnp.float32)
-            position = jnp.sum(member.astype(jnp.float32) * before, axis=1, keepdims=True).astype(jnp.int32)
+            before = jnp.dot(member, later, preferred_element_type=jnp.float32)
+            position = jnp.sum(member.astype(jnp.float32) * before, axis=0, keepdims=True).astype(jnp.int32)
             slot_index = targets * capacity + position
             spread = (
-                slot_index == lax.broadcasted_iota(jnp.int32, (tokens, devices * capacity), 1)
+                lax.broadcasted_iota(jnp.int32, (devices * capacity, tokens), 0) == slot_index
             ).astype(jnp.bfloat16)
-            down = (((0,), (0,)), ((), ()))
-            placed = lax.dot_general(spread, rows[...], down, preferred_element_type=jnp.float32)
+            placed = lax.dot_general(spread, rows[...], dims, preferred_element_type=jnp.float32)
             placed = placed.astype(jnp.bfloat16)
-            tagged = member * (slots + 1.0).astype(jnp.bfloat16)
-            spot = (position == lax.broadcasted_iota(jnp.int32, (tokens, lanes), 1)).astype(jnp.bfloat16)
-            labels = lax.dot_general(tagged, spot, down, preferred_element_type=jnp.float32)
+            tagged = member * (slots + 1).astype(jnp.bfloat16)
+            spot = (lax.broadcasted_iota(jnp.int32, (lanes, tokens), 0) == position).astype(jnp.bfloat16)
+            labels = lax.dot_general(tagged, spot, dims, preferred_element_type=jnp.float32)
             labels = labels.astype(jnp.bfloat16)
             for d in range(devices):
                 out_ref[d, :capacity, :] = placed[d * capacity:(d + 1) * capacity, :]
@@ -139,7 +136,7 @@
         ],
         out_specs=pl.BlockSpec((devices, capacity + 1, 2 * rank_width), lambda i, table: (0, 0, 0)),
         scratch_shapes=[
-            pltpu.VMEM((local_tokens, 2 * rank_width), jnp.bfloat16),
+            pltpu.VMEM((2 * rank_width, local_tokens), jnp.bfloat16),
             pltpu.VMEM((devices, rank_width, width), jnp.bfloat16),
             pltpu.VMEM((rank_width, features), jnp.bfloat16),
             pltpu.VMEM((rank_width, outputs), jnp.bfloat16),

time: 55.2 us -> 55.2 us (level)
  no operation moved by 1% of the time
where the time goes in v11:
time: 55.2 us; the launch traced here: 54.9 us
  waiting for transfers between devices  23.8 us (43%)
  starting transfers between devices  15.7 us (28%)
  Pallas kernels  10.6 us (19%)
  other arithmetic  2.14 us (4%)
  local copies, waits for them, and re-layouts  2.05 us (4%)
    ppermute x4, waiting for transfers between devices, ring_gather(): moving = lax.ppermute(moving, 'dp', forward)  11.6 us
    pallas_call x1, Pallas kernels, project_rows(): pl.pallas_call(projection_kernel(count, devices, features // devices, out...  10.6 us
    all_to_all x1, waiting for transfers between devices, local(): arrived = lax.all_to_all(packed, 'dp', 0, 0, tiled=True)  9.51 us
    ppermute x4, starting transfers between devices, ring_gather(): moving = lax.ppermute(moving, 'dp', forward)  8.76 us
    all_to_all x1, starting transfers between devices, local(): arrived = lax.all_to_all(packed, 'dp', 0, 0, tiled=True)  6.44 us
    ppermute x1, waiting for transfers between devices, ring_gather(): other = lax.ppermute(mine, 'dp', swap)  2.65 us
  transfers between devices with their start and end apart: 9, of which 6 were waited for; matrix products, arithmetic and copies ran while one was open for 2% of the time, Pallas kernels for 0%

profile of v11, /device:TPU:0, one launch (start us, length us, event | category | flops | bytes accessed | tf_op | source)
XLA Modules:
  0.0 54.9 jit_solution(14694490206707200673)
XLA Ops:
  0.0 1.0 %pad_maximum_fusion.refs_0_ = bf16[64,944]{1,0:T(8,128)(2,1)S(1)} fusion(bf16[64,256]{1,0:T(8,128)(2,1)} %param.10, bf16[64,688]{1,0:T(8,128)(2,1)} %param.9), kind=kLoop, calls=%fused_computation.3 | loop fusion | flops 241664 | bytes 241664 | tf_op jit(solution)/shard_map/concatenate | solution.py:159
  1.0 3.1 %collective-permute-start = (bf16[64,944]{1,0:T(8,128)(2,1)S(1)}, bf16[64,944]{1,0:T(8,128)(2,1)S(1)}, u32[]{:S(2)}, u32[]{:S(2)}) collective-permute-start(bf16[64,944]{1,0:T(8,128)(2,1)S(1)} %pad_maximum_fusion.refs_0_), channel_id=1, source_target_pairs={{0,4},{4,8},{8,12},{12,14},{14,10},{10,6},{6,2},{2,0},{1,5},{5,9},... | collective-permute-start | bytes 362504 | tf_op jit(solution)/shard_map/ppermute | solution.py:38
  4.1 1.0 %bitcast_dynamic-update-slice_fusion.7 = bf16[8,64,944]{2,1,0:T(8,128)(2,1)S(1)} fusion(bf16[64,256]{1,0:T(8,128)(2,1)} %param.10, bf16[64,688]{1,0:T(8,128)(2,1)} %param.9), kind=kLoop, calls=%fused_computation.11 | loop fusion | flops 241663 | bytes 251904
  5.1 2.4 %collective-permute-done.refs_1_ = bf16[64,944]{1,0:T(8,128)(2,1)S(1)} collective-permute-done((bf16[64,944]{1,0:T(8,128)(2,1)S(1)}, bf16[64,944]{1,0:T(8,128)(2,1)S(1)}, u32[]{:S(2)}, u32[]{:S(2)}) %collective-permute-start) | collective-permute-done | bytes 120864 | tf_op jit(solution)/shard_map/ppermute | solution.py:38
  7.5 1.8 %collective-permute-start.1 = (bf16[64,944]{1,0:T(8,128)(2,1)S(1)}, bf16[64,944]{1,0:T(8,128)(2,1)S(1)}, u32[]{:S(2)}, u32[]{:S(2)}) collective-permute-start(bf16[64,944]{1,0:T(8,128)(2,1)S(1)} %collective-permute-done.refs_1_), channel_id=1, source_target_pairs={{0,4},{4,8},{8,12},{12,14},{14,10},{10,6},{6,2},{2,0},{1,5},{5,9},... | collective-permute-start | bytes 362504 | tf_op jit(solution)/shard_map/ppermute | solution.py:38
  9.3 0.2 collective-permute-start.5
  9.6 2.9 %collective-permute-done.1.refs_2_ = bf16[64,944]{1,0:T(8,128)(2,1)S(1)} collective-permute-done((bf16[64,944]{1,0:T(8,128)(2,1)S(1)}, bf16[64,944]{1,0:T(8,128)(2,1)S(1)}, u32[]{:S(2)}, u32[]{:S(2)}) %collective-permute-start.1) | collective-permute-done | bytes 120864 | tf_op jit(solution)/shard_map/ppermute | solution.py:38
  12.5 1.8 %collective-permute-start.2 = (bf16[64,944]{1,0:T(8,128)(2,1)S(1)}, bf16[64,944]{1,0:T(8,128)(2,1)S(1)}, u32[]{:S(2)}, u32[]{:S(2)}) collective-permute-start(bf16[64,944]{1,0:T(8,128)(2,1)S(1)} %collective-permute-done.1.refs_2_), channel_id=1, source_target_pairs={{0,4},{4,8},{8,12},{12,14},{14,10},{10,6},{6,2},{2,0},{1,5},{5,9},... | collective-permute-start | bytes 362504 | tf_op jit(solution)/shard_map/ppermute | solution.py:38
  14.3 0.2 collective-permute-start.6
  14.5 3.3 %collective-permute-done.2.refs_3_ = bf16[64,944]{1,0:T(8,128)(2,1)S(1)} collective-permute-done((bf16[64,944]{1,0:T(8,128)(2,1)S(1)}, bf16[64,944]{1,0:T(8,128)(2,1)S(1)}, u32[]{:S(2)}, u32[]{:S(2)}) %collective-permute-start.2) | collective-permute-done | bytes 120864 | tf_op jit(solution)/shard_map/ppermute | solution.py:38
  17.9 2.1 %collective-permute-start.3 = (bf16[64,944]{1,0:T(8,128)(2,1)S(1)}, bf16[64,944]{1,0:T(8,128)(2,1)S(1)}, u32[]{:S(2)}, u32[]{:S(2)}) collective-permute-start(bf16[64,944]{1,0:T(8,128)(2,1)S(1)} %collective-permute-done.2.refs_3_), channel_id=1, source_target_pairs={{0,4},{4,8},{8,12},{12,14},{14,10},{10,6},{6,2},{2,0},{1,5},{5,9},... | collective-permute-start | bytes 362504 | tf_op jit(solution)/shard_map/ppermute | solution.py:38
  20.0 2.9 %collective-permute-done.3.refs_4_ = bf16[64,944]{1,0:T(8,128)(2,1)S(1)} collective-permute-done((bf16[64,944]{1,0:T(8,128)(2,1)S(1)}, bf16[64,944]{1,0:T(8,128)(2,1)S(1)}, u32[]{:S(2)}, u32[]{:S(2)}) %collective-permute-start.3) | collective-permute-done | bytes 120864 | tf_op jit(solution)/shard_map/ppermute | solution.py:38
  23.0 0.1 collective-permute-start.7
  23.1 2.6 %collective-permute-done.7.refs_8_ = bf16[8,64,944]{2,1,0:T(8,128)(2,1)S(1)} collective-permute-done((bf16[8,64,944]{2,1,0:T(8,128)(2,1)S(1)}, bf16[8,64,944]{2,1,0:T(8,128)(2,1)S(1)}, u32[]{:S(2)}, u32[]{:S(2)}) %collective-permute-start.7) | collective-permute-done | bytes 966688 | tf_op jit(solution)/shard_map/ppermute | solution.py:57
  25.8 0.9 %copy-done = bf16[8,64,944]{2,1,0:T(8,128)(2,1)} copy-done((bf16[8,64,944]{2,1,0:T(8,128)(2,1)}, bf16[8,64,944]{2,1,0:T(8,128)(2,1)S(1)}, u32[]{:S(2)}) %copy-start) | copy-done | bytes 966680
  26.7 10.6 %shard_map.73 = bf16[16,49,128]{2,1,0:T(8,128)(2,1)} custom-call(s32[256]{0:T(256)} %constant.4.clone.table, bf16[64,944]{1,0:T(8,128)(2,1)} %copy-done.1, bf16[64,944]{1,0:T(8,128)(2,1)} %copy-done.2, bf16[64,944]{1,0:T(8,128)(2,1)} %copy-done.4, bf16[64,944]{1,0:T(8,128)(2,1)} %copy-done.6, bf16[64,944]{1,0:T(8,128)(2,1)} %copy-done.8, ...), custom_call_target="tpu_custom_call" | custom-call | tf_op jit(solution)/shard_map/pallas_call | solution.py:145
  37.3 6.4 %all-to-all-start = ((bf16[16,49,128]{2,1,0:T(8,128)(2,1)}), bf16[16,49,128]{2,1,0:T(8,128)(2,1)S(1)}, u32[]{:S(2)}, u32[]{:S(2)}) async-start(bf16[16,49,128]{2,1,0:T(8,128)(2,1)} %shard_map.73), calls=%async_computation | async-start | bytes 458752 | tf_op jit(solution)/shard_map/all_to_all | solution.py:161
  43.7 9.5 %all-to-all-done = bf16[16,49,128]{2,1,0:T(8,128)(2,1)S(1)} async-done(((bf16[16,49,128]{2,1,0:T(8,128)(2,1)}), bf16[16,49,128]{2,1,0:T(8,128)(2,1)S(1)}, u32[]{:S(2)}, u32[]{:S(2)}) %all-to-all-start) | async-done | bytes 200736 | tf_op jit(solution)/shard_map/all_to_all | solution.py:161
  53.3 0.1 copy.8
  53.4 0.1 eq.19
  53.5 0.1 compare_convert_fusion
  53.6 0.1 broadcast_multiply_fusion
  53.7 0.4 fusion
  54.1 0.8 %reshape.53 = f32[8,4096]{1,0:T(8,128)} reshape(f32[512,64]{1,0:T(8,128)S(1)} %fusion) | data formatting | bytes 262144 | tf_op jit(solution)/shard_map/reshape | solution.py:172
  (31 shorter events, 0.2 us)
Async XLA Ops:
  1.0 24.8 %copy-start.1 = (bf16[64,944]{1,0:T(8,128)(2,1)}, bf16[64,944]{1,0:T(8,128)(2,1)S(1)}, u32[]{:S(2)}) copy-start(bf16[64,944]{1,0:T(8,128)(2,1)S(1)} %pad_maximum_fusion.refs_0_) | copy-start | bytes 362500
  1.0 6.5 %collective-permute-start = (bf16[64,944]{1,0:T(8,128)(2,1)S(1)}, bf16[64,944]{1,0:T(8,128)(2,1)S(1)}, u32[]{:S(2)}, u32[]{:S(2)}) collective-permute-start(bf16[64,944]{1,0:T(8,128)(2,1)S(1)} %pad_maximum_fusion.refs_0_), channel_id=1, source_target_pairs={{0,4},{4,8},{8,12},{12,14},{14,10},{10,6},{6,2},{2,0},{1,5},{5,9},... | collective-permute-start | bytes 362504 | tf_op jit(solution)/shard_map/ppermute | solution.py:38
  4.1 5.2 %collective-permute-start.4 = (bf16[64,944]{1,0:T(8,128)(2,1)S(1)}, bf16[64,944]{1,0:T(8,128)(2,1)S(1)}, u32[]{:S(2)}, u32[]{:S(2)}) collective-permute-start(bf16[64,944]{1,0:T(8,128)(2,1)S(1)} %pad_maximum_fusion.refs_0_), channel_id=1, source_target_pairs={{0,2},{4,0},{8,4},{12,8},{14,12},{10,14},{6,10},{2,6},{1,3},{5,1},... | collective-permute-start | bytes 362504 | tf_op jit(solution)/shard_map/ppermute | solution.py:43
  7.5 18.2 %copy-start.2 = (bf16[64,944]{1,0:T(8,128)(2,1)}, bf16[64,944]{1,0:T(8,128)(2,1)S(1)}, u32[]{:S(2)}) copy-start(bf16[64,944]{1,0:T(8,128)(2,1)S(1)} %collective-permute-done.refs_1_) | copy-start | bytes 362500
  7.5 5.0 %collective-permute-start.1 = (bf16[64,944]{1,0:T(8,128)(2,1)S(1)}, bf16[64,944]{1,0:T(8,128)(2,1)S(1)}, u32[]{:S(2)}, u32[]{:S(2)}) collective-permute-start(bf16[64,944]{1,0:T(8,128)(2,1)S(1)} %collective-permute-done.refs_1_), channel_id=1, source_target_pairs={{0,4},{4,8},{8,12},{12,14},{14,10},{10,6},{6,2},{2,0},{1,5},{5,9},... | collective-permute-start | bytes 362504 | tf_op jit(solution)/shard_map/ppermute | solution.py:38
  9.3 16.4 %copy-start.3 = (bf16[64,944]{1,0:T(8,128)(2,1)}, bf16[64,944]{1,0:T(8,128)(2,1)S(1)}, u32[]{:S(2)}) copy-start(bf16[64,944]{1,0:T(8,128)(2,1)S(1)} %collective-permute-done.4.refs_5_) | copy-start | bytes 362500
  9.3 5.0 %collective-permute-start.5 = (bf16[64,944]{1,0:T(8,128)(2,1)S(1)}, bf16[64,944]{1,0:T(8,128)(2,1)S(1)}, u32[]{:S(2)}, u32[]{:S(2)}) collective-permute-start(bf16[64,944]{1,0:T(8,128)(2,1)S(1)} %collective-permute-done.4.refs_5_), channel_id=1, source_target_pairs={{0,2},{4,0},{8,4},{12,8},{14,12},{10,14},{6,10},{2,6},{1,3},{5,1},... | collective-permute-start | bytes 362504 | tf_op jit(solution)/shard_map/ppermute | solution.py:43
  12.5 13.3 %copy-start.4 = (bf16[64,944]{1,0:T(8,128)(2,1)}, bf16[64,944]{1,0:T(8,128)(2,1)S(1)}, u32[]{:S(2)}) copy-start(bf16[64,944]{1,0:T(8,128)(2,1)S(1)} %collective-permute-done.1.refs_2_) | copy-start | bytes 362500
  12.5 5.4 %collective-permute-start.2 = (bf16[64,944]{1,0:T(8,128)(2,1)S(1)}, bf16[64,944]{1,0:T(8,128)(2,1)S(1)}, u32[]{:S(2)}, u32[]{:S(2)}) collective-permute-start(bf16[64,944]{1,0:T(8,128)(2,1)S(1)} %collective-permute-done.1.refs_2_), channel_id=1, source_target_pairs={{0,4},{4,8},{8,12},{12,14},{14,10},{10,6},{6,2},{2,0},{1,5},{5,9},... | collective-permute-start | bytes 362504 | tf_op jit(solution)/shard_map/ppermute | solution.py:38
  14.3 11.5 %copy-start.5 = (bf16[64,944]{1,0:T(8,128)(2,1)}, bf16[64,944]{1,0:T(8,128)(2,1)S(1)}, u32[]{:S(2)}) copy-start(bf16[64,944]{1,0:T(8,128)(2,1)S(1)} %collective-permute-done.5.refs_6_) | copy-start | bytes 362500
  14.3 8.7 %collective-permute-start.6 = (bf16[64,944]{1,0:T(8,128)(2,1)S(1)}, bf16[64,944]{1,0:T(8,128)(2,1)S(1)}, u32[]{:S(2)}, u32[]{:S(2)}) collective-permute-start(bf16[64,944]{1,0:T(8,128)(2,1)S(1)} %collective-permute-done.5.refs_6_), channel_id=1, source_target_pairs={{0,2},{4,0},{8,4},{12,8},{14,12},{10,14},{6,10},{2,6},{1,3},{5,1},... | collective-permute-start | bytes 362504 | tf_op jit(solution)/shard_map/ppermute | solution.py:43
  17.9 7.9 %copy-start.6 = (bf16[64,944]{1,0:T(8,128)(2,1)}, bf16[64,944]{1,0:T(8,128)(2,1)S(1)}, u32[]{:S(2)}) copy-start(bf16[64,944]{1,0:T(8,128)(2,1)S(1)} %collective-permute-done.2.refs_3_) | copy-start | bytes 362500
  17.9 5.0 %collective-permute-start.3 = (bf16[64,944]{1,0:T(8,128)(2,1)S(1)}, bf16[64,944]{1,0:T(8,128)(2,1)S(1)}, u32[]{:S(2)}, u32[]{:S(2)}) collective-permute-start(bf16[64,944]{1,0:T(8,128)(2,1)S(1)} %collective-permute-done.2.refs_3_), channel_id=1, source_target_pairs={{0,4},{4,8},{8,12},{12,14},{14,10},{10,6},{6,2},{2,0},{1,5},{5,9},... | collective-permute-start | bytes 362504 | tf_op jit(solution)/shard_map/ppermute | solution.py:38
  22.9 2.9 %copy-start.8 = (bf16[64,944]{1,0:T(8,128)(2,1)}, bf16[64,944]{1,0:T(8,128)(2,1)S(1)}, u32[]{:S(2)}) copy-start(bf16[64,944]{1,0:T(8,128)(2,1)S(1)} %collective-permute-done.3.refs_4_) | copy-start | bytes 362500
  23.0 2.8 %copy-start.7 = (bf16[64,944]{1,0:T(8,128)(2,1)}, bf16[64,944]{1,0:T(8,128)(2,1)S(1)}, u32[]{:S(2)}) copy-start(bf16[64,944]{1,0:T(8,128)(2,1)S(1)} %collective-permute-done.6.refs_7_) | copy-start | bytes 362500
  23.0 2.7 %collective-permute-start.7 = (bf16[8,64,944]{2,1,0:T(8,128)(2,1)S(1)}, bf16[8,64,944]{2,1,0:T(8,128)(2,1)S(1)}, u32[]{:S(2)}, u32[]{:S(2)}) collective-permute-start(bf16[8,64,944]{2,1,0:T(8,128)(2,1)S(1)} %bitcast_dynamic-update-slice_fusion), channel_id=1, source_target_pairs={{0,1},{4,5},{8,9},{12,13},{14,15},{10,11},{6,7},{2,3},{1,0},{5,4},... | collective-permute-start | bytes 2899976 | tf_op jit(solution)/shard_map/ppermute | solution.py:57
  25.8 1.0 %copy-start = (bf16[8,64,944]{2,1,0:T(8,128)(2,1)}, bf16[8,64,944]{2,1,0:T(8,128)(2,1)S(1)}, u32[]{:S(2)}) copy-start(bf16[8,64,944]{2,1,0:T(8,128)(2,1)S(1)} %collective-permute-done.7.refs_8_) | copy-start | bytes 2899972
  37.3 16.0 %all-to-all-start = ((bf16[16,49,128]{2,1,0:T(8,128)(2,1)}), bf16[16,49,128]{2,1,0:T(8,128)(2,1)S(1)}, u32[]{:S(2)}, u32[]{:S(2)}) async-start(bf16[16,49,128]{2,1,0:T(8,128)(2,1)} %shard_map.73), calls=%async_computation | async-start | bytes 458752 | tf_op jit(solution)/shard_map/all_to_all | solution.py:161

commit v12 on v11

--- a/solution.py
+++ b/solution.py
@@ -31,18 +31,20 @@
             plane_of[member] = plane
     forward = [(ring[t], ring[(t + 1) % length]) for ring in planes for t in range(length)]
     backward = [(ring[t], ring[(t - 1) % length]) for ring in planes for t in range(length)]
-    blocks = [block]
-    shifts = [0]
-    moving = block
+    early, late = [block], []
+    early_shifts, late_shifts = [0], []
+    split = max(1, length // 4)
+    ahead = behind = block
     for step in range(1, length // 2 + 1):
-        moving = lax.ppermute(moving, "dp", forward)
-        blocks.append(moving)
-        shifts.append(-step)
-    moving = block
-    for step in range(1, length - length // 2):
-        moving = lax.ppermute(moving, "dp", backward)
-        blocks.append(moving)
-        shifts.append(step)
+        ahead = lax.ppermute(ahead, "dp", forward)
+        (early if step <= split else late).append(ahead)
+        (early_shifts if step <= split else late_shifts).append(-step)
+        if step < length - length // 2:
+            behind = lax.ppermute(behind, "dp", backward)
+            (early if step <= split else late).append(behind)
+            (early_shifts if step <= split else late_shifts).append(step)
+    blocks = early + late
+    shifts = early_shifts + late_shifts
     table = np.zeros((devices, len(shifts) * len(planes)), np.int32)
     for member in range(devices):
         for k, shift in enumerate(shifts):
@@ -52,9 +54,8 @@
     owners = jnp.asarray(table.reshape(-1))
     if len(planes) == 1:
         return blocks, None, owners
-    mine = jnp.stack(blocks)
     swap = list(zip(planes[0], planes[1])) + list(zip(planes[1], planes[0]))
-    other = lax.ppermute(mine, "dp", swap)
+    other = [lax.ppermute(jnp.stack(group), "dp", swap) for group in (early, late) if group]
     return blocks, other, owners
 
 
@@ -65,7 +66,7 @@
         blocks = refs[:count]
         rest = refs[count:]
         if paired:
-            other_ref, rest = rest[0], rest[1:]
+            other_refs, rest = rest[:len(paired)], rest[len(paired):]
         hidden_ref, grad_ref, owner_ref, slot_ref, out_ref, rows, stacked, hidden_full, output_full = rest
         step = pl.program_id(0)
         tile = hidden_ref.shape[0]
@@ -75,8 +76,11 @@
         def _():
             for k in range(count):
                 stacked[table[me * width + k]] = blocks[k][...]
-                if paired:
-                    stacked[table[me * width + count + k]] = other_ref[k]
+            at = count
+            for other_ref, size in zip(other_refs if paired else (), paired):
+                for k in range(size):
+                    stacked[table[me * width + at + k]] = other_ref[k]
+                at += size
             for d in range(devices):
                 hidden_full[:, d * hidden_cols:(d + 1) * hidden_cols] = stacked[d, :, :hidden_cols]
                 output_full[:, d * output_cols:(d + 1) * output_cols] = stacked[d, :, hidden_cols:]
@@ -119,7 +123,7 @@
 
 def project_rows(blocks, other, table, hidden, out_grad, owner_ids, doc_slot, devices, capacity):
     count = len(blocks)
-    paired = other is not None
+    paired = tuple(part.shape[0] for part in other) if other is not None else ()
     rank_width, width = blocks[0].shape
     local_tokens, features = hidden.shape
     outputs = out_grad.shape[1]
@@ -128,7 +132,7 @@
     grid_spec = pltpu.PrefetchScalarGridSpec(
         num_scalar_prefetch=1,
         grid=(local_tokens // tile,),
-        in_specs=[whole] * count + [pl.BlockSpec((count, rank_width, width), lambda i, table: (0, 0, 0))] * paired + [
+        in_specs=[whole] * count + [pl.BlockSpec(part.shape, lambda i, table: (0, 0, 0)) for part in (other or [])] + [
             pl.BlockSpec((tile, features), lambda i, table: (i, 0)),
             pl.BlockSpec((tile, outputs), lambda i, table: (i, 0)),
             pl.BlockSpec((1, local_tokens), lambda i, table: (0, 0)),
@@ -147,7 +151,7 @@
         grid_spec=grid_spec,
         out_shape=jax.ShapeDtypeStruct((devices, capacity + 1, 2 * rank_width), jnp.bfloat16),
         compiler_params=pltpu.CompilerParams(dimension_semantics=("arbitrary",)),
-    )(table, *blocks, *([other] if paired else []), hidden, out_grad, owner_ids.reshape(1, -1), doc_slot)
+    )(table, *blocks, *(other or []), hidden, out_grad, owner_ids.reshape(1, -1), doc_slot)
 
 
 def local(hidden, out_grad, hidden_basis, output_basis, owner_ids, doc_slot):

time: 55.2 us -> 53.9 us (0.976)
  waiting for transfers between devices: 23.8 us -> 22.7 us
    ppermute x8 -> x9, waiting for transfers between devices: 14.3 us -> 13.2 us  [the longest x4 11.5 us: ring_gather(): ahead = lax.ppermute(ahead, 'dp', forward)]
    ppermute x8 -> x9, starting transfers between devices: 9.3 us -> 9.37 us  [the longest x4 8.76 us: ring_gather(): ahead = lax.ppermute(ahead, 'dp', forward)]
  transfers between devices with their start and end apart: 9 -> 10, of which waited for: 6 -> 6; matrix products, arithmetic and copies ran while one was open for 2% -> 2% of each run, Pallas kernels for 0% -> 0%
where the time goes in v12:
time: 53.9 us; the launch traced here: 53.6 us
  waiting for transfers between devices  22.7 us (42%)
  starting transfers between devices  15.8 us (29%)
  Pallas kernels  10.5 us (19%)
  other arithmetic  2.19 us (4%)
  local copies, waits for them, and re-layouts  1.8 us (3%)
    ppermute x4, waiting for transfers between devices, ring_gather(): ahead = lax.ppermute(ahead, 'dp', forward)  11.5 us
    pallas_call x1, Pallas kernels, project_rows(): pl.pallas_call(projection_kernel(count, devices, features // devices, out...  10.5 us
    all_to_all x1, waiting for transfers between devices, local(): arrived = lax.all_to_all(packed, 'dp', 0, 0, tiled=True)  9.51 us
    ppermute x4, starting transfers between devices, ring_gather(): ahead = lax.ppermute(ahead, 'dp', forward)  8.76 us
    all_to_all x1, starting transfers between devices, local(): arrived = lax.all_to_all(packed, 'dp', 0, 0, tiled=True)  6.44 us
    ppermute x2, waiting for transfers between devices, ring_gather(): lax.ppermute(jnp.stack(group), 'dp', swap)  1.69 us
  transfers between devices with their start and end apart: 10, of which 6 were waited for; matrix products, arithmetic and copies ran while one was open for 2% of the time, Pallas kernels for 0%

profile of v12, /device:TPU:0, one launch (start us, length us, event | category | flops | bytes accessed | tf_op | source)
XLA Modules:
  0.0 53.6 jit_solution(13433264749581830630)
XLA Ops:
  0.0 1.0 %pad_maximum_fusion.1.refs_0_ = bf16[64,944]{1,0:T(8,128)(2,1)S(1)} fusion(bf16[64,256]{1,0:T(8,128)(2,1)} %param.10, bf16[64,688]{1,0:T(8,128)(2,1)} %param.9), kind=kLoop, calls=%fused_computation.4 | loop fusion | flops 241664 | bytes 241664 | tf_op jit(solution)/shard_map/concatenate | solution.py:163
  1.0 3.1 %collective-permute-start = (bf16[64,944]{1,0:T(8,128)(2,1)S(1)}, bf16[64,944]{1,0:T(8,128)(2,1)S(1)}, u32[]{:S(2)}, u32[]{:S(2)}) collective-permute-start(bf16[64,944]{1,0:T(8,128)(2,1)S(1)} %pad_maximum_fusion.1.refs_0_), channel_id=1, source_target_pairs={{0,4},{4,8},{8,12},{12,14},{14,10},{10,6},{6,2},{2,0},{1,5},{5,9},... | collective-permute-start | bytes 362504 | tf_op jit(solution)/shard_map/ppermute | solution.py:39
  4.1 1.0 %bitcast_dynamic-update-slice_fusion.4 = bf16[5,64,944]{2,1,0:T(8,128)(2,1)S(1)} fusion(bf16[64,256]{1,0:T(8,128)(2,1)} %param.10, bf16[64,688]{1,0:T(8,128)(2,1)} %param.9), kind=kLoop, calls=%fused_computation.9 | loop fusion | flops 241663 | bytes 251904
  5.1 2.4 %collective-permute-done.refs_1_ = bf16[64,944]{1,0:T(8,128)(2,1)S(1)} collective-permute-done((bf16[64,944]{1,0:T(8,128)(2,1)S(1)}, bf16[64,944]{1,0:T(8,128)(2,1)S(1)}, u32[]{:S(2)}, u32[]{:S(2)}) %collective-permute-start) | collective-permute-done | bytes 120864 | tf_op jit(solution)/shard_map/ppermute | solution.py:39
  7.5 1.8 %collective-permute-start.2 = (bf16[64,944]{1,0:T(8,128)(2,1)S(1)}, bf16[64,944]{1,0:T(8,128)(2,1)S(1)}, u32[]{:S(2)}, u32[]{:S(2)}) collective-permute-start(bf16[64,944]{1,0:T(8,128)(2,1)S(1)} %collective-permute-done.refs_1_), channel_id=1, source_target_pairs={{0,4},{4,8},{8,12},{12,14},{14,10},{10,6},{6,2},{2,0},{1,5},{5,9},... | collective-permute-start | bytes 362504 | tf_op jit(solution)/shard_map/ppermute | solution.py:39
  9.3 0.2 collective-permute-start.3
  9.6 2.9 %collective-permute-done.2.refs_3_ = bf16[64,944]{1,0:T(8,128)(2,1)S(1)} collective-permute-done((bf16[64,944]{1,0:T(8,128)(2,1)S(1)}, bf16[64,944]{1,0:T(8,128)(2,1)S(1)}, u32[]{:S(2)}, u32[]{:S(2)}) %collective-permute-start.2) | collective-permute-done | bytes 120864 | tf_op jit(solution)/shard_map/ppermute | solution.py:39
  12.5 1.8 %collective-permute-start.4 = (bf16[64,944]{1,0:T(8,128)(2,1)S(1)}, bf16[64,944]{1,0:T(8,128)(2,1)S(1)}, u32[]{:S(2)}, u32[]{:S(2)}) collective-permute-start(bf16[64,944]{1,0:T(8,128)(2,1)S(1)} %collective-permute-done.2.refs_3_), channel_id=1, source_target_pairs={{0,4},{4,8},{8,12},{12,14},{14,10},{10,6},{6,2},{2,0},{1,5},{5,9},... | collective-permute-start | bytes 362504 | tf_op jit(solution)/shard_map/ppermute | solution.py:39
  14.3 0.2 collective-permute-start.5
  14.5 3.3 %collective-permute-done.4.refs_5_ = bf16[64,944]{1,0:T(8,128)(2,1)S(1)} collective-permute-done((bf16[64,944]{1,0:T(8,128)(2,1)S(1)}, bf16[64,944]{1,0:T(8,128)(2,1)S(1)}, u32[]{:S(2)}, u32[]{:S(2)}) %collective-permute-start.4) | collective-permute-done | bytes 120864 | tf_op jit(solution)/shard_map/ppermute | solution.py:39
  17.9 2.1 %collective-permute-start.6 = (bf16[64,944]{1,0:T(8,128)(2,1)S(1)}, bf16[64,944]{1,0:T(8,128)(2,1)S(1)}, u32[]{:S(2)}, u32[]{:S(2)}) collective-permute-start(bf16[64,944]{1,0:T(8,128)(2,1)S(1)} %collective-permute-done.4.refs_5_), channel_id=1, source_target_pairs={{0,4},{4,8},{8,12},{12,14},{14,10},{10,6},{6,2},{2,0},{1,5},{5,9},... | collective-permute-start | bytes 362504 | tf_op jit(solution)/shard_map/ppermute | solution.py:39
  20.0 0.1 collective-permute-start.7
  20.1 2.8 %collective-permute-done.6.refs_7_ = bf16[64,944]{1,0:T(8,128)(2,1)S(1)} collective-permute-done((bf16[64,944]{1,0:T(8,128)(2,1)S(1)}, bf16[64,944]{1,0:T(8,128)(2,1)S(1)}, u32[]{:S(2)}, u32[]{:S(2)}) %collective-permute-start.6) | collective-permute-done | bytes 120864 | tf_op jit(solution)/shard_map/ppermute | solution.py:39
  23.0 0.1 collective-permute-start.8
  23.1 1.7 %collective-permute-done.8.refs_9_ = bf16[3,64,944]{2,1,0:T(8,128)(2,1)S(1)} collective-permute-done((bf16[3,64,944]{2,1,0:T(8,128)(2,1)S(1)}, bf16[3,64,944]{2,1,0:T(8,128)(2,1)S(1)}, u32[]{:S(2)}, u32[]{:S(2)}) %collective-permute-start.8) | collective-permute-done | bytes 362528 | tf_op jit(solution)/shard_map/ppermute | solution.py:58
  24.9 0.7 %copy-done.9 = bf16[3,64,944]{2,1,0:T(8,128)(2,1)} copy-done((bf16[3,64,944]{2,1,0:T(8,128)(2,1)}, bf16[3,64,944]{2,1,0:T(8,128)(2,1)S(1)}, u32[]{:S(2)}) %copy-start.9) | copy-done | bytes 362520
  25.5 10.5 %shard_map.73 = bf16[16,49,128]{2,1,0:T(8,128)(2,1)} custom-call(s32[256]{0:T(256)} %constant.4.clone.table, bf16[64,944]{1,0:T(8,128)(2,1)} %copy-done.1, bf16[64,944]{1,0:T(8,128)(2,1)} %copy-done.2, bf16[64,944]{1,0:T(8,128)(2,1)} %copy-done.3, bf16[64,944]{1,0:T(8,128)(2,1)} %copy-done.4, bf16[64,944]{1,0:T(8,128)(2,1)} %copy-done.5, ...), custom_call_target="tpu_custom_call" | custom-call | tf_op jit(solution)/shard_map/pallas_call | solution.py:149
  36.0 6.4 %all-to-all-start = ((bf16[16,49,128]{2,1,0:T(8,128)(2,1)}), bf16[16,49,128]{2,1,0:T(8,128)(2,1)S(1)}, u32[]{:S(2)}, u32[]{:S(2)}) async-start(bf16[16,49,128]{2,1,0:T(8,128)(2,1)} %shard_map.73), calls=%async_computation | async-start | bytes 458752 | tf_op jit(solution)/shard_map/all_to_all | solution.py:165
  42.5 9.5 %all-to-all-done = bf16[16,49,128]{2,1,0:T(8,128)(2,1)S(1)} async-done(((bf16[16,49,128]{2,1,0:T(8,128)(2,1)}), bf16[16,49,128]{2,1,0:T(8,128)(2,1)S(1)}, u32[]{:S(2)}, u32[]{:S(2)}) %all-to-all-start) | async-done | bytes 200736 | tf_op jit(solution)/shard_map/all_to_all | solution.py:165
  52.0 0.1 copy.8
  52.2 0.1 eq.19
  52.3 0.1 compare_convert_fusion
  52.4 0.4 fusion
  52.9 0.8 %reshape.53 = f32[8,4096]{1,0:T(8,128)} reshape(f32[512,64]{1,0:T(8,128)S(1)} %fusion) | data formatting | bytes 262144 | tf_op jit(solution)/shard_map/reshape | solution.py:176
  (33 shorter events, 0.3 us)
Async XLA Ops:
  1.0 23.8 %copy-start.1 = (bf16[64,944]{1,0:T(8,128)(2,1)}, bf16[64,944]{1,0:T(8,128)(2,1)S(1)}, u32[]{:S(2)}) copy-start(bf16[64,944]{1,0:T(8,128)(2,1)S(1)} %pad_maximum_fusion.1.refs_0_) | copy-start | bytes 362500
  1.0 6.5 %collective-permute-start = (bf16[64,944]{1,0:T(8,128)(2,1)S(1)}, bf16[64,944]{1,0:T(8,128)(2,1)S(1)}, u32[]{:S(2)}, u32[]{:S(2)}) collective-permute-start(bf16[64,944]{1,0:T(8,128)(2,1)S(1)} %pad_maximum_fusion.1.refs_0_), channel_id=1, source_target_pairs={{0,4},{4,8},{8,12},{12,14},{14,10},{10,6},{6,2},{2,0},{1,5},{5,9},... | collective-permute-start | bytes 362504 | tf_op jit(solution)/shard_map/ppermute | solution.py:39
  4.1 5.2 %collective-permute-start.1 = (bf16[64,944]{1,0:T(8,128)(2,1)S(1)}, bf16[64,944]{1,0:T(8,128)(2,1)S(1)}, u32[]{:S(2)}, u32[]{:S(2)}) collective-permute-start(bf16[64,944]{1,0:T(8,128)(2,1)S(1)} %pad_maximum_fusion.1.refs_0_), channel_id=1, source_target_pairs={{0,2},{4,0},{8,4},{12,8},{14,12},{10,14},{6,10},{2,6},{1,3},{5,1},... | collective-permute-start | bytes 362504 | tf_op jit(solution)/shard_map/ppermute | solution.py:43
  7.5 17.3 %copy-start.2 = (bf16[64,944]{1,0:T(8,128)(2,1)}, bf16[64,944]{1,0:T(8,128)(2,1)S(1)}, u32[]{:S(2)}) copy-start(bf16[64,944]{1,0:T(8,128)(2,1)S(1)} %collective-permute-done.refs_1_) | copy-start | bytes 362500
  7.5 5.0 %collective-permute-start.2 = (bf16[64,944]{1,0:T(8,128)(2,1)S(1)}, bf16[64,944]{1,0:T(8,128)(2,1)S(1)}, u32[]{:S(2)}, u32[]{:S(2)}) collective-permute-start(bf16[64,944]{1,0:T(8,128)(2,1)S(1)} %collective-permute-done.refs_1_), channel_id=1, source_target_pairs={{0,4},{4,8},{8,12},{12,14},{14,10},{10,6},{6,2},{2,0},{1,5},{5,9},... | collective-permute-start | bytes 362504 | tf_op jit(solution)/shard_map/ppermute | solution.py:39
  9.3 15.5 %copy-start.3 = (bf16[64,944]{1,0:T(8,128)(2,1)}, bf16[64,944]{1,0:T(8,128)(2,1)S(1)}, u32[]{:S(2)}) copy-start(bf16[64,944]{1,0:T(8,128)(2,1)S(1)} %collective-permute-done.1.refs_2_) | copy-start | bytes 362500
  9.3 5.0 %collective-permute-start.3 = (bf16[64,944]{1,0:T(8,128)(2,1)S(1)}, bf16[64,944]{1,0:T(8,128)(2,1)S(1)}, u32[]{:S(2)}, u32[]{:S(2)}) collective-permute-start(bf16[64,944]{1,0:T(8,128)(2,1)S(1)} %collective-permute-done.1.refs_2_), channel_id=1, source_target_pairs={{0,2},{4,0},{8,4},{12,8},{14,12},{10,14},{6,10},{2,6},{1,3},{5,1},... | collective-permute-start | bytes 362504 | tf_op jit(solution)/shard_map/ppermute | solution.py:43
  12.5 12.3 %copy-start.4 = (bf16[64,944]{1,0:T(8,128)(2,1)}, bf16[64,944]{1,0:T(8,128)(2,1)S(1)}, u32[]{:S(2)}) copy-start(bf16[64,944]{1,0:T(8,128)(2,1)S(1)} %collective-permute-done.2.refs_3_) | copy-start | bytes 362500
  12.5 5.4 %collective-permute-start.4 = (bf16[64,944]{1,0:T(8,128)(2,1)S(1)}, bf16[64,944]{1,0:T(8,128)(2,1)S(1)}, u32[]{:S(2)}, u32[]{:S(2)}) collective-permute-start(bf16[64,944]{1,0:T(8,128)(2,1)S(1)} %collective-permute-done.2.refs_3_), channel_id=1, source_target_pairs={{0,4},{4,8},{8,12},{12,14},{14,10},{10,6},{6,2},{2,0},{1,5},{5,9},... | collective-permute-start | bytes 362504 | tf_op jit(solution)/shard_map/ppermute | solution.py:39
  14.3 10.5 %copy-start.5 = (bf16[64,944]{1,0:T(8,128)(2,1)}, bf16[64,944]{1,0:T(8,128)(2,1)S(1)}, u32[]{:S(2)}) copy-start(bf16[64,944]{1,0:T(8,128)(2,1)S(1)} %collective-permute-done.3.refs_4_) | copy-start | bytes 362500
  14.3 5.8 %collective-permute-start.5 = (bf16[64,944]{1,0:T(8,128)(2,1)S(1)}, bf16[64,944]{1,0:T(8,128)(2,1)S(1)}, u32[]{:S(2)}, u32[]{:S(2)}) collective-permute-start(bf16[64,944]{1,0:T(8,128)(2,1)S(1)} %collective-permute-done.3.refs_4_), channel_id=1, source_target_pairs={{0,2},{4,0},{8,4},{12,8},{14,12},{10,14},{6,10},{2,6},{1,3},{5,1},... | collective-permute-start | bytes 362504 | tf_op jit(solution)/shard_map/ppermute | solution.py:43
  17.9 6.9 %copy-start.6 = (bf16[64,944]{1,0:T(8,128)(2,1)}, bf16[64,944]{1,0:T(8,128)(2,1)S(1)}, u32[]{:S(2)}) copy-start(bf16[64,944]{1,0:T(8,128)(2,1)S(1)} %collective-permute-done.4.refs_5_) | copy-start | bytes 362500
  17.9 5.0 %collective-permute-start.6 = (bf16[64,944]{1,0:T(8,128)(2,1)S(1)}, bf16[64,944]{1,0:T(8,128)(2,1)S(1)}, u32[]{:S(2)}, u32[]{:S(2)}) collective-permute-start(bf16[64,944]{1,0:T(8,128)(2,1)S(1)} %collective-permute-done.4.refs_5_), channel_id=1, source_target_pairs={{0,4},{4,8},{8,12},{12,14},{14,10},{10,6},{6,2},{2,0},{1,5},{5,9},... | collective-permute-start | bytes 362504 | tf_op jit(solution)/shard_map/ppermute | solution.py:39
  20.0 3.1 %collective-permute-start.7 = (bf16[5,64,944]{2,1,0:T(8,128)(2,1)S(1)}, bf16[5,64,944]{2,1,0:T(8,128)(2,1)S(1)}, u32[]{:S(2)}, u32[]{:S(2)}) collective-permute-start(bf16[5,64,944]{2,1,0:T(8,128)(2,1)S(1)} %bitcast_dynamic-update-slice_fusion), channel_id=1, source_target_pairs={{0,1},{4,5},{8,9},{12,13},{14,15},{10,11},{6,7},{2,3},{1,0},{5,4},... | collective-permute-start | bytes 1812488 | tf_op jit(solution)/shard_map/ppermute | solution.py:58
  20.1 4.7 %copy-start.7 = (bf16[64,944]{1,0:T(8,128)(2,1)}, bf16[64,944]{1,0:T(8,128)(2,1)S(1)}, u32[]{:S(2)}) copy-start(bf16[64,944]{1,0:T(8,128)(2,1)S(1)} %collective-permute-done.5.refs_6_) | copy-start | bytes 362500
  22.9 1.9 %copy-start.8 = (bf16[64,944]{1,0:T(8,128)(2,1)}, bf16[64,944]{1,0:T(8,128)(2,1)S(1)}, u32[]{:S(2)}) copy-start(bf16[64,944]{1,0:T(8,128)(2,1)S(1)} %collective-permute-done.6.refs_7_) | copy-start | bytes 362500
  23.0 1.8 %collective-permute-start.8 = (bf16[3,64,944]{2,1,0:T(8,128)(2,1)S(1)}, bf16[3,64,944]{2,1,0:T(8,128)(2,1)S(1)}, u32[]{:S(2)}, u32[]{:S(2)}) collective-permute-start(bf16[3,64,944]{2,1,0:T(8,128)(2,1)S(1)} %pad_maximum_fusion), channel_id=1, source_target_pairs={{0,1},{4,5},{8,9},{12,13},{14,15},{10,11},{6,7},{2,3},{1,0},{5,4},... | collective-permute-start | bytes 1087496 | tf_op jit(solution)/shard_map/ppermute | solution.py:58
  23.1 1.8 %copy-start = (bf16[5,64,944]{2,1,0:T(8,128)(2,1)}, bf16[5,64,944]{2,1,0:T(8,128)(2,1)S(1)}, u32[]{:S(2)}) copy-start(bf16[5,64,944]{2,1,0:T(8,128)(2,1)S(1)} %collective-permute-done.7.refs_8_) | copy-start | bytes 1812484
  24.8 0.8 %copy-start.9 = (bf16[3,64,944]{2,1,0:T(8,128)(2,1)}, bf16[3,64,944]{2,1,0:T(8,128)(2,1)S(1)}, u32[]{:S(2)}) copy-start(bf16[3,64,944]{2,1,0:T(8,128)(2,1)S(1)} %collective-permute-done.8.refs_9_) | copy-start | bytes 1087492
  36.0 16.0 %all-to-all-start = ((bf16[16,49,128]{2,1,0:T(8,128)(2,1)}), bf16[16,49,128]{2,1,0:T(8,128)(2,1)S(1)}, u32[]{:S(2)}, u32[]{:S(2)}) async-start(bf16[16,49,128]{2,1,0:T(8,128)(2,1)} %shard_map.73), calls=%async_computation | async-start | bytes 458752 | tf_op jit(solution)/shard_map/all_to_all | solution.py:165

commit v13 on v12

--- a/solution.py
+++ b/solution.py
@@ -33,7 +33,7 @@
     backward = [(ring[t], ring[(t - 1) % length]) for ring in planes for t in range(length)]
     early, late = [block], []
     early_shifts, late_shifts = [0], []
-    split = max(1, length // 4)
+    split = max(1, length // 2 - 1)
     ahead = behind = block
     for step in range(1, length // 2 + 1):
         ahead = lax.ppermute(ahead, "dp", forward)

time: 53.9 us -> 54.6 us (1.013)
  waiting for transfers between devices: 22.7 us -> 25.2 us
  starting transfers between devices: 15.8 us -> 13.8 us
    ppermute x3, waiting for transfers between devices: 0.01 us -> 1.94 us  [ring_gather(): behind = lax.ppermute(behind, 'dp', backward)]
    all_to_all x1, starting transfers between devices: 6.44 us -> 4.93 us  [local(): arrived = lax.all_to_all(packed, 'dp', 0, 0, tiled=True)]
    ppermute x4, waiting for transfers between devices: 11.5 us -> 12.4 us  [ring_gather(): ahead = lax.ppermute(ahead, 'dp', forward)]
  transfers between devices with their start and end apart: 10 -> 10, of which waited for: 6 -> 8; matrix products, arithmetic and copies ran while one was open for 2% -> 2% of each run, Pallas kernels for 0% -> 0%
where the time goes in v13:
time: 54.6 us; the launch traced here: 54.3 us
  waiting for transfers between devices  25.2 us (46%)
  starting transfers between devices  13.8 us (25%)
  Pallas kernels  10.5 us (19%)
  other arithmetic  2.14 us (4%)
  local copies, waits for them, and re-layouts  2.03 us (4%)
    ppermute x4, waiting for transfers between devices, ring_gather(): ahead = lax.ppermute(ahead, 'dp', forward)  12.4 us
    pallas_call x1, Pallas kernels, project_rows(): pl.pallas_call(projection_kernel(count, devices, features // devices, out...  10.5 us
    all_to_all x1, waiting for transfers between devices, local(): arrived = lax.all_to_all(packed, 'dp', 0, 0, tiled=True)  9.51 us
    ppermute x4, starting transfers between devices, ring_gather(): ahead = lax.ppermute(ahead, 'dp', forward)  8.3 us
    all_to_all x1, starting transfers between devices, local(): arrived = lax.all_to_all(packed, 'dp', 0, 0, tiled=True)  4.93 us
    ppermute x3, waiting for transfers between devices, ring_gather(): behind = lax.ppermute(behind, 'dp', backward)  1.94 us
    ppermute x2, waiting for transfers between devices, ring_gather(): lax.ppermute(jnp.stack(group), 'dp', swap)  1.35 us
  transfers between devices with their start and end apart: 10, of which 8 were waited for; matrix products, arithmetic and copies ran while one was open for 2% of the time, Pallas kernels for 0%

profile of v13, /device:TPU:0, one launch (start us, length us, event | category | flops | bytes accessed | tf_op | source)
XLA Modules:
  0.0 54.3 jit_solution(1614719479772255691)
XLA Ops:
  0.0 1.0 %pad_maximum_fusion.refs_0_ = bf16[64,944]{1,0:T(8,128)(2,1)S(1)} fusion(bf16[64,256]{1,0:T(8,128)(2,1)} %param.10, bf16[64,688]{1,0:T(8,128)(2,1)} %param.9), kind=kLoop, calls=%fused_computation.3 | loop fusion | flops 241664 | bytes 241664 | tf_op jit(solution)/shard_map/concatenate | solution.py:163
  1.0 3.1 %collective-permute-start = (bf16[64,944]{1,0:T(8,128)(2,1)S(1)}, bf16[64,944]{1,0:T(8,128)(2,1)S(1)}, u32[]{:S(2)}, u32[]{:S(2)}) collective-permute-start(bf16[64,944]{1,0:T(8,128)(2,1)S(1)} %pad_maximum_fusion.refs_0_), channel_id=1, source_target_pairs={{0,4},{4,8},{8,12},{12,14},{14,10},{10,6},{6,2},{2,0},{1,5},{5,9},... | collective-permute-start | bytes 362504 | tf_op jit(solution)/shard_map/ppermute | solution.py:39
  4.1 1.0 %bitcast_dynamic-update-slice_fusion.6 = bf16[7,64,944]{2,1,0:T(8,128)(2,1)S(1)} fusion(bf16[64,256]{1,0:T(8,128)(2,1)} %param.10, bf16[64,688]{1,0:T(8,128)(2,1)} %param.9), kind=kLoop, calls=%fused_computation.10 | loop fusion | flops 241663 | bytes 251904
  5.1 2.4 %collective-permute-done.refs_1_ = bf16[64,944]{1,0:T(8,128)(2,1)S(1)} collective-permute-done((bf16[64,944]{1,0:T(8,128)(2,1)S(1)}, bf16[64,944]{1,0:T(8,128)(2,1)S(1)}, u32[]{:S(2)}, u32[]{:S(2)}) %collective-permute-start) | collective-permute-done | bytes 120864 | tf_op jit(solution)/shard_map/ppermute | solution.py:39
  7.5 1.8 %collective-permute-start.2 = (bf16[64,944]{1,0:T(8,128)(2,1)S(1)}, bf16[64,944]{1,0:T(8,128)(2,1)S(1)}, u32[]{:S(2)}, u32[]{:S(2)}) collective-permute-start(bf16[64,944]{1,0:T(8,128)(2,1)S(1)} %collective-permute-done.refs_1_), channel_id=1, source_target_pairs={{0,4},{4,8},{8,12},{12,14},{14,10},{10,6},{6,2},{2,0},{1,5},{5,9},... | collective-permute-start | bytes 362504 | tf_op jit(solution)/shard_map/ppermute | solution.py:39
  9.4 0.3 collective-permute-start.3
  9.7 2.8 %collective-permute-done.2.refs_3_ = bf16[64,944]{1,0:T(8,128)(2,1)S(1)} collective-permute-done((bf16[64,944]{1,0:T(8,128)(2,1)S(1)}, bf16[64,944]{1,0:T(8,128)(2,1)S(1)}, u32[]{:S(2)}, u32[]{:S(2)}) %collective-permute-start.2) | collective-permute-done | bytes 120864 | tf_op jit(solution)/shard_map/ppermute | solution.py:39
  12.5 1.8 %collective-permute-start.4 = (bf16[64,944]{1,0:T(8,128)(2,1)S(1)}, bf16[64,944]{1,0:T(8,128)(2,1)S(1)}, u32[]{:S(2)}, u32[]{:S(2)}) collective-permute-start(bf16[64,944]{1,0:T(8,128)(2,1)S(1)} %collective-permute-done.2.refs_3_), channel_id=1, source_target_pairs={{0,4},{4,8},{8,12},{12,14},{14,10},{10,6},{6,2},{2,0},{1,5},{5,9},... | collective-permute-start | bytes 362504 | tf_op jit(solution)/shard_map/ppermute | solution.py:39
  14.4 0.2 collective-permute-start.5
  14.6 2.8 %collective-permute-done.4.refs_5_ = bf16[64,944]{1,0:T(8,128)(2,1)S(1)} collective-permute-done((bf16[64,944]{1,0:T(8,128)(2,1)S(1)}, bf16[64,944]{1,0:T(8,128)(2,1)S(1)}, u32[]{:S(2)}, u32[]{:S(2)}) %collective-permute-start.4) | collective-permute-done | bytes 120864 | tf_op jit(solution)/shard_map/ppermute | solution.py:39
  17.5 1.9 %collective-permute-done.5.refs_6_ = bf16[64,944]{1,0:T(8,128)(2,1)S(1)} collective-permute-done((bf16[64,944]{1,0:T(8,128)(2,1)S(1)}, bf16[64,944]{1,0:T(8,128)(2,1)S(1)}, u32[]{:S(2)}, u32[]{:S(2)}) %collective-permute-start.5) | collective-permute-done | bytes 120864 | tf_op jit(solution)/shard_map/ppermute | solution.py:43
  19.4 1.6 %collective-permute-start.6 = (bf16[64,944]{1,0:T(8,128)(2,1)S(1)}, bf16[64,944]{1,0:T(8,128)(2,1)S(1)}, u32[]{:S(2)}, u32[]{:S(2)}) collective-permute-start(bf16[64,944]{1,0:T(8,128)(2,1)S(1)} %collective-permute-done.4.refs_5_), channel_id=1, source_target_pairs={{0,4},{4,8},{8,12},{12,14},{14,10},{10,6},{6,2},{2,0},{1,5},{5,9},... | collective-permute-start | bytes 362504 | tf_op jit(solution)/shard_map/ppermute | solution.py:39
  21.1 4.3 %collective-permute-done.6.refs_7_ = bf16[64,944]{1,0:T(8,128)(2,1)S(1)} collective-permute-done((bf16[64,944]{1,0:T(8,128)(2,1)S(1)}, bf16[64,944]{1,0:T(8,128)(2,1)S(1)}, u32[]{:S(2)}, u32[]{:S(2)}) %collective-permute-start.6) | collective-permute-done | bytes 120864 | tf_op jit(solution)/shard_map/ppermute | solution.py:39
  25.4 1.3 %collective-permute-done.8.refs_9_ = bf16[1,64,944]{2,1,0:T(8,128)(2,1)S(1)} collective-permute-done((bf16[1,64,944]{2,1,0:T(8,128)(2,1)S(1)}, bf16[1,64,944]{2,1,0:T(8,128)(2,1)S(1)}, u32[]{:S(2)}, u32[]{:S(2)}) %collective-permute-start.8) | collective-permute-done | bytes 120864 | tf_op jit(solution)/shard_map/ppermute | solution.py:58
  26.8 0.6 %copy-done.9 = bf16[1,64,944]{2,1,0:T(8,128)(2,1)} copy-done((bf16[1,64,944]{2,1,0:T(8,128)(2,1)}, bf16[1,64,944]{2,1,0:T(8,128)(2,1)S(1)}, u32[]{:S(2)}) %copy-start.9) | copy-done | bytes 120856
  27.4 0.3 copy-done
  27.7 10.5 %shard_map.73 = bf16[16,49,128]{2,1,0:T(8,128)(2,1)} custom-call(s32[256]{0:T(256)} %constant.4.clone.table, bf16[64,944]{1,0:T(8,128)(2,1)} %copy-done.1, bf16[64,944]{1,0:T(8,128)(2,1)} %copy-done.2, bf16[64,944]{1,0:T(8,128)(2,1)} %copy-done.3, bf16[64,944]{1,0:T(8,128)(2,1)} %copy-done.4, bf16[64,944]{1,0:T(8,128)(2,1)} %copy-done.5, ...), custom_call_target="tpu_custom_call" | custom-call | tf_op jit(solution)/shard_map/pallas_call | solution.py:149
  38.2 4.9 %all-to-all-start = ((bf16[16,49,128]{2,1,0:T(8,128)(2,1)}), bf16[16,49,128]{2,1,0:T(8,128)(2,1)S(1)}, u32[]{:S(2)}, u32[]{:S(2)}) async-start(bf16[16,49,128]{2,1,0:T(8,128)(2,1)} %shard_map.73), calls=%async_computation | async-start | bytes 458752 | tf_op jit(solution)/shard_map/all_to_all | solution.py:165
  43.1 9.5 %all-to-all-done = bf16[16,49,128]{2,1,0:T(8,128)(2,1)S(1)} async-done(((bf16[16,49,128]{2,1,0:T(8,128)(2,1)}), bf16[16,49,128]{2,1,0:T(8,128)(2,1)S(1)}, u32[]{:S(2)}, u32[]{:S(2)}) %all-to-all-start) | async-done | bytes 200736 | tf_op jit(solution)/shard_map/all_to_all | solution.py:165
  52.6 0.1 copy.8
  52.8 0.1 eq.19
  52.9 0.1 compare_convert_fusion
  53.0 0.4 fusion
  53.5 0.8 %reshape.53 = f32[8,4096]{1,0:T(8,128)} reshape(f32[512,64]{1,0:T(8,128)S(1)} %fusion) | data formatting | bytes 262144 | tf_op jit(solution)/shard_map/reshape | solution.py:176
  (34 shorter events, 0.4 us)
Async XLA Ops:
  1.0 25.7 %copy-start.1 = (bf16[64,944]{1,0:T(8,128)(2,1)}, bf16[64,944]{1,0:T(8,128)(2,1)S(1)}, u32[]{:S(2)}) copy-start(bf16[64,944]{1,0:T(8,128)(2,1)S(1)} %pad_maximum_fusion.refs_0_) | copy-start | bytes 362500
  1.0 6.5 %collective-permute-start = (bf16[64,944]{1,0:T(8,128)(2,1)S(1)}, bf16[64,944]{1,0:T(8,128)(2,1)S(1)}, u32[]{:S(2)}, u32[]{:S(2)}) collective-permute-start(bf16[64,944]{1,0:T(8,128)(2,1)S(1)} %pad_maximum_fusion.refs_0_), channel_id=1, source_target_pairs={{0,4},{4,8},{8,12},{12,14},{14,10},{10,6},{6,2},{2,0},{1,5},{5,9},... | collective-permute-start | bytes 362504 | tf_op jit(solution)/shard_map/ppermute | solution.py:39
  4.1 5.3 %collective-permute-start.1 = (bf16[64,944]{1,0:T(8,128)(2,1)S(1)}, bf16[64,944]{1,0:T(8,128)(2,1)S(1)}, u32[]{:S(2)}, u32[]{:S(2)}) collective-permute-start(bf16[64,944]{1,0:T(8,128)(2,1)S(1)} %pad_maximum_fusion.refs_0_), channel_id=1, source_target_pairs={{0,2},{4,0},{8,4},{12,8},{14,12},{10,14},{6,10},{2,6},{1,3},{5,1},... | collective-permute-start | bytes 362504 | tf_op jit(solution)/shard_map/ppermute | solution.py:43
  7.5 19.2 %copy-start.2 = (bf16[64,944]{1,0:T(8,128)(2,1)}, bf16[64,944]{1,0:T(8,128)(2,1)S(1)}, u32[]{:S(2)}) copy-start(bf16[64,944]{1,0:T(8,128)(2,1)S(1)} %collective-permute-done.refs_1_) | copy-start | bytes 362500
  7.5 5.0 %collective-permute-start.2 = (bf16[64,944]{1,0:T(8,128)(2,1)S(1)}, bf16[64,944]{1,0:T(8,128)(2,1)S(1)}, u32[]{:S(2)}, u32[]{:S(2)}) collective-permute-start(bf16[64,944]{1,0:T(8,128)(2,1)S(1)} %collective-permute-done.refs_1_), channel_id=1, source_target_pairs={{0,4},{4,8},{8,12},{12,14},{14,10},{10,6},{6,2},{2,0},{1,5},{5,9},... | collective-permute-start | bytes 362504 | tf_op jit(solution)/shard_map/ppermute | solution.py:39
  9.4 17.4 %copy-start.3 = (bf16[64,944]{1,0:T(8,128)(2,1)}, bf16[64,944]{1,0:T(8,128)(2,1)S(1)}, u32[]{:S(2)}) copy-start(bf16[64,944]{1,0:T(8,128)(2,1)S(1)} %collective-permute-done.1.refs_2_) | copy-start | bytes 362500
  9.4 5.0 %collective-permute-start.3 = (bf16[64,944]{1,0:T(8,128)(2,1)S(1)}, bf16[64,944]{1,0:T(8,128)(2,1)S(1)}, u32[]{:S(2)}, u32[]{:S(2)}) collective-permute-start(bf16[64,944]{1,0:T(8,128)(2,1)S(1)} %collective-permute-done.1.refs_2_), channel_id=1, source_target_pairs={{0,2},{4,0},{8,4},{12,8},{14,12},{10,14},{6,10},{2,6},{1,3},{5,1},... | collective-permute-start | bytes 362504 | tf_op jit(solution)/shard_map/ppermute | solution.py:43
  12.5 14.2 %copy-start.4 = (bf16[64,944]{1,0:T(8,128)(2,1)}, bf16[64,944]{1,0:T(8,128)(2,1)S(1)}, u32[]{:S(2)}) copy-start(bf16[64,944]{1,0:T(8,128)(2,1)S(1)} %collective-permute-done.2.refs_3_) | copy-start | bytes 362500
  12.5 5.0 %collective-permute-start.4 = (bf16[64,944]{1,0:T(8,128)(2,1)S(1)}, bf16[64,944]{1,0:T(8,128)(2,1)S(1)}, u32[]{:S(2)}, u32[]{:S(2)}) collective-permute-start(bf16[64,944]{1,0:T(8,128)(2,1)S(1)} %collective-permute-done.2.refs_3_), channel_id=1, source_target_pairs={{0,4},{4,8},{8,12},{12,14},{14,10},{10,6},{6,2},{2,0},{1,5},{5,9},... | collective-permute-start | bytes 362504 | tf_op jit(solution)/shard_map/ppermute | solution.py:39
  14.4 12.4 %copy-start.5 = (bf16[64,944]{1,0:T(8,128)(2,1)}, bf16[64,944]{1,0:T(8,128)(2,1)S(1)}, u32[]{:S(2)}) copy-start(bf16[64,944]{1,0:T(8,128)(2,1)S(1)} %collective-permute-done.3.refs_4_) | copy-start | bytes 362500
  14.4 5.0 %collective-permute-start.5 = (bf16[64,944]{1,0:T(8,128)(2,1)S(1)}, bf16[64,944]{1,0:T(8,128)(2,1)S(1)}, u32[]{:S(2)}, u32[]{:S(2)}) collective-permute-start(bf16[64,944]{1,0:T(8,128)(2,1)S(1)} %collective-permute-done.3.refs_4_), channel_id=1, source_target_pairs={{0,2},{4,0},{8,4},{12,8},{14,12},{10,14},{6,10},{2,6},{1,3},{5,1},... | collective-permute-start | bytes 362504 | tf_op jit(solution)/shard_map/ppermute | solution.py:43
  17.5 9.3 %copy-start.6 = (bf16[64,944]{1,0:T(8,128)(2,1)}, bf16[64,944]{1,0:T(8,128)(2,1)S(1)}, u32[]{:S(2)}) copy-start(bf16[64,944]{1,0:T(8,128)(2,1)S(1)} %collective-permute-done.4.refs_5_) | copy-start | bytes 362500
  19.4 7.4 %copy-start.7 = (bf16[64,944]{1,0:T(8,128)(2,1)}, bf16[64,944]{1,0:T(8,128)(2,1)S(1)}, u32[]{:S(2)}) copy-start(bf16[64,944]{1,0:T(8,128)(2,1)S(1)} %collective-permute-done.5.refs_6_) | copy-start | bytes 362500
  19.4 7.3 %collective-permute-start.7 = (bf16[7,64,944]{2,1,0:T(8,128)(2,1)S(1)}, bf16[7,64,944]{2,1,0:T(8,128)(2,1)S(1)}, u32[]{:S(2)}, u32[]{:S(2)}) collective-permute-start(bf16[7,64,944]{2,1,0:T(8,128)(2,1)S(1)} %bitcast_dynamic-update-slice_fusion), channel_id=1, source_target_pairs={{0,1},{4,5},{8,9},{12,13},{14,15},{10,11},{6,7},{2,3},{1,0},{5,4},... | collective-permute-start | bytes 2537480 | tf_op jit(solution)/shard_map/ppermute | solution.py:58
  19.4 5.9 %collective-permute-start.6 = (bf16[64,944]{1,0:T(8,128)(2,1)S(1)}, bf16[64,944]{1,0:T(8,128)(2,1)S(1)}, u32[]{:S(2)}, u32[]{:S(2)}) collective-permute-start(bf16[64,944]{1,0:T(8,128)(2,1)S(1)} %collective-permute-done.4.refs_5_), channel_id=1, source_target_pairs={{0,4},{4,8},{8,12},{12,14},{14,10},{10,6},{6,2},{2,0},{1,5},{5,9},... | collective-permute-start | bytes 362504 | tf_op jit(solution)/shard_map/ppermute | solution.py:39
  25.3 1.4 %copy-start.8 = (bf16[64,944]{1,0:T(8,128)(2,1)}, bf16[64,944]{1,0:T(8,128)(2,1)S(1)}, u32[]{:S(2)}) copy-start(bf16[64,944]{1,0:T(8,128)(2,1)S(1)} %collective-permute-done.6.refs_7_) | copy-start | bytes 362500
  25.3 1.3 %collective-permute-start.8 = (bf16[1,64,944]{2,1,0:T(8,128)(2,1)S(1)}, bf16[1,64,944]{2,1,0:T(8,128)(2,1)S(1)}, u32[]{:S(2)}, u32[]{:S(2)}) collective-permute-start(bf16[1,64,944]{2,1,0:T(8,128)(2,1)S(1)} %bitcast.23), channel_id=1, source_target_pairs={{0,1},{4,5},{8,9},{12,13},{14,15},{10,11},{6,7},{2,3},{1,0},{5,4},... | collective-permute-start | bytes 362504 | tf_op jit(solution)/shard_map/ppermute | solution.py:58
  26.7 0.7 %copy-start.9 = (bf16[1,64,944]{2,1,0:T(8,128)(2,1)}, bf16[1,64,944]{2,1,0:T(8,128)(2,1)S(1)}, u32[]{:S(2)}) copy-start(bf16[1,64,944]{2,1,0:T(8,128)(2,1)S(1)} %collective-permute-done.8.refs_9_) | copy-start | bytes 362500
  26.7 1.0 %copy-start = (bf16[7,64,944]{2,1,0:T(8,128)(2,1)}, bf16[7,64,944]{2,1,0:T(8,128)(2,1)S(1)}, u32[]{:S(2)}) copy-start(bf16[7,64,944]{2,1,0:T(8,128)(2,1)S(1)} %collective-permute-done.7.refs_8_) | copy-start | bytes 2537476
  38.2 14.5 %all-to-all-start = ((bf16[16,49,128]{2,1,0:T(8,128)(2,1)}), bf16[16,49,128]{2,1,0:T(8,128)(2,1)S(1)}, u32[]{:S(2)}, u32[]{:S(2)}) async-start(bf16[16,49,128]{2,1,0:T(8,128)(2,1)} %shard_map.73), calls=%async_computation | async-start | bytes 458752 | tf_op jit(solution)/shard_map/all_to_all | solution.py:165

commit v14 on v12

--- a/solution.py
+++ b/solution.py
@@ -82,8 +82,8 @@
                     stacked[table[me * width + at + k]] = other_ref[k]
                 at += size
             for d in range(devices):
-                hidden_full[:, d * hidden_cols:(d + 1) * hidden_cols] = stacked[d, :, :hidden_cols]
-                output_full[:, d * output_cols:(d + 1) * output_cols] = stacked[d, :, hidden_cols:]
+                hidden_full[:, d * hidden_cols:(d + 1) * hidden_cols] = stacked[d, :, output_cols:]
+                output_full[:, d * output_cols:(d + 1) * output_cols] = stacked[d, :, :output_cols]
 
         dims = (((1,), (1,)), ((), ()))
         left = lax.dot_general(hidden_full[...], hidden_ref[...], dims, preferred_element_type=jnp.float32)
@@ -160,7 +160,7 @@
     capacity = 2 * local_tokens // devices
     rank_width = hidden_basis.shape[0]
     buffer_len = devices * capacity
-    blocks, other, table = ring_gather(jnp.concatenate([hidden_basis, output_basis], axis=1), devices)
+    blocks, other, table = ring_gather(jnp.concatenate([output_basis, hidden_basis], axis=1), devices)
     packed = project_rows(blocks, other, table, hidden, out_grad, owner_ids, doc_slot, devices, capacity)
     arrived = lax.all_to_all(packed, "dp", 0, 0, tiled=True)
     rows_in = arrived[:, :capacity, :].reshape(buffer_len, 2 * rank_width)

time: 53.9 us -> 54.4 us (level)
  other arithmetic: 2.19 us -> 0.19 us
  local copies, waits for them, and re-layouts: 1.8 us -> 3.46 us
  waiting for transfers between devices: 22.7 us -> 23.7 us
    unnamed x1 -> x0, other arithmetic: 1 us -> none
    concatenate x1 -> x0, other arithmetic: 1 us -> none  [local(): jnp.concatenate([hidden_basis, output_basis], axis=1)]
    concatenate x0 -> x1, local copies, waits for them, and re-layouts: none -> 0.9 us  [local(): jnp.concatenate([output_basis, hidden_basis], axis=1)]
    ppermute x4, waiting for transfers between devices: 11.5 us -> 12.4 us  [ring_gather(): ahead = lax.ppermute(ahead, 'dp', forward)]
    unnamed x23 -> x25, local copies, waits for them, and re-layouts: 0.76 us -> 1.52 us
  transfers between devices with their start and end apart: 10 -> 10, of which waited for: 6 -> 7; matrix products, arithmetic and copies ran while one was open for 2% -> 0% of each run, Pallas kernels for 0% -> 0%
where the time goes in v14:
time: 54.4 us; the launch traced here: 54 us
  waiting for transfers between devices  23.7 us (44%)
  starting transfers between devices  15.8 us (29%)
  Pallas kernels  10.2 us (19%)
  local copies, waits for them, and re-layouts  3.46 us (6%)
    ppermute x4, waiting for transfers between devices, ring_gather(): ahead = lax.ppermute(ahead, 'dp', forward)  12.4 us
    pallas_call x1, Pallas kernels, project_rows(): pl.pallas_call(projection_kernel(count, devices, features // devices, out...  10.2 us
    all_to_all x1, waiting for transfers between devices, local(): arrived = lax.all_to_all(packed, 'dp', 0, 0, tiled=True)  9.51 us
    ppermute x4, starting transfers between devices, ring_gather(): ahead = lax.ppermute(ahead, 'dp', forward)  8.71 us
    all_to_all x1, starting transfers between devices, local(): arrived = lax.all_to_all(packed, 'dp', 0, 0, tiled=True)  6.44 us
    ppermute x2, waiting for transfers between devices, ring_gather(): lax.ppermute(jnp.stack(group), 'dp', swap)  1.69 us
    unnamed x25, local copies, waits for them, and re-layouts  1.52 us
  transfers between devices with their start and end apart: 10, of which 7 were waited for; matrix products, arithmetic and copies ran while one was open for 0% of the time, Pallas kernels for 0%

profile of v14, /device:TPU:0, one launch (start us, length us, event | category | flops | bytes accessed | tf_op | source)
XLA Modules:
  0.0 54.0 jit_solution(4917978310187995983)
XLA Ops:
  0.0 0.8 %constant_dynamic-update-slice_fusion.1 = bf16[64,944]{1,0:T(8,128)(2,1)S(1)} fusion(bf16[64,256]{1,0:T(8,128)(2,1)} %param.10), kind=kLoop, calls=%fused_computation.11 | loop fusion | bytes 65536
  0.8 0.9 %constant_dynamic-update-slice_fusion.refs_0_ = bf16[64,944]{1,0:T(8,128)(2,1)S(1)} fusion(bf16[64,944]{1,0:T(8,128)(2,1)S(1)} %constant_dynamic-update-slice_fusion.1, bf16[64,688]{1,0:T(8,128)(2,1)} %param.9), kind=kLoop, calls=%fused_computation.10 | loop fusion | bytes 186368 | tf_op jit(solution)/shard_map/concatenate | solution.py:163
  1.7 3.1 %collective-permute-start = (bf16[64,944]{1,0:T(8,128)(2,1)S(1)}, bf16[64,944]{1,0:T(8,128)(2,1)S(1)}, u32[]{:S(2)}, u32[]{:S(2)}) collective-permute-start(bf16[64,944]{1,0:T(8,128)(2,1)S(1)} %constant_dynamic-update-slice_fusion.refs_0_), channel_id=1, source_target_pairs={{0,4},{4,8},{8,12},{12,14},{14,10},{10,6},{6,2},{2,0},{1,5},{5,9},... | collective-permute-start | bytes 362504 | tf_op jit(solution)/shard_map/ppermute | solution.py:39
  4.8 3.4 %collective-permute-done.refs_1_ = bf16[64,944]{1,0:T(8,128)(2,1)S(1)} collective-permute-done((bf16[64,944]{1,0:T(8,128)(2,1)S(1)}, bf16[64,944]{1,0:T(8,128)(2,1)S(1)}, u32[]{:S(2)}, u32[]{:S(2)}) %collective-permute-start) | collective-permute-done | bytes 120864 | tf_op jit(solution)/shard_map/ppermute | solution.py:39
  8.2 1.8 %collective-permute-start.2 = (bf16[64,944]{1,0:T(8,128)(2,1)S(1)}, bf16[64,944]{1,0:T(8,128)(2,1)S(1)}, u32[]{:S(2)}, u32[]{:S(2)}) collective-permute-start(bf16[64,944]{1,0:T(8,128)(2,1)S(1)} %collective-permute-done.refs_1_), channel_id=1, source_target_pairs={{0,4},{4,8},{8,12},{12,14},{14,10},{10,6},{6,2},{2,0},{1,5},{5,9},... | collective-permute-start | bytes 362504 | tf_op jit(solution)/shard_map/ppermute | solution.py:39
  10.0 0.3 collective-permute-start.3
  10.3 2.8 %collective-permute-done.2.refs_3_ = bf16[64,944]{1,0:T(8,128)(2,1)S(1)} collective-permute-done((bf16[64,944]{1,0:T(8,128)(2,1)S(1)}, bf16[64,944]{1,0:T(8,128)(2,1)S(1)}, u32[]{:S(2)}, u32[]{:S(2)}) %collective-permute-start.2) | collective-permute-done | bytes 120864 | tf_op jit(solution)/shard_map/ppermute | solution.py:39
  13.2 1.8 %collective-permute-start.4 = (bf16[64,944]{1,0:T(8,128)(2,1)S(1)}, bf16[64,944]{1,0:T(8,128)(2,1)S(1)}, u32[]{:S(2)}, u32[]{:S(2)}) collective-permute-start(bf16[64,944]{1,0:T(8,128)(2,1)S(1)} %collective-permute-done.2.refs_3_), channel_id=1, source_target_pairs={{0,4},{4,8},{8,12},{12,14},{14,10},{10,6},{6,2},{2,0},{1,5},{5,9},... | collective-permute-start | bytes 362504 | tf_op jit(solution)/shard_map/ppermute | solution.py:39
  15.0 0.1 collective-permute-done.3.refs_4_
  15.0 0.2 collective-permute-start.5
  15.3 3.2 %collective-permute-done.4.refs_5_ = bf16[64,944]{1,0:T(8,128)(2,1)S(1)} collective-permute-done((bf16[64,944]{1,0:T(8,128)(2,1)S(1)}, bf16[64,944]{1,0:T(8,128)(2,1)S(1)}, u32[]{:S(2)}, u32[]{:S(2)}) %collective-permute-start.4) | collective-permute-done | bytes 120864 | tf_op jit(solution)/shard_map/ppermute | solution.py:39
  18.5 2.0 %collective-permute-start.6 = (bf16[64,944]{1,0:T(8,128)(2,1)S(1)}, bf16[64,944]{1,0:T(8,128)(2,1)S(1)}, u32[]{:S(2)}, u32[]{:S(2)}) collective-permute-start(bf16[64,944]{1,0:T(8,128)(2,1)S(1)} %collective-permute-done.4.refs_5_), channel_id=1, source_target_pairs={{0,4},{4,8},{8,12},{12,14},{14,10},{10,6},{6,2},{2,0},{1,5},{5,9},... | collective-permute-start | bytes 362504 | tf_op jit(solution)/shard_map/ppermute | solution.py:39
  20.6 0.1 collective-permute-start.7
  20.7 2.9 %collective-permute-done.6.refs_7_ = bf16[64,944]{1,0:T(8,128)(2,1)S(1)} collective-permute-done((bf16[64,944]{1,0:T(8,128)(2,1)S(1)}, bf16[64,944]{1,0:T(8,128)(2,1)S(1)}, u32[]{:S(2)}, u32[]{:S(2)}) %collective-permute-start.6) | collective-permute-done | bytes 120864 | tf_op jit(solution)/shard_map/ppermute | solution.py:39
  23.7 1.7 %collective-permute-done.8.refs_9_ = bf16[3,64,944]{2,1,0:T(8,128)(2,1)S(1)} collective-permute-done((bf16[3,64,944]{2,1,0:T(8,128)(2,1)S(1)}, bf16[3,64,944]{2,1,0:T(8,128)(2,1)S(1)}, u32[]{:S(2)}, u32[]{:S(2)}) %collective-permute-start.8) | collective-permute-done | bytes 362528 | tf_op jit(solution)/shard_map/ppermute | solution.py:58
  25.5 0.7 %copy-done.9 = bf16[3,64,944]{2,1,0:T(8,128)(2,1)} copy-done((bf16[3,64,944]{2,1,0:T(8,128)(2,1)}, bf16[3,64,944]{2,1,0:T(8,128)(2,1)S(1)}, u32[]{:S(2)}) %copy-start.9) | copy-done | bytes 362520
  26.2 10.2 %shard_map.73 = bf16[16,49,128]{2,1,0:T(8,128)(2,1)} custom-call(s32[256]{0:T(256)} %constant.4.clone.table, bf16[64,944]{1,0:T(8,128)(2,1)} %copy-done, bf16[64,944]{1,0:T(8,128)(2,1)} %copy-done.2, bf16[64,944]{1,0:T(8,128)(2,1)} %copy-done.3, bf16[64,944]{1,0:T(8,128)(2,1)} %copy-done.4, bf16[64,944]{1,0:T(8,128)(2,1)} %copy-done.5, ...), custom_call_target="tpu_custom_call" | custom-call | tf_op jit(solution)/shard_map/pallas_call | solution.py:149
  36.4 6.4 %all-to-all-start = ((bf16[16,49,128]{2,1,0:T(8,128)(2,1)}), bf16[16,49,128]{2,1,0:T(8,128)(2,1)S(1)}, u32[]{:S(2)}, u32[]{:S(2)}) async-start(bf16[16,49,128]{2,1,0:T(8,128)(2,1)} %shard_map.73), calls=%async_computation | async-start | bytes 458752 | tf_op jit(solution)/shard_map/all_to_all | solution.py:165
  42.9 9.5 %all-to-all-done = bf16[16,49,128]{2,1,0:T(8,128)(2,1)S(1)} async-done(((bf16[16,49,128]{2,1,0:T(8,128)(2,1)}), bf16[16,49,128]{2,1,0:T(8,128)(2,1)S(1)}, u32[]{:S(2)}, u32[]{:S(2)}) %all-to-all-start) | async-done | bytes 200736 | tf_op jit(solution)/shard_map/all_to_all | solution.py:165
  52.4 0.1 copy.8
  52.6 0.1 eq.19
  52.7 0.1 compare_convert_fusion
  52.8 0.4 fusion
  53.3 0.8 %reshape.53 = f32[8,4096]{1,0:T(8,128)} reshape(f32[512,64]{1,0:T(8,128)S(1)} %fusion) | data formatting | bytes 262144 | tf_op jit(solution)/shard_map/reshape | solution.py:176
  (34 shorter events, 0.3 us)
Async XLA Ops:
  1.7 23.8 %copy-start = (bf16[64,944]{1,0:T(8,128)(2,1)}, bf16[64,944]{1,0:T(8,128)(2,1)S(1)}, u32[]{:S(2)}) copy-start(bf16[64,944]{1,0:T(8,128)(2,1)S(1)} %constant_dynamic-update-slice_fusion.refs_0_) | copy-start | bytes 362500
  1.7 6.5 %collective-permute-start = (bf16[64,944]{1,0:T(8,128)(2,1)S(1)}, bf16[64,944]{1,0:T(8,128)(2,1)S(1)}, u32[]{:S(2)}, u32[]{:S(2)}) collective-permute-start(bf16[64,944]{1,0:T(8,128)(2,1)S(1)} %constant_dynamic-update-slice_fusion.refs_0_), channel_id=1, source_target_pairs={{0,4},{4,8},{8,12},{12,14},{14,10},{10,6},{6,2},{2,0},{1,5},{5,9},... | collective-permute-start | bytes 362504 | tf_op jit(solution)/shard_map/ppermute | solution.py:39
  4.7 5.3 %collective-permute-start.1 = (bf16[64,944]{1,0:T(8,128)(2,1)S(1)}, bf16[64,944]{1,0:T(8,128)(2,1)S(1)}, u32[]{:S(2)}, u32[]{:S(2)}) collective-permute-start(bf16[64,944]{1,0:T(8,128)(2,1)S(1)} %constant_dynamic-update-slice_fusion.refs_0_), channel_id=1, source_target_pairs={{0,2},{4,0},{8,4},{12,8},{14,12},{10,14},{6,10},{2,6},{1,3},{5,1},... | collective-permute-start | bytes 362504 | tf_op jit(solution)/shard_map/ppermute | solution.py:43
  8.2 17.3 %copy-start.2 = (bf16[64,944]{1,0:T(8,128)(2,1)}, bf16[64,944]{1,0:T(8,128)(2,1)S(1)}, u32[]{:S(2)}) copy-start(bf16[64,944]{1,0:T(8,128)(2,1)S(1)} %collective-permute-done.refs_1_) | copy-start | bytes 362500
  8.2 5.0 %collective-permute-start.2 = (bf16[64,944]{1,0:T(8,128)(2,1)S(1)}, bf16[64,944]{1,0:T(8,128)(2,1)S(1)}, u32[]{:S(2)}, u32[]{:S(2)}) collective-permute-start(bf16[64,944]{1,0:T(8,128)(2,1)S(1)} %collective-permute-done.refs_1_), channel_id=1, source_target_pairs={{0,4},{4,8},{8,12},{12,14},{14,10},{10,6},{6,2},{2,0},{1,5},{5,9},... | collective-permute-start | bytes 362504 | tf_op jit(solution)/shard_map/ppermute | solution.py:39
  10.0 15.4 %copy-start.3 = (bf16[64,944]{1,0:T(8,128)(2,1)}, bf16[64,944]{1,0:T(8,128)(2,1)S(1)}, u32[]{:S(2)}) copy-start(bf16[64,944]{1,0:T(8,128)(2,1)S(1)} %collective-permute-done.1.refs_2_) | copy-start | bytes 362500
  10.0 5.0 %collective-permute-start.3 = (bf16[64,944]{1,0:T(8,128)(2,1)S(1)}, bf16[64,944]{1,0:T(8,128)(2,1)S(1)}, u32[]{:S(2)}, u32[]{:S(2)}) collective-permute-start(bf16[64,944]{1,0:T(8,128)(2,1)S(1)} %collective-permute-done.1.refs_2_), channel_id=1, source_target_pairs={{0,2},{4,0},{8,4},{12,8},{14,12},{10,14},{6,10},{2,6},{1,3},{5,1},... | collective-permute-start | bytes 362504 | tf_op jit(solution)/shard_map/ppermute | solution.py:43
  13.2 12.3 %copy-start.4 = (bf16[64,944]{1,0:T(8,128)(2,1)}, bf16[64,944]{1,0:T(8,128)(2,1)S(1)}, u32[]{:S(2)}) copy-start(bf16[64,944]{1,0:T(8,128)(2,1)S(1)} %collective-permute-done.2.refs_3_) | copy-start | bytes 362500
  13.2 5.3 %collective-permute-start.4 = (bf16[64,944]{1,0:T(8,128)(2,1)S(1)}, bf16[64,944]{1,0:T(8,128)(2,1)S(1)}, u32[]{:S(2)}, u32[]{:S(2)}) collective-permute-start(bf16[64,944]{1,0:T(8,128)(2,1)S(1)} %collective-permute-done.2.refs_3_), channel_id=1, source_target_pairs={{0,4},{4,8},{8,12},{12,14},{14,10},{10,6},{6,2},{2,0},{1,5},{5,9},... | collective-permute-start | bytes 362504 | tf_op jit(solution)/shard_map/ppermute | solution.py:39
  15.0 10.4 %copy-start.5 = (bf16[64,944]{1,0:T(8,128)(2,1)}, bf16[64,944]{1,0:T(8,128)(2,1)S(1)}, u32[]{:S(2)}) copy-start(bf16[64,944]{1,0:T(8,128)(2,1)S(1)} %collective-permute-done.3.refs_4_) | copy-start | bytes 362500
  15.0 5.6 %collective-permute-start.5 = (bf16[64,944]{1,0:T(8,128)(2,1)S(1)}, bf16[64,944]{1,0:T(8,128)(2,1)S(1)}, u32[]{:S(2)}, u32[]{:S(2)}) collective-permute-start(bf16[64,944]{1,0:T(8,128)(2,1)S(1)} %collective-permute-done.3.refs_4_), channel_id=1, source_target_pairs={{0,2},{4,0},{8,4},{12,8},{14,12},{10,14},{6,10},{2,6},{1,3},{5,1},... | collective-permute-start | bytes 362504 | tf_op jit(solution)/shard_map/ppermute | solution.py:43
  18.5 7.0 %copy-start.6 = (bf16[64,944]{1,0:T(8,128)(2,1)}, bf16[64,944]{1,0:T(8,128)(2,1)S(1)}, u32[]{:S(2)}) copy-start(bf16[64,944]{1,0:T(8,128)(2,1)S(1)} %collective-permute-done.4.refs_5_) | copy-start | bytes 362500
  18.5 5.1 %collective-permute-start.6 = (bf16[64,944]{1,0:T(8,128)(2,1)S(1)}, bf16[64,944]{1,0:T(8,128)(2,1)S(1)}, u32[]{:S(2)}, u32[]{:S(2)}) collective-permute-start(bf16[64,944]{1,0:T(8,128)(2,1)S(1)} %collective-permute-done.4.refs_5_), channel_id=1, source_target_pairs={{0,4},{4,8},{8,12},{12,14},{14,10},{10,6},{6,2},{2,0},{1,5},{5,9},... | collective-permute-start | bytes 362504 | tf_op jit(solution)/shard_map/ppermute | solution.py:39
  20.6 3.2 %collective-permute-start.7 = (bf16[5,64,944]{2,1,0:T(8,128)(2,1)S(1)}, bf16[5,64,944]{2,1,0:T(8,128)(2,1)S(1)}, u32[]{:S(2)}, u32[]{:S(2)}) collective-permute-start(bf16[5,64,944]{2,1,0:T(8,128)(2,1)S(1)} %bitcast_dynamic-update-slice_fusion), channel_id=1, source_target_pairs={{0,1},{4,5},{8,9},{12,13},{14,15},{10,11},{6,7},{2,3},{1,0},{5,4},... | collective-permute-start | bytes 1812488 | tf_op jit(solution)/shard_map/ppermute | solution.py:58
  20.6 4.8 %copy-start.7 = (bf16[64,944]{1,0:T(8,128)(2,1)}, bf16[64,944]{1,0:T(8,128)(2,1)S(1)}, u32[]{:S(2)}) copy-start(bf16[64,944]{1,0:T(8,128)(2,1)S(1)} %collective-permute-done.5.refs_6_) | copy-start | bytes 362500
  23.6 1.9 %copy-start.8 = (bf16[64,944]{1,0:T(8,128)(2,1)}, bf16[64,944]{1,0:T(8,128)(2,1)S(1)}, u32[]{:S(2)}) copy-start(bf16[64,944]{1,0:T(8,128)(2,1)S(1)} %collective-permute-done.6.refs_7_) | copy-start | bytes 362500
  23.6 1.8 %collective-permute-start.8 = (bf16[3,64,944]{2,1,0:T(8,128)(2,1)S(1)}, bf16[3,64,944]{2,1,0:T(8,128)(2,1)S(1)}, u32[]{:S(2)}, u32[]{:S(2)}) collective-permute-start(bf16[3,64,944]{2,1,0:T(8,128)(2,1)S(1)} %pad_maximum_fusion), channel_id=1, source_target_pairs={{0,1},{4,5},{8,9},{12,13},{14,15},{10,11},{6,7},{2,3},{1,0},{5,4},... | collective-permute-start | bytes 1087496 | tf_op jit(solution)/shard_map/ppermute | solution.py:58
  23.7 1.8 %copy-start.1 = (bf16[5,64,944]{2,1,0:T(8,128)(2,1)}, bf16[5,64,944]{2,1,0:T(8,128)(2,1)S(1)}, u32[]{:S(2)}) copy-start(bf16[5,64,944]{2,1,0:T(8,128)(2,1)S(1)} %collective-permute-done.7.refs_8_) | copy-start | bytes 1812484
  25.4 0.8 %copy-start.9 = (bf16[3,64,944]{2,1,0:T(8,128)(2,1)}, bf16[3,64,944]{2,1,0:T(8,128)(2,1)S(1)}, u32[]{:S(2)}) copy-start(bf16[3,64,944]{2,1,0:T(8,128)(2,1)S(1)} %collective-permute-done.8.refs_9_) | copy-start | bytes 1087492
  36.4 16.0 %all-to-all-start = ((bf16[16,49,128]{2,1,0:T(8,128)(2,1)}), bf16[16,49,128]{2,1,0:T(8,128)(2,1)S(1)}, u32[]{:S(2)}, u32[]{:S(2)}) async-start(bf16[16,49,128]{2,1,0:T(8,128)(2,1)} %shard_map.73), calls=%async_computation | async-start | bytes 458752 | tf_op jit(solution)/shard_map/all_to_all | solution.py:165

commit v15 on v12

--- a/solution.py
+++ b/solution.py
@@ -170,10 +170,25 @@
     wanted = (jnp.arange(DOCS_DEV, dtype=jnp.int32) + 1).astype(jnp.bfloat16)[None, :]
     selector = (label_in == wanted).astype(jnp.bfloat16)
     weighted = (selector[:, :, None] * left_in[:, None, :]).reshape(buffer_len, DOCS_DEV * rank_width)
-    grads = lax.dot_general(
-        weighted, right_in, (((0,), (0,)), ((), ())), preferred_element_type=jnp.float32
-    )
-    return grads.reshape(DOCS_DEV, rank_width * rank_width)
+    return doc_grads(weighted, right_in, rank_width)
+
+
+def doc_grads(weighted, right_in, rank_width):
+    def kernel(weighted_ref, right_ref, out_ref, grads):
+        grads[...] = lax.dot_general(
+            weighted_ref[...], right_ref[...], (((0,), (0,)), ((), ())), preferred_element_type=jnp.float32
+        )
+        lanes = 2 * rank_width
+        for pair in range(rank_width // 2):
+            even = grads[pl.ds(2 * pair, DOCS_DEV, stride=rank_width), :]
+            odd = grads[pl.ds(2 * pair + 1, DOCS_DEV, stride=rank_width), :]
+            out_ref[:, pair * lanes:(pair + 1) * lanes] = jnp.concatenate([even, odd], axis=1)
+
+    return pl.pallas_call(
+        kernel,
+        out_shape=jax.ShapeDtypeStruct((DOCS_DEV, rank_width * rank_width), jnp.float32),
+        scratch_shapes=[pltpu.VMEM((DOCS_DEV * rank_width, rank_width), jnp.float32)],
+    )(weighted, right_in)
 
 
 def solution(mesh):

time: 53.9 us -> 57.1 us (1.059)
  Pallas kernels: 10.5 us -> 12.8 us
  local copies, waits for them, and re-layouts: 1.8 us -> 2.99 us
    pallas_call x0 -> x1, Pallas kernels: none -> 2.36 us  [doc_grads(): pl.pallas_call(kernel, out_shape=jax.ShapeDtypeStruct((DOCS_DEV, rank_wid...]
    mul x0 -> x1, local copies, waits for them, and re-layouts: none -> 1.17 us  [local(): selector[:, :, None] * left_in[:, None, :]]
    slice x0 -> x1, local copies, waits for them, and re-layouts: none -> 0.8 us  [local(): right_in = rows_in[:, rank_width:]]
    reshape x1 -> x0, local copies, waits for them, and re-layouts: 0.77 us -> none  [local(): return grads.reshape(DOCS_DEV, rank_width * rank_width)]
where the time goes in v15:
time: 57.1 us; the launch traced here: 56.8 us
  waiting for transfers between devices  22.7 us (40%)
  starting transfers between devices  15.8 us (28%)
  Pallas kernels  12.8 us (22%)
  local copies, waits for them, and re-layouts  2.99 us (5%)
  other arithmetic  2.19 us (4%)
    ppermute x4, waiting for transfers between devices, ring_gather(): ahead = lax.ppermute(ahead, 'dp', forward)  11.5 us
    pallas_call x1, Pallas kernels, project_rows(): pl.pallas_call(projection_kernel(count, devices, features // devices, out...  10.5 us
    all_to_all x1, waiting for transfers between devices, local(): arrived = lax.all_to_all(packed, 'dp', 0, 0, tiled=True)  9.51 us
    ppermute x4, starting transfers between devices, ring_gather(): ahead = lax.ppermute(ahead, 'dp', forward)  8.76 us
    all_to_all x1, starting transfers between devices, local(): arrived = lax.all_to_all(packed, 'dp', 0, 0, tiled=True)  6.44 us
    pallas_call x1, Pallas kernels, doc_grads(): pl.pallas_call(kernel, out_shape=jax.ShapeDtypeStruct((DOCS_DEV, rank_wid...  2.36 us
    ppermute x2, waiting for transfers between devices, ring_gather(): lax.ppermute(jnp.stack(group), 'dp', swap)  1.69 us
    mul x1, local copies, waits for them, and re-layouts, local(): selector[:, :, None] * left_in[:, None, :]  1.17 us
  transfers between devices with their start and end apart: 10, of which 6 were waited for; matrix products, arithmetic and copies ran while one was open for 2% of the time, Pallas kernels for 0%

profile of v15, /device:TPU:0, one launch (start us, length us, event | category | flops | bytes accessed | tf_op | source)
XLA Modules:
  0.0 56.8 jit_solution(10320295496243955329)
XLA Ops:
  0.0 1.0 %pad_maximum_fusion.1.refs_0_ = bf16[64,944]{1,0:T(8,128)(2,1)S(1)} fusion(bf16[64,256]{1,0:T(8,128)(2,1)} %param.10, bf16[64,688]{1,0:T(8,128)(2,1)} %param.9), kind=kLoop, calls=%fused_computation.2 | loop fusion | flops 241664 | bytes 241664 | tf_op jit(solution)/shard_map/concatenate | solution.py:163
  1.0 3.1 %collective-permute-start = (bf16[64,944]{1,0:T(8,128)(2,1)S(1)}, bf16[64,944]{1,0:T(8,128)(2,1)S(1)}, u32[]{:S(2)}, u32[]{:S(2)}) collective-permute-start(bf16[64,944]{1,0:T(8,128)(2,1)S(1)} %pad_maximum_fusion.1.refs_0_), channel_id=1, source_target_pairs={{0,4},{4,8},{8,12},{12,14},{14,10},{10,6},{6,2},{2,0},{1,5},{5,9},... | collective-permute-start | bytes 362504 | tf_op jit(solution)/shard_map/ppermute | solution.py:39
  4.1 1.0 %bitcast_dynamic-update-slice_fusion.4 = bf16[5,64,944]{2,1,0:T(8,128)(2,1)S(1)} fusion(bf16[64,256]{1,0:T(8,128)(2,1)} %param.10, bf16[64,688]{1,0:T(8,128)(2,1)} %param.9), kind=kLoop, calls=%fused_computation.7 | loop fusion | flops 241663 | bytes 251904
  5.1 2.4 %collective-permute-done.refs_1_ = bf16[64,944]{1,0:T(8,128)(2,1)S(1)} collective-permute-done((bf16[64,944]{1,0:T(8,128)(2,1)S(1)}, bf16[64,944]{1,0:T(8,128)(2,1)S(1)}, u32[]{:S(2)}, u32[]{:S(2)}) %collective-permute-start) | collective-permute-done | bytes 120864 | tf_op jit(solution)/shard_map/ppermute | solution.py:39
  7.5 1.8 %collective-permute-start.2 = (bf16[64,944]{1,0:T(8,128)(2,1)S(1)}, bf16[64,944]{1,0:T(8,128)(2,1)S(1)}, u32[]{:S(2)}, u32[]{:S(2)}) collective-permute-start(bf16[64,944]{1,0:T(8,128)(2,1)S(1)} %collective-permute-done.refs_1_), channel_id=1, source_target_pairs={{0,4},{4,8},{8,12},{12,14},{14,10},{10,6},{6,2},{2,0},{1,5},{5,9},... | collective-permute-start | bytes 362504 | tf_op jit(solution)/shard_map/ppermute | solution.py:39
  9.3 0.2 collective-permute-start.3
  9.6 2.9 %collective-permute-done.2.refs_3_ = bf16[64,944]{1,0:T(8,128)(2,1)S(1)} collective-permute-done((bf16[64,944]{1,0:T(8,128)(2,1)S(1)}, bf16[64,944]{1,0:T(8,128)(2,1)S(1)}, u32[]{:S(2)}, u32[]{:S(2)}) %collective-permute-start.2) | collective-permute-done | bytes 120864 | tf_op jit(solution)/shard_map/ppermute | solution.py:39
  12.5 1.8 %collective-permute-start.4 = (bf16[64,944]{1,0:T(8,128)(2,1)S(1)}, bf16[64,944]{1,0:T(8,128)(2,1)S(1)}, u32[]{:S(2)}, u32[]{:S(2)}) collective-permute-start(bf16[64,944]{1,0:T(8,128)(2,1)S(1)} %collective-permute-done.2.refs_3_), channel_id=1, source_target_pairs={{0,4},{4,8},{8,12},{12,14},{14,10},{10,6},{6,2},{2,0},{1,5},{5,9},... | collective-permute-start | bytes 362504 | tf_op jit(solution)/shard_map/ppermute | solution.py:39
  14.3 0.2 collective-permute-start.5
  14.5 3.3 %collective-permute-done.4.refs_5_ = bf16[64,944]{1,0:T(8,128)(2,1)S(1)} collective-permute-done((bf16[64,944]{1,0:T(8,128)(2,1)S(1)}, bf16[64,944]{1,0:T(8,128)(2,1)S(1)}, u32[]{:S(2)}, u32[]{:S(2)}) %collective-permute-start.4) | collective-permute-done | bytes 120864 | tf_op jit(solution)/shard_map/ppermute | solution.py:39
  17.9 2.1 %collective-permute-start.6 = (bf16[64,944]{1,0:T(8,128)(2,1)S(1)}, bf16[64,944]{1,0:T(8,128)(2,1)S(1)}, u32[]{:S(2)}, u32[]{:S(2)}) collective-permute-start(bf16[64,944]{1,0:T(8,128)(2,1)S(1)} %collective-permute-done.4.refs_5_), channel_id=1, source_target_pairs={{0,4},{4,8},{8,12},{12,14},{14,10},{10,6},{6,2},{2,0},{1,5},{5,9},... | collective-permute-start | bytes 362504 | tf_op jit(solution)/shard_map/ppermute | solution.py:39
  20.0 0.1 collective-permute-start.7
  20.1 2.8 %collective-permute-done.6.refs_7_ = bf16[64,944]{1,0:T(8,128)(2,1)S(1)} collective-permute-done((bf16[64,944]{1,0:T(8,128)(2,1)S(1)}, bf16[64,944]{1,0:T(8,128)(2,1)S(1)}, u32[]{:S(2)}, u32[]{:S(2)}) %collective-permute-start.6) | collective-permute-done | bytes 120864 | tf_op jit(solution)/shard_map/ppermute | solution.py:39
  23.1 1.7 %collective-permute-done.8.refs_9_ = bf16[3,64,944]{2,1,0:T(8,128)(2,1)S(1)} collective-permute-done((bf16[3,64,944]{2,1,0:T(8,128)(2,1)S(1)}, bf16[3,64,944]{2,1,0:T(8,128)(2,1)S(1)}, u32[]{:S(2)}, u32[]{:S(2)}) %collective-permute-start.8) | collective-permute-done | bytes 362528 | tf_op jit(solution)/shard_map/ppermute | solution.py:58
  24.9 0.7 %copy-done.9 = bf16[3,64,944]{2,1,0:T(8,128)(2,1)} copy-done((bf16[3,64,944]{2,1,0:T(8,128)(2,1)}, bf16[3,64,944]{2,1,0:T(8,128)(2,1)S(1)}, u32[]{:S(2)}) %copy-start.9) | copy-done | bytes 362520
  25.5 10.5 %shard_map.73 = bf16[16,49,128]{2,1,0:T(8,128)(2,1)} custom-call(s32[256]{0:T(256)} %constant.4.clone.table, bf16[64,944]{1,0:T(8,128)(2,1)} %copy-done.1, bf16[64,944]{1,0:T(8,128)(2,1)} %copy-done.2, bf16[64,944]{1,0:T(8,128)(2,1)} %copy-done.3, bf16[64,944]{1,0:T(8,128)(2,1)} %copy-done.4, bf16[64,944]{1,0:T(8,128)(2,1)} %copy-done.5, ...), custom_call_target="tpu_custom_call" | custom-call | tf_op jit(solution)/shard_map/pallas_call | solution.py:149
  36.0 6.4 %all-to-all-start = ((bf16[16,49,128]{2,1,0:T(8,128)(2,1)}), bf16[16,49,128]{2,1,0:T(8,128)(2,1)S(1)}, u32[]{:S(2)}, u32[]{:S(2)}) async-start(bf16[16,49,128]{2,1,0:T(8,128)(2,1)} %shard_map.73), calls=%async_computation | async-start | bytes 458752 | tf_op jit(solution)/shard_map/all_to_all | solution.py:165
  42.5 9.5 %all-to-all-done = bf16[16,49,128]{2,1,0:T(8,128)(2,1)S(1)} async-done(((bf16[16,49,128]{2,1,0:T(8,128)(2,1)}), bf16[16,49,128]{2,1,0:T(8,128)(2,1)S(1)}, u32[]{:S(2)}, u32[]{:S(2)}) %all-to-all-start) | async-done | bytes 200736 | tf_op jit(solution)/shard_map/all_to_all | solution.py:165
  52.0 0.8 %fusion = (bf16[768,64]{1,0:T(8,128)(2,1)}, bf16[768,64]{1,0:T(8,128)(2,1)S(1)}) fusion(bf16[768,128]{1,0:T(8,128)(2,1)S(1)} %bitcast.17), kind=kLoop, calls=%fused_computation.11 | loop fusion | bytes 393216 | tf_op jit(solution)/shard_map/slice | solution.py:169
  52.8 0.1 copy.8
  53.0 0.1 eq.19
  53.1 0.1 compare_convert_fusion
  53.2 1.2 %copy.9.weighted_ref = bf16[768,512]{1,0:T(8,128)(2,1)} copy(bf16[768,512]{0,1:T(8,128)(2,1)S(1)} %bitcast.16) | data formatting | bytes 1572864 | tf_op jit(solution)/shard_map/mul | solution.py:172
  54.4 2.4 %shard_map.74 = f32[8,4096]{1,0:T(8,128)} custom-call(bf16[768,512]{1,0:T(8,128)(2,1)} %copy.9.weighted_ref, bf16[768,64]{1,0:T(8,128)(2,1)} %get-tuple-element.5.right_ref), custom_call_target="tpu_custom_call" | custom-call | tf_op jit(solution)/shard_map/pallas_call | solution.py:187
  (34 shorter events, 0.3 us)
Async XLA Ops:
  1.0 23.8 %copy-start.1 = (bf16[64,944]{1,0:T(8,128)(2,1)}, bf16[64,944]{1,0:T(8,128)(2,1)S(1)}, u32[]{:S(2)}) copy-start(bf16[64,944]{1,0:T(8,128)(2,1)S(1)} %pad_maximum_fusion.1.refs_0_) | copy-start | bytes 362500
  1.0 6.5 %collective-permute-start = (bf16[64,944]{1,0:T(8,128)(2,1)S(1)}, bf16[64,944]{1,0:T(8,128)(2,1)S(1)}, u32[]{:S(2)}, u32[]{:S(2)}) collective-permute-start(bf16[64,944]{1,0:T(8,128)(2,1)S(1)} %pad_maximum_fusion.1.refs_0_), channel_id=1, source_target_pairs={{0,4},{4,8},{8,12},{12,14},{14,10},{10,6},{6,2},{2,0},{1,5},{5,9},... | collective-permute-start | bytes 362504 | tf_op jit(solution)/shard_map/ppermute | solution.py:39
  4.1 5.2 %collective-permute-start.1 = (bf16[64,944]{1,0:T(8,128)(2,1)S(1)}, bf16[64,944]{1,0:T(8,128)(2,1)S(1)}, u32[]{:S(2)}, u32[]{:S(2)}) collective-permute-start(bf16[64,944]{1,0:T(8,128)(2,1)S(1)} %pad_maximum_fusion.1.refs_0_), channel_id=1, source_target_pairs={{0,2},{4,0},{8,4},{12,8},{14,12},{10,14},{6,10},{2,6},{1,3},{5,1},... | collective-permute-start | bytes 362504 | tf_op jit(solution)/shard_map/ppermute | solution.py:43
  7.5 17.3 %copy-start.2 = (bf16[64,944]{1,0:T(8,128)(2,1)}, bf16[64,944]{1,0:T(8,128)(2,1)S(1)}, u32[]{:S(2)}) copy-start(bf16[64,944]{1,0:T(8,128)(2,1)S(1)} %collective-permute-done.refs_1_) | copy-start | bytes 362500
  7.5 5.0 %collective-permute-start.2 = (bf16[64,944]{1,0:T(8,128)(2,1)S(1)}, bf16[64,944]{1,0:T(8,128)(2,1)S(1)}, u32[]{:S(2)}, u32[]{:S(2)}) collective-permute-start(bf16[64,944]{1,0:T(8,128)(2,1)S(1)} %collective-permute-done.refs_1_), channel_id=1, source_target_pairs={{0,4},{4,8},{8,12},{12,14},{14,10},{10,6},{6,2},{2,0},{1,5},{5,9},... | collective-permute-start | bytes 362504 | tf_op jit(solution)/shard_map/ppermute | solution.py:39
  9.3 15.5 %copy-start.3 = (bf16[64,944]{1,0:T(8,128)(2,1)}, bf16[64,944]{1,0:T(8,128)(2,1)S(1)}, u32[]{:S(2)}) copy-start(bf16[64,944]{1,0:T(8,128)(2,1)S(1)} %collective-permute-done.1.refs_2_) | copy-start | bytes 362500
  9.3 5.0 %collective-permute-start.3 = (bf16[64,944]{1,0:T(8,128)(2,1)S(1)}, bf16[64,944]{1,0:T(8,128)(2,1)S(1)}, u32[]{:S(2)}, u32[]{:S(2)}) collective-permute-start(bf16[64,944]{1,0:T(8,128)(2,1)S(1)} %collective-permute-done.1.refs_2_), channel_id=1, source_target_pairs={{0,2},{4,0},{8,4},{12,8},{14,12},{10,14},{6,10},{2,6},{1,3},{5,1},... | collective-permute-start | bytes 362504 | tf_op jit(solution)/shard_map/ppermute | solution.py:43
  12.5 12.3 %copy-start.4 = (bf16[64,944]{1,0:T(8,128)(2,1)}, bf16[64,944]{1,0:T(8,128)(2,1)S(1)}, u32[]{:S(2)}) copy-start(bf16[64,944]{1,0:T(8,128)(2,1)S(1)} %collective-permute-done.2.refs_3_) | copy-start | bytes 362500
  12.5 5.4 %collective-permute-start.4 = (bf16[64,944]{1,0:T(8,128)(2,1)S(1)}, bf16[64,944]{1,0:T(8,128)(2,1)S(1)}, u32[]{:S(2)}, u32[]{:S(2)}) collective-permute-start(bf16[64,944]{1,0:T(8,128)(2,1)S(1)} %collective-permute-done.2.refs_3_), channel_id=1, source_target_pairs={{0,4},{4,8},{8,12},{12,14},{14,10},{10,6},{6,2},{2,0},{1,5},{5,9},... | collective-permute-start | bytes 362504 | tf_op jit(solution)/shard_map/ppermute | solution.py:39
  14.3 10.5 %copy-start.5 = (bf16[64,944]{1,0:T(8,128)(2,1)}, bf16[64,944]{1,0:T(8,128)(2,1)S(1)}, u32[]{:S(2)}) copy-start(bf16[64,944]{1,0:T(8,128)(2,1)S(1)} %collective-permute-done.3.refs_4_) | copy-start | bytes 362500
  14.3 5.8 %collective-permute-start.5 = (bf16[64,944]{1,0:T(8,128)(2,1)S(1)}, bf16[64,944]{1,0:T(8,128)(2,1)S(1)}, u32[]{:S(2)}, u32[]{:S(2)}) collective-permute-start(bf16[64,944]{1,0:T(8,128)(2,1)S(1)} %collective-permute-done.3.refs_4_), channel_id=1, source_target_pairs={{0,2},{4,0},{8,4},{12,8},{14,12},{10,14},{6,10},{2,6},{1,3},{5,1},... | collective-permute-start | bytes 362504 | tf_op jit(solution)/shard_map/ppermute | solution.py:43
  17.9 6.9 %copy-start.6 = (bf16[64,944]{1,0:T(8,128)(2,1)}, bf16[64,944]{1,0:T(8,128)(2,1)S(1)}, u32[]{:S(2)}) copy-start(bf16[64,944]{1,0:T(8,128)(2,1)S(1)} %collective-permute-done.4.refs_5_) | copy-start | bytes 362500
  17.9 5.0 %collective-permute-start.6 = (bf16[64,944]{1,0:T(8,128)(2,1)S(1)}, bf16[64,944]{1,0:T(8,128)(2,1)S(1)}, u32[]{:S(2)}, u32[]{:S(2)}) collective-permute-start(bf16[64,944]{1,0:T(8,128)(2,1)S(1)} %collective-permute-done.4.refs_5_), channel_id=1, source_target_pairs={{0,4},{4,8},{8,12},{12,14},{14,10},{10,6},{6,2},{2,0},{1,5},{5,9},... | collective-permute-start | bytes 362504 | tf_op jit(solution)/shard_map/ppermute | solution.py:39
  20.0 3.1 %collective-permute-start.7 = (bf16[5,64,944]{2,1,0:T(8,128)(2,1)S(1)}, bf16[5,64,944]{2,1,0:T(8,128)(2,1)S(1)}, u32[]{:S(2)}, u32[]{:S(2)}) collective-permute-start(bf16[5,64,944]{2,1,0:T(8,128)(2,1)S(1)} %bitcast_dynamic-update-slice_fusion), channel_id=1, source_target_pairs={{0,1},{4,5},{8,9},{12,13},{14,15},{10,11},{6,7},{2,3},{1,0},{5,4},... | collective-permute-start | bytes 1812488 | tf_op jit(solution)/shard_map/ppermute | solution.py:58
  20.1 4.7 %copy-start.7 = (bf16[64,944]{1,0:T(8,128)(2,1)}, bf16[64,944]{1,0:T(8,128)(2,1)S(1)}, u32[]{:S(2)}) copy-start(bf16[64,944]{1,0:T(8,128)(2,1)S(1)} %collective-permute-done.5.refs_6_) | copy-start | bytes 362500
  22.9 1.9 %copy-start.8 = (bf16[64,944]{1,0:T(8,128)(2,1)}, bf16[64,944]{1,0:T(8,128)(2,1)S(1)}, u32[]{:S(2)}) copy-start(bf16[64,944]{1,0:T(8,128)(2,1)S(1)} %collective-permute-done.6.refs_7_) | copy-start | bytes 362500
  23.0 1.8 %collective-permute-start.8 = (bf16[3,64,944]{2,1,0:T(8,128)(2,1)S(1)}, bf16[3,64,944]{2,1,0:T(8,128)(2,1)S(1)}, u32[]{:S(2)}, u32[]{:S(2)}) collective-permute-start(bf16[3,64,944]{2,1,0:T(8,128)(2,1)S(1)} %pad_maximum_fusion), channel_id=1, source_target_pairs={{0,1},{4,5},{8,9},{12,13},{14,15},{10,11},{6,7},{2,3},{1,0},{5,4},... | collective-permute-start | bytes 1087496 | tf_op jit(solution)/shard_map/ppermute | solution.py:58
  23.1 1.8 %copy-start = (bf16[5,64,944]{2,1,0:T(8,128)(2,1)}, bf16[5,64,944]{2,1,0:T(8,128)(2,1)S(1)}, u32[]{:S(2)}) copy-start(bf16[5,64,944]{2,1,0:T(8,128)(2,1)S(1)} %collective-permute-done.7.refs_8_) | copy-start | bytes 1812484
  24.8 0.8 %copy-start.9 = (bf16[3,64,944]{2,1,0:T(8,128)(2,1)}, bf16[3,64,944]{2,1,0:T(8,128)(2,1)S(1)}, u32[]{:S(2)}) copy-start(bf16[3,64,944]{2,1,0:T(8,128)(2,1)S(1)} %collective-permute-done.8.refs_9_) | copy-start | bytes 1087492
  36.0 16.0 %all-to-all-start = ((bf16[16,49,128]{2,1,0:T(8,128)(2,1)}), bf16[16,49,128]{2,1,0:T(8,128)(2,1)S(1)}, u32[]{:S(2)}, u32[]{:S(2)}) async-start(bf16[16,49,128]{2,1,0:T(8,128)(2,1)} %shard_map.73), calls=%async_computation | async-start | bytes 458752 | tf_op jit(solution)/shard_map/all_to_all | solution.py:165

commit v16 on v13

--- a/solution.py
+++ b/solution.py
@@ -31,20 +31,21 @@
             plane_of[member] = plane
     forward = [(ring[t], ring[(t + 1) % length]) for ring in planes for t in range(length)]
     backward = [(ring[t], ring[(t - 1) % length]) for ring in planes for t in range(length)]
-    early, late = [block], []
-    early_shifts, late_shifts = [0], []
-    split = max(1, length // 2 - 1)
+    cuts = (max(1, length // 8), max(1, length // 4))
+    groups = [[block], [], []]
+    group_shifts = [[0], [], []]
     ahead = behind = block
     for step in range(1, length // 2 + 1):
+        group = sum(step > cut for cut in cuts)
         ahead = lax.ppermute(ahead, "dp", forward)
-        (early if step <= split else late).append(ahead)
-        (early_shifts if step <= split else late_shifts).append(-step)
+        groups[group].append(ahead)
+        group_shifts[group].append(-step)
         if step < length - length // 2:
             behind = lax.ppermute(behind, "dp", backward)
-            (early if step <= split else late).append(behind)
-            (early_shifts if step <= split else late_shifts).append(step)
-    blocks = early + late
-    shifts = early_shifts + late_shifts
+            groups[group].append(behind)
+            group_shifts[group].append(step)
+    blocks = [got for group in groups for got in group]
+    shifts = [shift for group in group_shifts for shift in group]
     table = np.zeros((devices, len(shifts) * len(planes)), np.int32)
     for member in range(devices):
         for k, shift in enumerate(shifts):
@@ -55,7 +56,7 @@
     if len(planes) == 1:
         return blocks, None, owners
     swap = list(zip(planes[0], planes[1])) + list(zip(planes[1], planes[0]))
-    other = [lax.ppermute(jnp.stack(group), "dp", swap) for group in (early, late) if group]
+    other = [lax.ppermute(jnp.stack(group), "dp", swap) for group in groups if group]
     return blocks, other, owners
 
 

time: 54.6 us -> 54.5 us (level)
  starting transfers between devices: 13.8 us -> 16.4 us
  waiting for transfers between devices: 25.2 us -> 23.5 us
  other arithmetic: 2.14 us -> 1.27 us
    ppermute x3, waiting for transfers between devices: 1.94 us -> 0.01 us  [ring_gather(): behind = lax.ppermute(behind, 'dp', backward)]
    all_to_all x1, starting transfers between devices: 4.93 us -> 6.44 us  [local(): arrived = lax.all_to_all(packed, 'dp', 0, 0, tiled=True)]
    another operation x0 -> x4, other arithmetic: none -> 1.12 us  [ring_gather(): jnp.stack(group)]
    unnamed x1 -> x0, other arithmetic: 1 us -> none
    concatenate x1 -> x0, other arithmetic: 1 us -> none  [local(): jnp.concatenate([hidden_basis, output_basis], axis=1)]
    ppermute x2 -> x3, starting transfers between devices: 0.07 us -> 0.7 us  [ring_gather(): lax.ppermute(jnp.stack(group), 'dp', swap)]
    ppermute x2 -> x3, waiting for transfers between devices: 1.35 us -> 1.5 us  [ring_gather(): lax.ppermute(jnp.stack(group), 'dp', swap)]
  transfers between devices with their start and end apart: 10 -> 11, of which waited for: 8 -> 6; matrix products, arithmetic and copies ran while one was open for 2% -> 0% of each run, Pallas kernels for 0% -> 0%
where the time goes in v16:
time: 54.5 us; the launch traced here: 54.3 us
  waiting for transfers between devices  23.5 us (43%)
  starting transfers between devices  16.4 us (30%)
  Pallas kernels  10.5 us (19%)
  local copies, waits for them, and re-layouts  1.94 us (4%)
  other arithmetic  1.27 us (2%)
    ppermute x4, waiting for transfers between devices, ring_gather(): ahead = lax.ppermute(ahead, 'dp', forward)  12.5 us
    pallas_call x1, Pallas kernels, project_rows(): pl.pallas_call(projection_kernel(count, devices, features // devices, out...  10.5 us
    all_to_all x1, waiting for transfers between devices, local(): arrived = lax.all_to_all(packed, 'dp', 0, 0, tiled=True)  9.51 us
    ppermute x4, starting transfers between devices, ring_gather(): ahead = lax.ppermute(ahead, 'dp', forward)  8.76 us
    all_to_all x1, starting transfers between devices, local(): arrived = lax.all_to_all(packed, 'dp', 0, 0, tiled=True)  6.44 us
    ppermute x3, waiting for transfers between devices, ring_gather(): lax.ppermute(jnp.stack(group), 'dp', swap)  1.5 us
    another operation x4, other arithmetic, ring_gather(): jnp.stack(group)  1.12 us
  transfers between devices with their start and end apart: 11, of which 6 were waited for; matrix products, arithmetic and copies ran while one was open for 0% of the time, Pallas kernels for 0%

profile of v16, /device:TPU:0, one launch (start us, length us, event | category | flops | bytes accessed | tf_op | source)
XLA Modules:
  0.0 54.3 jit_solution(201615874429779938)
XLA Ops:
  0.0 1.0 %fusion.2 = (bf16[1,64,944]{2,1,0:T(8,128)(2,1)S(1)}, bf16[64,944]{1,0:T(8,128)(2,1)S(1)}) fusion(bf16[64,256]{1,0:T(8,128)(2,1)} %param.10, bf16[64,688]{1,0:T(8,128)(2,1)} %param.9), kind=kLoop, calls=%fused_computation.10 | loop fusion | flops 241664 | bytes 362496 | tf_op jit(solution)/shard_map/stack | solution.py:59
  1.0 3.1 %collective-permute-start = (bf16[64,944]{1,0:T(8,128)(2,1)S(1)}, bf16[64,944]{1,0:T(8,128)(2,1)S(1)}, u32[]{:S(2)}, u32[]{:S(2)}) collective-permute-start(bf16[64,944]{1,0:T(8,128)(2,1)S(1)} %get-tuple-element.6.refs_0_), channel_id=1, source_target_pairs={{0,4},{4,8},{8,12},{12,14},{14,10},{10,6},{6,2},{2,0},{1,5},{5,9},... | collective-permute-start | bytes 362504 | tf_op jit(solution)/shard_map/ppermute | solution.py:40
  4.1 3.4 %collective-permute-done.refs_1_ = bf16[64,944]{1,0:T(8,128)(2,1)S(1)} collective-permute-done((bf16[64,944]{1,0:T(8,128)(2,1)S(1)}, bf16[64,944]{1,0:T(8,128)(2,1)S(1)}, u32[]{:S(2)}, u32[]{:S(2)}) %collective-permute-start) | collective-permute-done | bytes 120864 | tf_op jit(solution)/shard_map/ppermute | solution.py:40
  7.5 1.8 %collective-permute-start.2 = (bf16[64,944]{1,0:T(8,128)(2,1)S(1)}, bf16[64,944]{1,0:T(8,128)(2,1)S(1)}, u32[]{:S(2)}, u32[]{:S(2)}) collective-permute-start(bf16[64,944]{1,0:T(8,128)(2,1)S(1)} %collective-permute-done.refs_1_), channel_id=1, source_target_pairs={{0,4},{4,8},{8,12},{12,14},{14,10},{10,6},{6,2},{2,0},{1,5},{5,9},... | collective-permute-start | bytes 362504 | tf_op jit(solution)/shard_map/ppermute | solution.py:40
  9.3 0.2 collective-permute-start.3
  9.6 2.9 %collective-permute-done.2.refs_3_ = bf16[64,944]{1,0:T(8,128)(2,1)S(1)} collective-permute-done((bf16[64,944]{1,0:T(8,128)(2,1)S(1)}, bf16[64,944]{1,0:T(8,128)(2,1)S(1)}, u32[]{:S(2)}, u32[]{:S(2)}) %collective-permute-start.2) | collective-permute-done | bytes 120864 | tf_op jit(solution)/shard_map/ppermute | solution.py:40
  12.5 1.8 %collective-permute-start.4 = (bf16[64,944]{1,0:T(8,128)(2,1)S(1)}, bf16[64,944]{1,0:T(8,128)(2,1)S(1)}, u32[]{:S(2)}, u32[]{:S(2)}) collective-permute-start(bf16[64,944]{1,0:T(8,128)(2,1)S(1)} %collective-permute-done.2.refs_3_), channel_id=1, source_target_pairs={{0,4},{4,8},{8,12},{12,14},{14,10},{10,6},{6,2},{2,0},{1,5},{5,9},... | collective-permute-start | bytes 362504 | tf_op jit(solution)/shard_map/ppermute | solution.py:40
  14.3 0.2 collective-permute-start.5
  14.5 3.4 %collective-permute-done.4.refs_5_ = bf16[64,944]{1,0:T(8,128)(2,1)S(1)} collective-permute-done((bf16[64,944]{1,0:T(8,128)(2,1)S(1)}, bf16[64,944]{1,0:T(8,128)(2,1)S(1)}, u32[]{:S(2)}, u32[]{:S(2)}) %collective-permute-start.4) | collective-permute-done | bytes 120864 | tf_op jit(solution)/shard_map/ppermute | solution.py:40
  17.9 2.1 %collective-permute-start.6 = (bf16[64,944]{1,0:T(8,128)(2,1)S(1)}, bf16[64,944]{1,0:T(8,128)(2,1)S(1)}, u32[]{:S(2)}, u32[]{:S(2)}) collective-permute-start(bf16[64,944]{1,0:T(8,128)(2,1)S(1)} %collective-permute-done.4.refs_5_), channel_id=1, source_target_pairs={{0,4},{4,8},{8,12},{12,14},{14,10},{10,6},{6,2},{2,0},{1,5},{5,9},... | collective-permute-start | bytes 362504 | tf_op jit(solution)/shard_map/ppermute | solution.py:40
  20.1 2.8 %collective-permute-done.6.refs_7_ = bf16[64,944]{1,0:T(8,128)(2,1)S(1)} collective-permute-done((bf16[64,944]{1,0:T(8,128)(2,1)S(1)}, bf16[64,944]{1,0:T(8,128)(2,1)S(1)}, u32[]{:S(2)}, u32[]{:S(2)}) %collective-permute-start.6) | collective-permute-done | bytes 120864 | tf_op jit(solution)/shard_map/ppermute | solution.py:40
  23.1 0.6 %collective-permute-start.8 = (bf16[2,64,944]{2,1,0:T(8,128)(2,1)S(1)}, bf16[2,64,944]{2,1,0:T(8,128)(2,1)S(1)}, u32[]{:S(2)}, u32[]{:S(2)}) collective-permute-start(bf16[2,64,944]{2,1,0:T(8,128)(2,1)S(1)} %pad_maximum_fusion.2), channel_id=1, source_target_pairs={{0,1},{4,5},{8,9},{12,13},{14,15},{10,11},{6,7},{2,3},{1,0},{5,4},... | collective-permute-start | bytes 725000 | tf_op jit(solution)/shard_map/ppermute | solution.py:59
  23.7 1.5 %collective-permute-done.8.refs_9_ = bf16[2,64,944]{2,1,0:T(8,128)(2,1)S(1)} collective-permute-done((bf16[2,64,944]{2,1,0:T(8,128)(2,1)S(1)}, bf16[2,64,944]{2,1,0:T(8,128)(2,1)S(1)}, u32[]{:S(2)}, u32[]{:S(2)}) %collective-permute-start.8) | collective-permute-done | bytes 241696 | tf_op jit(solution)/shard_map/ppermute | solution.py:59
  25.3 0.6 %copy-done.10 = bf16[2,64,944]{2,1,0:T(8,128)(2,1)} copy-done((bf16[2,64,944]{2,1,0:T(8,128)(2,1)}, bf16[2,64,944]{2,1,0:T(8,128)(2,1)S(1)}, u32[]{:S(2)}) %copy-start.10) | copy-done | bytes 241688
  25.9 0.2 copy-done.8
  26.0 0.1 copy-done.9
  26.1 10.5 %shard_map.73 = bf16[16,49,128]{2,1,0:T(8,128)(2,1)} custom-call(s32[256]{0:T(256)} %constant.4.clone.table, bf16[64,944]{1,0:T(8,128)(2,1)} %copy-done, bf16[64,944]{1,0:T(8,128)(2,1)} %copy-done.1, bf16[64,944]{1,0:T(8,128)(2,1)} %copy-done.2, bf16[64,944]{1,0:T(8,128)(2,1)} %copy-done.3, bf16[64,944]{1,0:T(8,128)(2,1)} %copy-done.4, ...), custom_call_target="tpu_custom_call" | custom-call | tf_op jit(solution)/shard_map/pallas_call | solution.py:150
  36.7 6.4 %all-to-all-start = ((bf16[16,49,128]{2,1,0:T(8,128)(2,1)}), bf16[16,49,128]{2,1,0:T(8,128)(2,1)S(1)}, u32[]{:S(2)}, u32[]{:S(2)}) async-start(bf16[16,49,128]{2,1,0:T(8,128)(2,1)} %shard_map.73), calls=%async_computation | async-start | bytes 458752 | tf_op jit(solution)/shard_map/all_to_all | solution.py:166
  43.1 9.5 %all-to-all-done = bf16[16,49,128]{2,1,0:T(8,128)(2,1)S(1)} async-done(((bf16[16,49,128]{2,1,0:T(8,128)(2,1)}), bf16[16,49,128]{2,1,0:T(8,128)(2,1)S(1)}, u32[]{:S(2)}, u32[]{:S(2)}) %all-to-all-start) | async-done | bytes 200736 | tf_op jit(solution)/shard_map/all_to_all | solution.py:166
  52.6 0.1 copy.8
  52.8 0.1 eq.19
  52.9 0.1 compare_convert_fusion
  53.0 0.4 fusion
  53.5 0.8 %reshape.53 = f32[8,4096]{1,0:T(8,128)} reshape(f32[512,64]{1,0:T(8,128)S(1)} %fusion) | data formatting | bytes 262144 | tf_op jit(solution)/shard_map/reshape | solution.py:177
  (34 shorter events, 0.4 us)
Async XLA Ops:
  1.0 24.2 %copy-start = (bf16[64,944]{1,0:T(8,128)(2,1)}, bf16[64,944]{1,0:T(8,128)(2,1)S(1)}, u32[]{:S(2)}) copy-start(bf16[64,944]{1,0:T(8,128)(2,1)S(1)} %get-tuple-element.6.refs_0_) | copy-start | bytes 362500
  1.0 6.5 %collective-permute-start = (bf16[64,944]{1,0:T(8,128)(2,1)S(1)}, bf16[64,944]{1,0:T(8,128)(2,1)S(1)}, u32[]{:S(2)}, u32[]{:S(2)}) collective-permute-start(bf16[64,944]{1,0:T(8,128)(2,1)S(1)} %get-tuple-element.6.refs_0_), channel_id=1, source_target_pairs={{0,4},{4,8},{8,12},{12,14},{14,10},{10,6},{6,2},{2,0},{1,5},{5,9},... | collective-permute-start | bytes 362504 | tf_op jit(solution)/shard_map/ppermute | solution.py:40
  4.1 5.2 %collective-permute-start.1 = (bf16[64,944]{1,0:T(8,128)(2,1)S(1)}, bf16[64,944]{1,0:T(8,128)(2,1)S(1)}, u32[]{:S(2)}, u32[]{:S(2)}) collective-permute-start(bf16[64,944]{1,0:T(8,128)(2,1)S(1)} %get-tuple-element.6.refs_0_), channel_id=1, source_target_pairs={{0,2},{4,0},{8,4},{12,8},{14,12},{10,14},{6,10},{2,6},{1,3},{5,1},... | collective-permute-start | bytes 362504 | tf_op jit(solution)/shard_map/ppermute | solution.py:44
  7.5 17.7 %copy-start.1 = (bf16[64,944]{1,0:T(8,128)(2,1)}, bf16[64,944]{1,0:T(8,128)(2,1)S(1)}, u32[]{:S(2)}) copy-start(bf16[64,944]{1,0:T(8,128)(2,1)S(1)} %collective-permute-done.refs_1_) | copy-start | bytes 362500
  7.5 5.0 %collective-permute-start.2 = (bf16[64,944]{1,0:T(8,128)(2,1)S(1)}, bf16[64,944]{1,0:T(8,128)(2,1)S(1)}, u32[]{:S(2)}, u32[]{:S(2)}) collective-permute-start(bf16[64,944]{1,0:T(8,128)(2,1)S(1)} %collective-permute-done.refs_1_), channel_id=1, source_target_pairs={{0,4},{4,8},{8,12},{12,14},{14,10},{10,6},{6,2},{2,0},{1,5},{5,9},... | collective-permute-start | bytes 362504 | tf_op jit(solution)/shard_map/ppermute | solution.py:40
  9.3 15.9 %copy-start.2 = (bf16[64,944]{1,0:T(8,128)(2,1)}, bf16[64,944]{1,0:T(8,128)(2,1)S(1)}, u32[]{:S(2)}) copy-start(bf16[64,944]{1,0:T(8,128)(2,1)S(1)} %collective-permute-done.1.refs_2_) | copy-start | bytes 362500
  9.3 5.0 %collective-permute-start.3 = (bf16[64,944]{1,0:T(8,128)(2,1)S(1)}, bf16[64,944]{1,0:T(8,128)(2,1)S(1)}, u32[]{:S(2)}, u32[]{:S(2)}) collective-permute-start(bf16[64,944]{1,0:T(8,128)(2,1)S(1)} %collective-permute-done.1.refs_2_), channel_id=1, source_target_pairs={{0,2},{4,0},{8,4},{12,8},{14,12},{10,14},{6,10},{2,6},{1,3},{5,1},... | collective-permute-start | bytes 362504 | tf_op jit(solution)/shard_map/ppermute | solution.py:44
  12.5 12.7 %copy-start.3 = (bf16[64,944]{1,0:T(8,128)(2,1)}, bf16[64,944]{1,0:T(8,128)(2,1)S(1)}, u32[]{:S(2)}) copy-start(bf16[64,944]{1,0:T(8,128)(2,1)S(1)} %collective-permute-done.2.refs_3_) | copy-start | bytes 362500
  12.5 5.4 %collective-permute-start.4 = (bf16[64,944]{1,0:T(8,128)(2,1)S(1)}, bf16[64,944]{1,0:T(8,128)(2,1)S(1)}, u32[]{:S(2)}, u32[]{:S(2)}) collective-permute-start(bf16[64,944]{1,0:T(8,128)(2,1)S(1)} %collective-permute-done.2.refs_3_), channel_id=1, source_target_pairs={{0,4},{4,8},{8,12},{12,14},{14,10},{10,6},{6,2},{2,0},{1,5},{5,9},... | collective-permute-start | bytes 362504 | tf_op jit(solution)/shard_map/ppermute | solution.py:40
  14.3 10.9 %copy-start.4 = (bf16[64,944]{1,0:T(8,128)(2,1)}, bf16[64,944]{1,0:T(8,128)(2,1)S(1)}, u32[]{:S(2)}) copy-start(bf16[64,944]{1,0:T(8,128)(2,1)S(1)} %collective-permute-done.3.refs_4_) | copy-start | bytes 362500
  14.3 5.8 %collective-permute-start.5 = (bf16[64,944]{1,0:T(8,128)(2,1)S(1)}, bf16[64,944]{1,0:T(8,128)(2,1)S(1)}, u32[]{:S(2)}, u32[]{:S(2)}) collective-permute-start(bf16[64,944]{1,0:T(8,128)(2,1)S(1)} %collective-permute-done.3.refs_4_), channel_id=1, source_target_pairs={{0,2},{4,0},{8,4},{12,8},{14,12},{10,14},{6,10},{2,6},{1,3},{5,1},... | collective-permute-start | bytes 362504 | tf_op jit(solution)/shard_map/ppermute | solution.py:44
  17.9 7.3 %copy-start.5 = (bf16[64,944]{1,0:T(8,128)(2,1)}, bf16[64,944]{1,0:T(8,128)(2,1)S(1)}, u32[]{:S(2)}) copy-start(bf16[64,944]{1,0:T(8,128)(2,1)S(1)} %collective-permute-done.4.refs_5_) | copy-start | bytes 362500
  17.9 5.0 %collective-permute-start.6 = (bf16[64,944]{1,0:T(8,128)(2,1)S(1)}, bf16[64,944]{1,0:T(8,128)(2,1)S(1)}, u32[]{:S(2)}, u32[]{:S(2)}) collective-permute-start(bf16[64,944]{1,0:T(8,128)(2,1)S(1)} %collective-permute-done.4.refs_5_), channel_id=1, source_target_pairs={{0,4},{4,8},{8,12},{12,14},{14,10},{10,6},{6,2},{2,0},{1,5},{5,9},... | collective-permute-start | bytes 362504 | tf_op jit(solution)/shard_map/ppermute | solution.py:40
  20.0 5.1 %collective-permute-start.7 = (bf16[3,64,944]{2,1,0:T(8,128)(2,1)S(1)}, bf16[3,64,944]{2,1,0:T(8,128)(2,1)S(1)}, u32[]{:S(2)}, u32[]{:S(2)}) collective-permute-start(bf16[3,64,944]{2,1,0:T(8,128)(2,1)S(1)} %pad_maximum_fusion), channel_id=1, source_target_pairs={{0,1},{4,5},{8,9},{12,13},{14,15},{10,11},{6,7},{2,3},{1,0},{5,4},... | collective-permute-start | bytes 1087496 | tf_op jit(solution)/shard_map/ppermute | solution.py:59
  20.1 5.1 %copy-start.6 = (bf16[64,944]{1,0:T(8,128)(2,1)}, bf16[64,944]{1,0:T(8,128)(2,1)S(1)}, u32[]{:S(2)}) copy-start(bf16[64,944]{1,0:T(8,128)(2,1)S(1)} %collective-permute-done.5.refs_6_) | copy-start | bytes 362500
  22.9 2.3 %copy-start.7 = (bf16[64,944]{1,0:T(8,128)(2,1)}, bf16[64,944]{1,0:T(8,128)(2,1)S(1)}, u32[]{:S(2)}) copy-start(bf16[64,944]{1,0:T(8,128)(2,1)S(1)} %collective-permute-done.6.refs_7_) | copy-start | bytes 362500
  23.0 2.2 %collective-permute-start.9 = (bf16[3,64,944]{2,1,0:T(8,128)(2,1)S(1)}, bf16[3,64,944]{2,1,0:T(8,128)(2,1)S(1)}, u32[]{:S(2)}, u32[]{:S(2)}) collective-permute-start(bf16[3,64,944]{2,1,0:T(8,128)(2,1)S(1)} %pad_maximum_fusion.1), channel_id=1, source_target_pairs={{0,1},{4,5},{8,9},{12,13},{14,15},{10,11},{6,7},{2,3},{1,0},{5,4},... | collective-permute-start | bytes 1087496 | tf_op jit(solution)/shard_map/ppermute | solution.py:59
  23.1 2.0 %collective-permute-start.8 = (bf16[2,64,944]{2,1,0:T(8,128)(2,1)S(1)}, bf16[2,64,944]{2,1,0:T(8,128)(2,1)S(1)}, u32[]{:S(2)}, u32[]{:S(2)}) collective-permute-start(bf16[2,64,944]{2,1,0:T(8,128)(2,1)S(1)} %pad_maximum_fusion.2), channel_id=1, source_target_pairs={{0,1},{4,5},{8,9},{12,13},{14,15},{10,11},{6,7},{2,3},{1,0},{5,4},... | collective-permute-start | bytes 725000 | tf_op jit(solution)/shard_map/ppermute | solution.py:59
  25.2 0.7 %copy-start.10 = (bf16[2,64,944]{2,1,0:T(8,128)(2,1)}, bf16[2,64,944]{2,1,0:T(8,128)(2,1)S(1)}, u32[]{:S(2)}) copy-start(bf16[2,64,944]{2,1,0:T(8,128)(2,1)S(1)} %collective-permute-done.8.refs_9_) | copy-start | bytes 724996
  25.2 0.8 %copy-start.8 = (bf16[3,64,944]{2,1,0:T(8,128)(2,1)}, bf16[3,64,944]{2,1,0:T(8,128)(2,1)S(1)}, u32[]{:S(2)}) copy-start(bf16[3,64,944]{2,1,0:T(8,128)(2,1)S(1)} %collective-permute-done.7.refs_8_) | copy-start | bytes 1087492
  25.2 1.0 %copy-start.9 = (bf16[3,64,944]{2,1,0:T(8,128)(2,1)}, bf16[3,64,944]{2,1,0:T(8,128)(2,1)S(1)}, u32[]{:S(2)}) copy-start(bf16[3,64,944]{2,1,0:T(8,128)(2,1)S(1)} %collective-permute-done.9.refs_10_) | copy-start | bytes 1087492
  36.7 16.0 %all-to-all-start = ((bf16[16,49,128]{2,1,0:T(8,128)(2,1)}), bf16[16,49,128]{2,1,0:T(8,128)(2,1)S(1)}, u32[]{:S(2)}, u32[]{:S(2)}) async-start(bf16[16,49,128]{2,1,0:T(8,128)(2,1)} %shard_map.73), calls=%async_computation | async-start | bytes 458752 | tf_op jit(solution)/shard_map/all_to_all | solution.py:166

commit v17 on v12

--- a/solution.py
+++ b/solution.py
@@ -35,7 +35,14 @@
     early_shifts, late_shifts = [0], []
     split = max(1, length // 4)
     ahead = behind = block
+    half = block.shape[0] // 2
     for step in range(1, length // 2 + 1):
+        if step == length - step and half * 2 == block.shape[0] and step > 1:
+            top = lax.ppermute(ahead[:half], "dp", forward)
+            bottom = lax.ppermute(behind[half:], "dp", backward)
+            late.append(jnp.concatenate([top, bottom], axis=0))
+            late_shifts.append(-step)
+            continue
         ahead = lax.ppermute(ahead, "dp", forward)
         (early if step <= split else late).append(ahead)
         (early_shifts if step <= split else late_shifts).append(-step)

time: 53.9 us -> 54.4 us (level)
  waiting for transfers between devices: 22.7 us -> 24.3 us
  starting transfers between devices: 15.8 us -> 14.5 us
    ppermute x0 -> x2, waiting for transfers between devices: none -> 4.45 us  [the longest x1 2.4 us: ring_gather(): bottom = lax.ppermute(behind[half:], 'dp', backward)]
    ppermute x4 -> x3, waiting for transfers between devices: 11.5 us -> 8.6 us  [ring_gather(): ahead = lax.ppermute(ahead, 'dp', forward)]
    ppermute x0 -> x2, starting transfers between devices: none -> 2.21 us  [the longest x1 2.15 us: ring_gather(): top = lax.ppermute(ahead[:half], 'dp', forward)]
    ppermute x4 -> x3, starting transfers between devices: 8.76 us -> 6.67 us  [ring_gather(): ahead = lax.ppermute(ahead, 'dp', forward)]
    all_to_all x1, starting transfers between devices: 6.44 us -> 4.98 us  [local(): arrived = lax.all_to_all(packed, 'dp', 0, 0, tiled=True)]
  transfers between devices with their start and end apart: 10 -> 11, of which waited for: 6 -> 7; matrix products, arithmetic and copies ran while one was open for 2% -> 2% of each run, Pallas kernels for 0% -> 0%
where the time goes in v17:
time: 54.4 us; the launch traced here: 54.1 us
  waiting for transfers between devices  24.3 us (45%)
  starting transfers between devices  14.5 us (27%)
  Pallas kernels  10.5 us (19%)
  other arithmetic  2.19 us (4%)
  local copies, waits for them, and re-layouts  2.02 us (4%)
    pallas_call x1, Pallas kernels, project_rows(): pl.pallas_call(projection_kernel(count, devices, features // devices, out...  10.5 us
    all_to_all x1, waiting for transfers between devices, local(): arrived = lax.all_to_all(packed, 'dp', 0, 0, tiled=True)  9.51 us
    ppermute x3, waiting for transfers between devices, ring_gather(): ahead = lax.ppermute(ahead, 'dp', forward)  8.6 us
    ppermute x3, starting transfers between devices, ring_gather(): ahead = lax.ppermute(ahead, 'dp', forward)  6.67 us
    all_to_all x1, starting transfers between devices, local(): arrived = lax.all_to_all(packed, 'dp', 0, 0, tiled=True)  4.98 us
    ppermute x1, waiting for transfers between devices, ring_gather(): bottom = lax.ppermute(behind[half:], 'dp', backward)  2.4 us
    ppermute x1, starting transfers between devices, ring_gather(): top = lax.ppermute(ahead[:half], 'dp', forward)  2.15 us
    ppermute x1, waiting for transfers between devices, ring_gather(): top = lax.ppermute(ahead[:half], 'dp', forward)  2.05 us
  transfers between devices with their start and end apart: 11, of which 7 were waited for; matrix products, arithmetic and copies ran while one was open for 2% of the time, Pallas kernels for 0%

profile of v17, /device:TPU:0, one launch (start us, length us, event | category | flops | bytes accessed | tf_op | source)
XLA Modules:
  0.0 54.1 jit_solution(11386333758561293105)
XLA Ops:
  0.0 1.0 %pad_maximum_fusion.1.refs_0_ = bf16[64,944]{1,0:T(8,128)(2,1)S(1)} fusion(bf16[64,256]{1,0:T(8,128)(2,1)} %param.10, bf16[64,688]{1,0:T(8,128)(2,1)} %param.9), kind=kLoop, calls=%fused_computation.4 | loop fusion | flops 241664 | bytes 241664 | tf_op jit(solution)/shard_map/concatenate | solution.py:170
  1.0 3.1 %collective-permute-start = (bf16[64,944]{1,0:T(8,128)(2,1)S(1)}, bf16[64,944]{1,0:T(8,128)(2,1)S(1)}, u32[]{:S(2)}, u32[]{:S(2)}) collective-permute-start(bf16[64,944]{1,0:T(8,128)(2,1)S(1)} %pad_maximum_fusion.1.refs_0_), channel_id=1, source_target_pairs={{0,4},{4,8},{8,12},{12,14},{14,10},{10,6},{6,2},{2,0},{1,5},{5,9},... | collective-permute-start | bytes 362504 | tf_op jit(solution)/shard_map/ppermute | solution.py:46
  4.1 1.0 %bitcast_dynamic-update-slice_fusion.4 = bf16[5,64,944]{2,1,0:T(8,128)(2,1)S(1)} fusion(bf16[64,256]{1,0:T(8,128)(2,1)} %param.10, bf16[64,688]{1,0:T(8,128)(2,1)} %param.9), kind=kLoop, calls=%fused_computation.9 | loop fusion | flops 241663 | bytes 251904
  5.1 2.4 %collective-permute-done.refs_1_ = bf16[64,944]{1,0:T(8,128)(2,1)S(1)} collective-permute-done((bf16[64,944]{1,0:T(8,128)(2,1)S(1)}, bf16[64,944]{1,0:T(8,128)(2,1)S(1)}, u32[]{:S(2)}, u32[]{:S(2)}) %collective-permute-start) | collective-permute-done | bytes 120864 | tf_op jit(solution)/shard_map/ppermute | solution.py:46
  7.5 1.8 %collective-permute-start.2 = (bf16[64,944]{1,0:T(8,128)(2,1)S(1)}, bf16[64,944]{1,0:T(8,128)(2,1)S(1)}, u32[]{:S(2)}, u32[]{:S(2)}) collective-permute-start(bf16[64,944]{1,0:T(8,128)(2,1)S(1)} %collective-permute-done.refs_1_), channel_id=1, source_target_pairs={{0,4},{4,8},{8,12},{12,14},{14,10},{10,6},{6,2},{2,0},{1,5},{5,9},... | collective-permute-start | bytes 362504 | tf_op jit(solution)/shard_map/ppermute | solution.py:46
  9.3 0.2 collective-permute-start.3
  9.6 2.9 %collective-permute-done.2.refs_3_ = bf16[64,944]{1,0:T(8,128)(2,1)S(1)} collective-permute-done((bf16[64,944]{1,0:T(8,128)(2,1)S(1)}, bf16[64,944]{1,0:T(8,128)(2,1)S(1)}, u32[]{:S(2)}, u32[]{:S(2)}) %collective-permute-start.2) | collective-permute-done | bytes 120864 | tf_op jit(solution)/shard_map/ppermute | solution.py:46
  12.5 1.8 %collective-permute-start.4 = (bf16[64,944]{1,0:T(8,128)(2,1)S(1)}, bf16[64,944]{1,0:T(8,128)(2,1)S(1)}, u32[]{:S(2)}, u32[]{:S(2)}) collective-permute-start(bf16[64,944]{1,0:T(8,128)(2,1)S(1)} %collective-permute-done.2.refs_3_), channel_id=1, source_target_pairs={{0,4},{4,8},{8,12},{12,14},{14,10},{10,6},{6,2},{2,0},{1,5},{5,9},... | collective-permute-start | bytes 362504 | tf_op jit(solution)/shard_map/ppermute | solution.py:46
  14.3 0.2 collective-permute-start.5
  14.5 3.3 %collective-permute-done.4.refs_5_ = bf16[64,944]{1,0:T(8,128)(2,1)S(1)} collective-permute-done((bf16[64,944]{1,0:T(8,128)(2,1)S(1)}, bf16[64,944]{1,0:T(8,128)(2,1)S(1)}, u32[]{:S(2)}, u32[]{:S(2)}) %collective-permute-start.4) | collective-permute-done | bytes 120864 | tf_op jit(solution)/shard_map/ppermute | solution.py:46
  17.8 2.1 %collective-permute-start.6 = (bf16[32,944]{1,0:T(8,128)(2,1)S(1)}, bf16[32,944]{1,0:T(8,128)(2,1)S(1)}, u32[]{:S(2)}, u32[]{:S(2)}) collective-permute-start(bf16[32,944]{1,0:T(8,128)(2,1)S(1)} %slice.24), channel_id=1, source_target_pairs={{0,4},{4,8},{8,12},{12,14},{14,10},{10,6},{6,2},{2,0},{1,5},{5,9},... | collective-permute-start | bytes 181256 | tf_op jit(solution)/shard_map/ppermute | solution.py:41
  20.2 2.0 %collective-permute-done.6 = bf16[32,944]{1,0:T(8,128)(2,1)S(1)} collective-permute-done((bf16[32,944]{1,0:T(8,128)(2,1)S(1)}, bf16[32,944]{1,0:T(8,128)(2,1)S(1)}, u32[]{:S(2)}, u32[]{:S(2)}) %collective-permute-start.6) | collective-permute-done | bytes 60448 | tf_op jit(solution)/shard_map/ppermute | solution.py:41
  22.2 2.4 %collective-permute-done.7 = bf16[32,944]{1,0:T(8,128)(2,1)S(1)} collective-permute-done((bf16[32,944]{1,0:T(8,128)(2,1)S(1)}, bf16[32,944]{1,0:T(8,128)(2,1)S(1)}, u32[]{:S(2)}, u32[]{:S(2)}) %collective-permute-start.7) | collective-permute-done | bytes 60448 | tf_op jit(solution)/shard_map/ppermute | solution.py:42
  24.8 1.7 %collective-permute-done.9.refs_9_ = bf16[3,64,944]{2,1,0:T(8,128)(2,1)S(1)} collective-permute-done((bf16[3,64,944]{2,1,0:T(8,128)(2,1)S(1)}, bf16[3,64,944]{2,1,0:T(8,128)(2,1)S(1)}, u32[]{:S(2)}, u32[]{:S(2)}) %collective-permute-start.9) | collective-permute-done | bytes 362528 | tf_op jit(solution)/shard_map/ppermute | solution.py:65
  26.6 0.7 %copy-done.9 = bf16[3,64,944]{2,1,0:T(8,128)(2,1)} copy-done((bf16[3,64,944]{2,1,0:T(8,128)(2,1)}, bf16[3,64,944]{2,1,0:T(8,128)(2,1)S(1)}, u32[]{:S(2)}) %copy-start.9) | copy-done | bytes 362520
  27.2 0.2 copy-done.3
  27.5 10.5 %shard_map.73 = bf16[16,49,128]{2,1,0:T(8,128)(2,1)} custom-call(s32[256]{0:T(256)} %constant.4.clone.table, bf16[64,944]{1,0:T(8,128)(2,1)} %copy-done.4, bf16[64,944]{1,0:T(8,128)(2,1)} %copy-done.5, bf16[64,944]{1,0:T(8,128)(2,1)} %copy-done.6, bf16[64,944]{1,0:T(8,128)(2,1)} %copy-done.7, bf16[64,944]{1,0:T(8,128)(2,1)} %copy-done.8, ...), custom_call_target="tpu_custom_call" | custom-call | tf_op jit(solution)/shard_map/pallas_call | solution.py:156
  37.9 5.0 %all-to-all-start = ((bf16[16,49,128]{2,1,0:T(8,128)(2,1)}), bf16[16,49,128]{2,1,0:T(8,128)(2,1)S(1)}, u32[]{:S(2)}, u32[]{:S(2)}) async-start(bf16[16,49,128]{2,1,0:T(8,128)(2,1)} %shard_map.73), calls=%async_computation | async-start | bytes 458752 | tf_op jit(solution)/shard_map/all_to_all | solution.py:172
  42.9 9.5 %all-to-all-done = bf16[16,49,128]{2,1,0:T(8,128)(2,1)S(1)} async-done(((bf16[16,49,128]{2,1,0:T(8,128)(2,1)}), bf16[16,49,128]{2,1,0:T(8,128)(2,1)S(1)}, u32[]{:S(2)}, u32[]{:S(2)}) %all-to-all-start) | async-done | bytes 200736 | tf_op jit(solution)/shard_map/all_to_all | solution.py:172
  52.5 0.1 copy.8
  52.6 0.1 eq.19
  52.7 0.1 compare_convert_fusion
  52.9 0.4 fusion
  53.3 0.8 %reshape.53 = f32[8,4096]{1,0:T(8,128)} reshape(f32[512,64]{1,0:T(8,128)S(1)} %fusion) | data formatting | bytes 262144 | tf_op jit(solution)/shard_map/reshape | solution.py:183
  (39 shorter events, 0.5 us)
Async XLA Ops:
  1.0 25.5 %copy-start.4 = (bf16[64,944]{1,0:T(8,128)(2,1)}, bf16[64,944]{1,0:T(8,128)(2,1)S(1)}, u32[]{:S(2)}) copy-start(bf16[64,944]{1,0:T(8,128)(2,1)S(1)} %pad_maximum_fusion.1.refs_0_) | copy-start | bytes 362500
  1.0 6.5 %collective-permute-start = (bf16[64,944]{1,0:T(8,128)(2,1)S(1)}, bf16[64,944]{1,0:T(8,128)(2,1)S(1)}, u32[]{:S(2)}, u32[]{:S(2)}) collective-permute-start(bf16[64,944]{1,0:T(8,128)(2,1)S(1)} %pad_maximum_fusion.1.refs_0_), channel_id=1, source_target_pairs={{0,4},{4,8},{8,12},{12,14},{14,10},{10,6},{6,2},{2,0},{1,5},{5,9},... | collective-permute-start | bytes 362504 | tf_op jit(solution)/shard_map/ppermute | solution.py:46
  4.1 5.2 %collective-permute-start.1 = (bf16[64,944]{1,0:T(8,128)(2,1)S(1)}, bf16[64,944]{1,0:T(8,128)(2,1)S(1)}, u32[]{:S(2)}, u32[]{:S(2)}) collective-permute-start(bf16[64,944]{1,0:T(8,128)(2,1)S(1)} %pad_maximum_fusion.1.refs_0_), channel_id=1, source_target_pairs={{0,2},{4,0},{8,4},{12,8},{14,12},{10,14},{6,10},{2,6},{1,3},{5,1},... | collective-permute-start | bytes 362504 | tf_op jit(solution)/shard_map/ppermute | solution.py:50
  7.5 19.0 %copy-start.5 = (bf16[64,944]{1,0:T(8,128)(2,1)}, bf16[64,944]{1,0:T(8,128)(2,1)S(1)}, u32[]{:S(2)}) copy-start(bf16[64,944]{1,0:T(8,128)(2,1)S(1)} %collective-permute-done.refs_1_) | copy-start | bytes 362500
  7.5 5.0 %collective-permute-start.2 = (bf16[64,944]{1,0:T(8,128)(2,1)S(1)}, bf16[64,944]{1,0:T(8,128)(2,1)S(1)}, u32[]{:S(2)}, u32[]{:S(2)}) collective-permute-start(bf16[64,944]{1,0:T(8,128)(2,1)S(1)} %collective-permute-done.refs_1_), channel_id=1, source_target_pairs={{0,4},{4,8},{8,12},{12,14},{14,10},{10,6},{6,2},{2,0},{1,5},{5,9},... | collective-permute-start | bytes 362504 | tf_op jit(solution)/shard_map/ppermute | solution.py:46
  9.3 17.2 %copy-start.6 = (bf16[64,944]{1,0:T(8,128)(2,1)}, bf16[64,944]{1,0:T(8,128)(2,1)S(1)}, u32[]{:S(2)}) copy-start(bf16[64,944]{1,0:T(8,128)(2,1)S(1)} %collective-permute-done.1.refs_2_) | copy-start | bytes 362500
  9.3 5.0 %collective-permute-start.3 = (bf16[64,944]{1,0:T(8,128)(2,1)S(1)}, bf16[64,944]{1,0:T(8,128)(2,1)S(1)}, u32[]{:S(2)}, u32[]{:S(2)}) collective-permute-start(bf16[64,944]{1,0:T(8,128)(2,1)S(1)} %collective-permute-done.1.refs_2_), channel_id=1, source_target_pairs={{0,2},{4,0},{8,4},{12,8},{14,12},{10,14},{6,10},{2,6},{1,3},{5,1},... | collective-permute-start | bytes 362504 | tf_op jit(solution)/shard_map/ppermute | solution.py:50
  12.5 14.0 %copy-start.7 = (bf16[64,944]{1,0:T(8,128)(2,1)}, bf16[64,944]{1,0:T(8,128)(2,1)S(1)}, u32[]{:S(2)}) copy-start(bf16[64,944]{1,0:T(8,128)(2,1)S(1)} %collective-permute-done.2.refs_3_) | copy-start | bytes 362500
  12.5 5.3 %collective-permute-start.4 = (bf16[64,944]{1,0:T(8,128)(2,1)S(1)}, bf16[64,944]{1,0:T(8,128)(2,1)S(1)}, u32[]{:S(2)}, u32[]{:S(2)}) collective-permute-start(bf16[64,944]{1,0:T(8,128)(2,1)S(1)} %collective-permute-done.2.refs_3_), channel_id=1, source_target_pairs={{0,4},{4,8},{8,12},{12,14},{14,10},{10,6},{6,2},{2,0},{1,5},{5,9},... | collective-permute-start | bytes 362504 | tf_op jit(solution)/shard_map/ppermute | solution.py:46
  14.3 12.2 %copy-start.8 = (bf16[64,944]{1,0:T(8,128)(2,1)}, bf16[64,944]{1,0:T(8,128)(2,1)S(1)}, u32[]{:S(2)}) copy-start(bf16[64,944]{1,0:T(8,128)(2,1)S(1)} %collective-permute-done.3.refs_4_) | copy-start | bytes 362500
  14.3 5.8 %collective-permute-start.5 = (bf16[64,944]{1,0:T(8,128)(2,1)S(1)}, bf16[64,944]{1,0:T(8,128)(2,1)S(1)}, u32[]{:S(2)}, u32[]{:S(2)}) collective-permute-start(bf16[64,944]{1,0:T(8,128)(2,1)S(1)} %collective-permute-done.3.refs_4_), channel_id=1, source_target_pairs={{0,2},{4,0},{8,4},{12,8},{14,12},{10,14},{6,10},{2,6},{1,3},{5,1},... | collective-permute-start | bytes 362504 | tf_op jit(solution)/shard_map/ppermute | solution.py:50
  17.8 8.7 %copy-start = (bf16[64,944]{1,0:T(8,128)(2,1)}, bf16[64,944]{1,0:T(8,128)(2,1)S(1)}, u32[]{:S(2)}) copy-start(bf16[64,944]{1,0:T(8,128)(2,1)S(1)} %collective-permute-done.4.refs_5_) | copy-start | bytes 362500
  17.8 4.4 %collective-permute-start.6 = (bf16[32,944]{1,0:T(8,128)(2,1)S(1)}, bf16[32,944]{1,0:T(8,128)(2,1)S(1)}, u32[]{:S(2)}, u32[]{:S(2)}) collective-permute-start(bf16[32,944]{1,0:T(8,128)(2,1)S(1)} %slice.24), channel_id=1, source_target_pairs={{0,4},{4,8},{8,12},{12,14},{14,10},{10,6},{6,2},{2,0},{1,5},{5,9},... | collective-permute-start | bytes 181256 | tf_op jit(solution)/shard_map/ppermute | solution.py:41
  20.0 6.5 %collective-permute-start.8 = (bf16[5,64,944]{2,1,0:T(8,128)(2,1)S(1)}, bf16[5,64,944]{2,1,0:T(8,128)(2,1)S(1)}, u32[]{:S(2)}, u32[]{:S(2)}) collective-permute-start(bf16[5,64,944]{2,1,0:T(8,128)(2,1)S(1)} %bitcast_dynamic-update-slice_fusion), channel_id=1, source_target_pairs={{0,1},{4,5},{8,9},{12,13},{14,15},{10,11},{6,7},{2,3},{1,0},{5,4},... | collective-permute-start | bytes 1812488 | tf_op jit(solution)/shard_map/ppermute | solution.py:65
  20.1 6.5 %copy-start.1 = (bf16[64,944]{1,0:T(8,128)(2,1)}, bf16[64,944]{1,0:T(8,128)(2,1)S(1)}, u32[]{:S(2)}) copy-start(bf16[64,944]{1,0:T(8,128)(2,1)S(1)} %collective-permute-done.5.refs_6_) | copy-start | bytes 362500
  20.1 4.5 %collective-permute-start.7 = (bf16[32,944]{1,0:T(8,128)(2,1)S(1)}, bf16[32,944]{1,0:T(8,128)(2,1)S(1)}, u32[]{:S(2)}, u32[]{:S(2)}) collective-permute-start(bf16[32,944]{1,0:T(8,128)(2,1)S(1)} %slice.25), channel_id=1, source_target_pairs={{0,2},{4,0},{8,4},{12,8},{14,12},{10,14},{6,10},{2,6},{1,3},{5,1},... | collective-permute-start | bytes 181256 | tf_op jit(solution)/shard_map/ppermute | solution.py:42
  24.6 1.9 %copy-start.2 = (bf16[64,944]{1,0:T(8,128)(2,1)}, bf16[64,944]{1,0:T(8,128)(2,1)S(1)}, u32[]{:S(2)}) copy-start(bf16[64,944]{1,0:T(8,128)(2,1)S(1)} %constant_dynamic-update-slice_fusion.refs_7_) | copy-start | bytes 362500
  24.7 1.8 %collective-permute-start.9 = (bf16[3,64,944]{2,1,0:T(8,128)(2,1)S(1)}, bf16[3,64,944]{2,1,0:T(8,128)(2,1)S(1)}, u32[]{:S(2)}, u32[]{:S(2)}) collective-permute-start(bf16[3,64,944]{2,1,0:T(8,128)(2,1)S(1)} %pad_maximum_fusion), channel_id=1, source_target_pairs={{0,1},{4,5},{8,9},{12,13},{14,15},{10,11},{6,7},{2,3},{1,0},{5,4},... | collective-permute-start | bytes 1087496 | tf_op jit(solution)/shard_map/ppermute | solution.py:65
  26.5 0.8 %copy-start.9 = (bf16[3,64,944]{2,1,0:T(8,128)(2,1)}, bf16[3,64,944]{2,1,0:T(8,128)(2,1)S(1)}, u32[]{:S(2)}) copy-start(bf16[3,64,944]{2,1,0:T(8,128)(2,1)S(1)} %collective-permute-done.9.refs_9_) | copy-start | bytes 1087492
  26.5 1.0 %copy-start.3 = (bf16[5,64,944]{2,1,0:T(8,128)(2,1)}, bf16[5,64,944]{2,1,0:T(8,128)(2,1)S(1)}, u32[]{:S(2)}) copy-start(bf16[5,64,944]{2,1,0:T(8,128)(2,1)S(1)} %collective-permute-done.8.refs_8_) | copy-start | bytes 1812484
  37.9 14.5 %all-to-all-start = ((bf16[16,49,128]{2,1,0:T(8,128)(2,1)}), bf16[16,49,128]{2,1,0:T(8,128)(2,1)S(1)}, u32[]{:S(2)}, u32[]{:S(2)}) async-start(bf16[16,49,128]{2,1,0:T(8,128)(2,1)} %shard_map.73), calls=%async_computation | async-start | bytes 458752 | tf_op jit(solution)/shard_map/all_to_all | solution.py:172

commit v18 on v17

--- a/solution.py
+++ b/solution.py
@@ -89,8 +89,8 @@
                     stacked[table[me * width + at + k]] = other_ref[k]
                 at += size
             for d in range(devices):
-                hidden_full[:, d * hidden_cols:(d + 1) * hidden_cols] = stacked[d, :, :hidden_cols]
-                output_full[:, d * output_cols:(d + 1) * output_cols] = stacked[d, :, hidden_cols:]
+                hidden_full[:, d * hidden_cols:(d + 1) * hidden_cols] = stacked[d, :, output_cols:]
+                output_full[:, d * output_cols:(d + 1) * output_cols] = stacked[d, :, :output_cols]
 
         dims = (((1,), (1,)), ((), ()))
         left = lax.dot_general(hidden_full[...], hidden_ref[...], dims, preferred_element_type=jnp.float32)
@@ -167,7 +167,7 @@
     capacity = 2 * local_tokens // devices
     rank_width = hidden_basis.shape[0]
     buffer_len = devices * capacity
-    blocks, other, table = ring_gather(jnp.concatenate([hidden_basis, output_basis], axis=1), devices)
+    blocks, other, table = ring_gather(jnp.concatenate([output_basis, hidden_basis], axis=1), devices)
     packed = project_rows(blocks, other, table, hidden, out_grad, owner_ids, doc_slot, devices, capacity)
     arrived = lax.all_to_all(packed, "dp", 0, 0, tiled=True)
     rows_in = arrived[:, :capacity, :].reshape(buffer_len, 2 * rank_width)

time: 54.4 us -> 54.8 us (level)
  other arithmetic: 2.19 us -> 0.19 us
  local copies, waits for them, and re-layouts: 2.02 us -> 3.69 us
  waiting for transfers between devices: 24.3 us -> 25.3 us
    unnamed x1 -> x0, other arithmetic: 1 us -> none
    concatenate x1 -> x0, other arithmetic: 1 us -> none  [local(): jnp.concatenate([hidden_basis, output_basis], axis=1)]
    ppermute x3, waiting for transfers between devices: 8.6 us -> 9.59 us  [ring_gather(): ahead = lax.ppermute(ahead, 'dp', forward)]
    concatenate x0 -> x1, local copies, waits for them, and re-layouts: none -> 0.9 us  [local(): jnp.concatenate([output_basis, hidden_basis], axis=1)]
    unnamed x24 -> x26, local copies, waits for them, and re-layouts: 0.96 us -> 1.73 us
  transfers between devices with their start and end apart: 11 -> 11, of which waited for: 7 -> 7; matrix products, arithmetic and copies ran while one was open for 2% -> 0% of each run, Pallas kernels for 0% -> 0%
where the time goes in v18:
time: 54.8 us; the launch traced here: 54.5 us
  waiting for transfers between devices  25.3 us (46%)
  starting transfers between devices  14.5 us (26%)
  Pallas kernels  10.2 us (19%)
  local copies, waits for them, and re-layouts  3.69 us (7%)
    pallas_call x1, Pallas kernels, project_rows(): pl.pallas_call(projection_kernel(count, devices, features // devices, out...  10.2 us
    ppermute x3, waiting for transfers between devices, ring_gather(): ahead = lax.ppermute(ahead, 'dp', forward)  9.59 us
    all_to_all x1, waiting for transfers between devices, local(): arrived = lax.all_to_all(packed, 'dp', 0, 0, tiled=True)  9.51 us
    ppermute x3, starting transfers between devices, ring_gather(): ahead = lax.ppermute(ahead, 'dp', forward)  6.67 us
    all_to_all x1, starting transfers between devices, local(): arrived = lax.all_to_all(packed, 'dp', 0, 0, tiled=True)  4.99 us
    ppermute x1, waiting for transfers between devices, ring_gather(): bottom = lax.ppermute(behind[half:], 'dp', backward)  2.4 us
    ppermute x1, starting transfers between devices, ring_gather(): top = lax.ppermute(ahead[:half], 'dp', forward)  2.15 us
    ppermute x1, waiting for transfers between devices, ring_gather(): top = lax.ppermute(ahead[:half], 'dp', forward)  2.05 us
  transfers between devices with their start and end apart: 11, of which 7 were waited for; matrix products, arithmetic and copies ran while one was open for 0% of the time, Pallas kernels for 0%

profile of v18, /device:TPU:0, one launch (start us, length us, event | category | flops | bytes accessed | tf_op | source)
XLA Modules:
  0.0 54.5 jit_solution(17592720857279933242)
XLA Ops:
  0.0 0.8 %constant_dynamic-update-slice_fusion.1 = bf16[64,944]{1,0:T(8,128)(2,1)S(1)} fusion(bf16[64,256]{1,0:T(8,128)(2,1)} %param.10), kind=kLoop, calls=%fused_computation.11 | loop fusion | bytes 65536
  0.8 0.9 %constant_dynamic-update-slice_fusion.refs_0_ = bf16[64,944]{1,0:T(8,128)(2,1)S(1)} fusion(bf16[64,944]{1,0:T(8,128)(2,1)S(1)} %constant_dynamic-update-slice_fusion.1, bf16[64,688]{1,0:T(8,128)(2,1)} %param.9), kind=kLoop, calls=%fused_computation.10 | loop fusion | bytes 186368 | tf_op jit(solution)/shard_map/concatenate | solution.py:170
  1.7 3.1 %collective-permute-start = (bf16[64,944]{1,0:T(8,128)(2,1)S(1)}, bf16[64,944]{1,0:T(8,128)(2,1)S(1)}, u32[]{:S(2)}, u32[]{:S(2)}) collective-permute-start(bf16[64,944]{1,0:T(8,128)(2,1)S(1)} %constant_dynamic-update-slice_fusion.refs_0_), channel_id=1, source_target_pairs={{0,4},{4,8},{8,12},{12,14},{14,10},{10,6},{6,2},{2,0},{1,5},{5,9},... | collective-permute-start | bytes 362504 | tf_op jit(solution)/shard_map/ppermute | solution.py:46
  4.8 3.4 %collective-permute-done.refs_1_ = bf16[64,944]{1,0:T(8,128)(2,1)S(1)} collective-permute-done((bf16[64,944]{1,0:T(8,128)(2,1)S(1)}, bf16[64,944]{1,0:T(8,128)(2,1)S(1)}, u32[]{:S(2)}, u32[]{:S(2)}) %collective-permute-start) | collective-permute-done | bytes 120864 | tf_op jit(solution)/shard_map/ppermute | solution.py:46
  8.2 1.8 %collective-permute-start.2 = (bf16[64,944]{1,0:T(8,128)(2,1)S(1)}, bf16[64,944]{1,0:T(8,128)(2,1)S(1)}, u32[]{:S(2)}, u32[]{:S(2)}) collective-permute-start(bf16[64,944]{1,0:T(8,128)(2,1)S(1)} %collective-permute-done.refs_1_), channel_id=1, source_target_pairs={{0,4},{4,8},{8,12},{12,14},{14,10},{10,6},{6,2},{2,0},{1,5},{5,9},... | collective-permute-start | bytes 362504 | tf_op jit(solution)/shard_map/ppermute | solution.py:46
  10.0 0.2 collective-permute-start.3
  10.2 2.9 %collective-permute-done.2.refs_3_ = bf16[64,944]{1,0:T(8,128)(2,1)S(1)} collective-permute-done((bf16[64,944]{1,0:T(8,128)(2,1)S(1)}, bf16[64,944]{1,0:T(8,128)(2,1)S(1)}, u32[]{:S(2)}, u32[]{:S(2)}) %collective-permute-start.2) | collective-permute-done | bytes 120864 | tf_op jit(solution)/shard_map/ppermute | solution.py:46
  13.2 1.8 %collective-permute-start.4 = (bf16[64,944]{1,0:T(8,128)(2,1)S(1)}, bf16[64,944]{1,0:T(8,128)(2,1)S(1)}, u32[]{:S(2)}, u32[]{:S(2)}) collective-permute-start(bf16[64,944]{1,0:T(8,128)(2,1)S(1)} %collective-permute-done.2.refs_3_), channel_id=1, source_target_pairs={{0,4},{4,8},{8,12},{12,14},{14,10},{10,6},{6,2},{2,0},{1,5},{5,9},... | collective-permute-start | bytes 362504 | tf_op jit(solution)/shard_map/ppermute | solution.py:46
  15.0 0.2 collective-permute-start.5
  15.2 3.3 %collective-permute-done.4.refs_5_ = bf16[64,944]{1,0:T(8,128)(2,1)S(1)} collective-permute-done((bf16[64,944]{1,0:T(8,128)(2,1)S(1)}, bf16[64,944]{1,0:T(8,128)(2,1)S(1)}, u32[]{:S(2)}, u32[]{:S(2)}) %collective-permute-start.4) | collective-permute-done | bytes 120864 | tf_op jit(solution)/shard_map/ppermute | solution.py:46
  18.5 2.1 %collective-permute-start.6 = (bf16[32,944]{1,0:T(8,128)(2,1)S(1)}, bf16[32,944]{1,0:T(8,128)(2,1)S(1)}, u32[]{:S(2)}, u32[]{:S(2)}) collective-permute-start(bf16[32,944]{1,0:T(8,128)(2,1)S(1)} %slice.24), channel_id=1, source_target_pairs={{0,4},{4,8},{8,12},{12,14},{14,10},{10,6},{6,2},{2,0},{1,5},{5,9},... | collective-permute-start | bytes 181256 | tf_op jit(solution)/shard_map/ppermute | solution.py:41
  20.8 2.0 %collective-permute-done.6 = bf16[32,944]{1,0:T(8,128)(2,1)S(1)} collective-permute-done((bf16[32,944]{1,0:T(8,128)(2,1)S(1)}, bf16[32,944]{1,0:T(8,128)(2,1)S(1)}, u32[]{:S(2)}, u32[]{:S(2)}) %collective-permute-start.6) | collective-permute-done | bytes 60448 | tf_op jit(solution)/shard_map/ppermute | solution.py:41
  22.9 2.4 %collective-permute-done.7 = bf16[32,944]{1,0:T(8,128)(2,1)S(1)} collective-permute-done((bf16[32,944]{1,0:T(8,128)(2,1)S(1)}, bf16[32,944]{1,0:T(8,128)(2,1)S(1)}, u32[]{:S(2)}, u32[]{:S(2)}) %collective-permute-start.7) | collective-permute-done | bytes 60448 | tf_op jit(solution)/shard_map/ppermute | solution.py:42
  25.4 1.7 %collective-permute-done.9.refs_9_ = bf16[3,64,944]{2,1,0:T(8,128)(2,1)S(1)} collective-permute-done((bf16[3,64,944]{2,1,0:T(8,128)(2,1)S(1)}, bf16[3,64,944]{2,1,0:T(8,128)(2,1)S(1)}, u32[]{:S(2)}, u32[]{:S(2)}) %collective-permute-start.9) | collective-permute-done | bytes 362528 | tf_op jit(solution)/shard_map/ppermute | solution.py:65
  27.2 0.7 %copy-done.9 = bf16[3,64,944]{2,1,0:T(8,128)(2,1)} copy-done((bf16[3,64,944]{2,1,0:T(8,128)(2,1)}, bf16[3,64,944]{2,1,0:T(8,128)(2,1)S(1)}, u32[]{:S(2)}) %copy-start.9) | copy-done | bytes 362520
  27.9 0.2 copy-done.4
  28.1 10.2 %shard_map.73 = bf16[16,49,128]{2,1,0:T(8,128)(2,1)} custom-call(s32[256]{0:T(256)} %constant.4.clone.table, bf16[64,944]{1,0:T(8,128)(2,1)} %copy-done.3, bf16[64,944]{1,0:T(8,128)(2,1)} %copy-done.5, bf16[64,944]{1,0:T(8,128)(2,1)} %copy-done.6, bf16[64,944]{1,0:T(8,128)(2,1)} %copy-done.7, bf16[64,944]{1,0:T(8,128)(2,1)} %copy-done.8, ...), custom_call_target="tpu_custom_call" | custom-call | tf_op jit(solution)/shard_map/pallas_call | solution.py:156
  38.3 5.0 %all-to-all-start = ((bf16[16,49,128]{2,1,0:T(8,128)(2,1)}), bf16[16,49,128]{2,1,0:T(8,128)(2,1)S(1)}, u32[]{:S(2)}, u32[]{:S(2)}) async-start(bf16[16,49,128]{2,1,0:T(8,128)(2,1)} %shard_map.73), calls=%async_computation | async-start | bytes 458752 | tf_op jit(solution)/shard_map/all_to_all | solution.py:172
  43.4 9.5 %all-to-all-done = bf16[16,49,128]{2,1,0:T(8,128)(2,1)S(1)} async-done(((bf16[16,49,128]{2,1,0:T(8,128)(2,1)}), bf16[16,49,128]{2,1,0:T(8,128)(2,1)S(1)}, u32[]{:S(2)}, u32[]{:S(2)}) %all-to-all-start) | async-done | bytes 200736 | tf_op jit(solution)/shard_map/all_to_all | solution.py:172
  52.9 0.1 copy.8
  53.0 0.1 eq.19
  53.1 0.1 compare_convert_fusion
  53.3 0.4 fusion
  53.7 0.8 %reshape.53 = f32[8,4096]{1,0:T(8,128)} reshape(f32[512,64]{1,0:T(8,128)S(1)} %fusion) | data formatting | bytes 262144 | tf_op jit(solution)/shard_map/reshape | solution.py:183
  (40 shorter events, 0.5 us)
Async XLA Ops:
  1.7 25.5 %copy-start.3 = (bf16[64,944]{1,0:T(8,128)(2,1)}, bf16[64,944]{1,0:T(8,128)(2,1)S(1)}, u32[]{:S(2)}) copy-start(bf16[64,944]{1,0:T(8,128)(2,1)S(1)} %constant_dynamic-update-slice_fusion.refs_0_) | copy-start | bytes 362500
  1.7 6.5 %collective-permute-start = (bf16[64,944]{1,0:T(8,128)(2,1)S(1)}, bf16[64,944]{1,0:T(8,128)(2,1)S(1)}, u32[]{:S(2)}, u32[]{:S(2)}) collective-permute-start(bf16[64,944]{1,0:T(8,128)(2,1)S(1)} %constant_dynamic-update-slice_fusion.refs_0_), channel_id=1, source_target_pairs={{0,4},{4,8},{8,12},{12,14},{14,10},{10,6},{6,2},{2,0},{1,5},{5,9},... | collective-permute-start | bytes 362504 | tf_op jit(solution)/shard_map/ppermute | solution.py:46
  4.7 5.2 %collective-permute-start.1 = (bf16[64,944]{1,0:T(8,128)(2,1)S(1)}, bf16[64,944]{1,0:T(8,128)(2,1)S(1)}, u32[]{:S(2)}, u32[]{:S(2)}) collective-permute-start(bf16[64,944]{1,0:T(8,128)(2,1)S(1)} %constant_dynamic-update-slice_fusion.refs_0_), channel_id=1, source_target_pairs={{0,2},{4,0},{8,4},{12,8},{14,12},{10,14},{6,10},{2,6},{1,3},{5,1},... | collective-permute-start | bytes 362504 | tf_op jit(solution)/shard_map/ppermute | solution.py:50
  8.2 19.0 %copy-start.5 = (bf16[64,944]{1,0:T(8,128)(2,1)}, bf16[64,944]{1,0:T(8,128)(2,1)S(1)}, u32[]{:S(2)}) copy-start(bf16[64,944]{1,0:T(8,128)(2,1)S(1)} %collective-permute-done.refs_1_) | copy-start | bytes 362500
  8.2 5.0 %collective-permute-start.2 = (bf16[64,944]{1,0:T(8,128)(2,1)S(1)}, bf16[64,944]{1,0:T(8,128)(2,1)S(1)}, u32[]{:S(2)}, u32[]{:S(2)}) collective-permute-start(bf16[64,944]{1,0:T(8,128)(2,1)S(1)} %collective-permute-done.refs_1_), channel_id=1, source_target_pairs={{0,4},{4,8},{8,12},{12,14},{14,10},{10,6},{6,2},{2,0},{1,5},{5,9},... | collective-permute-start | bytes 362504 | tf_op jit(solution)/shard_map/ppermute | solution.py:46
  10.0 17.2 %copy-start.6 = (bf16[64,944]{1,0:T(8,128)(2,1)}, bf16[64,944]{1,0:T(8,128)(2,1)S(1)}, u32[]{:S(2)}) copy-start(bf16[64,944]{1,0:T(8,128)(2,1)S(1)} %collective-permute-done.1.refs_2_) | copy-start | bytes 362500
  10.0 5.0 %collective-permute-start.3 = (bf16[64,944]{1,0:T(8,128)(2,1)S(1)}, bf16[64,944]{1,0:T(8,128)(2,1)S(1)}, u32[]{:S(2)}, u32[]{:S(2)}) collective-permute-start(bf16[64,944]{1,0:T(8,128)(2,1)S(1)} %collective-permute-done.1.refs_2_), channel_id=1, source_target_pairs={{0,2},{4,0},{8,4},{12,8},{14,12},{10,14},{6,10},{2,6},{1,3},{5,1},... | collective-permute-start | bytes 362504 | tf_op jit(solution)/shard_map/ppermute | solution.py:50
  13.2 14.0 %copy-start.7 = (bf16[64,944]{1,0:T(8,128)(2,1)}, bf16[64,944]{1,0:T(8,128)(2,1)S(1)}, u32[]{:S(2)}) copy-start(bf16[64,944]{1,0:T(8,128)(2,1)S(1)} %collective-permute-done.2.refs_3_) | copy-start | bytes 362500
  13.2 5.3 %collective-permute-start.4 = (bf16[64,944]{1,0:T(8,128)(2,1)S(1)}, bf16[64,944]{1,0:T(8,128)(2,1)S(1)}, u32[]{:S(2)}, u32[]{:S(2)}) collective-permute-start(bf16[64,944]{1,0:T(8,128)(2,1)S(1)} %collective-permute-done.2.refs_3_), channel_id=1, source_target_pairs={{0,4},{4,8},{8,12},{12,14},{14,10},{10,6},{6,2},{2,0},{1,5},{5,9},... | collective-permute-start | bytes 362504 | tf_op jit(solution)/shard_map/ppermute | solution.py:46
  15.0 12.2 %copy-start.8 = (bf16[64,944]{1,0:T(8,128)(2,1)}, bf16[64,944]{1,0:T(8,128)(2,1)S(1)}, u32[]{:S(2)}) copy-start(bf16[64,944]{1,0:T(8,128)(2,1)S(1)} %collective-permute-done.3.refs_4_) | copy-start | bytes 362500
  15.0 5.8 %collective-permute-start.5 = (bf16[64,944]{1,0:T(8,128)(2,1)S(1)}, bf16[64,944]{1,0:T(8,128)(2,1)S(1)}, u32[]{:S(2)}, u32[]{:S(2)}) collective-permute-start(bf16[64,944]{1,0:T(8,128)(2,1)S(1)} %collective-permute-done.3.refs_4_), channel_id=1, source_target_pairs={{0,2},{4,0},{8,4},{12,8},{14,12},{10,14},{6,10},{2,6},{1,3},{5,1},... | collective-permute-start | bytes 362504 | tf_op jit(solution)/shard_map/ppermute | solution.py:50
  18.5 8.7 %copy-start = (bf16[64,944]{1,0:T(8,128)(2,1)}, bf16[64,944]{1,0:T(8,128)(2,1)S(1)}, u32[]{:S(2)}) copy-start(bf16[64,944]{1,0:T(8,128)(2,1)S(1)} %collective-permute-done.4.refs_5_) | copy-start | bytes 362500
  18.5 4.4 %collective-permute-start.6 = (bf16[32,944]{1,0:T(8,128)(2,1)S(1)}, bf16[32,944]{1,0:T(8,128)(2,1)S(1)}, u32[]{:S(2)}, u32[]{:S(2)}) collective-permute-start(bf16[32,944]{1,0:T(8,128)(2,1)S(1)} %slice.24), channel_id=1, source_target_pairs={{0,4},{4,8},{8,12},{12,14},{14,10},{10,6},{6,2},{2,0},{1,5},{5,9},... | collective-permute-start | bytes 181256 | tf_op jit(solution)/shard_map/ppermute | solution.py:41
  20.6 6.5 %collective-permute-start.8 = (bf16[5,64,944]{2,1,0:T(8,128)(2,1)S(1)}, bf16[5,64,944]{2,1,0:T(8,128)(2,1)S(1)}, u32[]{:S(2)}, u32[]{:S(2)}) collective-permute-start(bf16[5,64,944]{2,1,0:T(8,128)(2,1)S(1)} %bitcast_dynamic-update-slice_fusion), channel_id=1, source_target_pairs={{0,1},{4,5},{8,9},{12,13},{14,15},{10,11},{6,7},{2,3},{1,0},{5,4},... | collective-permute-start | bytes 1812488 | tf_op jit(solution)/shard_map/ppermute | solution.py:65
  20.7 6.5 %copy-start.1 = (bf16[64,944]{1,0:T(8,128)(2,1)}, bf16[64,944]{1,0:T(8,128)(2,1)S(1)}, u32[]{:S(2)}) copy-start(bf16[64,944]{1,0:T(8,128)(2,1)S(1)} %collective-permute-done.5.refs_6_) | copy-start | bytes 362500
  20.8 4.5 %collective-permute-start.7 = (bf16[32,944]{1,0:T(8,128)(2,1)S(1)}, bf16[32,944]{1,0:T(8,128)(2,1)S(1)}, u32[]{:S(2)}, u32[]{:S(2)}) collective-permute-start(bf16[32,944]{1,0:T(8,128)(2,1)S(1)} %slice.25), channel_id=1, source_target_pairs={{0,2},{4,0},{8,4},{12,8},{14,12},{10,14},{6,10},{2,6},{1,3},{5,1},... | collective-permute-start | bytes 181256 | tf_op jit(solution)/shard_map/ppermute | solution.py:42
  25.3 1.9 %copy-start.2 = (bf16[64,944]{1,0:T(8,128)(2,1)}, bf16[64,944]{1,0:T(8,128)(2,1)S(1)}, u32[]{:S(2)}) copy-start(bf16[64,944]{1,0:T(8,128)(2,1)S(1)} %constant_dynamic-update-slice_fusion.2.refs_7_) | copy-start | bytes 362500
  25.3 1.8 %collective-permute-start.9 = (bf16[3,64,944]{2,1,0:T(8,128)(2,1)S(1)}, bf16[3,64,944]{2,1,0:T(8,128)(2,1)S(1)}, u32[]{:S(2)}, u32[]{:S(2)}) collective-permute-start(bf16[3,64,944]{2,1,0:T(8,128)(2,1)S(1)} %pad_maximum_fusion), channel_id=1, source_target_pairs={{0,1},{4,5},{8,9},{12,13},{14,15},{10,11},{6,7},{2,3},{1,0},{5,4},... | collective-permute-start | bytes 1087496 | tf_op jit(solution)/shard_map/ppermute | solution.py:65
  27.1 0.8 %copy-start.9 = (bf16[3,64,944]{2,1,0:T(8,128)(2,1)}, bf16[3,64,944]{2,1,0:T(8,128)(2,1)S(1)}, u32[]{:S(2)}) copy-start(bf16[3,64,944]{2,1,0:T(8,128)(2,1)S(1)} %collective-permute-done.9.refs_9_) | copy-start | bytes 1087492
  27.1 1.0 %copy-start.4 = (bf16[5,64,944]{2,1,0:T(8,128)(2,1)}, bf16[5,64,944]{2,1,0:T(8,128)(2,1)S(1)}, u32[]{:S(2)}) copy-start(bf16[5,64,944]{2,1,0:T(8,128)(2,1)S(1)} %collective-permute-done.8.refs_8_) | copy-start | bytes 1812484
  38.3 14.5 %all-to-all-start = ((bf16[16,49,128]{2,1,0:T(8,128)(2,1)}), bf16[16,49,128]{2,1,0:T(8,128)(2,1)S(1)}, u32[]{:S(2)}, u32[]{:S(2)}) async-start(bf16[16,49,128]{2,1,0:T(8,128)(2,1)} %shard_map.73), calls=%async_computation | async-start | bytes 458752 | tf_op jit(solution)/shard_map/all_to_all | solution.py:172

commit v19 on v13

--- a/solution.py
+++ b/solution.py
@@ -33,7 +33,7 @@
     backward = [(ring[t], ring[(t - 1) % length]) for ring in planes for t in range(length)]
     early, late = [block], []
     early_shifts, late_shifts = [0], []
-    split = max(1, length // 2 - 1)
+    split = max(1, length // 8)
     ahead = behind = block
     for step in range(1, length // 2 + 1):
         ahead = lax.ppermute(ahead, "dp", forward)

time: 54.6 us -> 55 us (level)
  starting transfers between devices: 13.8 us -> 16.3 us
  waiting for transfers between devices: 25.2 us -> 24.1 us
  other arithmetic: 2.14 us -> 1.19 us
    ppermute x3, waiting for transfers between devices: 1.94 us -> 0.01 us  [ring_gather(): behind = lax.ppermute(behind, 'dp', backward)]
    all_to_all x1, starting transfers between devices: 4.93 us -> 6.44 us  [local(): arrived = lax.all_to_all(packed, 'dp', 0, 0, tiled=True)]
    another operation x0 -> x2, other arithmetic: none -> 1.05 us  [ring_gather(): jnp.stack(group)]
    unnamed x1 -> x0, other arithmetic: 1 us -> none
    concatenate x1 -> x0, other arithmetic: 1 us -> none  [local(): jnp.concatenate([hidden_basis, output_basis], axis=1)]
    ppermute x2, waiting for transfers between devices: 1.35 us -> 2.04 us  [ring_gather(): lax.ppermute(jnp.stack(group), 'dp', swap)]
    ppermute x2, starting transfers between devices: 0.07 us -> 0.63 us  [ring_gather(): lax.ppermute(jnp.stack(group), 'dp', swap)]
  transfers between devices with their start and end apart: 10 -> 10, of which waited for: 8 -> 6; matrix products, arithmetic and copies ran while one was open for 2% -> 0% of each run, Pallas kernels for 0% -> 0%
where the time goes in v19:
time: 55 us; the launch traced here: 54.8 us
  waiting for transfers between devices  24.1 us (44%)
  starting transfers between devices  16.3 us (30%)
  Pallas kernels  10.5 us (19%)
  local copies, waits for them, and re-layouts  2.01 us (4%)
  other arithmetic  1.19 us (2%)
    ppermute x4, waiting for transfers between devices, ring_gather(): ahead = lax.ppermute(ahead, 'dp', forward)  12.5 us
    pallas_call x1, Pallas kernels, project_rows(): pl.pallas_call(projection_kernel(count, devices, features // devices, out...  10.5 us
    all_to_all x1, waiting for transfers between devices, local(): arrived = lax.all_to_all(packed, 'dp', 0, 0, tiled=True)  9.51 us
    ppermute x4, starting transfers between devices, ring_gather(): ahead = lax.ppermute(ahead, 'dp', forward)  8.76 us
    all_to_all x1, starting transfers between devices, local(): arrived = lax.all_to_all(packed, 'dp', 0, 0, tiled=True)  6.44 us
    ppermute x2, waiting for transfers between devices, ring_gather(): lax.ppermute(jnp.stack(group), 'dp', swap)  2.04 us
  transfers between devices with their start and end apart: 10, of which 6 were waited for; matrix products, arithmetic and copies ran while one was open for 0% of the time, Pallas kernels for 0%

profile of v19, /device:TPU:0, one launch (start us, length us, event | category | flops | bytes accessed | tf_op | source)
XLA Modules:
  0.0 54.8 jit_solution(5826792551425199512)
XLA Ops:
  0.0 1.0 %fusion.2 = (bf16[1,64,944]{2,1,0:T(8,128)(2,1)S(1)}, bf16[64,944]{1,0:T(8,128)(2,1)S(1)}) fusion(bf16[64,256]{1,0:T(8,128)(2,1)} %param.10, bf16[64,688]{1,0:T(8,128)(2,1)} %param.9), kind=kLoop, calls=%fused_computation.13 | loop fusion | flops 241664 | bytes 362496 | tf_op jit(solution)/shard_map/stack | solution.py:58
  1.0 3.1 %collective-permute-start = (bf16[64,944]{1,0:T(8,128)(2,1)S(1)}, bf16[64,944]{1,0:T(8,128)(2,1)S(1)}, u32[]{:S(2)}, u32[]{:S(2)}) collective-permute-start(bf16[64,944]{1,0:T(8,128)(2,1)S(1)} %get-tuple-element.6.refs_0_), channel_id=1, source_target_pairs={{0,4},{4,8},{8,12},{12,14},{14,10},{10,6},{6,2},{2,0},{1,5},{5,9},... | collective-permute-start | bytes 362504 | tf_op jit(solution)/shard_map/ppermute | solution.py:39
  4.1 3.4 %collective-permute-done.refs_1_ = bf16[64,944]{1,0:T(8,128)(2,1)S(1)} collective-permute-done((bf16[64,944]{1,0:T(8,128)(2,1)S(1)}, bf16[64,944]{1,0:T(8,128)(2,1)S(1)}, u32[]{:S(2)}, u32[]{:S(2)}) %collective-permute-start) | collective-permute-done | bytes 120864 | tf_op jit(solution)/shard_map/ppermute | solution.py:39
  7.5 1.8 %collective-permute-start.2 = (bf16[64,944]{1,0:T(8,128)(2,1)S(1)}, bf16[64,944]{1,0:T(8,128)(2,1)S(1)}, u32[]{:S(2)}, u32[]{:S(2)}) collective-permute-start(bf16[64,944]{1,0:T(8,128)(2,1)S(1)} %collective-permute-done.refs_1_), channel_id=1, source_target_pairs={{0,4},{4,8},{8,12},{12,14},{14,10},{10,6},{6,2},{2,0},{1,5},{5,9},... | collective-permute-start | bytes 362504 | tf_op jit(solution)/shard_map/ppermute | solution.py:39
  9.3 0.2 collective-permute-start.3
  9.6 2.9 %collective-permute-done.2.refs_3_ = bf16[64,944]{1,0:T(8,128)(2,1)S(1)} collective-permute-done((bf16[64,944]{1,0:T(8,128)(2,1)S(1)}, bf16[64,944]{1,0:T(8,128)(2,1)S(1)}, u32[]{:S(2)}, u32[]{:S(2)}) %collective-permute-start.2) | collective-permute-done | bytes 120864 | tf_op jit(solution)/shard_map/ppermute | solution.py:39
  12.5 1.8 %collective-permute-start.4 = (bf16[64,944]{1,0:T(8,128)(2,1)S(1)}, bf16[64,944]{1,0:T(8,128)(2,1)S(1)}, u32[]{:S(2)}, u32[]{:S(2)}) collective-permute-start(bf16[64,944]{1,0:T(8,128)(2,1)S(1)} %collective-permute-done.2.refs_3_), channel_id=1, source_target_pairs={{0,4},{4,8},{8,12},{12,14},{14,10},{10,6},{6,2},{2,0},{1,5},{5,9},... | collective-permute-start | bytes 362504 | tf_op jit(solution)/shard_map/ppermute | solution.py:39
  14.3 0.3 collective-permute-start.5
  14.6 3.3 %collective-permute-done.4.refs_5_ = bf16[64,944]{1,0:T(8,128)(2,1)S(1)} collective-permute-done((bf16[64,944]{1,0:T(8,128)(2,1)S(1)}, bf16[64,944]{1,0:T(8,128)(2,1)S(1)}, u32[]{:S(2)}, u32[]{:S(2)}) %collective-permute-start.4) | collective-permute-done | bytes 120864 | tf_op jit(solution)/shard_map/ppermute | solution.py:39
  17.9 2.1 %collective-permute-start.6 = (bf16[64,944]{1,0:T(8,128)(2,1)S(1)}, bf16[64,944]{1,0:T(8,128)(2,1)S(1)}, u32[]{:S(2)}, u32[]{:S(2)}) collective-permute-start(bf16[64,944]{1,0:T(8,128)(2,1)S(1)} %collective-permute-done.4.refs_5_), channel_id=1, source_target_pairs={{0,4},{4,8},{8,12},{12,14},{14,10},{10,6},{6,2},{2,0},{1,5},{5,9},... | collective-permute-start | bytes 362504 | tf_op jit(solution)/shard_map/ppermute | solution.py:39
  20.0 2.9 %collective-permute-done.6.refs_7_ = bf16[64,944]{1,0:T(8,128)(2,1)S(1)} collective-permute-done((bf16[64,944]{1,0:T(8,128)(2,1)S(1)}, bf16[64,944]{1,0:T(8,128)(2,1)S(1)}, u32[]{:S(2)}, u32[]{:S(2)}) %collective-permute-start.6) | collective-permute-done | bytes 120864 | tf_op jit(solution)/shard_map/ppermute | solution.py:39
  23.0 0.1 collective-permute-start.8
  23.1 0.6 %collective-permute-start.7 = (bf16[3,64,944]{2,1,0:T(8,128)(2,1)S(1)}, bf16[3,64,944]{2,1,0:T(8,128)(2,1)S(1)}, u32[]{:S(2)}, u32[]{:S(2)}) collective-permute-start(bf16[3,64,944]{2,1,0:T(8,128)(2,1)S(1)} %pad_maximum_fusion), channel_id=1, source_target_pairs={{0,1},{4,5},{8,9},{12,13},{14,15},{10,11},{6,7},{2,3},{1,0},{5,4},... | collective-permute-start | bytes 1087496 | tf_op jit(solution)/shard_map/ppermute | solution.py:58
  23.7 2.0 %collective-permute-done.7.refs_8_ = bf16[3,64,944]{2,1,0:T(8,128)(2,1)S(1)} collective-permute-done((bf16[3,64,944]{2,1,0:T(8,128)(2,1)S(1)}, bf16[3,64,944]{2,1,0:T(8,128)(2,1)S(1)}, u32[]{:S(2)}, u32[]{:S(2)}) %collective-permute-start.7) | collective-permute-done | bytes 362528 | tf_op jit(solution)/shard_map/ppermute | solution.py:58
  25.8 0.7 %copy-done.9 = bf16[3,64,944]{2,1,0:T(8,128)(2,1)} copy-done((bf16[3,64,944]{2,1,0:T(8,128)(2,1)}, bf16[3,64,944]{2,1,0:T(8,128)(2,1)S(1)}, u32[]{:S(2)}) %copy-start.9) | copy-done | bytes 362520
  26.4 0.2 copy-done
  26.7 10.5 %shard_map.73 = bf16[16,49,128]{2,1,0:T(8,128)(2,1)} custom-call(s32[256]{0:T(256)} %constant.4.clone.table, bf16[64,944]{1,0:T(8,128)(2,1)} %copy-done.1, bf16[64,944]{1,0:T(8,128)(2,1)} %copy-done.7, bf16[64,944]{1,0:T(8,128)(2,1)} %copy-done.8, bf16[64,944]{1,0:T(8,128)(2,1)} %copy-done.2, bf16[64,944]{1,0:T(8,128)(2,1)} %copy-done.3, ...), custom_call_target="tpu_custom_call" | custom-call | tf_op jit(solution)/shard_map/pallas_call | solution.py:149
  37.1 6.4 %all-to-all-start = ((bf16[16,49,128]{2,1,0:T(8,128)(2,1)}), bf16[16,49,128]{2,1,0:T(8,128)(2,1)S(1)}, u32[]{:S(2)}, u32[]{:S(2)}) async-start(bf16[16,49,128]{2,1,0:T(8,128)(2,1)} %shard_map.73), calls=%async_computation | async-start | bytes 458752 | tf_op jit(solution)/shard_map/all_to_all | solution.py:165
  43.6 9.5 %all-to-all-done = bf16[16,49,128]{2,1,0:T(8,128)(2,1)S(1)} async-done(((bf16[16,49,128]{2,1,0:T(8,128)(2,1)}), bf16[16,49,128]{2,1,0:T(8,128)(2,1)S(1)}, u32[]{:S(2)}, u32[]{:S(2)}) %all-to-all-start) | async-done | bytes 200736 | tf_op jit(solution)/shard_map/all_to_all | solution.py:165
  53.1 0.1 copy.8
  53.3 0.1 eq.19
  53.4 0.1 compare_convert_fusion
  53.5 0.4 fusion
  54.0 0.8 %reshape.53 = f32[8,4096]{1,0:T(8,128)} reshape(f32[512,64]{1,0:T(8,128)S(1)} %fusion) | data formatting | bytes 262144 | tf_op jit(solution)/shard_map/reshape | solution.py:176
  (33 shorter events, 0.3 us)
Async XLA Ops:
  1.0 24.7 %copy-start.1 = (bf16[64,944]{1,0:T(8,128)(2,1)}, bf16[64,944]{1,0:T(8,128)(2,1)S(1)}, u32[]{:S(2)}) copy-start(bf16[64,944]{1,0:T(8,128)(2,1)S(1)} %get-tuple-element.6.refs_0_) | copy-start | bytes 362500
  1.0 6.5 %collective-permute-start = (bf16[64,944]{1,0:T(8,128)(2,1)S(1)}, bf16[64,944]{1,0:T(8,128)(2,1)S(1)}, u32[]{:S(2)}, u32[]{:S(2)}) collective-permute-start(bf16[64,944]{1,0:T(8,128)(2,1)S(1)} %get-tuple-element.6.refs_0_), channel_id=1, source_target_pairs={{0,4},{4,8},{8,12},{12,14},{14,10},{10,6},{6,2},{2,0},{1,5},{5,9},... | collective-permute-start | bytes 362504 | tf_op jit(solution)/shard_map/ppermute | solution.py:39
  4.1 5.2 %collective-permute-start.1 = (bf16[64,944]{1,0:T(8,128)(2,1)S(1)}, bf16[64,944]{1,0:T(8,128)(2,1)S(1)}, u32[]{:S(2)}, u32[]{:S(2)}) collective-permute-start(bf16[64,944]{1,0:T(8,128)(2,1)S(1)} %get-tuple-element.6.refs_0_), channel_id=1, source_target_pairs={{0,2},{4,0},{8,4},{12,8},{14,12},{10,14},{6,10},{2,6},{1,3},{5,1},... | collective-permute-start | bytes 362504 | tf_op jit(solution)/shard_map/ppermute | solution.py:43
  7.5 18.2 %copy-start.7 = (bf16[64,944]{1,0:T(8,128)(2,1)}, bf16[64,944]{1,0:T(8,128)(2,1)S(1)}, u32[]{:S(2)}) copy-start(bf16[64,944]{1,0:T(8,128)(2,1)S(1)} %collective-permute-done.refs_1_) | copy-start | bytes 362500
  7.5 5.0 %collective-permute-start.2 = (bf16[64,944]{1,0:T(8,128)(2,1)S(1)}, bf16[64,944]{1,0:T(8,128)(2,1)S(1)}, u32[]{:S(2)}, u32[]{:S(2)}) collective-permute-start(bf16[64,944]{1,0:T(8,128)(2,1)S(1)} %collective-permute-done.refs_1_), channel_id=1, source_target_pairs={{0,4},{4,8},{8,12},{12,14},{14,10},{10,6},{6,2},{2,0},{1,5},{5,9},... | collective-permute-start | bytes 362504 | tf_op jit(solution)/shard_map/ppermute | solution.py:39
  9.3 16.4 %copy-start.8 = (bf16[64,944]{1,0:T(8,128)(2,1)}, bf16[64,944]{1,0:T(8,128)(2,1)S(1)}, u32[]{:S(2)}) copy-start(bf16[64,944]{1,0:T(8,128)(2,1)S(1)} %collective-permute-done.1.refs_2_) | copy-start | bytes 362500
  9.3 5.0 %collective-permute-start.3 = (bf16[64,944]{1,0:T(8,128)(2,1)S(1)}, bf16[64,944]{1,0:T(8,128)(2,1)S(1)}, u32[]{:S(2)}, u32[]{:S(2)}) collective-permute-start(bf16[64,944]{1,0:T(8,128)(2,1)S(1)} %collective-permute-done.1.refs_2_), channel_id=1, source_target_pairs={{0,2},{4,0},{8,4},{12,8},{14,12},{10,14},{6,10},{2,6},{1,3},{5,1},... | collective-permute-start | bytes 362504 | tf_op jit(solution)/shard_map/ppermute | solution.py:43
  12.5 13.2 %copy-start.2 = (bf16[64,944]{1,0:T(8,128)(2,1)}, bf16[64,944]{1,0:T(8,128)(2,1)S(1)}, u32[]{:S(2)}) copy-start(bf16[64,944]{1,0:T(8,128)(2,1)S(1)} %collective-permute-done.2.refs_3_) | copy-start | bytes 362500
  12.5 5.4 %collective-permute-start.4 = (bf16[64,944]{1,0:T(8,128)(2,1)S(1)}, bf16[64,944]{1,0:T(8,128)(2,1)S(1)}, u32[]{:S(2)}, u32[]{:S(2)}) collective-permute-start(bf16[64,944]{1,0:T(8,128)(2,1)S(1)} %collective-permute-done.2.refs_3_), channel_id=1, source_target_pairs={{0,4},{4,8},{8,12},{12,14},{14,10},{10,6},{6,2},{2,0},{1,5},{5,9},... | collective-permute-start | bytes 362504 | tf_op jit(solution)/shard_map/ppermute | solution.py:39
  14.3 11.4 %copy-start.3 = (bf16[64,944]{1,0:T(8,128)(2,1)}, bf16[64,944]{1,0:T(8,128)(2,1)S(1)}, u32[]{:S(2)}) copy-start(bf16[64,944]{1,0:T(8,128)(2,1)S(1)} %collective-permute-done.3.refs_4_) | copy-start | bytes 362500
  14.3 5.7 %collective-permute-start.5 = (bf16[64,944]{1,0:T(8,128)(2,1)S(1)}, bf16[64,944]{1,0:T(8,128)(2,1)S(1)}, u32[]{:S(2)}, u32[]{:S(2)}) collective-permute-start(bf16[64,944]{1,0:T(8,128)(2,1)S(1)} %collective-permute-done.3.refs_4_), channel_id=1, source_target_pairs={{0,2},{4,0},{8,4},{12,8},{14,12},{10,14},{6,10},{2,6},{1,3},{5,1},... | collective-permute-start | bytes 362504 | tf_op jit(solution)/shard_map/ppermute | solution.py:43
  17.9 7.8 %copy-start.4 = (bf16[64,944]{1,0:T(8,128)(2,1)}, bf16[64,944]{1,0:T(8,128)(2,1)S(1)}, u32[]{:S(2)}) copy-start(bf16[64,944]{1,0:T(8,128)(2,1)S(1)} %collective-permute-done.4.refs_5_) | copy-start | bytes 362500
  17.9 5.0 %collective-permute-start.6 = (bf16[64,944]{1,0:T(8,128)(2,1)S(1)}, bf16[64,944]{1,0:T(8,128)(2,1)S(1)}, u32[]{:S(2)}, u32[]{:S(2)}) collective-permute-start(bf16[64,944]{1,0:T(8,128)(2,1)S(1)} %collective-permute-done.4.refs_5_), channel_id=1, source_target_pairs={{0,4},{4,8},{8,12},{12,14},{14,10},{10,6},{6,2},{2,0},{1,5},{5,9},... | collective-permute-start | bytes 362504 | tf_op jit(solution)/shard_map/ppermute | solution.py:39
  20.0 5.7 %copy-start.5 = (bf16[64,944]{1,0:T(8,128)(2,1)}, bf16[64,944]{1,0:T(8,128)(2,1)S(1)}, u32[]{:S(2)}) copy-start(bf16[64,944]{1,0:T(8,128)(2,1)S(1)} %collective-permute-done.5.refs_6_) | copy-start | bytes 362500
  22.9 2.8 %copy-start.6 = (bf16[64,944]{1,0:T(8,128)(2,1)}, bf16[64,944]{1,0:T(8,128)(2,1)S(1)}, u32[]{:S(2)}) copy-start(bf16[64,944]{1,0:T(8,128)(2,1)S(1)} %collective-permute-done.6.refs_7_) | copy-start | bytes 362500
  23.0 2.7 %collective-permute-start.8 = (bf16[5,64,944]{2,1,0:T(8,128)(2,1)S(1)}, bf16[5,64,944]{2,1,0:T(8,128)(2,1)S(1)}, u32[]{:S(2)}, u32[]{:S(2)}) collective-permute-start(bf16[5,64,944]{2,1,0:T(8,128)(2,1)S(1)} %bitcast_dynamic-update-slice_fusion), channel_id=1, source_target_pairs={{0,1},{4,5},{8,9},{12,13},{14,15},{10,11},{6,7},{2,3},{1,0},{5,4},... | collective-permute-start | bytes 1812488 | tf_op jit(solution)/shard_map/ppermute | solution.py:58
  23.1 2.6 %collective-permute-start.7 = (bf16[3,64,944]{2,1,0:T(8,128)(2,1)S(1)}, bf16[3,64,944]{2,1,0:T(8,128)(2,1)S(1)}, u32[]{:S(2)}, u32[]{:S(2)}) collective-permute-start(bf16[3,64,944]{2,1,0:T(8,128)(2,1)S(1)} %pad_maximum_fusion), channel_id=1, source_target_pairs={{0,1},{4,5},{8,9},{12,13},{14,15},{10,11},{6,7},{2,3},{1,0},{5,4},... | collective-permute-start | bytes 1087496 | tf_op jit(solution)/shard_map/ppermute | solution.py:58
  25.7 0.8 %copy-start.9 = (bf16[3,64,944]{2,1,0:T(8,128)(2,1)}, bf16[3,64,944]{2,1,0:T(8,128)(2,1)S(1)}, u32[]{:S(2)}) copy-start(bf16[3,64,944]{2,1,0:T(8,128)(2,1)S(1)} %collective-permute-done.7.refs_8_) | copy-start | bytes 1087492
  25.7 1.0 %copy-start = (bf16[5,64,944]{2,1,0:T(8,128)(2,1)}, bf16[5,64,944]{2,1,0:T(8,128)(2,1)S(1)}, u32[]{:S(2)}) copy-start(bf16[5,64,944]{2,1,0:T(8,128)(2,1)S(1)} %collective-permute-done.8.refs_9_) | copy-start | bytes 1812484
  37.1 16.0 %all-to-all-start = ((bf16[16,49,128]{2,1,0:T(8,128)(2,1)}), bf16[16,49,128]{2,1,0:T(8,128)(2,1)S(1)}, u32[]{:S(2)}, u32[]{:S(2)}) async-start(bf16[16,49,128]{2,1,0:T(8,128)(2,1)} %shard_map.73), calls=%async_computation | async-start | bytes 458752 | tf_op jit(solution)/shard_map/all_to_all | solution.py:165
